TPU v7x, 32 devices: a whole 2x2x4 slice. The times are simulated.
32 devices in a mesh: groups: 2 (over x), seq: 4 (over y, core), sp: 4 (over z).
Axes of the slice: x: 2, y: 2, z: 4, core: 2. Of those that a mesh axis runs over, the one named last changes fastest.
Arguments:
- queries: bfloat16 [4096, 5120], P(('groups', 'seq', 'sp')), parts along dimension 0, may hold values from -19 to 19
- new_keys: bfloat16 [4096, 5120], P(('groups', 'seq'), 'sp'), parts along dimension 0, may hold values from -6 to 6
- new_values: bfloat16 [4096, 5120], P(('groups', 'seq'), 'sp'), parts along dimension 0, may hold values from -6 to 6
- cache_keys: bfloat16 [4096, 5120], P(('groups', 'seq'), 'sp'), parts along dimension 0, may hold values from -6 to 6
- cache_values: bfloat16 [4096, 5120], P(('groups', 'seq'), 'sp'), parts along dimension 0, may hold values from -6 to 6
- sources: int32 [8, 6], P(('groups', 'seq')), parts along dimension 0, may hold values from -1 to 7, as said below
Outputs:
- attended: bfloat16 [4096, 5120], P(('groups', 'seq', 'sp')), parts along dimension 0
There are 2 independent parts, one for each index of `groups`. A program takes and returns all parts, laid end to end along the dimension named above; each array names one. Nothing has to cross between parts.
Inputs may be any that keep to these rules, and one draw needn't show every extreme that they name: `sources`: row q lists the 2 blocks of frame 0, then for each of 2 frames ending with the query block's own frame (frame (q + 4) // 2) its 2 blocks, or -1 for each of them where the frame lies outside the row's window or is frame 0. A window is 1 to 2 frames and always holds the own frame; all blocks of one frame share a window; entries other than -1 in a row are distinct.
All inputs are finite; a program needn't handle non-finite values.
Results may differ from a plain program's by a relative error of at most 0.006.
Values may be sent and summed in bfloat16 or wider, within the bound.
No kernel may reach another device: no remote copies, remote signals or barrier semaphores. Data moves between devices by JAX's collectives and lax.ppermute only.
A program may use at most 320 MiB of HBM per device.

v0:
```python
import math

import jax
import jax.numpy as jnp
from jax import lax
from jax.sharding import PartitionSpec as P

HEAD_DIM = 128
FB = 2
WMAX = 2


def shifted(x, axis, by):
    length = lax.axis_size(axis)
    return lax.ppermute(x, axis, [(i, (i + by) % length) for i in range(length)])


def local(queries, new_keys, new_values, cache_keys, cache_values, sources):
    head_width = cache_keys.shape[1]
    gathered = lax.all_gather(queries, "sp", axis=0, tiled=True)
    offset = lax.axis_index("sp") * head_width
    query_part = lax.dynamic_slice_in_dim(gathered, offset, head_width, 1)
    block_rows = query_part.shape[0]
    nheads = head_width // HEAD_DIM
    query_heads = query_part.reshape(block_rows, nheads, HEAD_DIM)
    seq_count = lax.axis_size("seq")
    seq_place = lax.axis_index("seq")
    listed = sources[0]
    score_scale = 1.0 / math.sqrt(HEAD_DIM)
    own_block = seq_count + seq_place

    def attend(running, key_rows, value_rows, block_ids):
        count_rows = key_rows.shape[0]
        allowed = jnp.any(listed[None, :] == block_ids[:, None], axis=1)
        key_heads = key_rows.reshape(count_rows, nheads, HEAD_DIM)
        value_heads = value_rows.reshape(count_rows, nheads, HEAD_DIM)
        scores = (
            jnp.einsum("qhd,khd->hqk", query_heads, key_heads, preferred_element_type=jnp.float32)
            * score_scale
        )
        scores = jnp.where(allowed[None, None, :], scores, -1e30)
        top_old, total_old, summed_old = running
        top_new = jnp.maximum(top_old, jnp.max(scores, axis=-1))
        weights = jnp.where(allowed[None, None, :], jnp.exp(scores - top_new[:, :, None]), 0.0)
        fading = jnp.exp(top_old - top_new)
        total_new = total_old * fading + jnp.sum(weights, axis=-1)
        product = jnp.einsum(
            "hqk,khd->hqd",
            weights.astype(jnp.bfloat16),
            value_heads,
            preferred_element_type=jnp.float32,
        )
        return (top_new, total_new, summed_old * fading[:, :, None] + product)

    running = (
        jnp.full((nheads, block_rows), -1e30, jnp.float32),
        jnp.zeros((nheads, block_rows), jnp.float32),
        jnp.zeros((nheads, block_rows, HEAD_DIM), jnp.float32),
    )
    running = attend(running, new_keys, new_values, jnp.full((block_rows,), own_block, jnp.int32))
    pieces = (
        lax.all_gather(cache_keys, "seq", axis=0, tiled=True),
        lax.all_gather(cache_values, "seq", axis=0, tiled=True),
    )
    count_rows = pieces[0].shape[0]
    fold_block_ids = jnp.arange(count_rows, dtype=jnp.int32) // block_rows
    running = attend(running, pieces[0], pieces[1], fold_block_ids)
    window_running = running
    for distance in range(1 - FB, WMAX * FB):
        if distance == 0:
            continue
        send_keys, send_values = (new_keys, new_values)
        got_keys, got_values = shifted((send_keys, send_values), "seq", distance)
        source_block = own_block - distance
        usable = (source_block >= seq_count) & (source_block < 2 * seq_count)
        block_ids = jnp.full((block_rows,), jnp.where(usable, source_block, -2), jnp.int32)
        window_running = attend(window_running, got_keys, got_values, block_ids)
    running = window_running
    top_final, total_final, summed_final = running
    heads_out = summed_final / total_final[:, :, None]
    heads_out = (
        jnp.transpose(heads_out, (1, 0, 2)).reshape(block_rows, head_width).astype(jnp.bfloat16)
    )
    return lax.all_to_all(heads_out, "sp", split_axis=0, concat_axis=1, tiled=True)


def solution(mesh):
    return jax.shard_map(
        local,
        mesh=mesh,
        in_specs=(
            P(("groups", "seq", "sp"), None),
            P(("groups", "seq"), "sp"),
            P(("groups", "seq"), "sp"),
            P(("groups", "seq"), "sp"),
            P(("groups", "seq"), "sp"),
            P(("groups", "seq"), None),
        ),
        out_specs=P(("groups", "seq", "sp"), None),
        check_vma=False,
    )
```

profile of v0, /device:TPU:0, one launch (start us, length us, event | category | flops | bytes accessed | tf_op | source)
XLA Modules:
  0.0 351.2 jit_solution(14756906117489997197)
XLA Ops:
  6.5 2.5 copy.117
  9.2 2.4 copy.124
  11.7 1.6 copy.118
  13.3 3.0 collective-permute-start.4
  16.3 0.5 collective-permute-start.2
  16.8 1.5 copy.121
  18.3 1.2 collective-permute-start.1
  19.5 2.6 copy.127
  22.2 0.7 compare_reduce_fusion.1
  23.0 86.6 %all-gather.4.cloned.1.call-done = bf16[512,5120]{0,1:T(8,128)(2,1)} async-done(((bf16[128,5120]{0,1:T(8,128)(2,1)}), bf16[512,5120]{0,1:T(8,128)(2,1)}) %all-gather.4.cloned.1.call-update) | async-done | bytes 5242896 | tf_op jit(solution)/shard_map/all_gather | solution.py:20
  109.7 1.4 constant_dynamic-slice_fusion
  111.1 6.8 %fusion.6 = (f32[10,512]{1,0:T(8,128)S(1)}, f32[10,512,512]{1,2,0:T(8,128)}) fusion(pred[]{:T(512)} %get-tuple-element.10, bf16[512,10,128]{0,2,1:T(8,128)(2,1)S(1)} %bitcast.166, bf16[512,10,128]{0,2,1:T(8,128)(2,1)S(1)} %bitcast.172), kind=kOutput, calls=%fused_computation.17 | convolution fusion | flops 678947840 | bytes 13127681 | tf_op jit(solution)/shard_map/qhd,khd->hqk/dot_general | solution.py:38
  117.9 1.3 collective-permute-start.5
  119.2 7.5 %fusion.8 = (f32[10,512]{1,0:T(8,128)S(1)}, f32[10,512,512]{1,2,0:T(8,128)}) fusion(pred[]{:T(512)} %get-tuple-element.13, bf16[512,10,128]{0,2,1:T(8,128)(2,1)S(1)} %bitcast.167, bf16[512,10,128]{0,2,1:T(8,128)(2,1)} %bitcast.18), kind=kOutput, calls=%fused_computation.19 | convolution fusion | flops 678947840 | bytes 13127681 | tf_op jit(solution)/shard_map/qhd,khd->hqk/dot_general | solution.py:38
  126.7 7.5 %fusion.7 = (f32[10,512]{1,0:T(8,128)S(1)}, f32[10,512,512]{1,2,0:T(8,128)}) fusion(pred[]{:T(512)} %get-tuple-element.12, bf16[512,10,128]{0,2,1:T(8,128)(2,1)S(1)} %bitcast.168, bf16[512,10,128]{0,2,1:T(8,128)(2,1)} %bitcast.14), kind=kOutput, calls=%fused_computation.18 | convolution fusion | flops 678947840 | bytes 13127681 | tf_op jit(solution)/shard_map/qhd,khd->hqk/dot_general | solution.py:38
  134.2 7.7 %select_reduce_fusion = (f32[10,512]{1,0:T(8,128)S(1)}, f32[10,512]{1,0:T(8,128)S(1)}, f32[10,512,512]{1,2,0:T(8,128)}) fusion(pred[]{:T(512)} %get-tuple-element.9, pred[]{:T(512)} %get-tuple-element.11, bf16[512,10,128]{0,2,1:T(8,128)(2,1)S(1)} %bitcast.169, bf16[512,10,128]{0,2,1:T(8,128)(2,1)} %bitcast.10), kind=kOutput, calls=%fused_computation.15 | convolution fusion | flops 684185600 | bytes 13148162 | tf_op jit(solution)/shard_map/qhd,khd->hqk/dot_general | solution.py:38
  141.8 35.8 %all-gather.6.cloned.1.call-done = bf16[2048,1280]{0,1:T(8,128)(2,1)} async-done(((bf16[512,1280]{0,1:T(8,128)(2,1)}), bf16[2048,1280]{0,1:T(8,128)(2,1)}) %all-gather.6.cloned.1.call-update) | async-done | bytes 5242896 | tf_op jit(solution)/shard_map/all_gather | solution.py:62
  177.6 20.9 %fusion = (f32[10,512]{1,0:T(8,128)S(1)}, f32[10,512,2048]{2,1,0:T(8,128)}) fusion(pred[2048]{0:T(1024)(128)(4,1)S(1)} %compare_reduce_fusion, bf16[512,10,128]{0,2,1:T(8,128)(2,1)S(1)} %bitcast.170, bf16[2048,10,128]{0,2,1:T(8,128)(2,1)} %bitcast.171), kind=kOutput, calls=%fused_computation.2 | convolution fusion | flops 2715806720 | bytes 48519168 | tf_op jit(solution)/shard_map/qhd,khd->hqk/dot_general | solution.py:38
  198.5 18.6 %fusion.1 = f32[10,512]{1,0:T(8,128)S(1)} fusion(f32[10,512,2048]{2,1,0:T(8,128)} %get-tuple-element.34, f32[10,512]{1,0:T(8,128)S(1)} %get-tuple-element.23, pred[2048]{0:T(1024)(128)(4,1)S(1)} %compare_reduce_fusion), kind=kLoop, calls=%fused_computation.3 | loop fusion | flops 52423680 | bytes 41986048 | tf_op jit(solution)/shard_map/reduce_sum | solution.py:46
  217.1 1.0 all-gather.8.cloned.1.call-done
  218.1 19.1 %fusion.3 = f32[10,512,128]{2,1,0:T(8,128)} fusion(bf16[2048,10,128]{0,2,1:T(8,128)(2,1)} %bitcast.175, f32[10,512,2048]{2,1,0:T(8,128)} %get-tuple-element.34, f32[10,512]{1,0:T(8,128)S(1)} %get-tuple-element.23, pred[2048]{0:T(1024)(128)(4,1)S(1)} %compare_reduce_fusion), kind=kOutput, calls=%fused_computation.5 | convolution fusion | flops 2736783360 | bytes 49829888 | tf_op jit(solution)/shard_map/hqk,khd->hqd/dot_general | solution.py:47
  237.2 14.6 %fusion.11 = (f32[10,512]{1,0:T(8,128)S(1)}, f32[10,512]{1,0:T(8,128)S(1)}, f32[10,512]{1,0:T(8,128)S(1)}) fusion(f32[10,512,512]{1,2,0:T(8,128)} %get-tuple-element.28, f32[10,512]{1,0:T(8,128)S(1)} %get-tuple-element.22, pred[]{:T(512)} %get-tuple-element.11, f32[10,512]{1,0:T(8,128)S(1)} %get-tuple-element.19, pred[]{:T(512)} %get-tuple-element.9, ...), kind=kLoop, calls=%fused_computation.22 | loop fusion | flops 36684800 | bytes 21094404 | tf_op jit(solution)/shard_map/reduce_sum | solution.py:46
  251.8 10.9 %fusion.13 = (f32[10,512]{1,0:T(8,128)S(1)}, f32[10,512]{1,0:T(8,128)S(1)}) fusion(f32[10,512,512]{1,2,0:T(8,128)} %get-tuple-element.32, f32[10,512]{1,0:T(8,128)S(1)} %get-tuple-element.21, pred[]{:T(512)} %get-tuple-element.12, f32[10,512]{1,0:T(8,128)S(1)} %get-tuple-element.20, f32[10,512,512]{1,2,0:T(8,128)} %get-tuple-element.30, pred[]{:T(512)} %get-tuple-element.13), kind=kLoop, calls=%fused_computation.24 | loop fusion | flops 26204160 | bytes 21053442 | tf_op jit(solution)/shard_map/reduce_sum | solution.py:46
  262.8 5.4 %fusion.27 = f32[10,512,128]{2,1,0:T(8,128)S(1)} fusion(bf16[512,10,128]{0,2,1:T(8,128)(2,1)} %bitcast.4, f32[10,512,512]{1,2,0:T(8,128)S(1)} %bitcast.165, f32[10,512]{1,0:T(8,128)S(1)} %get-tuple-element.27, pred[]{:T(512)} %get-tuple-element.10), kind=kOutput, calls=%fused_computation.34 | convolution fusion | flops 684195840 | bytes 14438401 | tf_op jit(solution)/shard_map/hqk,khd->hqd/dot_general | solution.py:47
  268.2 9.9 %fusion.25 = f32[10,512,128]{2,1,0:T(8,128)} fusion(bf16[512,10,128]{0,2,1:T(8,128)(2,1)} %bitcast.12, f32[10,512,512]{1,2,0:T(8,128)} %get-tuple-element.28, f32[10,512]{1,0:T(8,128)S(1)} %get-tuple-element.22, pred[]{:T(512)} %get-tuple-element.11), kind=kOutput, calls=%fused_computation.33 | convolution fusion | flops 684195840 | bytes 14438401 | tf_op jit(solution)/shard_map/hqk,khd->hqd/dot_general | solution.py:47
  278.2 9.4 %fusion.23 = f32[10,512,128]{2,1,0:T(8,128)} fusion(bf16[512,10,128]{0,2,1:T(8,128)(2,1)} %bitcast.16, f32[10,512,512]{1,2,0:T(8,128)} %get-tuple-element.32, f32[10,512]{1,0:T(8,128)S(1)} %get-tuple-element.21, pred[]{:T(512)} %get-tuple-element.12), kind=kOutput, calls=%fused_computation.32 | convolution fusion | flops 684195840 | bytes 14438401 | tf_op jit(solution)/shard_map/hqk,khd->hqd/dot_general | solution.py:47
  287.6 6.3 %fusion.21 = f32[10,512,128]{2,1,0:T(8,128)} fusion(bf16[512,10,128]{0,2,1:T(8,128)(2,1)} %bitcast.20, f32[10,512,512]{1,2,0:T(8,128)S(1)} %bitcast.163, f32[10,512]{1,0:T(8,128)S(1)} %get-tuple-element.20, pred[]{:T(512)} %get-tuple-element.13), kind=kOutput, calls=%fused_computation.31 | convolution fusion | flops 684195840 | bytes 14438401 | tf_op jit(solution)/shard_map/hqk,khd->hqd/dot_general | solution.py:47
  294.0 11.9 %fusion.35 = bf16[512,10,128]{2,0,1:T(8,128)(2,1)S(1)} fusion(f32[10,512,128]{2,1,0:T(8,128)} %fusion.21, f32[10,512,128]{2,1,0:T(8,128)} %fusion.23, f32[10,512,128]{2,1,0:T(8,128)} %fusion.25, f32[10,512,128]{2,1,0:T(8,128)} %fusion.3, f32[10,512,128]{2,1,0:T(8,128)S(1)} %fusion.27, bf16[512,10,128]{0,2,1:T(8,128)(2,1)} %bitcast.12, ...), kind=kOutput, calls=%fused_computation.42 | convolution fusion | flops 692715520 | bytes 26378240 | tf_op jit(solution)/shard_map/hqk,khd->hqd/dot_general | solution.py:47
  305.9 0.6 copy.149
  306.5 0.3 convert_element_type.32
  307.1 36.2 %all_to_all.16 = bf16[4,128,1280]{1,2,0:T(8,128)(2,1)S(1)} all-to-all(bf16[4,128,1280]{1,2,0:T(8,128)(2,1)S(1)} %copy.150), channel_id=1, replica_groups=mesh['groups'=2,'seq'=4,'sp'=4] {'sp'}, dimensions={0} | all-to-all | bytes 2621440 | tf_op jit(solution)/shard_map/all_to_all | solution.py:84
  343.2 1.4 copy.151
  (38 shorter events, 0.6 us)
Async XLA Ops:
  6.5 10.3 %copy-start = (bf16[512,1280]{1,0:T(8,128)(2,1)S(1)}, bf16[512,1280]{1,0:T(8,128)(2,1)}, u32[]{:S(2)}) copy-start(bf16[512,1280]{1,0:T(8,128)(2,1)} %param.8) | copy-start | bytes 3932164
  6.5 15.6 %copy-start.1 = (s32[1,6]{1,0:T(1,128)S(1)}, s32[1,6]{1,0:T(1,128)}, u32[]{:S(2)}) copy-start(s32[1,6]{1,0:T(1,128)} %param.11) | copy-start | bytes 76
  6.5 103.1 %all-gather.4.cloned.1.call-start = ((), (), s32[]{:S(2)}) async-start(), calls=%async_computation.1 | async-start | bytes 6553600 | tf_op jit(solution)/shard_map/all_gather | solution.py:20
  9.1 168.5 %all-gather.6.cloned.1.call-start = ((), (), s32[]{:S(2)}) async-start(), calls=%async_computation.2 | async-start | bytes 6553600 | tf_op jit(solution)/shard_map/all_gather | solution.py:62
  11.6 206.5 %all-gather.8.cloned.1.call-start = ((), (), s32[]{:S(2)}) async-start(), calls=%async_computation.3 | async-start | bytes 6553600 | tf_op jit(solution)/shard_map/all_gather | solution.py:63
  13.3 104.6 %collective-permute-start.4 = (bf16[512,1280]{0,1:T(8,128)(2,1)S(1)}, bf16[512,1280]{0,1:T(8,128)(2,1)}, u32[]{:S(2)}, u32[]{:S(2)}) collective-permute-start(bf16[512,1280]{0,1:T(8,128)(2,1)S(1)} %copy.118), channel_id=1, source_target_pairs={{0,8},{4,12},{8,0},{12,4},{1,9},{5,13},{9,1},{13,5},{2,10},{6,14},... | collective-permute-start | bytes 3932168 | tf_op jit(solution)/shard_map/ppermute | solution.py:15
  16.3 117.9 %collective-permute-start = (bf16[512,1280]{0,1:T(8,128)(2,1)S(1)}, bf16[512,1280]{0,1:T(8,128)(2,1)}, u32[]{:S(2)}, u32[]{:S(2)}) collective-permute-start(bf16[512,1280]{0,1:T(8,128)(2,1)S(1)} %copy.118), channel_id=1, source_target_pairs={{0,12},{4,0},{8,4},{12,8},{1,13},{5,1},{9,5},{13,9},{2,14},{6,2},{... | collective-permute-start | bytes 3932168 | tf_op jit(solution)/shard_map/ppermute | solution.py:15
  16.3 110.3 %collective-permute-start.2 = (bf16[512,1280]{0,1:T(8,128)(2,1)S(1)}, bf16[512,1280]{0,1:T(8,128)(2,1)}, u32[]{:S(2)}, u32[]{:S(2)}) collective-permute-start(bf16[512,1280]{0,1:T(8,128)(2,1)S(1)} %copy.118), channel_id=1, source_target_pairs={{0,4},{4,8},{8,12},{12,0},{1,5},{5,9},{9,13},{13,1},{2,6},{6,10},{... | collective-permute-start | bytes 3932168 | tf_op jit(solution)/shard_map/ppermute | solution.py:15
  18.3 249.9 %collective-permute-start.1 = (bf16[512,1280]{0,1:T(8,128)(2,1)}, bf16[512,1280]{0,1:T(8,128)(2,1)}, u32[]{:S(2)}, u32[]{:S(2)}) collective-permute-start(bf16[512,1280]{0,1:T(8,128)(2,1)} %copy.121), channel_id=1, source_target_pairs={{0,12},{4,0},{8,4},{12,8},{1,13},{5,1},{9,5},{13,9},{2,14},{6,2},{... | collective-permute-start | bytes 3932168 | tf_op jit(solution)/shard_map/ppermute | solution.py:15
  19.5 258.6 %collective-permute-start.3 = (bf16[512,1280]{0,1:T(8,128)(2,1)}, bf16[512,1280]{0,1:T(8,128)(2,1)}, u32[]{:S(2)}, u32[]{:S(2)}) collective-permute-start(bf16[512,1280]{0,1:T(8,128)(2,1)} %copy.121), channel_id=1, source_target_pairs={{0,4},{4,8},{8,12},{12,0},{1,5},{5,9},{9,13},{13,1},{2,6},{6,10},{... | collective-permute-start | bytes 3932168 | tf_op jit(solution)/shard_map/ppermute | solution.py:15
  117.9 169.7 %collective-permute-start.5 = (bf16[512,1280]{0,1:T(8,128)(2,1)}, bf16[512,1280]{0,1:T(8,128)(2,1)}, u32[]{:S(2)}, u32[]{:S(2)}) collective-permute-start(bf16[512,1280]{0,1:T(8,128)(2,1)} %copy.121), channel_id=1, source_target_pairs={{0,8},{4,12},{8,0},{12,4},{1,9},{5,13},{9,1},{13,5},{2,10},{6,14},... | collective-permute-start | bytes 3932168 | tf_op jit(solution)/shard_map/ppermute | solution.py:15
  237.2 25.5 %slice-start.3 = ((s8[10485760]{0:T(1024)(128)(4,1)}), s8[4194304]{0:T(1024)(128)(4,1)S(1)}, s32[]{:S(2)}) async-start(s8[10485760]{0:T(1024)(128)(4,1)} %bitcast.164), calls=%async_computation.7 | async-start | bytes 8388608
  237.2 25.5 %slice-start.4 = ((s8[10485760]{0:T(1024)(128)(4,1)}), s8[4194304]{0:T(1024)(128)(4,1)S(1)}, s32[]{:S(2)}) async-start(s8[10485760]{0:T(1024)(128)(4,1)} %bitcast.164), calls=%async_computation.8 | async-start | bytes 8388608
  251.8 10.9 %slice-start.5 = ((s8[10485760]{0:T(1024)(128)(4,1)}), s8[2097152]{0:T(1024)(128)(4,1)S(1)}, s32[]{:S(2)}) async-start(s8[10485760]{0:T(1024)(128)(4,1)} %bitcast.164), calls=%async_computation.9 | async-start | bytes 4194304
  268.2 19.4 %slice-start = ((s8[10485760]{0:T(1024)(128)(4,1)}), s8[4194304]{0:T(1024)(128)(4,1)S(1)}, s32[]{:S(2)}) async-start(s8[10485760]{0:T(1024)(128)(4,1)} %bitcast.162), calls=%async_computation.4 | async-start | bytes 8388608
  268.2 19.4 %slice-start.1 = ((s8[10485760]{0:T(1024)(128)(4,1)}), s8[4194304]{0:T(1024)(128)(4,1)S(1)}, s32[]{:S(2)}) async-start(s8[10485760]{0:T(1024)(128)(4,1)} %bitcast.162), calls=%async_computation.5 | async-start | bytes 8388608
  278.2 9.5 %slice-start.2 = ((s8[10485760]{0:T(1024)(128)(4,1)}), s8[2097152]{0:T(1024)(128)(4,1)S(1)}, s32[]{:S(2)}) async-start(s8[10485760]{0:T(1024)(128)(4,1)} %bitcast.162), calls=%async_computation.6 | async-start | bytes 4194304
Sparse Core Ops, SparseCore 0:
  9.2 100.3 all-gather.3
  111.2 66.3 all-gather.5
  179.2 38.8 all-gather.7
where the time goes:
time: 352 us; the launch traced here: 351 us
  waiting for transfers between devices  123 us (35%)
  matrix products  112 us (32%)
  other arithmetic  45 us (13%)
  blocking collectives  36.2 us (10%)
  local copies, waits for them, and re-layouts  14.6 us (4%)
  between operations  13.3 us (4%)
  starting transfers between devices  6.19 us (2%)
    all_gather x1, waiting for transfers between devices, local(): gathered = lax.all_gather(queries, 'sp', axis=0, tiled=True)  86.6 us
    dot_general x6, matrix products, attend(): jnp.einsum('hqk,khd->hqd', weights.astype(jnp.bfloat16), value_heads, pre...  62.1 us
    dot_general x5, matrix products, attend(): jnp.einsum('qhd,khd->hqk', query_heads, key_heads, preferred_element_type...  50.3 us
    reduce_sum x3, other arithmetic, attend(): total_new = total_old * fading + jnp.sum(weights, axis=-1)  44.1 us
    all_to_all x1, blocking collectives, local(): lax.all_to_all(heads_out, 'sp', split_axis=0, concat_axis=1, tiled=True)  36.2 us
    all_gather x1, waiting for transfers between devices, local(): lax.all_gather(cache_keys, 'seq', axis=0, tiled=True)  35.8 us
    unnamed x21, local copies, waits for them, and re-layouts  10.7 us
  transfers between devices with their start and end apart: 9, of which 3 were waited for; matrix products, arithmetic and copies ran while one was open for 42% of the time, Pallas kernels for 0%

commit v1 on v0

v1 whole, which is shorter than its diff:
```python
import math

import jax
import jax.numpy as jnp
from jax import lax
from jax.experimental import pallas as pl
from jax.experimental.pallas import tpu as pltpu
from jax.sharding import PartitionSpec as P

HEAD_DIM = 128
NSRC = 6
ROW_SPLIT = 2


def attention_kernel(flags_ref, q_ref, *refs):
    key_refs = refs[:NSRC]
    value_refs = refs[NSRC : 2 * NSRC]
    out_ref = refs[2 * NSRC]
    score_ref = refs[2 * NSRC + 1]
    score_scale = 1.0 / math.sqrt(HEAD_DIM)
    query = q_ref[...]
    top = None
    for j in range(NSRC):
        scores = lax.dot_general(
            query, key_refs[j][...], (((1,), (1,)), ((), ())), preferred_element_type=jnp.float32
        ) * score_scale
        scores = jnp.where(flags_ref[j] > 0, scores, -1e30)
        score_ref[j] = scores
        block_top = jnp.max(scores, axis=1, keepdims=True)
        top = block_top if top is None else jnp.maximum(top, block_top)
    total = None
    summed = None
    for j in range(NSRC):
        weights = jnp.exp(score_ref[j] - top)
        part_total = jnp.sum(weights, axis=1, keepdims=True)
        product = jnp.dot(
            weights.astype(jnp.bfloat16), value_refs[j][...], preferred_element_type=jnp.float32
        )
        total = part_total if total is None else total + part_total
        summed = product if summed is None else summed + product
    out_ref[...] = (summed / total).astype(out_ref.dtype)


def attend(flags, query_block, key_blocks, value_blocks):
    rows, width = query_block.shape
    block_rows = key_blocks[0].shape[0]
    nheads = width // HEAD_DIM
    row_tile = rows // ROW_SPLIT
    q_spec = pl.BlockSpec((row_tile, HEAD_DIM), lambda h, r, f: (r, h))
    kv_spec = pl.BlockSpec((block_rows, HEAD_DIM), lambda h, r, f: (0, h))
    grid_spec = pltpu.PrefetchScalarGridSpec(
        num_scalar_prefetch=1,
        grid=(nheads, ROW_SPLIT),
        in_specs=[q_spec] + [kv_spec] * (2 * NSRC),
        out_specs=q_spec,
        scratch_shapes=[pltpu.VMEM((NSRC, row_tile, block_rows), jnp.float32)],
    )
    return pl.pallas_call(
        attention_kernel,
        grid_spec=grid_spec,
        out_shape=jax.ShapeDtypeStruct((rows, width), jnp.bfloat16),
        compiler_params=pltpu.CompilerParams(dimension_semantics=("parallel", "arbitrary")),
    )(flags, query_block, *key_blocks, *value_blocks)


def local(queries, new_keys, new_values, cache_keys, cache_values, sources):
    head_width = new_keys.shape[1]
    sp_count = lax.axis_size("sp")
    sp_place = lax.axis_index("sp")
    seq_count = lax.axis_size("seq")
    seq_place = lax.axis_index("seq")
    chips = seq_count // 2

    query_parts = [lax.dynamic_slice_in_dim(queries, sp_place * head_width, head_width, 1)]
    for d in range(1, sp_count):
        columns = ((sp_place + d) % sp_count) * head_width
        piece = lax.dynamic_slice_in_dim(queries, columns, head_width, 1)
        query_parts.append(
            lax.ppermute(piece, "sp", [(i, (i + d) % sp_count) for i in range(sp_count)])
        )
    query_block = jnp.concatenate(query_parts, axis=0)

    swap = [(i, i ^ 1) for i in range(seq_count)]
    partner = lax.ppermute((new_keys, new_values), "seq", swap)

    first = (cache_keys, cache_values)
    span = 1
    while span < chips:
        pairs = [
            (2 * c + k, 2 * (c + span) + k)
            for c in range(span)
            if c + span < chips
            for k in range(2)
        ]
        got = lax.ppermute(first, "seq", pairs)
        chip = seq_place // 2
        taking = (chip >= span) & (chip < 2 * span)
        first = tuple(jnp.where(taking, b, a) for a, b in zip(first, got))
        span *= 2

    last_chip = seq_place >= seq_count - 2
    sending = tuple(
        jnp.where(last_chip, c, n) for c, n in zip((cache_keys, cache_values), (new_keys, new_values))
    )
    before = lax.ppermute(sending, "seq", [(i, (i + 2) % seq_count) for i in range(seq_count)])

    first_other, before_other = lax.ppermute((first, before), "seq", swap)

    other = seq_place ^ 1
    block_ids = jnp.stack(
        [
            seq_count + seq_place,
            seq_count + other,
            seq_place % 2,
            other % 2,
            seq_count + seq_place - 2,
            seq_count + other - 2,
        ]
    ).astype(jnp.int32)
    listed = sources[0]
    flags = jnp.any(listed[None, :] == block_ids[:, None], axis=1).astype(jnp.int32)

    held = [(new_keys, new_values), partner, first, first_other, before, before_other]
    heads_out = attend(flags, query_block, [k for k, _ in held], [v for _, v in held])

    rows = queries.shape[0]
    result = jnp.zeros((rows, queries.shape[1]), jnp.bfloat16)
    for d in range(sp_count):
        piece = heads_out[d * rows : (d + 1) * rows]
        if d:
            piece = lax.ppermute(piece, "sp", [(i, (i - d) % sp_count) for i in range(sp_count)])
        columns = ((sp_place + d) % sp_count) * head_width
        result = lax.dynamic_update_slice_in_dim(result, piece, columns, 1)
    return result


def solution(mesh):
    return jax.shard_map(
        local,
        mesh=mesh,
        in_specs=(
            P(("groups", "seq", "sp"), None),
            P(("groups", "seq"), "sp"),
            P(("groups", "seq"), "sp"),
            P(("groups", "seq"), "sp"),
            P(("groups", "seq"), "sp"),
            P(("groups", "seq"), None),
        ),
        out_specs=P(("groups", "seq", "sp"), None),
        check_vma=False,
    )
```

time: 352 us -> 190 us (0.54)
  matrix products: 112 us -> 0 us
  other arithmetic: 45 us -> 7.58 us
  blocking collectives: 36.2 us -> 0 us
  Pallas kernels: 0 us -> 33.1 us
  starting transfers between devices: 6.19 us -> 21.6 us
  between operations: 13.3 us -> 0.17 us
  local copies, waits for them, and re-layouts: 14.6 us -> 5.49 us
    all_gather x3 -> x0, waiting for transfers between devices: 123 us -> none  [the longest x1 86.6 us: local(): gathered = lax.all_gather(queries, 'sp', axis=0, tiled=True)]
    ppermute x6 -> x16, waiting for transfers between devices: 0.02 us -> 121 us  [the longest x2 49.6 us: local(): got = lax.ppermute(first, 'seq', pairs)]
    dot_general x11 -> x0, matrix products: 112 us -> none  [the longest x6 62.1 us: attend(): jnp.einsum('hqk,khd->hqd', weights.astype(jnp.bfloat16), value_heads, pre...]
    reduce_sum x3 -> x0, other arithmetic: 44.1 us -> none  [attend(): total_new = total_old * fading + jnp.sum(weights, axis=-1)]
    all_to_all x1 -> x0, blocking collectives: 36.2 us -> none  [local(): lax.all_to_all(heads_out, 'sp', split_axis=0, concat_axis=1, tiled=True)]
    pallas_call x0 -> x1, Pallas kernels: none -> 33.1 us  [attend(): pl.pallas_call(attention_kernel, grid_spec=grid_spec, out_shape=jax.Shape...]
    ppermute x6 -> x16, starting transfers between devices: 6.11 us -> 21.6 us  [the longest x2 7.28 us: local(): got = lax.ppermute(first, 'seq', pairs)]
    unnamed x21 -> x18, local copies, waits for them, and re-layouts: 10.7 us -> 2.94 us
  transfers between devices with their start and end apart: 9 -> 16, of which waited for: 3 -> 9; matrix products, arithmetic and copies ran while one was open for 42% -> 5% of each run, Pallas kernels for 0% -> 0%
where the time goes in v1:
time: 190 us; the launch traced here: 189 us
  waiting for transfers between devices  121 us (64%)
  Pallas kernels  33.1 us (17%)
  starting transfers between devices  21.6 us (11%)
  other arithmetic  7.58 us (4%)
  local copies, waits for them, and re-layouts  5.49 us (3%)
    ppermute x2, waiting for transfers between devices, local(): got = lax.ppermute(first, 'seq', pairs)  49.6 us
    pallas_call x1, Pallas kernels, attend(): pl.pallas_call(attention_kernel, grid_spec=grid_spec, out_shape=jax.Shape...  33.1 us
    ppermute x3, waiting for transfers between devices, local(): lax.ppermute(piece, 'sp', [(i, (i - d) % sp_count) for i in range(sp_coun...  27.2 us
    ppermute x3, waiting for transfers between devices, local(): lax.ppermute(piece, 'sp', [(i, (i + d) % sp_count) for i in range(sp_coun...  26.2 us
    ppermute x2, waiting for transfers between devices, local(): lax.ppermute(sending, 'seq', [(i, (i + 2) % seq_count) for i in range(seq...  17.8 us
    ppermute x2, starting transfers between devices, local(): got = lax.ppermute(first, 'seq', pairs)  7.28 us
    ppermute x2, starting transfers between devices, local(): lax.ppermute(sending, 'seq', [(i, (i + 2) % seq_count) for i in range(seq...  4.86 us
    select_n x2, other arithmetic, local(): jnp.where(last_chip, c, n)  4.68 us
  transfers between devices with their start and end apart: 16, of which 9 were waited for; matrix products, arithmetic and copies ran while one was open for 5% of the time, Pallas kernels for 0%

profile of v1, /device:TPU:0, one launch (start us, length us, event | category | flops | bytes accessed | tf_op | source)
XLA Modules:
  0.0 189.1 jit_solution(12051091587206737558)
XLA Ops:
  0.0 5.9 %collective-permute-start.9 = (bf16[512,1280]{1,0:T(8,128)(2,1)}, bf16[512,1280]{1,0:T(8,128)(2,1)}, u32[]{:S(2)}, u32[]{:S(2)}) collective-permute-start(bf16[512,1280]{1,0:T(8,128)(2,1)} %param.10), channel_id=1, source_target_pairs={{0,8},{4,12},{1,9},{5,13},{2,10},{6,14},{3,11},{7,15},{16,24},{20,... | collective-permute-start | bytes 3932168 | tf_op jit(solution)/shard_map/ppermute | solution.py:95
  5.9 1.4 collective-permute-start.4
  7.4 26.9 %collective-permute-done.9 = bf16[512,1280]{1,0:T(8,128)(2,1)} collective-permute-done((bf16[512,1280]{1,0:T(8,128)(2,1)}, bf16[512,1280]{1,0:T(8,128)(2,1)}, u32[]{:S(2)}, u32[]{:S(2)}) %collective-permute-start.9) | collective-permute-done | bytes 1310752 | tf_op jit(solution)/shard_map/ppermute | solution.py:95
  34.3 3.0 %broadcast_select_fusion = (bf16[512,1280]{1,0:T(8,128)(2,1)}, bf16[512,1280]{1,0:T(8,128)(2,1)S(1)}) fusion(bf16[512,1280]{1,0:T(8,128)(2,1)} %param.10, bf16[512,1280]{1,0:T(8,128)(2,1)} %refs_6_.1, pred[]{:T(512)S(6)} %ge.7, bf16[512,1280]{1,0:T(8,128)(2,1)} %collective-permute-done.9, pred[]{:T(512)S(6)} %and.44), kind=kLoop, calls=%fused_computation.1 | loop fusion | flops 1310720 | bytes 6553602 | tf_op jit(solution)/shard_map/jit(_where)/select_n | solution.py:103
  37.3 2.5 %collective-permute-start.11 = (bf16[512,1280]{1,0:T(8,128)(2,1)}, bf16[512,1280]{1,0:T(8,128)(2,1)}, u32[]{:S(2)}, u32[]{:S(2)}) collective-permute-start(bf16[512,1280]{1,0:T(8,128)(2,1)} %get-tuple-element.9), channel_id=1, source_target_pairs={{0,8},{4,12},{8,0},{12,4},{1,9},{5,13},{9,1},{13,5},{2,10},{6,14},... | collective-permute-start | bytes 3932168 | tf_op jit(solution)/shard_map/ppermute | solution.py:105
  39.8 22.6 %collective-permute-done.4 = bf16[512,1280]{1,0:T(8,128)(2,1)S(1)} collective-permute-done((bf16[512,1280]{1,0:T(8,128)(2,1)}, bf16[512,1280]{1,0:T(8,128)(2,1)S(1)}, u32[]{:S(2)}, u32[]{:S(2)}) %collective-permute-start.4) | collective-permute-done | bytes 1310752 | tf_op jit(solution)/shard_map/ppermute | solution.py:95
  62.4 1.7 broadcast_select_fusion.1
  64.1 2.4 %collective-permute-start.6 = (bf16[512,1280]{1,0:T(8,128)(2,1)}, bf16[512,1280]{1,0:T(8,128)(2,1)}, u32[]{:S(2)}, u32[]{:S(2)}) collective-permute-start(bf16[512,1280]{1,0:T(8,128)(2,1)} %get-tuple-element.11), channel_id=1, source_target_pairs={{0,8},{4,12},{8,0},{12,4},{1,9},{5,13},{9,1},{13,5},{2,10},{6,14},... | collective-permute-start | bytes 3932168 | tf_op jit(solution)/shard_map/ppermute | solution.py:105
  66.5 1.5 constant_dynamic-slice_fusion.3
  68.0 1.6 collective-permute-start
  69.6 2.6 %collective-permute-start.1 = (bf16[128,1280]{1,0:T(8,128)(2,1)S(1)}, bf16[128,1280]{1,0:T(8,128)(2,1)S(1)}, u32[]{:S(2)}, u32[]{:S(2)}) collective-permute-start(bf16[128,1280]{1,0:T(8,128)(2,1)S(1)} %get-tuple-element.16), channel_id=1, source_target_pairs={{0,2},{1,3},{2,0},{3,1},{4,6},{5,7},{6,4},{7,5},{8,10},{9,11},{10,... | collective-permute-start | bytes 983048 | tf_op jit(solution)/shard_map/ppermute | solution.py:79
  72.2 8.3 %collective-permute-done = bf16[128,1280]{1,0:T(8,128)(2,1)S(1)} collective-permute-done((bf16[128,1280]{1,0:T(8,128)(2,1)S(1)}, bf16[128,1280]{1,0:T(8,128)(2,1)S(1)}, u32[]{:S(2)}, u32[]{:S(2)}) %collective-permute-start) | collective-permute-done | bytes 327712 | tf_op jit(solution)/shard_map/ppermute | solution.py:79
  80.5 10.6 %collective-permute-done.1 = bf16[128,1280]{1,0:T(8,128)(2,1)S(1)} collective-permute-done((bf16[128,1280]{1,0:T(8,128)(2,1)S(1)}, bf16[128,1280]{1,0:T(8,128)(2,1)S(1)}, u32[]{:S(2)}, u32[]{:S(2)}) %collective-permute-start.1) | collective-permute-done | bytes 327712 | tf_op jit(solution)/shard_map/ppermute | solution.py:79
  91.2 7.2 %collective-permute-done.2 = bf16[128,1280]{1,0:T(8,128)(2,1)S(1)} collective-permute-done((bf16[128,1280]{1,0:T(8,128)(2,1)S(1)}, bf16[128,1280]{1,0:T(8,128)(2,1)S(1)}, u32[]{:S(2)}, u32[]{:S(2)}) %collective-permute-start.2) | collective-permute-done | bytes 327712 | tf_op jit(solution)/shard_map/ppermute | solution.py:79
  98.5 0.7 copy-done.7
  99.2 0.5 collective-permute-start.12
  99.7 17.8 %collective-permute-done.6.refs_4_ = bf16[512,1280]{1,0:T(8,128)(2,1)} collective-permute-done((bf16[512,1280]{1,0:T(8,128)(2,1)}, bf16[512,1280]{1,0:T(8,128)(2,1)}, u32[]{:S(2)}, u32[]{:S(2)}) %collective-permute-start.6) | collective-permute-done | bytes 1310752 | tf_op jit(solution)/shard_map/ppermute | solution.py:105
  117.5 0.1 stack.27
  117.6 0.2 compare_reduce_fusion
  117.7 0.5 convert_element_type.3.flags_ref
  118.3 2.2 %pad_maximum_fusion.q_ref = bf16[512,1280]{1,0:T(8,128)(2,1)} fusion(bf16[128,1280]{1,0:T(8,128)(2,1)} %copy-done.7, bf16[128,1280]{1,0:T(8,128)(2,1)} %copy-done.6, bf16[128,1280]{1,0:T(8,128)(2,1)S(1)} %collective-permute-done, bf16[128,1280]{1,0:T(8,128)(2,1)S(1)} %get-tuple-element.13), kind=kLoop, calls=%fused_computation | loop fusion | flops 5242880 | bytes 2621440 | tf_op jit(solution)/shard_map/concatenate | solution.py:81
  120.5 0.4 collective-permute-done.7.refs_5_
  120.8 33.1 %shard_map.64 = bf16[512,1280]{1,0:T(8,128)(2,1)} custom-call(s32[6]{0:T(128)} %convert_element_type.3.flags_ref, bf16[512,1280]{1,0:T(8,128)(2,1)} %pad_maximum_fusion.q_ref, bf16[512,1280]{1,0:T(8,128)(2,1)} %refs_0_.1, bf16[512,1280]{1,0:T(8,128)(2,1)} %collective-permute-done.3.refs_1_, bf16[512,1280]{1,0:T(8,128)(2,1)} %get-tuple-element.12.refs_2_, ...), custom_call_target="tpu_custom_call" | custom-call | tf_op jit(solution)/shard_map/pallas_call | solution.py:58
  154.0 0.1 broadcast_in_dim.4
  154.1 1.2 copy-done.3
  155.3 0.1 fusion
  155.4 3.7 %collective-permute-start.13 = (bf16[128,1280]{1,0:T(8,128)(2,1)S(1)}, bf16[128,1280]{1,0:T(8,128)(2,1)S(1)}, u32[]{:S(2)}, u32[]{:S(2)}) collective-permute-start(bf16[128,1280]{1,0:T(8,128)(2,1)S(1)} %get-tuple-element.7), channel_id=1, source_target_pairs={{0,3},{1,0},{2,1},{3,2},{4,7},{5,4},{6,5},{7,6},{8,11},{9,8},{10,9... | collective-permute-start | bytes 983048 | tf_op jit(solution)/shard_map/ppermute | solution.py:131
  159.0 1.0 collective-permute-start.15
  160.0 7.1 %collective-permute-done.13 = bf16[128,1280]{1,0:T(8,128)(2,1)S(1)} collective-permute-done((bf16[128,1280]{1,0:T(8,128)(2,1)S(1)}, bf16[128,1280]{1,0:T(8,128)(2,1)S(1)}, u32[]{:S(2)}, u32[]{:S(2)}) %collective-permute-start.13) | collective-permute-done | bytes 327712 | tf_op jit(solution)/shard_map/ppermute | solution.py:131
  167.2 20.1 %collective-permute-done.14 = bf16[128,1280]{1,0:T(8,128)(2,1)S(1)} collective-permute-done((bf16[128,1280]{1,0:T(8,128)(2,1)S(1)}, bf16[128,1280]{1,0:T(8,128)(2,1)S(1)}, u32[]{:S(2)}, u32[]{:S(2)}) %collective-permute-start.14) | collective-permute-done | bytes 327712 | tf_op jit(solution)/shard_map/ppermute | solution.py:131
  187.3 1.0 copy-done.4
  188.4 0.7 constant_dynamic-update-slice_fusion
  (31 shorter events, 0.2 us)
Async XLA Ops:
  0.0 34.3 %collective-permute-start.9 = (bf16[512,1280]{1,0:T(8,128)(2,1)}, bf16[512,1280]{1,0:T(8,128)(2,1)}, u32[]{:S(2)}, u32[]{:S(2)}) collective-permute-start(bf16[512,1280]{1,0:T(8,128)(2,1)} %param.10), channel_id=1, source_target_pairs={{0,8},{4,12},{1,9},{5,13},{2,10},{6,14},{3,11},{7,15},{16,24},{20,... | collective-permute-start | bytes 3932168 | tf_op jit(solution)/shard_map/ppermute | solution.py:95
  5.9 56.5 %collective-permute-start.4 = (bf16[512,1280]{1,0:T(8,128)(2,1)}, bf16[512,1280]{1,0:T(8,128)(2,1)S(1)}, u32[]{:S(2)}, u32[]{:S(2)}) collective-permute-start(bf16[512,1280]{1,0:T(8,128)(2,1)} %param.9), channel_id=1, source_target_pairs={{0,8},{4,12},{1,9},{5,13},{2,10},{6,14},{3,11},{7,15},{16,24},{20,... | collective-permute-start | bytes 3932168 | tf_op jit(solution)/shard_map/ppermute | solution.py:95
  7.3 91.2 %collective-permute-start.3 = (bf16[512,1280]{1,0:T(8,128)(2,1)}, bf16[512,1280]{1,0:T(8,128)(2,1)}, u32[]{:S(2)}, u32[]{:S(2)}) collective-permute-start(bf16[512,1280]{1,0:T(8,128)(2,1)} %refs_0_.1), channel_id=1, source_target_pairs={{0,4},{4,0},{8,12},{12,8},{1,5},{5,1},{9,13},{13,9},{2,6},{6,2},{1... | collective-permute-start | bytes 3932168 | tf_op jit(solution)/shard_map/ppermute | solution.py:84
  7.4 55.0 %copy-start = (bf16[512,1280]{1,0:T(8,128)(2,1)S(1)}, bf16[512,1280]{1,0:T(8,128)(2,1)}, u32[]{:S(2)}) copy-start(bf16[512,1280]{1,0:T(8,128)(2,1)} %refs_0_.1) | copy-start | bytes 3932164
  7.4 55.0 %copy-start.5 = (bf16[512,1280]{1,0:T(8,128)(2,1)S(1)}, bf16[512,1280]{1,0:T(8,128)(2,1)}, u32[]{:S(2)}) copy-start(bf16[512,1280]{1,0:T(8,128)(2,1)} %param.9) | copy-start | bytes 3932164
  37.3 61.1 %copy-start.2 = (bf16[512,1280]{1,0:T(8,128)(2,1)}, bf16[512,1280]{1,0:T(8,128)(2,1)S(1)}, u32[]{:S(2)}) copy-start(bf16[512,1280]{1,0:T(8,128)(2,1)S(1)} %get-tuple-element.10.refs_8_) | copy-start | bytes 3932164
  37.3 61.8 %collective-permute-start.11 = (bf16[512,1280]{1,0:T(8,128)(2,1)}, bf16[512,1280]{1,0:T(8,128)(2,1)}, u32[]{:S(2)}, u32[]{:S(2)}) collective-permute-start(bf16[512,1280]{1,0:T(8,128)(2,1)} %get-tuple-element.9), channel_id=1, source_target_pairs={{0,8},{4,12},{8,0},{12,4},{1,9},{5,13},{9,1},{13,5},{2,10},{6,14},... | collective-permute-start | bytes 3932168 | tf_op jit(solution)/shard_map/ppermute | solution.py:105
  64.1 53.3 %collective-permute-start.6 = (bf16[512,1280]{1,0:T(8,128)(2,1)}, bf16[512,1280]{1,0:T(8,128)(2,1)}, u32[]{:S(2)}, u32[]{:S(2)}) collective-permute-start(bf16[512,1280]{1,0:T(8,128)(2,1)} %get-tuple-element.11), channel_id=1, source_target_pairs={{0,8},{4,12},{8,0},{12,4},{1,9},{5,13},{9,1},{13,5},{2,10},{6,14},... | collective-permute-start | bytes 3932168 | tf_op jit(solution)/shard_map/ppermute | solution.py:105
  66.5 24.7 %copy-start.1 = (bf16[512,1280]{1,0:T(8,128)(2,1)S(1)}, bf16[512,1280]{1,0:T(8,128)(2,1)}, u32[]{:S(2)}) copy-start(bf16[512,1280]{1,0:T(8,128)(2,1)} %refs_6_.1) | copy-start | bytes 3932164
  66.5 51.0 %copy-start.8 = (s32[1,6]{1,0:T(1,128)S(1)}, s32[1,6]{1,0:T(1,128)}, u32[]{:S(2)}) copy-start(s32[1,6]{1,0:T(1,128)} %param.11) | copy-start | bytes 76
  68.0 12.6 %collective-permute-start = (bf16[128,1280]{1,0:T(8,128)(2,1)S(1)}, bf16[128,1280]{1,0:T(8,128)(2,1)S(1)}, u32[]{:S(2)}, u32[]{:S(2)}) collective-permute-start(bf16[128,1280]{1,0:T(8,128)(2,1)S(1)} %get-tuple-element.14), channel_id=1, source_target_pairs={{0,1},{1,2},{2,3},{3,0},{4,5},{5,6},{6,7},{7,4},{8,9},{9,10},{10,1... | collective-permute-start | bytes 983048 | tf_op jit(solution)/shard_map/ppermute | solution.py:79
  69.6 21.6 %collective-permute-start.1 = (bf16[128,1280]{1,0:T(8,128)(2,1)S(1)}, bf16[128,1280]{1,0:T(8,128)(2,1)S(1)}, u32[]{:S(2)}, u32[]{:S(2)}) collective-permute-start(bf16[128,1280]{1,0:T(8,128)(2,1)S(1)} %get-tuple-element.16), channel_id=1, source_target_pairs={{0,2},{1,3},{2,0},{3,1},{4,6},{5,7},{6,4},{7,5},{8,10},{9,11},{10,... | collective-permute-start | bytes 983048 | tf_op jit(solution)/shard_map/ppermute | solution.py:79
  80.5 17.9 %collective-permute-start.2 = (bf16[128,1280]{1,0:T(8,128)(2,1)S(1)}, bf16[128,1280]{1,0:T(8,128)(2,1)S(1)}, u32[]{:S(2)}, u32[]{:S(2)}) collective-permute-start(bf16[128,1280]{1,0:T(8,128)(2,1)S(1)} %get-tuple-element.15), channel_id=1, source_target_pairs={{0,3},{1,0},{2,1},{3,2},{4,7},{5,4},{6,5},{7,6},{8,11},{9,8},{10,9... | collective-permute-start | bytes 983048 | tf_op jit(solution)/shard_map/ppermute | solution.py:79
  91.2 7.3 %copy-start.6 = (bf16[128,1280]{1,0:T(8,128)(2,1)}, bf16[128,1280]{1,0:T(8,128)(2,1)S(1)}, u32[]{:S(2)}) copy-start(bf16[128,1280]{1,0:T(8,128)(2,1)S(1)} %collective-permute-done.1) | copy-start | bytes 983044
  91.2 29.3 %collective-permute-start.8 = (bf16[512,1280]{1,0:T(8,128)(2,1)S(1)}, bf16[512,1280]{1,0:T(8,128)(2,1)}, u32[]{:S(2)}, u32[]{:S(2)}) collective-permute-start(bf16[512,1280]{1,0:T(8,128)(2,1)S(1)} %copy-done.1), channel_id=1, source_target_pairs={{0,4},{4,0},{8,12},{12,8},{1,5},{5,1},{9,13},{13,9},{2,6},{6,2},{1... | collective-permute-start | bytes 3932168 | tf_op jit(solution)/shard_map/ppermute | solution.py:84
  98.4 0.7 copy-start.7
  98.4 22.0 %collective-permute-start.10 = (bf16[512,1280]{1,0:T(8,128)(2,1)S(1)}, bf16[512,1280]{1,0:T(8,128)(2,1)}, u32[]{:S(2)}, u32[]{:S(2)}) collective-permute-start(bf16[512,1280]{1,0:T(8,128)(2,1)S(1)} %get-tuple-element.10.refs_8_), channel_id=1, source_target_pairs={{0,4},{4,0},{8,12},{12,8},{1,5},{5,1},{9,13},{13,9},{2,6},{6,2},{1... | collective-permute-start | bytes 3932168 | tf_op jit(solution)/shard_map/ppermute | solution.py:107
  99.2 21.3 %collective-permute-start.5 = (bf16[512,1280]{1,0:T(8,128)(2,1)}, bf16[512,1280]{1,0:T(8,128)(2,1)}, u32[]{:S(2)}, u32[]{:S(2)}) collective-permute-start(bf16[512,1280]{1,0:T(8,128)(2,1)} %get-tuple-element.12.refs_2_), channel_id=1, source_target_pairs={{0,4},{4,0},{8,12},{12,8},{1,5},{5,1},{9,13},{13,9},{2,6},{6,2},{1... | collective-permute-start | bytes 3932168 | tf_op jit(solution)/shard_map/ppermute | solution.py:107
  99.2 21.3 %collective-permute-start.12 = (bf16[512,1280]{1,0:T(8,128)(2,1)}, bf16[512,1280]{1,0:T(8,128)(2,1)}, u32[]{:S(2)}, u32[]{:S(2)}) collective-permute-start(bf16[512,1280]{1,0:T(8,128)(2,1)} %collective-permute-done.11.refs_10_), channel_id=1, source_target_pairs={{0,4},{4,0},{8,12},{12,8},{1,5},{5,1},{9,13},{13,9},{2,6},{6,2},{1... | collective-permute-start | bytes 3932168 | tf_op jit(solution)/shard_map/ppermute | solution.py:107
  117.5 3.4 %collective-permute-start.7 = (bf16[512,1280]{1,0:T(8,128)(2,1)}, bf16[512,1280]{1,0:T(8,128)(2,1)}, u32[]{:S(2)}, u32[]{:S(2)}) collective-permute-start(bf16[512,1280]{1,0:T(8,128)(2,1)} %collective-permute-done.6.refs_4_), channel_id=1, source_target_pairs={{0,4},{4,0},{8,12},{12,8},{1,5},{5,1},{9,13},{13,9},{2,6},{6,2},{1... | collective-permute-start | bytes 3932168 | tf_op jit(solution)/shard_map/ppermute | solution.py:107
  153.9 1.3 copy-start.3
  155.4 11.8 %collective-permute-start.13 = (bf16[128,1280]{1,0:T(8,128)(2,1)S(1)}, bf16[128,1280]{1,0:T(8,128)(2,1)S(1)}, u32[]{:S(2)}, u32[]{:S(2)}) collective-permute-start(bf16[128,1280]{1,0:T(8,128)(2,1)S(1)} %get-tuple-element.7), channel_id=1, source_target_pairs={{0,3},{1,0},{2,1},{3,2},{4,7},{5,4},{6,5},{7,6},{8,11},{9,8},{10,9... | collective-permute-start | bytes 983048 | tf_op jit(solution)/shard_map/ppermute | solution.py:131
  159.0 28.3 %collective-permute-start.14 = (bf16[128,1280]{1,0:T(8,128)(2,1)S(1)}, bf16[128,1280]{1,0:T(8,128)(2,1)S(1)}, u32[]{:S(2)}, u32[]{:S(2)}) collective-permute-start(bf16[128,1280]{1,0:T(8,128)(2,1)S(1)} %get-tuple-element.6), channel_id=1, source_target_pairs={{0,2},{1,3},{2,0},{3,1},{4,6},{5,7},{6,4},{7,5},{8,10},{9,11},{10,... | collective-permute-start | bytes 983048 | tf_op jit(solution)/shard_map/ppermute | solution.py:131
  159.0 28.3 %collective-permute-start.15 = (bf16[128,1280]{1,0:T(8,128)(2,1)S(1)}, bf16[128,1280]{1,0:T(8,128)(2,1)S(1)}, u32[]{:S(2)}, u32[]{:S(2)}) collective-permute-start(bf16[128,1280]{1,0:T(8,128)(2,1)S(1)} %get-tuple-element.5), channel_id=1, source_target_pairs={{0,1},{1,2},{2,3},{3,0},{4,5},{5,6},{6,7},{7,4},{8,9},{9,10},{10,1... | collective-permute-start | bytes 983048 | tf_op jit(solution)/shard_map/ppermute | solution.py:131
  187.3 1.1 copy-start.4

commit v2 on v1

v2 whole, which is shorter than its diff:
```python
import math

import jax
import jax.numpy as jnp
from jax import lax
from jax.experimental import pallas as pl
from jax.experimental.pallas import tpu as pltpu
from jax.sharding import PartitionSpec as P

HEAD_DIM = 128
ROW_SPLIT = 2
STAT_ROWS = 8


def partial_kernel(nsrc, flags_ref, q_ref, *refs):
    key_refs = refs[:nsrc]
    value_refs = refs[nsrc : 2 * nsrc]
    out_ref, lse_ref = refs[2 * nsrc : 2 * nsrc + 2]
    score_ref, top_ref, total_ref, summed_ref = refs[2 * nsrc + 2 :]
    score_scale = 1.0 / math.sqrt(HEAD_DIM)
    query = q_ref[...]
    top_ref[...] = jnp.full(top_ref.shape, -1e30, jnp.float32)
    total_ref[...] = jnp.zeros(total_ref.shape, jnp.float32)
    summed_ref[...] = jnp.zeros(summed_ref.shape, jnp.float32)
    for j in range(nsrc):

        @pl.when(flags_ref[j] > 0)
        def _():
            scores = lax.dot_general(
                query, key_refs[j][...], (((1,), (1,)), ((), ())), preferred_element_type=jnp.float32
            ) * score_scale
            score_ref[j] = scores
            top_ref[...] = jnp.maximum(top_ref[...], jnp.max(scores, axis=1, keepdims=True))

    for j in range(nsrc):

        @pl.when(flags_ref[j] > 0)
        def _():
            weights = jnp.exp(score_ref[j] - top_ref[...])
            total_ref[...] += jnp.sum(weights, axis=1, keepdims=True)
            summed_ref[...] += jnp.dot(
                weights.astype(jnp.bfloat16), value_refs[j][...], preferred_element_type=jnp.float32
            )

    total = total_ref[...]
    filled = total > 0
    safe = jnp.where(filled, total, 1.0)
    out_ref[...] = jnp.where(filled, summed_ref[...] / safe, 0.0).astype(out_ref.dtype)
    lse = jnp.where(filled, top_ref[...] + jnp.log(safe), -1e30)
    wide = jnp.broadcast_to(lse, (lse.shape[0], 128))
    lse_ref[...] = jnp.transpose(wide)[:STAT_ROWS]


def attend_partial(flags, query_block, key_blocks, value_blocks, out_dtype):
    nsrc = len(key_blocks)
    rows, width = query_block.shape
    block_rows = key_blocks[0].shape[0]
    nheads = width // HEAD_DIM
    row_tile = rows // ROW_SPLIT
    q_spec = pl.BlockSpec((row_tile, HEAD_DIM), lambda h, r, f: (r, h))
    kv_spec = pl.BlockSpec((block_rows, HEAD_DIM), lambda h, r, f: (0, h))
    lse_spec = pl.BlockSpec((None, STAT_ROWS, row_tile), lambda h, r, f: (h, 0, r))
    grid_spec = pltpu.PrefetchScalarGridSpec(
        num_scalar_prefetch=1,
        grid=(nheads, ROW_SPLIT),
        in_specs=[q_spec] + [kv_spec] * (2 * nsrc),
        out_specs=[q_spec, lse_spec],
        scratch_shapes=[
            pltpu.VMEM((nsrc, row_tile, block_rows), jnp.float32),
            pltpu.VMEM((row_tile, 1), jnp.float32),
            pltpu.VMEM((row_tile, 1), jnp.float32),
            pltpu.VMEM((row_tile, HEAD_DIM), jnp.float32),
        ],
    )
    return pl.pallas_call(
        lambda *a: partial_kernel(nsrc, *a),
        grid_spec=grid_spec,
        out_shape=[
            jax.ShapeDtypeStruct((rows, width), out_dtype),
            jax.ShapeDtypeStruct((nheads, STAT_ROWS, rows), jnp.float32),
        ],
        compiler_params=pltpu.CompilerParams(dimension_semantics=("parallel", "arbitrary")),
    )(flags, query_block, *key_blocks, *value_blocks)


def membership(listed, block_ids, valid):
    hit = jnp.any(listed[None, :] == jnp.stack(block_ids)[:, None], axis=1)
    return (hit & jnp.stack(valid)).astype(jnp.int32)


def local(queries, new_keys, new_values, cache_keys, cache_values, sources):
    head_width = new_keys.shape[1]
    nheads = head_width // HEAD_DIM
    sp_count = lax.axis_size("sp")
    sp_place = lax.axis_index("sp")
    seq_count = lax.axis_size("seq")
    s = lax.axis_index("seq")
    chips = seq_count // 2
    chip = s // 2
    other = s ^ 1
    listed = sources[0]

    query_parts = [lax.dynamic_slice_in_dim(queries, sp_place * head_width, head_width, 1)]
    for d in range(1, sp_count):
        columns = ((sp_place + d) % sp_count) * head_width
        piece = lax.dynamic_slice_in_dim(queries, columns, head_width, 1)
        query_parts.append(
            lax.ppermute(piece, "sp", [(i, (i + d) % sp_count) for i in range(sp_count)])
        )
    query_block = jnp.concatenate(query_parts, axis=0)

    back = [(i, (i - 2) % seq_count) for i in range(seq_count)]
    forth = [(i, (i + 2) % seq_count) for i in range(seq_count)]
    t = (s - 2) % seq_count
    t_chip = t // 2
    remote_ids = [seq_count + t, seq_count + (t ^ 1), t, t ^ 1]
    remote_valid = [
        s >= 2,
        s >= 2,
        (t_chip == 0) | (t_chip == chips - 1),
        (t_chip == 0) | (t_chip == chips - 1),
    ]
    if chips > 2:
        remote_ids += [t % 2, 1 - t % 2]
        remote_valid += [(t_chip >= 1) & (t_chip <= chips - 2)] * 2
    remote_flags = membership(listed, remote_ids, remote_valid)
    got_query, got_flags = lax.ppermute((query_block, remote_flags), "seq", back)

    swap = [(i, i ^ 1) for i in range(seq_count)]
    partner_k, partner_v, partner_ck, partner_cv = lax.ppermute(
        (new_keys, new_values, cache_keys, cache_values), "seq", swap
    )
    keys = [new_keys, partner_k, cache_keys, partner_ck]
    values = [new_values, partner_v, cache_values, partner_cv]

    if chips > 2:
        first = (cache_keys, cache_values)
        span = 1
        while span < chips - 1:
            pairs = [
                (2 * c + k, 2 * (c + span) + k)
                for c in range(span)
                if c + span < chips - 1
                for k in range(2)
            ]
            got = lax.ppermute(first, "seq", pairs)
            taking = (chip >= span) & (chip < 2 * span)
            first = tuple(jnp.where(taking, b, a) for a, b in zip(first, got))
            span *= 2
        first_other = lax.ppermute(first, "seq", swap)
        remote_keys = keys + [first[0], first_other[0]]
        remote_values = values + [first[1], first_other[1]]
    else:
        remote_keys, remote_values = keys, values

    local_flags = membership(
        listed,
        [seq_count + s, seq_count + other, s, other],
        [s >= 0, s >= 0, chip == 0, chip == 0],
    )
    local_out, local_lse = attend_partial(local_flags, query_block, keys, values, jnp.float32)

    far_out, far_lse = attend_partial(got_flags, got_query, remote_keys, remote_values, jnp.bfloat16)
    far_out, far_lse = lax.ppermute((far_out, far_lse), "seq", forth)

    rows_all = query_block.shape[0]
    lse_a = local_lse[:, 0, :].T[:, :, None]
    lse_b = far_lse[:, 0, :].T[:, :, None]
    top = jnp.maximum(lse_a, lse_b)
    weight_a = jnp.exp(lse_a - top)
    weight_b = jnp.exp(lse_b - top)
    mixed = (
        local_out.reshape(rows_all, nheads, HEAD_DIM) * weight_a
        + far_out.astype(jnp.float32).reshape(rows_all, nheads, HEAD_DIM) * weight_b
    ) / (weight_a + weight_b)
    heads_out = mixed.reshape(rows_all, head_width).astype(jnp.bfloat16)

    rows = queries.shape[0]
    result = jnp.zeros((rows, queries.shape[1]), jnp.bfloat16)
    for d in range(sp_count):
        piece = heads_out[d * rows : (d + 1) * rows]
        if d:
            piece = lax.ppermute(piece, "sp", [(i, (i - d) % sp_count) for i in range(sp_count)])
        columns = ((sp_place + d) % sp_count) * head_width
        result = lax.dynamic_update_slice_in_dim(result, piece, columns, 1)
    return result


def solution(mesh):
    return jax.shard_map(
        local,
        mesh=mesh,
        in_specs=(
            P(("groups", "seq", "sp"), None),
            P(("groups", "seq"), "sp"),
            P(("groups", "seq"), "sp"),
            P(("groups", "seq"), "sp"),
            P(("groups", "seq"), "sp"),
            P(("groups", "seq"), None),
        ),
        out_specs=P(("groups", "seq", "sp"), None),
        check_vma=False,
    )
```

time: 190 us -> 229 us (1.21)
  Pallas kernels: 33.1 us -> 113 us
  waiting for transfers between devices: 121 us -> 79.5 us
  local copies, waits for them, and re-layouts: 5.49 us -> 12.9 us
  starting transfers between devices: 21.6 us -> 15.2 us
    pallas_call x1 -> x2, Pallas kernels: 33.1 us -> 113 us  [attend_partial(): pl.pallas_call(lambda *a: partial_kernel(nsrc, *a), grid_spec=grid_spec,...]
    ppermute x10 -> x8, waiting for transfers between devices: 67.7 us -> 29.6 us  [the longest x2 29.5 us: local(): lax.ppermute((query_block, remote_flags), 'seq', back)]
    ppermute x10 -> x8, starting transfers between devices: 12.7 us -> 5.58 us  [the longest x2 3.04 us: local(): lax.ppermute((query_block, remote_flags), 'seq', back)]
    convert_element_type x1 -> x3, other arithmetic: 0.51 us -> 5.93 us  [the longest x1 5.19 us: local(): heads_out = mixed.reshape(rows_all, head_width).astype(jnp.bfloat16)]
    mul x0 -> x4, local copies, waits for them, and re-layouts: none -> 4.89 us  [the longest x2 2.5 us: local(): local_out.reshape(rows_all, nheads, HEAD_DIM) * weight_a]
    select_n x2 -> x0, other arithmetic: 4.68 us -> none  [local(): jnp.where(last_chip, c, n)]
    ppermute x3, waiting for transfers between devices: 27.2 us -> 23.6 us  [local(): lax.ppermute(piece, 'sp', [(i, (i - d) % sp_count) for i in range(sp_coun...]
    div x0 -> x2, local copies, waits for them, and re-layouts: none -> 2.45 us  [local(): (local_out.reshape(rows_all, nheads, HEAD_DIM) * weight_a + far_out.astyp...]
  transfers between devices with their start and end apart: 16 -> 14, of which waited for: 9 -> 6; matrix products, arithmetic and copies ran while one was open for 5% -> 5% of each run, Pallas kernels for 0% -> 25%
where the time goes in v2:
time: 229 us; the launch traced here: 228 us
  Pallas kernels  113 us (49%)
  waiting for transfers between devices  79.5 us (35%)
  starting transfers between devices  15.2 us (7%)
  local copies, waits for them, and re-layouts  12.9 us (6%)
  other arithmetic  7.4 us (3%)
    pallas_call x2, Pallas kernels, attend_partial(): pl.pallas_call(lambda *a: partial_kernel(nsrc, *a), grid_spec=grid_spec,...  113 us
    ppermute x2, waiting for transfers between devices, local(): lax.ppermute((query_block, remote_flags), 'seq', back)  29.5 us
    ppermute x3, waiting for transfers between devices, local(): lax.ppermute(piece, 'sp', [(i, (i + d) % sp_count) for i in range(sp_coun...  26.3 us
    ppermute x3, waiting for transfers between devices, local(): lax.ppermute(piece, 'sp', [(i, (i - d) % sp_count) for i in range(sp_coun...  23.6 us
    ppermute x3, starting transfers between devices, local(): lax.ppermute(piece, 'sp', [(i, (i + d) % sp_count) for i in range(sp_coun...  6.08 us
    convert_element_type x1, other arithmetic, local(): heads_out = mixed.reshape(rows_all, head_width).astype(jnp.bfloat16)  5.19 us
  transfers between devices with their start and end apart: 14, of which 6 were waited for; matrix products, arithmetic and copies ran while one was open for 5% of the time, Pallas kernels for 25%

profile of v2, /device:TPU:0, one launch (start us, length us, event | category | flops | bytes accessed | tf_op | source)
XLA Modules:
  0.0 228.4 jit_solution(15964671653008174007)
XLA Ops:
  0.0 2.4 %constant_dynamic-slice_fusion.3 = (bf16[128,1280]{1,0:T(8,128)(2,1)S(1)}, bf16[128,1280]{1,0:T(8,128)(2,1)}, bf16[128,1280]{1,0:T(8,128)(2,1)}, bf16[128,1280]{1,0:T(8,128)(2,1)}) fusion(bf16[128,5120]{1,0:T(8,128)(2,1)} %param.6, s32[]{:T(128)S(6)} %select_n.55, s32[]{:T(128)S(6)} %select_n.57, s32[]{:T(128)S(6)} %select_n.61, s32[]{:T(128)S(6)} %select_n.59), kind=kLoop, calls=%fused_computation.14 | loop fusion | bytes 2621456 | tf_op jit(solution)/shard_map/dynamic_slice | solution.py:103
  2.4 5.1 %collective-permute-start.2 = (bf16[128,1280]{1,0:T(8,128)(2,1)}, bf16[128,1280]{1,0:T(8,128)(2,1)S(1)}, u32[]{:S(2)}, u32[]{:S(2)}) collective-permute-start(bf16[128,1280]{1,0:T(8,128)(2,1)} %get-tuple-element.24), channel_id=1, source_target_pairs={{0,3},{1,0},{2,1},{3,2},{4,7},{5,4},{6,5},{7,6},{8,11},{9,8},{10,9... | collective-permute-start | bytes 983048 | tf_op jit(solution)/shard_map/ppermute | solution.py:108
  7.5 1.0 collective-permute-start
  8.5 0.5 collective-permute-start.4
  9.1 0.2 compare_reduce_fusion.1
  9.4 6.6 %collective-permute-done.2 = bf16[128,1280]{1,0:T(8,128)(2,1)S(1)} collective-permute-done((bf16[128,1280]{1,0:T(8,128)(2,1)}, bf16[128,1280]{1,0:T(8,128)(2,1)S(1)}, u32[]{:S(2)}, u32[]{:S(2)}) %collective-permute-start.2) | collective-permute-done | bytes 327712 | tf_op jit(solution)/shard_map/ppermute | solution.py:108
  16.0 19.8 %collective-permute-done.1 = bf16[128,1280]{1,0:T(8,128)(2,1)} collective-permute-done((bf16[128,1280]{1,0:T(8,128)(2,1)}, bf16[128,1280]{1,0:T(8,128)(2,1)}, u32[]{:S(2)}, u32[]{:S(2)}) %collective-permute-start.1) | collective-permute-done | bytes 327712 | tf_op jit(solution)/shard_map/ppermute | solution.py:108
  35.7 1.5 collective-permute-start.7
  37.3 1.2 pad_maximum_fusion.a_1_
  38.4 0.8 collective-permute-done.7.a_0_
  39.3 1.5 collective-permute-start.8
  40.8 28.7 %collective-permute-done.8.a_1_ = bf16[512,1280]{1,0:T(8,128)(2,1)} collective-permute-done((bf16[512,1280]{1,0:T(8,128)(2,1)S(1)}, bf16[512,1280]{1,0:T(8,128)(2,1)}, u32[]{:S(2)}, u32[]{:S(2)}) %collective-permute-start.8) | collective-permute-done | bytes 1310752 | tf_op jit(solution)/shard_map/ppermute | solution.py:127
  69.5 56.6 %shard_map.65 = (bf16[512,1280]{1,0:T(8,128)(2,1)}, f32[10,8,512]{2,1,0:T(8,128)}) custom-call(s32[4]{0:T(128)} %copy-done.4, bf16[512,1280]{1,0:T(8,128)(2,1)} %collective-permute-done.8.a_1_, bf16[512,1280]{1,0:T(8,128)(2,1)} %a_2_.3, bf16[512,1280]{1,0:T(8,128)(2,1)} %collective-permute-done.3.a_3_, bf16[512,1280]{1,0:T(8,128)(2,1)} %a_4_.3, ...), custom_call_target="tpu_custom_call" | custom-call | tf_op jit(solution)/shard_map/pallas_call | solution.py:75
  126.2 2.0 collective-permute-start.9
  128.2 0.7 fusion.2.a_0_
  128.8 56.6 %shard_map.64 = (f32[512,1280]{1,0:T(8,128)}, f32[10,8,512]{2,1,0:T(8,128)}) custom-call(s32[4]{0:T(128)} %fusion.2.a_0_, bf16[512,1280]{1,0:T(8,128)(2,1)} %copy-done.2, bf16[512,1280]{1,0:T(8,128)(2,1)} %a_2_.3, bf16[512,1280]{1,0:T(8,128)(2,1)} %collective-permute-done.3.a_3_, bf16[512,1280]{1,0:T(8,128)(2,1)} %a_4_.3, ...), custom_call_target="tpu_custom_call" | custom-call | tf_op jit(solution)/shard_map/pallas_call | solution.py:75
  185.5 1.0 copy.15
  186.5 0.3 div.32
  186.9 2.1 copy.18
  189.0 0.3 mul.47
  189.3 2.1 copy.17
  191.4 0.3 mul.44
  191.7 2.2 copy.16
  193.9 5.2 %divide_convert_fusion = bf16[512,1280]{1,0:T(8,128)(2,1)S(1)} fusion(f32[512,1280]{1,0:T(8,128)} %copy.18, f32[512,1280]{1,0:T(8,128)} %copy.17, bf16[512,1280]{1,0:T(8,128)(2,1)} %collective-permute-done.10, f32[512,1280]{1,0:T(8,128)} %get-tuple-element.9, f32[512,1280]{1,0:T(8,128)} %copy.16), kind=kLoop, calls=%fused_computation | loop fusion | flops 3932160 | bytes 13107200 | tf_op jit(solution)/shard_map/convert_element_type | solution.py:176
  199.1 0.1 broadcast_in_dim.2
  199.2 0.1 fusion.7
  199.4 1.6 collective-permute-start.12
  201.0 1.9 collective-permute-start.13
  202.9 6.2 %collective-permute-done.11 = bf16[128,1280]{1,0:T(8,128)(2,1)S(1)} collective-permute-done((bf16[128,1280]{1,0:T(8,128)(2,1)S(1)}, bf16[128,1280]{1,0:T(8,128)(2,1)S(1)}, u32[]{:S(2)}, u32[]{:S(2)}) %collective-permute-start.11) | collective-permute-done | bytes 327712 | tf_op jit(solution)/shard_map/ppermute | solution.py:183
  209.2 17.4 %collective-permute-done.12 = bf16[128,1280]{1,0:T(8,128)(2,1)S(1)} collective-permute-done((bf16[128,1280]{1,0:T(8,128)(2,1)S(1)}, bf16[128,1280]{1,0:T(8,128)(2,1)S(1)}, u32[]{:S(2)}, u32[]{:S(2)}) %collective-permute-start.12) | collective-permute-done | bytes 327712 | tf_op jit(solution)/shard_map/ppermute | solution.py:183
  226.6 1.0 copy-done.3
  227.7 0.7 constant_dynamic-update-slice_fusion
  (31 shorter events, 0.4 us)
Async XLA Ops:
  0.0 8.5 %copy-start = (bf16[512,1280]{1,0:T(8,128)(2,1)S(1)}, bf16[512,1280]{1,0:T(8,128)(2,1)}, u32[]{:S(2)}) copy-start(bf16[512,1280]{1,0:T(8,128)(2,1)} %a_2_.3) | copy-start | bytes 3932164
  0.0 8.5 %copy-start.1 = (bf16[512,1280]{1,0:T(8,128)(2,1)S(1)}, bf16[512,1280]{1,0:T(8,128)(2,1)}, u32[]{:S(2)}) copy-start(bf16[512,1280]{1,0:T(8,128)(2,1)} %a_4_.3) | copy-start | bytes 3932164
  0.0 9.1 %copy-start.5 = (s32[1,6]{1,0:T(1,128)S(1)}, s32[1,6]{1,0:T(1,128)}, u32[]{:S(2)}) copy-start(s32[1,6]{1,0:T(1,128)} %param.11) | copy-start | bytes 76
  2.4 13.5 %collective-permute-start.2 = (bf16[128,1280]{1,0:T(8,128)(2,1)}, bf16[128,1280]{1,0:T(8,128)(2,1)S(1)}, u32[]{:S(2)}, u32[]{:S(2)}) collective-permute-start(bf16[128,1280]{1,0:T(8,128)(2,1)} %get-tuple-element.24), channel_id=1, source_target_pairs={{0,3},{1,0},{2,1},{3,2},{4,7},{5,4},{6,5},{7,6},{8,11},{9,8},{10,9... | collective-permute-start | bytes 983048 | tf_op jit(solution)/shard_map/ppermute | solution.py:108
  7.5 28.2 %collective-permute-start.1 = (bf16[128,1280]{1,0:T(8,128)(2,1)}, bf16[128,1280]{1,0:T(8,128)(2,1)}, u32[]{:S(2)}, u32[]{:S(2)}) collective-permute-start(bf16[128,1280]{1,0:T(8,128)(2,1)} %get-tuple-element.25), channel_id=1, source_target_pairs={{0,2},{1,3},{2,0},{3,1},{4,6},{5,7},{6,4},{7,5},{8,10},{9,11},{10,... | collective-permute-start | bytes 983048 | tf_op jit(solution)/shard_map/ppermute | solution.py:108
  7.5 28.2 %collective-permute-start = (bf16[128,1280]{1,0:T(8,128)(2,1)}, bf16[128,1280]{1,0:T(8,128)(2,1)}, u32[]{:S(2)}, u32[]{:S(2)}) collective-permute-start(bf16[128,1280]{1,0:T(8,128)(2,1)} %get-tuple-element.23), channel_id=1, source_target_pairs={{0,1},{1,2},{2,3},{3,0},{4,5},{5,6},{6,7},{7,4},{8,9},{9,10},{10,1... | collective-permute-start | bytes 983048 | tf_op jit(solution)/shard_map/ppermute | solution.py:108
  8.5 32.3 %collective-permute-start.3 = (bf16[512,1280]{1,0:T(8,128)(2,1)S(1)}, bf16[512,1280]{1,0:T(8,128)(2,1)}, u32[]{:S(2)}, u32[]{:S(2)}) collective-permute-start(bf16[512,1280]{1,0:T(8,128)(2,1)S(1)} %copy-done), channel_id=1, source_target_pairs={{0,4},{4,0},{8,12},{12,8},{1,5},{5,1},{9,13},{13,9},{2,6},{6,2},{1... | collective-permute-start | bytes 3932168 | tf_op jit(solution)/shard_map/ppermute | solution.py:130
  8.5 32.3 %collective-permute-start.4 = (bf16[512,1280]{1,0:T(8,128)(2,1)S(1)}, bf16[512,1280]{1,0:T(8,128)(2,1)}, u32[]{:S(2)}, u32[]{:S(2)}) collective-permute-start(bf16[512,1280]{1,0:T(8,128)(2,1)S(1)} %copy-done.1), channel_id=1, source_target_pairs={{0,4},{4,0},{8,12},{12,8},{1,5},{5,1},{9,13},{13,9},{2,6},{6,2},{1... | collective-permute-start | bytes 3932168 | tf_op jit(solution)/shard_map/ppermute | solution.py:130
  16.0 24.9 %collective-permute-start.5 = (bf16[512,1280]{1,0:T(8,128)(2,1)}, bf16[512,1280]{1,0:T(8,128)(2,1)}, u32[]{:S(2)}, u32[]{:S(2)}) collective-permute-start(bf16[512,1280]{1,0:T(8,128)(2,1)} %a_6_.3), channel_id=1, source_target_pairs={{0,4},{4,0},{8,12},{12,8},{1,5},{5,1},{9,13},{13,9},{2,6},{6,2},{1... | collective-permute-start | bytes 3932168 | tf_op jit(solution)/shard_map/ppermute | solution.py:130
  35.7 5.1 %collective-permute-start.6 = (bf16[512,1280]{1,0:T(8,128)(2,1)}, bf16[512,1280]{1,0:T(8,128)(2,1)}, u32[]{:S(2)}, u32[]{:S(2)}) collective-permute-start(bf16[512,1280]{1,0:T(8,128)(2,1)} %a_8_.3), channel_id=1, source_target_pairs={{0,4},{4,0},{8,12},{12,8},{1,5},{5,1},{9,13},{13,9},{2,6},{6,2},{1... | collective-permute-start | bytes 3932168 | tf_op jit(solution)/shard_map/ppermute | solution.py:130
  35.7 3.5 %collective-permute-start.7 = (s32[4]{0:T(128)S(1)}, s32[4]{0:T(128)S(1)}, u32[]{:S(2)}, u32[]{:S(2)}) collective-permute-start(s32[4]{0:T(128)S(1)} %fusion.3), channel_id=1, source_target_pairs={{0,8},{4,12},{8,0},{12,4},{1,9},{5,13},{9,1},{13,5},{2,10},{6,14},... | collective-permute-start | bytes 56 | tf_op jit(solution)/shard_map/ppermute | solution.py:127
  38.4 2.4 %copy-start.2 = (bf16[512,1280]{1,0:T(8,128)(2,1)}, bf16[512,1280]{1,0:T(8,128)(2,1)S(1)}, u32[]{:S(2)}) copy-start(bf16[512,1280]{1,0:T(8,128)(2,1)S(1)} %pad_maximum_fusion.a_1_) | copy-start | bytes 3932164
  39.3 30.3 %copy-start.4 = (s32[4]{0:T(128)}, s32[4]{0:T(128)S(1)}, u32[]{:S(2)}) copy-start(s32[4]{0:T(128)S(1)} %collective-permute-done.7.a_0_) | copy-start | bytes 52
  39.3 30.2 %collective-permute-start.8 = (bf16[512,1280]{1,0:T(8,128)(2,1)S(1)}, bf16[512,1280]{1,0:T(8,128)(2,1)}, u32[]{:S(2)}, u32[]{:S(2)}) collective-permute-start(bf16[512,1280]{1,0:T(8,128)(2,1)S(1)} %pad_maximum_fusion.a_1_), channel_id=1, source_target_pairs={{0,8},{4,12},{8,0},{12,4},{1,9},{5,13},{9,1},{13,5},{2,10},{6,14},... | collective-permute-start | bytes 3932168 | tf_op jit(solution)/shard_map/ppermute | solution.py:127
  126.1 67.8 %collective-permute-start.10 = (bf16[512,1280]{1,0:T(8,128)(2,1)}, bf16[512,1280]{1,0:T(8,128)(2,1)}, u32[]{:S(2)}, u32[]{:S(2)}) collective-permute-start(bf16[512,1280]{1,0:T(8,128)(2,1)} %get-tuple-element.12), channel_id=1, source_target_pairs={{0,8},{4,12},{8,0},{12,4},{1,9},{5,13},{9,1},{13,5},{2,10},{6,14},... | collective-permute-start | bytes 3932168 | tf_op jit(solution)/shard_map/ppermute | solution.py:164
  126.2 60.3 %collective-permute-start.9 = (f32[10,8,512]{2,1,0:T(8,128)}, f32[10,8,512]{2,1,0:T(8,128)S(1)}, u32[]{:S(2)}, u32[]{:S(2)}) collective-permute-start(f32[10,8,512]{2,1,0:T(8,128)} %get-tuple-element.11), channel_id=1, source_target_pairs={{0,8},{4,12},{8,0},{12,4},{1,9},{5,13},{9,1},{13,5},{2,10},{6,14},... | collective-permute-start | bytes 491528 | tf_op jit(solution)/shard_map/ppermute | solution.py:164
  199.3 9.8 %collective-permute-start.11 = (bf16[128,1280]{1,0:T(8,128)(2,1)S(1)}, bf16[128,1280]{1,0:T(8,128)(2,1)S(1)}, u32[]{:S(2)}, u32[]{:S(2)}) collective-permute-start(bf16[128,1280]{1,0:T(8,128)(2,1)S(1)} %get-tuple-element.20), channel_id=1, source_target_pairs={{0,3},{1,0},{2,1},{3,2},{4,7},{5,4},{6,5},{7,6},{8,11},{9,8},{10,9... | collective-permute-start | bytes 983048 | tf_op jit(solution)/shard_map/ppermute | solution.py:183
  199.4 27.2 %collective-permute-start.12 = (bf16[128,1280]{1,0:T(8,128)(2,1)S(1)}, bf16[128,1280]{1,0:T(8,128)(2,1)S(1)}, u32[]{:S(2)}, u32[]{:S(2)}) collective-permute-start(bf16[128,1280]{1,0:T(8,128)(2,1)S(1)} %get-tuple-element.19), channel_id=1, source_target_pairs={{0,2},{1,3},{2,0},{3,1},{4,6},{5,7},{6,4},{7,5},{8,10},{9,11},{10,... | collective-permute-start | bytes 983048 | tf_op jit(solution)/shard_map/ppermute | solution.py:183
  201.0 25.6 %collective-permute-start.13 = (bf16[128,1280]{1,0:T(8,128)(2,1)S(1)}, bf16[128,1280]{1,0:T(8,128)(2,1)S(1)}, u32[]{:S(2)}, u32[]{:S(2)}) collective-permute-start(bf16[128,1280]{1,0:T(8,128)(2,1)S(1)} %get-tuple-element.18), channel_id=1, source_target_pairs={{0,1},{1,2},{2,3},{3,0},{4,5},{5,6},{6,7},{7,4},{8,9},{9,10},{10,1... | collective-permute-start | bytes 983048 | tf_op jit(solution)/shard_map/ppermute | solution.py:183
  226.6 1.1 copy-start.3

commit v3 on v2

--- a/solution.py
+++ b/solution.py
@@ -16,37 +16,30 @@
     key_refs = refs[:nsrc]
     value_refs = refs[nsrc : 2 * nsrc]
     out_ref, lse_ref = refs[2 * nsrc : 2 * nsrc + 2]
-    score_ref, top_ref, total_ref, summed_ref = refs[2 * nsrc + 2 :]
+    score_ref = refs[2 * nsrc + 2]
     score_scale = 1.0 / math.sqrt(HEAD_DIM)
     query = q_ref[...]
-    top_ref[...] = jnp.full(top_ref.shape, -1e30, jnp.float32)
-    total_ref[...] = jnp.zeros(total_ref.shape, jnp.float32)
-    summed_ref[...] = jnp.zeros(summed_ref.shape, jnp.float32)
+    top = None
     for j in range(nsrc):
-
-        @pl.when(flags_ref[j] > 0)
-        def _():
-            scores = lax.dot_general(
-                query, key_refs[j][...], (((1,), (1,)), ((), ())), preferred_element_type=jnp.float32
-            ) * score_scale
-            score_ref[j] = scores
-            top_ref[...] = jnp.maximum(top_ref[...], jnp.max(scores, axis=1, keepdims=True))
-
+        scores = lax.dot_general(
+            query, key_refs[j][...], (((1,), (1,)), ((), ())), preferred_element_type=jnp.float32
+        ) * score_scale
+        scores = jnp.where(flags_ref[j] > 0, scores, -1e30)
+        score_ref[j] = scores
+        block_top = jnp.max(scores, axis=1, keepdims=True)
+        top = block_top if top is None else jnp.maximum(top, block_top)
+    total = None
+    summed = None
     for j in range(nsrc):
-
-        @pl.when(flags_ref[j] > 0)
-        def _():
-            weights = jnp.exp(score_ref[j] - top_ref[...])
-            total_ref[...] += jnp.sum(weights, axis=1, keepdims=True)
-            summed_ref[...] += jnp.dot(
-                weights.astype(jnp.bfloat16), value_refs[j][...], preferred_element_type=jnp.float32
-            )
-
-    total = total_ref[...]
-    filled = total > 0
-    safe = jnp.where(filled, total, 1.0)
-    out_ref[...] = jnp.where(filled, summed_ref[...] / safe, 0.0).astype(out_ref.dtype)
-    lse = jnp.where(filled, top_ref[...] + jnp.log(safe), -1e30)
+        weights = jnp.exp(score_ref[j] - top)
+        part_total = jnp.sum(weights, axis=1, keepdims=True)
+        product = jnp.dot(
+            weights.astype(jnp.bfloat16), value_refs[j][...], preferred_element_type=jnp.float32
+        )
+        total = part_total if total is None else total + part_total
+        summed = product if summed is None else summed + product
+    out_ref[...] = (summed / total).astype(out_ref.dtype)
+    lse = top + jnp.log(total)
     wide = jnp.broadcast_to(lse, (lse.shape[0], 128))
     lse_ref[...] = jnp.transpose(wide)[:STAT_ROWS]
 
@@ -65,12 +58,7 @@
         grid=(nheads, ROW_SPLIT),
         in_specs=[q_spec] + [kv_spec] * (2 * nsrc),
         out_specs=[q_spec, lse_spec],
-        scratch_shapes=[
-            pltpu.VMEM((nsrc, row_tile, block_rows), jnp.float32),
-            pltpu.VMEM((row_tile, 1), jnp.float32),
-            pltpu.VMEM((row_tile, 1), jnp.float32),
-            pltpu.VMEM((row_tile, HEAD_DIM), jnp.float32),
-        ],
+        scratch_shapes=[pltpu.VMEM((nsrc, row_tile, block_rows), jnp.float32)],
     )
     return pl.pallas_call(
         lambda *a: partial_kernel(nsrc, *a),
@@ -164,16 +152,13 @@
     far_out, far_lse = lax.ppermute((far_out, far_lse), "seq", forth)
 
     rows_all = query_block.shape[0]
-    lse_a = local_lse[:, 0, :].T[:, :, None]
-    lse_b = far_lse[:, 0, :].T[:, :, None]
+    lse_a = local_lse[:, 0, :].T
+    lse_b = far_lse[:, 0, :].T
     top = jnp.maximum(lse_a, lse_b)
-    weight_a = jnp.exp(lse_a - top)
-    weight_b = jnp.exp(lse_b - top)
-    mixed = (
-        local_out.reshape(rows_all, nheads, HEAD_DIM) * weight_a
-        + far_out.astype(jnp.float32).reshape(rows_all, nheads, HEAD_DIM) * weight_b
-    ) / (weight_a + weight_b)
-    heads_out = mixed.reshape(rows_all, head_width).astype(jnp.bfloat16)
+    weight_a = jnp.repeat(jnp.exp(lse_a - top), HEAD_DIM, axis=1)
+    weight_b = jnp.repeat(jnp.exp(lse_b - top), HEAD_DIM, axis=1)
+    mixed = (local_out * weight_a + far_out.astype(jnp.float32) * weight_b) / (weight_a + weight_b)
+    heads_out = mixed.astype(jnp.bfloat16)
 
     rows = queries.shape[0]
     result = jnp.zeros((rows, queries.shape[1]), jnp.bfloat16)

time: 229 us -> 173 us (0.76)
  Pallas kernels: 113 us -> 53.3 us
  starting transfers between devices: 15.2 us -> 21.8 us
  waiting for transfers between devices: 79.5 us -> 76.3 us
    pallas_call x2, Pallas kernels: 113 us -> 53.3 us  [attend_partial(): pl.pallas_call(lambda *a: partial_kernel(nsrc, *a), grid_spec=grid_spec,...]
    ppermute x3, waiting for transfers between devices: 26.3 us -> 19.4 us  [local(): lax.ppermute(piece, 'sp', [(i, (i + d) % sp_count) for i in range(sp_coun...]
    ppermute x3, starting transfers between devices: 3.59 us -> 9.21 us  [local(): lax.ppermute(piece, 'sp', [(i, (i - d) % sp_count) for i in range(sp_coun...]
    reshape x0 -> x2, local copies, waits for them, and re-layouts: none -> 5.4 us  [the longest x1 3.25 us: local(): weight_b = jnp.repeat(jnp.exp(lse_b - top), HEAD_DIM, axis=1)]
    mul x4 -> x0, local copies, waits for them, and re-layouts: 4.89 us -> none  [the longest x2 2.5 us: local(): local_out.reshape(rows_all, nheads, HEAD_DIM) * weight_a]
    broadcast_in_dim x0 -> x2, local copies, waits for them, and re-layouts: none -> 3.66 us  [the longest x1 1.86 us: local(): weight_a = jnp.repeat(jnp.exp(lse_a - top), HEAD_DIM, axis=1)]
    ppermute x2, waiting for transfers between devices: 0.01 us -> 2.54 us  [local(): far_out, far_lse = lax.ppermute((far_out, far_lse), 'seq', forth)]
    div x2 -> x0, local copies, waits for them, and re-layouts: 2.45 us -> none  [local(): (local_out.reshape(rows_all, nheads, HEAD_DIM) * weight_a + far_out.astyp...]
  transfers between devices with their start and end apart: 14 -> 14, of which waited for: 6 -> 7; matrix products, arithmetic and copies ran while one was open for 5% -> 7% of each run, Pallas kernels for 25% -> 16%
where the time goes in v3:
time: 173 us; the launch traced here: 172 us
  waiting for transfers between devices  76.3 us (44%)
  Pallas kernels  53.3 us (31%)
  starting transfers between devices  21.8 us (13%)
  local copies, waits for them, and re-layouts  14.6 us (8%)
  other arithmetic  5.72 us (3%)
    pallas_call x2, Pallas kernels, attend_partial(): pl.pallas_call(lambda *a: partial_kernel(nsrc, *a), grid_spec=grid_spec,...  53.3 us
    ppermute x2, waiting for transfers between devices, local(): lax.ppermute((query_block, remote_flags), 'seq', back)  29.5 us
    ppermute x3, waiting for transfers between devices, local(): lax.ppermute(piece, 'sp', [(i, (i - d) % sp_count) for i in range(sp_coun...  24.8 us
    ppermute x3, waiting for transfers between devices, local(): lax.ppermute(piece, 'sp', [(i, (i + d) % sp_count) for i in range(sp_coun...  19.4 us
    ppermute x3, starting transfers between devices, local(): lax.ppermute(piece, 'sp', [(i, (i - d) % sp_count) for i in range(sp_coun...  9.21 us
    ppermute x3, starting transfers between devices, local(): lax.ppermute(piece, 'sp', [(i, (i + d) % sp_count) for i in range(sp_coun...  6.98 us
    convert_element_type x1, other arithmetic, local(): heads_out = mixed.astype(jnp.bfloat16)  3.58 us
  transfers between devices with their start and end apart: 14, of which 7 were waited for; matrix products, arithmetic and copies ran while one was open for 7% of the time, Pallas kernels for 16%

profile of v3, /device:TPU:0, one launch (start us, length us, event | category | flops | bytes accessed | tf_op | source)
XLA Modules:
  0.0 171.9 jit_solution(2647485781581617576)
XLA Ops:
  0.0 2.4 %constant_dynamic-slice_fusion.3 = (bf16[128,1280]{1,0:T(8,128)(2,1)S(1)}, bf16[128,1280]{1,0:T(8,128)(2,1)}, bf16[128,1280]{1,0:T(8,128)(2,1)}, bf16[128,1280]{1,0:T(8,128)(2,1)}) fusion(bf16[128,5120]{1,0:T(8,128)(2,1)} %param.6, s32[]{:T(128)S(6)} %select_n.55, s32[]{:T(128)S(6)} %select_n.57, s32[]{:T(128)S(6)} %select_n.61, s32[]{:T(128)S(6)} %select_n.59), kind=kLoop, calls=%fused_computation.14 | loop fusion | bytes 2621456 | tf_op jit(solution)/shard_map/dynamic_slice | solution.py:91
  2.4 3.0 %collective-permute-start = (bf16[128,1280]{1,0:T(8,128)(2,1)}, bf16[128,1280]{1,0:T(8,128)(2,1)S(1)}, u32[]{:S(2)}, u32[]{:S(2)}) collective-permute-start(bf16[128,1280]{1,0:T(8,128)(2,1)} %get-tuple-element.20), channel_id=1, source_target_pairs={{0,1},{1,2},{2,3},{3,0},{4,5},{5,6},{6,7},{7,4},{8,9},{9,10},{10,1... | collective-permute-start | bytes 983048 | tf_op jit(solution)/shard_map/ppermute | solution.py:96
  5.4 2.6 %collective-permute-start.1 = (bf16[128,1280]{1,0:T(8,128)(2,1)}, bf16[128,1280]{1,0:T(8,128)(2,1)}, u32[]{:S(2)}, u32[]{:S(2)}) collective-permute-start(bf16[128,1280]{1,0:T(8,128)(2,1)} %get-tuple-element.22), channel_id=1, source_target_pairs={{0,2},{1,3},{2,0},{3,1},{4,6},{5,7},{6,4},{7,5},{8,10},{9,11},{10,... | collective-permute-start | bytes 983048 | tf_op jit(solution)/shard_map/ppermute | solution.py:96
  8.0 1.3 collective-permute-start.2
  9.4 0.5 collective-permute-start.4
  10.0 0.2 compare_reduce_fusion.1
  10.3 6.1 %collective-permute-done = bf16[128,1280]{1,0:T(8,128)(2,1)S(1)} collective-permute-done((bf16[128,1280]{1,0:T(8,128)(2,1)}, bf16[128,1280]{1,0:T(8,128)(2,1)S(1)}, u32[]{:S(2)}, u32[]{:S(2)}) %collective-permute-start) | collective-permute-done | bytes 327712 | tf_op jit(solution)/shard_map/ppermute | solution.py:96
  16.4 13.3 %collective-permute-done.1 = bf16[128,1280]{1,0:T(8,128)(2,1)} collective-permute-done((bf16[128,1280]{1,0:T(8,128)(2,1)}, bf16[128,1280]{1,0:T(8,128)(2,1)}, u32[]{:S(2)}, u32[]{:S(2)}) %collective-permute-start.1) | collective-permute-done | bytes 327712 | tf_op jit(solution)/shard_map/ppermute | solution.py:96
  29.7 1.5 collective-permute-start.7
  31.2 1.2 pad_maximum_fusion.a_1_
  32.4 0.9 collective-permute-done.7.a_0_
  33.2 1.5 collective-permute-start.8
  34.8 28.7 %collective-permute-done.8.a_1_ = bf16[512,1280]{1,0:T(8,128)(2,1)} collective-permute-done((bf16[512,1280]{1,0:T(8,128)(2,1)S(1)}, bf16[512,1280]{1,0:T(8,128)(2,1)}, u32[]{:S(2)}, u32[]{:S(2)}) %collective-permute-start.8) | collective-permute-done | bytes 1310752 | tf_op jit(solution)/shard_map/ppermute | solution.py:115
  63.5 26.6 %shard_map.65 = (bf16[512,1280]{1,0:T(8,128)(2,1)}, f32[10,8,512]{2,1,0:T(8,128)}) custom-call(s32[4]{0:T(128)} %copy-done.4, bf16[512,1280]{1,0:T(8,128)(2,1)} %collective-permute-done.8.a_1_, bf16[512,1280]{1,0:T(8,128)(2,1)} %a_2_.3, bf16[512,1280]{1,0:T(8,128)(2,1)} %collective-permute-done.3.a_3_, bf16[512,1280]{1,0:T(8,128)(2,1)} %a_4_.3, ...), custom_call_target="tpu_custom_call" | custom-call | tf_op jit(solution)/shard_map/pallas_call | solution.py:63
  90.0 1.5 collective-permute-start.10
  91.5 0.6 collective-permute-start.9
  92.1 0.6 fusion.2.a_0_
  92.7 26.8 %shard_map.64 = (f32[512,1280]{1,0:T(8,128)}, f32[10,8,512]{2,1,0:T(8,128)}) custom-call(s32[4]{0:T(128)} %fusion.2.a_0_, bf16[512,1280]{1,0:T(8,128)(2,1)} %copy-done.2, bf16[512,1280]{1,0:T(8,128)(2,1)} %a_2_.3, bf16[512,1280]{1,0:T(8,128)(2,1)} %collective-permute-done.3.a_3_, bf16[512,1280]{1,0:T(8,128)(2,1)} %a_4_.3, ...), custom_call_target="tpu_custom_call" | custom-call | tf_op jit(solution)/shard_map/pallas_call | solution.py:63
  119.5 1.0 copy.15
  120.5 2.5 %collective-permute-done.9 = f32[10,8,512]{2,1,0:T(8,128)S(1)} collective-permute-done((f32[10,8,512]{2,1,0:T(8,128)}, f32[10,8,512]{2,1,0:T(8,128)S(1)}, u32[]{:S(2)}, u32[]{:S(2)}) %collective-permute-start.9) | collective-permute-done | bytes 163872 | tf_op jit(solution)/shard_map/ppermute | solution.py:152
  123.1 1.9 %broadcast_in_dim.12 = f32[512,10,128]{0,2,1:T(8,128)} broadcast(f32[512,10]{0,1:T(8,128)S(1)} %get-tuple-element.24), dimensions={0,1} | broadcast | bytes 2641920 | tf_op jit(solution)/shard_map/broadcast_in_dim | solution.py:158
  124.9 2.1 %copy.16 = f32[512,1280]{1,0:T(8,128)S(1)} copy(f32[512,1280]{0,1:T(8,128)} %bitcast.28) | data formatting | bytes 5242880 | tf_op jit(solution)/shard_map/reshape | solution.py:158
  127.1 1.8 %broadcast_in_dim.13 = f32[512,10,128]{0,2,1:T(8,128)} broadcast(f32[512,10]{0,1:T(8,128)S(1)} %get-tuple-element.23), dimensions={0,1} | broadcast | bytes 2641920 | tf_op jit(solution)/shard_map/broadcast_in_dim | solution.py:159
  128.9 3.2 %copy.17 = f32[512,1280]{1,0:T(8,128)} copy(f32[512,1280]{0,1:T(8,128)} %bitcast.29) | data formatting | bytes 5242880 | tf_op jit(solution)/shard_map/reshape | solution.py:159
  132.1 3.6 %divide_convert_fusion = bf16[512,1280]{1,0:T(8,128)(2,1)S(1)} fusion(f32[512,1280]{1,0:T(8,128)S(1)} %copy.16, f32[512,1280]{1,0:T(8,128)} %copy.17, bf16[512,1280]{1,0:T(8,128)(2,1)} %collective-permute-done.10, f32[512,1280]{1,0:T(8,128)} %get-tuple-element.9), kind=kLoop, calls=%fused_computation | loop fusion | flops 4587520 | bytes 10485760 | tf_op jit(solution)/shard_map/convert_element_type | solution.py:161
  135.7 0.1 broadcast_in_dim.11
  136.0 8.6 %collective-permute-start.11 = (bf16[128,1280]{1,0:T(8,128)(2,1)S(1)}, bf16[128,1280]{1,0:T(8,128)(2,1)S(1)}, u32[]{:S(2)}, u32[]{:S(2)}) collective-permute-start(bf16[128,1280]{1,0:T(8,128)(2,1)S(1)} %get-tuple-element.17), channel_id=1, source_target_pairs={{0,3},{1,0},{2,1},{3,2},{4,7},{5,4},{6,5},{7,6},{8,11},{9,8},{10,9... | collective-permute-start | bytes 983048 | tf_op jit(solution)/shard_map/ppermute | solution.py:168
  144.5 0.6 collective-permute-start.13
  145.2 7.5 %collective-permute-done.11 = bf16[128,1280]{1,0:T(8,128)(2,1)S(1)} collective-permute-done((bf16[128,1280]{1,0:T(8,128)(2,1)S(1)}, bf16[128,1280]{1,0:T(8,128)(2,1)S(1)}, u32[]{:S(2)}, u32[]{:S(2)}) %collective-permute-start.11) | collective-permute-done | bytes 327712 | tf_op jit(solution)/shard_map/ppermute | solution.py:168
  152.7 17.3 %collective-permute-done.12 = bf16[128,1280]{1,0:T(8,128)(2,1)S(1)} collective-permute-done((bf16[128,1280]{1,0:T(8,128)(2,1)S(1)}, bf16[128,1280]{1,0:T(8,128)(2,1)S(1)}, u32[]{:S(2)}, u32[]{:S(2)}) %collective-permute-start.12) | collective-permute-done | bytes 327712 | tf_op jit(solution)/shard_map/ppermute | solution.py:168
  170.1 1.0 copy-done.3
  171.1 0.7 constant_dynamic-update-slice_fusion
  (29 shorter events, 0.4 us)
Async XLA Ops:
  0.0 9.4 %copy-start = (bf16[512,1280]{1,0:T(8,128)(2,1)S(1)}, bf16[512,1280]{1,0:T(8,128)(2,1)}, u32[]{:S(2)}) copy-start(bf16[512,1280]{1,0:T(8,128)(2,1)} %a_2_.3) | copy-start | bytes 3932164
  0.0 9.4 %copy-start.1 = (bf16[512,1280]{1,0:T(8,128)(2,1)S(1)}, bf16[512,1280]{1,0:T(8,128)(2,1)}, u32[]{:S(2)}) copy-start(bf16[512,1280]{1,0:T(8,128)(2,1)} %a_4_.3) | copy-start | bytes 3932164
  0.0 10.0 %copy-start.5 = (s32[1,6]{1,0:T(1,128)S(1)}, s32[1,6]{1,0:T(1,128)}, u32[]{:S(2)}) copy-start(s32[1,6]{1,0:T(1,128)} %param.11) | copy-start | bytes 76
  2.4 14.0 %collective-permute-start = (bf16[128,1280]{1,0:T(8,128)(2,1)}, bf16[128,1280]{1,0:T(8,128)(2,1)S(1)}, u32[]{:S(2)}, u32[]{:S(2)}) collective-permute-start(bf16[128,1280]{1,0:T(8,128)(2,1)} %get-tuple-element.20), channel_id=1, source_target_pairs={{0,1},{1,2},{2,3},{3,0},{4,5},{5,6},{6,7},{7,4},{8,9},{9,10},{10,1... | collective-permute-start | bytes 983048 | tf_op jit(solution)/shard_map/ppermute | solution.py:96
  5.4 24.2 %collective-permute-start.1 = (bf16[128,1280]{1,0:T(8,128)(2,1)}, bf16[128,1280]{1,0:T(8,128)(2,1)}, u32[]{:S(2)}, u32[]{:S(2)}) collective-permute-start(bf16[128,1280]{1,0:T(8,128)(2,1)} %get-tuple-element.22), channel_id=1, source_target_pairs={{0,2},{1,3},{2,0},{3,1},{4,6},{5,7},{6,4},{7,5},{8,10},{9,11},{10,... | collective-permute-start | bytes 983048 | tf_op jit(solution)/shard_map/ppermute | solution.py:96
  8.0 21.6 %collective-permute-start.2 = (bf16[128,1280]{1,0:T(8,128)(2,1)}, bf16[128,1280]{1,0:T(8,128)(2,1)}, u32[]{:S(2)}, u32[]{:S(2)}) collective-permute-start(bf16[128,1280]{1,0:T(8,128)(2,1)} %get-tuple-element.21), channel_id=1, source_target_pairs={{0,3},{1,0},{2,1},{3,2},{4,7},{5,4},{6,5},{7,6},{8,11},{9,8},{10,9... | collective-permute-start | bytes 983048 | tf_op jit(solution)/shard_map/ppermute | solution.py:96
  9.4 25.4 %collective-permute-start.3 = (bf16[512,1280]{1,0:T(8,128)(2,1)S(1)}, bf16[512,1280]{1,0:T(8,128)(2,1)}, u32[]{:S(2)}, u32[]{:S(2)}) collective-permute-start(bf16[512,1280]{1,0:T(8,128)(2,1)S(1)} %copy-done), channel_id=1, source_target_pairs={{0,4},{4,0},{8,12},{12,8},{1,5},{5,1},{9,13},{13,9},{2,6},{6,2},{1... | collective-permute-start | bytes 3932168 | tf_op jit(solution)/shard_map/ppermute | solution.py:118
  9.4 25.4 %collective-permute-start.4 = (bf16[512,1280]{1,0:T(8,128)(2,1)S(1)}, bf16[512,1280]{1,0:T(8,128)(2,1)}, u32[]{:S(2)}, u32[]{:S(2)}) collective-permute-start(bf16[512,1280]{1,0:T(8,128)(2,1)S(1)} %copy-done.1), channel_id=1, source_target_pairs={{0,4},{4,0},{8,12},{12,8},{1,5},{5,1},{9,13},{13,9},{2,6},{6,2},{1... | collective-permute-start | bytes 3932168 | tf_op jit(solution)/shard_map/ppermute | solution.py:118
  16.4 18.4 %collective-permute-start.5 = (bf16[512,1280]{1,0:T(8,128)(2,1)}, bf16[512,1280]{1,0:T(8,128)(2,1)}, u32[]{:S(2)}, u32[]{:S(2)}) collective-permute-start(bf16[512,1280]{1,0:T(8,128)(2,1)} %a_6_.3), channel_id=1, source_target_pairs={{0,4},{4,0},{8,12},{12,8},{1,5},{5,1},{9,13},{13,9},{2,6},{6,2},{1... | collective-permute-start | bytes 3932168 | tf_op jit(solution)/shard_map/ppermute | solution.py:118
  29.7 5.1 %collective-permute-start.6 = (bf16[512,1280]{1,0:T(8,128)(2,1)}, bf16[512,1280]{1,0:T(8,128)(2,1)}, u32[]{:S(2)}, u32[]{:S(2)}) collective-permute-start(bf16[512,1280]{1,0:T(8,128)(2,1)} %a_8_.3), channel_id=1, source_target_pairs={{0,4},{4,0},{8,12},{12,8},{1,5},{5,1},{9,13},{13,9},{2,6},{6,2},{1... | collective-permute-start | bytes 3932168 | tf_op jit(solution)/shard_map/ppermute | solution.py:118
  29.7 3.5 %collective-permute-start.7 = (s32[4]{0:T(128)S(1)}, s32[4]{0:T(128)S(1)}, u32[]{:S(2)}, u32[]{:S(2)}) collective-permute-start(s32[4]{0:T(128)S(1)} %fusion.3), channel_id=1, source_target_pairs={{0,8},{4,12},{8,0},{12,4},{1,9},{5,13},{9,1},{13,5},{2,10},{6,14},... | collective-permute-start | bytes 56 | tf_op jit(solution)/shard_map/ppermute | solution.py:115
  32.4 2.4 %copy-start.2 = (bf16[512,1280]{1,0:T(8,128)(2,1)}, bf16[512,1280]{1,0:T(8,128)(2,1)S(1)}, u32[]{:S(2)}) copy-start(bf16[512,1280]{1,0:T(8,128)(2,1)S(1)} %pad_maximum_fusion.a_1_) | copy-start | bytes 3932164
  33.2 30.3 %copy-start.4 = (s32[4]{0:T(128)}, s32[4]{0:T(128)S(1)}, u32[]{:S(2)}) copy-start(s32[4]{0:T(128)S(1)} %collective-permute-done.7.a_0_) | copy-start | bytes 52
  33.2 30.2 %collective-permute-start.8 = (bf16[512,1280]{1,0:T(8,128)(2,1)S(1)}, bf16[512,1280]{1,0:T(8,128)(2,1)}, u32[]{:S(2)}, u32[]{:S(2)}) collective-permute-start(bf16[512,1280]{1,0:T(8,128)(2,1)S(1)} %pad_maximum_fusion.a_1_), channel_id=1, source_target_pairs={{0,8},{4,12},{8,0},{12,4},{1,9},{5,13},{9,1},{13,5},{2,10},{6,14},... | collective-permute-start | bytes 3932168 | tf_op jit(solution)/shard_map/ppermute | solution.py:115
  90.0 42.1 %collective-permute-start.10 = (bf16[512,1280]{1,0:T(8,128)(2,1)}, bf16[512,1280]{1,0:T(8,128)(2,1)}, u32[]{:S(2)}, u32[]{:S(2)}) collective-permute-start(bf16[512,1280]{1,0:T(8,128)(2,1)} %get-tuple-element.12), channel_id=1, source_target_pairs={{0,8},{4,12},{8,0},{12,4},{1,9},{5,13},{9,1},{13,5},{2,10},{6,14},... | collective-permute-start | bytes 3932168 | tf_op jit(solution)/shard_map/ppermute | solution.py:152
  91.5 31.5 %collective-permute-start.9 = (f32[10,8,512]{2,1,0:T(8,128)}, f32[10,8,512]{2,1,0:T(8,128)S(1)}, u32[]{:S(2)}, u32[]{:S(2)}) collective-permute-start(f32[10,8,512]{2,1,0:T(8,128)} %get-tuple-element.11), channel_id=1, source_target_pairs={{0,8},{4,12},{8,0},{12,4},{1,9},{5,13},{9,1},{13,5},{2,10},{6,14},... | collective-permute-start | bytes 491528 | tf_op jit(solution)/shard_map/ppermute | solution.py:152
  136.0 16.7 %collective-permute-start.11 = (bf16[128,1280]{1,0:T(8,128)(2,1)S(1)}, bf16[128,1280]{1,0:T(8,128)(2,1)S(1)}, u32[]{:S(2)}, u32[]{:S(2)}) collective-permute-start(bf16[128,1280]{1,0:T(8,128)(2,1)S(1)} %get-tuple-element.17), channel_id=1, source_target_pairs={{0,3},{1,0},{2,1},{3,2},{4,7},{5,4},{6,5},{7,6},{8,11},{9,8},{10,9... | collective-permute-start | bytes 983048 | tf_op jit(solution)/shard_map/ppermute | solution.py:168
  144.5 25.5 %collective-permute-start.12 = (bf16[128,1280]{1,0:T(8,128)(2,1)S(1)}, bf16[128,1280]{1,0:T(8,128)(2,1)S(1)}, u32[]{:S(2)}, u32[]{:S(2)}) collective-permute-start(bf16[128,1280]{1,0:T(8,128)(2,1)S(1)} %get-tuple-element.16), channel_id=1, source_target_pairs={{0,2},{1,3},{2,0},{3,1},{4,6},{5,7},{6,4},{7,5},{8,10},{9,11},{10,... | collective-permute-start | bytes 983048 | tf_op jit(solution)/shard_map/ppermute | solution.py:168
  144.5 25.6 %collective-permute-start.13 = (bf16[128,1280]{1,0:T(8,128)(2,1)S(1)}, bf16[128,1280]{1,0:T(8,128)(2,1)S(1)}, u32[]{:S(2)}, u32[]{:S(2)}) collective-permute-start(bf16[128,1280]{1,0:T(8,128)(2,1)S(1)} %get-tuple-element.15), channel_id=1, source_target_pairs={{0,1},{1,2},{2,3},{3,0},{4,5},{5,6},{6,7},{7,4},{8,9},{9,10},{10,1... | collective-permute-start | bytes 983048 | tf_op jit(solution)/shard_map/ppermute | solution.py:168
  170.1 1.1 copy-start.3

commit v4 on v3

--- a/solution.py
+++ b/solution.py
@@ -8,7 +8,7 @@
 from jax.sharding import PartitionSpec as P
 
 HEAD_DIM = 128
-ROW_SPLIT = 2
+ROW_SPLIT = 1
 STAT_ROWS = 8
 
 
@@ -88,15 +88,7 @@
     other = s ^ 1
     listed = sources[0]
 
-    query_parts = [lax.dynamic_slice_in_dim(queries, sp_place * head_width, head_width, 1)]
-    for d in range(1, sp_count):
-        columns = ((sp_place + d) % sp_count) * head_width
-        piece = lax.dynamic_slice_in_dim(queries, columns, head_width, 1)
-        query_parts.append(
-            lax.ppermute(piece, "sp", [(i, (i + d) % sp_count) for i in range(sp_count)])
-        )
-    query_block = jnp.concatenate(query_parts, axis=0)
-
+    rows = queries.shape[0]
     back = [(i, (i - 2) % seq_count) for i in range(seq_count)]
     forth = [(i, (i + 2) % seq_count) for i in range(seq_count)]
     t = (s - 2) % seq_count
@@ -112,7 +104,7 @@
         remote_ids += [t % 2, 1 - t % 2]
         remote_valid += [(t_chip >= 1) & (t_chip <= chips - 2)] * 2
     remote_flags = membership(listed, remote_ids, remote_valid)
-    got_query, got_flags = lax.ppermute((query_block, remote_flags), "seq", back)
+    got_flags = lax.ppermute(remote_flags, "seq", back)
 
     swap = [(i, i ^ 1) for i in range(seq_count)]
     partner_k, partner_v, partner_ck, partner_cv = lax.ppermute(
@@ -146,24 +138,28 @@
         [seq_count + s, seq_count + other, s, other],
         [s >= 0, s >= 0, chip == 0, chip == 0],
     )
-    local_out, local_lse = attend_partial(local_flags, query_block, keys, values, jnp.float32)
 
-    far_out, far_lse = attend_partial(got_flags, got_query, remote_keys, remote_values, jnp.bfloat16)
-    far_out, far_lse = lax.ppermute((far_out, far_lse), "seq", forth)
-
-    rows_all = query_block.shape[0]
-    lse_a = local_lse[:, 0, :].T
-    lse_b = far_lse[:, 0, :].T
-    top = jnp.maximum(lse_a, lse_b)
-    weight_a = jnp.repeat(jnp.exp(lse_a - top), HEAD_DIM, axis=1)
-    weight_b = jnp.repeat(jnp.exp(lse_b - top), HEAD_DIM, axis=1)
-    mixed = (local_out * weight_a + far_out.astype(jnp.float32) * weight_b) / (weight_a + weight_b)
-    heads_out = mixed.astype(jnp.bfloat16)
-
-    rows = queries.shape[0]
     result = jnp.zeros((rows, queries.shape[1]), jnp.bfloat16)
     for d in range(sp_count):
-        piece = heads_out[d * rows : (d + 1) * rows]
+        columns = ((sp_place + d) % sp_count) * head_width
+        chunk = lax.dynamic_slice_in_dim(queries, columns, head_width, 1)
+        if d:
+            chunk = lax.ppermute(chunk, "sp", [(i, (i + d) % sp_count) for i in range(sp_count)])
+        got_chunk = lax.ppermute(chunk, "seq", back)
+        local_out, local_lse = attend_partial(local_flags, chunk, keys, values, jnp.float32)
+        far_out, far_lse = attend_partial(
+            got_flags, got_chunk, remote_keys, remote_values, jnp.bfloat16
+        )
+        far_out, far_lse = lax.ppermute((far_out, far_lse), "seq", forth)
+        lse_a = local_lse[:, 0, :].T
+        lse_b = far_lse[:, 0, :].T
+        top = jnp.maximum(lse_a, lse_b)
+        weight_a = jnp.repeat(jnp.exp(lse_a - top), HEAD_DIM, axis=1)
+        weight_b = jnp.repeat(jnp.exp(lse_b - top), HEAD_DIM, axis=1)
+        mixed = (local_out * weight_a + far_out.astype(jnp.float32) * weight_b) / (
+            weight_a + weight_b
+        )
+        piece = mixed.astype(jnp.bfloat16)
         if d:
             piece = lax.ppermute(piece, "sp", [(i, (i - d) % sp_count) for i in range(sp_count)])
         columns = ((sp_place + d) % sp_count) * head_width

time: 173 us -> 206 us (1.19)
  the two profiles are of different devices: /device:TPU:0 before, /device:TPU:8 now
where the time goes in v4:
time: 206 us; the launch traced here: 203 us
  Pallas kernels  98.4 us (48%)
  waiting for transfers between devices  51.9 us (25%)
  starting transfers between devices  28 us (14%)
  local copies, waits for them, and re-layouts  18.2 us (9%)
  other arithmetic  6.2 us (3%)
    pallas_call x8, Pallas kernels, attend_partial(): pl.pallas_call(lambda *a: partial_kernel(nsrc, *a), grid_spec=grid_spec,...  98.4 us
    ppermute x3, waiting for transfers between devices, local(): lax.ppermute(chunk, 'sp', [(i, (i + d) % sp_count) for i in range(sp_coun...  25.9 us
    ppermute x3, waiting for transfers between devices, local(): lax.ppermute(piece, 'sp', [(i, (i - d) % sp_count) for i in range(sp_coun...  15.9 us
    ppermute x8, starting transfers between devices, local(): far_out, far_lse = lax.ppermute((far_out, far_lse), 'seq', forth)  8.6 us
    ppermute x3, starting transfers between devices, local(): lax.ppermute(piece, 'sp', [(i, (i - d) % sp_count) for i in range(sp_coun...  6.85 us
    ppermute x4, waiting for transfers between devices, local(): got_chunk = lax.ppermute(chunk, 'seq', back)  6.64 us
    ppermute x4, starting transfers between devices, local(): got_chunk = lax.ppermute(chunk, 'seq', back)  5.07 us
    ppermute x3, starting transfers between devices, local(): lax.ppermute(chunk, 'sp', [(i, (i + d) % sp_count) for i in range(sp_coun...  5.05 us
  transfers between devices with their start and end apart: 23, of which 7 were waited for; matrix products, arithmetic and copies ran while one was open for 10% of the time, Pallas kernels for 48%

profile of v4, /device:TPU:8, one launch (start us, length us, event | category | flops | bytes accessed | tf_op | source)
XLA Modules:
  0.0 203.1 jit_solution(10398578755093526432)
XLA Ops:
  0.0 2.4 %constant_dynamic-slice_fusion = (bf16[128,1280]{1,0:T(8,128)(2,1)}, bf16[128,1280]{1,0:T(8,128)(2,1)}, bf16[128,1280]{1,0:T(8,128)(2,1)S(1)}, bf16[128,1280]{1,0:T(8,128)(2,1)}) fusion(bf16[128,5120]{1,0:T(8,128)(2,1)} %param.6, s32[]{:T(128)S(6)} %select_n.64, s32[]{:T(128)S(6)} %select_n.60, s32[]{:T(128)S(6)} %select_n.56, s32[]{:T(128)S(6)} %select_n.62), kind=kLoop, calls=%fused_computation.26 | loop fusion | bytes 2621456 | tf_op jit(solution)/shard_map/dynamic_slice | solution.py:145
  3.4 1.9 collective-permute-start.4
  5.3 1.6 collective-permute-done.4.a_0_
  6.9 5.1 %collective-permute-done.18.a_1_ = bf16[128,1280]{1,0:T(8,128)(2,1)S(1)} collective-permute-done((bf16[128,1280]{1,0:T(8,128)(2,1)}, bf16[128,1280]{1,0:T(8,128)(2,1)S(1)}, u32[]{:S(2)}, u32[]{:S(2)}) %collective-permute-start.18) | collective-permute-done | bytes 327712 | tf_op jit(solution)/shard_map/ppermute | solution.py:147
  12.1 4.4 %collective-permute-start.13 = (bf16[128,1280]{1,0:T(8,128)(2,1)}, bf16[128,1280]{1,0:T(8,128)(2,1)}, u32[]{:S(2)}, u32[]{:S(2)}) collective-permute-start(bf16[128,1280]{1,0:T(8,128)(2,1)} %get-tuple-element.42), channel_id=1, source_target_pairs={{0,2},{1,3},{2,0},{3,1},{4,6},{5,7},{6,4},{7,5},{8,10},{9,11},{10,... | collective-permute-start | bytes 983048 | tf_op jit(solution)/shard_map/ppermute | solution.py:147
  16.5 11.5 %collective-permute-done.13.a_1_ = bf16[128,1280]{1,0:T(8,128)(2,1)} collective-permute-done((bf16[128,1280]{1,0:T(8,128)(2,1)}, bf16[128,1280]{1,0:T(8,128)(2,1)}, u32[]{:S(2)}, u32[]{:S(2)}) %collective-permute-start.13) | collective-permute-done | bytes 327712 | tf_op jit(solution)/shard_map/ppermute | solution.py:147
  28.7 9.3 %collective-permute-done.8.a_1_ = bf16[128,1280]{1,0:T(8,128)(2,1)} collective-permute-done((bf16[128,1280]{1,0:T(8,128)(2,1)}, bf16[128,1280]{1,0:T(8,128)(2,1)}, u32[]{:S(2)}, u32[]{:S(2)}) %collective-permute-start.8) | collective-permute-done | bytes 327712 | tf_op jit(solution)/shard_map/ppermute | solution.py:147
  38.0 1.5 collective-permute-start.19
  39.5 6.6 %collective-permute-done.19.a_1_ = bf16[128,1280]{1,0:T(8,128)(2,1)S(1)} collective-permute-done((bf16[128,1280]{1,0:T(8,128)(2,1)S(1)}, bf16[128,1280]{1,0:T(8,128)(2,1)S(1)}, u32[]{:S(2)}, u32[]{:S(2)}) %collective-permute-start.19) | collective-permute-done | bytes 327712 | tf_op jit(solution)/shard_map/ppermute | solution.py:148
  46.1 1.5 collective-permute-start.14
  48.1 1.5 collective-permute-start.5
  49.7 12.3 %shard_map.71 = (bf16[128,1280]{1,0:T(8,128)(2,1)}, f32[10,8,128]{2,1,0:T(8,128)}) custom-call(s32[4]{0:T(128)} %copy-done.13, bf16[128,1280]{1,0:T(8,128)(2,1)} %copy-done.12, bf16[512,1280]{1,0:T(8,128)(2,1)} %a_2_.15, bf16[512,1280]{1,0:T(8,128)(2,1)} %collective-permute-done.a_3_, bf16[512,1280]{1,0:T(8,128)(2,1)} %a_4_.15, ...), custom_call_target="tpu_custom_call" | custom-call | tf_op jit(solution)/shard_map/pallas_call | solution.py:63
  63.2 12.3 %shard_map.70 = (f32[128,1280]{1,0:T(8,128)}, f32[10,8,128]{2,1,0:T(8,128)}) custom-call(s32[4]{0:T(128)} %fusion.9.a_0_, bf16[128,1280]{1,0:T(8,128)(2,1)} %copy-done.9, bf16[512,1280]{1,0:T(8,128)(2,1)} %a_2_.15, bf16[512,1280]{1,0:T(8,128)(2,1)} %collective-permute-done.a_3_, bf16[512,1280]{1,0:T(8,128)(2,1)} %a_4_.15, ...), custom_call_target="tpu_custom_call" | custom-call | tf_op jit(solution)/shard_map/pallas_call | solution.py:63
  76.3 1.6 collective-permute-start.21
  77.9 12.3 %shard_map.69 = (bf16[128,1280]{1,0:T(8,128)(2,1)}, f32[10,8,128]{2,1,0:T(8,128)}) custom-call(s32[4]{0:T(128)} %copy-done.13, bf16[128,1280]{1,0:T(8,128)(2,1)} %collective-permute-done.14.a_1_, bf16[512,1280]{1,0:T(8,128)(2,1)} %a_2_.15, bf16[512,1280]{1,0:T(8,128)(2,1)} %collective-permute-done.a_3_, bf16[512,1280]{1,0:T(8,128)(2,1)} %a_4_.15, ...), custom_call_target="tpu_custom_call" | custom-call | tf_op jit(solution)/shard_map/pallas_call | solution.py:63
  90.7 12.3 %shard_map.68 = (f32[128,1280]{1,0:T(8,128)}, f32[10,8,128]{2,1,0:T(8,128)}) custom-call(s32[4]{0:T(128)} %fusion.9.a_0_, bf16[128,1280]{1,0:T(8,128)(2,1)} %collective-permute-done.13.a_1_, bf16[512,1280]{1,0:T(8,128)(2,1)} %a_2_.15, bf16[512,1280]{1,0:T(8,128)(2,1)} %collective-permute-done.a_3_, bf16[512,1280]{1,0:T(8,128)(2,1)} %a_4_.15, ...), custom_call_target="tpu_custom_call" | custom-call | tf_op jit(solution)/shard_map/pallas_call | solution.py:63
  103.8 12.3 %shard_map.66 = (f32[128,1280]{1,0:T(8,128)}, f32[10,8,128]{2,1,0:T(8,128)}) custom-call(s32[4]{0:T(128)} %fusion.9.a_0_, bf16[128,1280]{1,0:T(8,128)(2,1)} %collective-permute-done.8.a_1_, bf16[512,1280]{1,0:T(8,128)(2,1)} %a_2_.15, bf16[512,1280]{1,0:T(8,128)(2,1)} %collective-permute-done.a_3_, bf16[512,1280]{1,0:T(8,128)(2,1)} %a_4_.15, ...), custom_call_target="tpu_custom_call" | custom-call | tf_op jit(solution)/shard_map/pallas_call | solution.py:63
  116.9 12.3 %shard_map.64 = (f32[128,1280]{1,0:T(8,128)}, f32[10,8,128]{2,1,0:T(8,128)}) custom-call(s32[4]{0:T(128)} %fusion.9.a_0_, bf16[128,1280]{1,0:T(8,128)(2,1)} %copy-done.4, bf16[512,1280]{1,0:T(8,128)(2,1)} %a_2_.15, bf16[512,1280]{1,0:T(8,128)(2,1)} %collective-permute-done.a_3_, bf16[512,1280]{1,0:T(8,128)(2,1)} %a_4_.15, ...), custom_call_target="tpu_custom_call" | custom-call | tf_op jit(solution)/shard_map/pallas_call | solution.py:63
  130.1 1.6 collective-permute-start.16
  131.6 12.2 %shard_map.67 = (bf16[128,1280]{1,0:T(8,128)(2,1)}, f32[10,8,128]{2,1,0:T(8,128)}) custom-call(s32[4]{0:T(128)} %copy-done.13, bf16[128,1280]{1,0:T(8,128)(2,1)} %copy-done.11, bf16[512,1280]{1,0:T(8,128)(2,1)} %a_2_.15, bf16[512,1280]{1,0:T(8,128)(2,1)} %collective-permute-done.a_3_, bf16[512,1280]{1,0:T(8,128)(2,1)} %a_4_.15, ...), custom_call_target="tpu_custom_call" | custom-call | tf_op jit(solution)/shard_map/pallas_call | solution.py:63
  144.7 12.3 %shard_map.65 = (bf16[128,1280]{1,0:T(8,128)(2,1)}, f32[10,8,128]{2,1,0:T(8,128)}) custom-call(s32[4]{0:T(128)} %copy-done.13, bf16[128,1280]{1,0:T(8,128)(2,1)} %copy-done.10, bf16[512,1280]{1,0:T(8,128)(2,1)} %a_2_.15, bf16[512,1280]{1,0:T(8,128)(2,1)} %collective-permute-done.a_3_, bf16[512,1280]{1,0:T(8,128)(2,1)} %a_4_.15, ...), custom_call_target="tpu_custom_call" | custom-call | tf_op jit(solution)/shard_map/pallas_call | solution.py:63
  156.9 1.4 collective-permute-start.11
  159.2 1.4 collective-permute-start.7
  163.8 1.3 copy.46
  165.1 1.8 collective-permute-done.6
  167.8 2.2 %copy.40 = f32[128,1280]{1,0:T(8,128)} copy(f32[128,1280]{0,1:T(8,128)} %bitcast.79) | data formatting | bytes 1310720 | tf_op jit(solution)/shard_map/reshape | solution.py:157
  170.9 2.2 %copy.41 = f32[128,1280]{1,0:T(8,128)} copy(f32[128,1280]{0,1:T(8,128)} %bitcast.80) | data formatting | bytes 1310720 | tf_op jit(solution)/shard_map/reshape | solution.py:158
  173.1 1.6 divide_convert_fusion
  174.7 2.8 %collective-permute-start.22 = (bf16[128,1280]{1,0:T(8,128)(2,1)S(1)}, bf16[128,1280]{1,0:T(8,128)(2,1)S(1)}, u32[]{:S(2)}, u32[]{:S(2)}) collective-permute-start(bf16[128,1280]{1,0:T(8,128)(2,1)S(1)} %divide_convert_fusion), channel_id=1, source_target_pairs={{0,1},{1,2},{2,3},{3,0},{4,5},{5,6},{6,7},{7,4},{8,9},{9,10},{10,1... | collective-permute-start | bytes 983048 | tf_op jit(solution)/shard_map/ppermute | solution.py:164
  178.7 2.0 %collective-permute-start.17 = (bf16[128,1280]{1,0:T(8,128)(2,1)S(1)}, bf16[128,1280]{1,0:T(8,128)(2,1)S(1)}, u32[]{:S(2)}, u32[]{:S(2)}) collective-permute-start(bf16[128,1280]{1,0:T(8,128)(2,1)S(1)} %divide_convert_fusion.1), channel_id=1, source_target_pairs={{0,2},{1,3},{2,0},{3,1},{4,6},{5,7},{6,4},{7,5},{8,10},{9,11},{10,... | collective-permute-start | bytes 983048 | tf_op jit(solution)/shard_map/ppermute | solution.py:164
  181.9 2.0 %collective-permute-start.12 = (bf16[128,1280]{1,0:T(8,128)(2,1)S(1)}, bf16[128,1280]{1,0:T(8,128)(2,1)S(1)}, u32[]{:S(2)}, u32[]{:S(2)}) collective-permute-start(bf16[128,1280]{1,0:T(8,128)(2,1)S(1)} %divide_convert_fusion.2), channel_id=1, source_target_pairs={{0,3},{1,0},{2,1},{3,2},{4,7},{5,4},{6,5},{7,6},{8,11},{9,8},{10,9... | collective-permute-start | bytes 983048 | tf_op jit(solution)/shard_map/ppermute | solution.py:164
  185.3 15.9 %collective-permute-done.12 = bf16[128,1280]{1,0:T(8,128)(2,1)S(1)} collective-permute-done((bf16[128,1280]{1,0:T(8,128)(2,1)S(1)}, bf16[128,1280]{1,0:T(8,128)(2,1)S(1)}, u32[]{:S(2)}, u32[]{:S(2)}) %collective-permute-start.12) | collective-permute-done | bytes 327712 | tf_op jit(solution)/shard_map/ppermute | solution.py:164
  (93 shorter events, 19.1 us)
Async XLA Ops:
  0.0 2.4 %copy-start = (bf16[512,1280]{1,0:T(8,128)(2,1)S(1)}, bf16[512,1280]{1,0:T(8,128)(2,1)}, u32[]{:S(2)}) copy-start(bf16[512,1280]{1,0:T(8,128)(2,1)} %a_2_.15) | copy-start | bytes 3932164
  0.0 2.5 %copy-start.1 = (bf16[512,1280]{1,0:T(8,128)(2,1)S(1)}, bf16[512,1280]{1,0:T(8,128)(2,1)}, u32[]{:S(2)}) copy-start(bf16[512,1280]{1,0:T(8,128)(2,1)} %a_4_.15) | copy-start | bytes 3932164
  0.0 3.1 %copy-start.14 = (s32[1,6]{1,0:T(1,128)S(1)}, s32[1,6]{1,0:T(1,128)}, u32[]{:S(2)}) copy-start(s32[1,6]{1,0:T(1,128)} %param.11) | copy-start | bytes 76
  2.4 59.5 %copy-start.4 = (bf16[128,1280]{1,0:T(8,128)(2,1)}, bf16[128,1280]{1,0:T(8,128)(2,1)S(1)}, u32[]{:S(2)}) copy-start(bf16[128,1280]{1,0:T(8,128)(2,1)S(1)} %get-tuple-element.41.a_1_) | copy-start | bytes 983044
  2.4 9.7 %collective-permute-start.18 = (bf16[128,1280]{1,0:T(8,128)(2,1)}, bf16[128,1280]{1,0:T(8,128)(2,1)S(1)}, u32[]{:S(2)}, u32[]{:S(2)}) collective-permute-start(bf16[128,1280]{1,0:T(8,128)(2,1)} %get-tuple-element.39), channel_id=1, source_target_pairs={{0,3},{1,0},{2,1},{3,2},{4,7},{5,4},{6,5},{7,6},{8,11},{9,8},{10,9... | collective-permute-start | bytes 983048 | tf_op jit(solution)/shard_map/ppermute | solution.py:147
  2.4 45.2 %collective-permute-start = (bf16[512,1280]{1,0:T(8,128)(2,1)S(1)}, bf16[512,1280]{1,0:T(8,128)(2,1)}, u32[]{:S(2)}, u32[]{:S(2)}) collective-permute-start(bf16[512,1280]{1,0:T(8,128)(2,1)S(1)} %copy-done), channel_id=1, source_target_pairs={{0,4},{4,0},{8,12},{12,8},{1,5},{5,1},{9,13},{13,9},{2,6},{6,2},{1... | collective-permute-start | bytes 3932168 | tf_op jit(solution)/shard_map/ppermute | solution.py:110
  2.5 45.6 %collective-permute-start.1 = (bf16[512,1280]{1,0:T(8,128)(2,1)S(1)}, bf16[512,1280]{1,0:T(8,128)(2,1)}, u32[]{:S(2)}, u32[]{:S(2)}) collective-permute-start(bf16[512,1280]{1,0:T(8,128)(2,1)S(1)} %copy-done.1), channel_id=1, source_target_pairs={{0,4},{4,0},{8,12},{12,8},{1,5},{5,1},{9,13},{13,9},{2,6},{6,2},{1... | collective-permute-start | bytes 3932168 | tf_op jit(solution)/shard_map/ppermute | solution.py:110
  3.4 3.6 %collective-permute-start.4 = (s32[4]{0:T(128)S(1)}, s32[4]{0:T(128)S(1)}, u32[]{:S(2)}, u32[]{:S(2)}) collective-permute-start(s32[4]{0:T(128)S(1)} %fusion.10), channel_id=1, source_target_pairs={{0,8},{4,12},{8,0},{12,4},{1,9},{5,13},{9,1},{13,5},{2,10},{6,14},... | collective-permute-start | bytes 56 | tf_op jit(solution)/shard_map/ppermute | solution.py:107
  5.3 44.4 %collective-permute-start.2 = (bf16[512,1280]{1,0:T(8,128)(2,1)}, bf16[512,1280]{1,0:T(8,128)(2,1)}, u32[]{:S(2)}, u32[]{:S(2)}) collective-permute-start(bf16[512,1280]{1,0:T(8,128)(2,1)} %a_6_.15), channel_id=1, source_target_pairs={{0,4},{4,0},{8,12},{12,8},{1,5},{5,1},{9,13},{13,9},{2,6},{6,2},{1... | collective-permute-start | bytes 3932168 | tf_op jit(solution)/shard_map/ppermute | solution.py:110
  6.9 42.7 %copy-start.13 = (s32[4]{0:T(128)}, s32[4]{0:T(128)S(1)}, u32[]{:S(2)}) copy-start(s32[4]{0:T(128)S(1)} %collective-permute-done.4.a_0_) | copy-start | bytes 52
  6.9 42.7 %collective-permute-start.3 = (bf16[512,1280]{1,0:T(8,128)(2,1)}, bf16[512,1280]{1,0:T(8,128)(2,1)}, u32[]{:S(2)}, u32[]{:S(2)}) collective-permute-start(bf16[512,1280]{1,0:T(8,128)(2,1)} %a_8_.15), channel_id=1, source_target_pairs={{0,4},{4,0},{8,12},{12,8},{1,5},{5,1},{9,13},{13,9},{2,6},{6,2},{1... | collective-permute-start | bytes 3932168 | tf_op jit(solution)/shard_map/ppermute | solution.py:110
  12.1 49.9 %copy-start.9 = (bf16[128,1280]{1,0:T(8,128)(2,1)}, bf16[128,1280]{1,0:T(8,128)(2,1)S(1)}, u32[]{:S(2)}) copy-start(bf16[128,1280]{1,0:T(8,128)(2,1)S(1)} %collective-permute-done.18.a_1_) | copy-start | bytes 983044
  12.1 15.9 %collective-permute-start.13 = (bf16[128,1280]{1,0:T(8,128)(2,1)}, bf16[128,1280]{1,0:T(8,128)(2,1)}, u32[]{:S(2)}, u32[]{:S(2)}) collective-permute-start(bf16[128,1280]{1,0:T(8,128)(2,1)} %get-tuple-element.42), channel_id=1, source_target_pairs={{0,2},{1,3},{2,0},{3,1},{4,6},{5,7},{6,4},{7,5},{8,10},{9,11},{10,... | collective-permute-start | bytes 983048 | tf_op jit(solution)/shard_map/ppermute | solution.py:147
  28.0 9.9 %collective-permute-start.8 = (bf16[128,1280]{1,0:T(8,128)(2,1)}, bf16[128,1280]{1,0:T(8,128)(2,1)}, u32[]{:S(2)}, u32[]{:S(2)}) collective-permute-start(bf16[128,1280]{1,0:T(8,128)(2,1)} %get-tuple-element.40), channel_id=1, source_target_pairs={{0,1},{1,2},{2,3},{3,0},{4,5},{5,6},{6,7},{7,4},{8,9},{9,10},{10,1... | collective-permute-start | bytes 983048 | tf_op jit(solution)/shard_map/ppermute | solution.py:147
  38.0 8.2 %collective-permute-start.19 = (bf16[128,1280]{1,0:T(8,128)(2,1)S(1)}, bf16[128,1280]{1,0:T(8,128)(2,1)S(1)}, u32[]{:S(2)}, u32[]{:S(2)}) collective-permute-start(bf16[128,1280]{1,0:T(8,128)(2,1)S(1)} %collective-permute-done.18.a_1_), channel_id=1, source_target_pairs={{0,8},{4,12},{8,0},{12,4},{1,9},{5,13},{9,1},{13,5},{2,10},{6,14},... | collective-permute-start | bytes 983048 | tf_op jit(solution)/shard_map/ppermute | solution.py:148
  46.1 31.8 %collective-permute-start.14 = (bf16[128,1280]{1,0:T(8,128)(2,1)}, bf16[128,1280]{1,0:T(8,128)(2,1)}, u32[]{:S(2)}, u32[]{:S(2)}) collective-permute-start(bf16[128,1280]{1,0:T(8,128)(2,1)} %collective-permute-done.13.a_1_), channel_id=1, source_target_pairs={{0,8},{4,12},{8,0},{12,4},{1,9},{5,13},{9,1},{13,5},{2,10},{6,14},... | collective-permute-start | bytes 983048 | tf_op jit(solution)/shard_map/ppermute | solution.py:148
  47.6 82.4 %collective-permute-start.9 = (bf16[128,1280]{1,0:T(8,128)(2,1)}, bf16[128,1280]{1,0:T(8,128)(2,1)S(1)}, u32[]{:S(2)}, u32[]{:S(2)}) collective-permute-start(bf16[128,1280]{1,0:T(8,128)(2,1)} %collective-permute-done.8.a_1_), channel_id=1, source_target_pairs={{0,8},{4,12},{8,0},{12,4},{1,9},{5,13},{9,1},{13,5},{2,10},{6,14},... | collective-permute-start | bytes 983048 | tf_op jit(solution)/shard_map/ppermute | solution.py:148
  48.1 95.8 %collective-permute-start.5 = (bf16[128,1280]{1,0:T(8,128)(2,1)S(1)}, bf16[128,1280]{1,0:T(8,128)(2,1)S(1)}, u32[]{:S(2)}, u32[]{:S(2)}) collective-permute-start(bf16[128,1280]{1,0:T(8,128)(2,1)S(1)} %get-tuple-element.41.a_1_), channel_id=1, source_target_pairs={{0,8},{4,12},{8,0},{12,4},{1,9},{5,13},{9,1},{13,5},{2,10},{6,14},... | collective-permute-start | bytes 983048 | tf_op jit(solution)/shard_map/ppermute | solution.py:148
  62.0 95.0 %collective-permute-start.20 = (f32[10,8,128]{2,1,0:T(8,128)}, f32[10,8,128]{2,1,0:T(8,128)S(1)}, u32[]{:S(2)}, u32[]{:S(2)}) collective-permute-start(f32[10,8,128]{2,1,0:T(8,128)} %get-tuple-element.35), channel_id=1, source_target_pairs={{0,8},{4,12},{8,0},{12,4},{1,9},{5,13},{9,1},{13,5},{2,10},{6,14},... | collective-permute-start | bytes 122888 | tf_op jit(solution)/shard_map/ppermute | solution.py:153
  76.3 96.8 %collective-permute-start.21 = (bf16[128,1280]{1,0:T(8,128)(2,1)}, bf16[128,1280]{1,0:T(8,128)(2,1)}, u32[]{:S(2)}, u32[]{:S(2)}) collective-permute-start(bf16[128,1280]{1,0:T(8,128)(2,1)} %get-tuple-element.36), channel_id=1, source_target_pairs={{0,8},{4,12},{8,0},{12,4},{1,9},{5,13},{9,1},{13,5},{2,10},{6,14},... | collective-permute-start | bytes 983048 | tf_op jit(solution)/shard_map/ppermute | solution.py:153
  90.1 68.2 %collective-permute-start.15 = (f32[10,8,128]{2,1,0:T(8,128)}, f32[10,8,128]{2,1,0:T(8,128)S(1)}, u32[]{:S(2)}, u32[]{:S(2)}) collective-permute-start(f32[10,8,128]{2,1,0:T(8,128)} %get-tuple-element.31), channel_id=1, source_target_pairs={{0,8},{4,12},{8,0},{12,4},{1,9},{5,13},{9,1},{13,5},{2,10},{6,14},... | collective-permute-start | bytes 122888 | tf_op jit(solution)/shard_map/ppermute | solution.py:153
  130.1 47.4 %collective-permute-start.16 = (bf16[128,1280]{1,0:T(8,128)(2,1)}, bf16[128,1280]{1,0:T(8,128)(2,1)}, u32[]{:S(2)}, u32[]{:S(2)}) collective-permute-start(bf16[128,1280]{1,0:T(8,128)(2,1)} %get-tuple-element.32), channel_id=1, source_target_pairs={{0,8},{4,12},{8,0},{12,4},{1,9},{5,13},{9,1},{13,5},{2,10},{6,14},... | collective-permute-start | bytes 983048 | tf_op jit(solution)/shard_map/ppermute | solution.py:153
  143.9 15.2 %collective-permute-start.10 = (f32[10,8,128]{2,1,0:T(8,128)}, f32[10,8,128]{2,1,0:T(8,128)S(1)}, u32[]{:S(2)}, u32[]{:S(2)}) collective-permute-start(f32[10,8,128]{2,1,0:T(8,128)} %get-tuple-element.27), channel_id=1, source_target_pairs={{0,8},{4,12},{8,0},{12,4},{1,9},{5,13},{9,1},{13,5},{2,10},{6,14},... | collective-permute-start | bytes 122888 | tf_op jit(solution)/shard_map/ppermute | solution.py:153
  156.9 23.8 %collective-permute-start.11 = (bf16[128,1280]{1,0:T(8,128)(2,1)}, bf16[128,1280]{1,0:T(8,128)(2,1)}, u32[]{:S(2)}, u32[]{:S(2)}) collective-permute-start(bf16[128,1280]{1,0:T(8,128)(2,1)} %get-tuple-element.28), channel_id=1, source_target_pairs={{0,8},{4,12},{8,0},{12,4},{1,9},{5,13},{9,1},{13,5},{2,10},{6,14},... | collective-permute-start | bytes 983048 | tf_op jit(solution)/shard_map/ppermute | solution.py:153
  158.4 8.5 %collective-permute-start.6 = (f32[10,8,128]{2,1,0:T(8,128)}, f32[10,8,128]{2,1,0:T(8,128)S(1)}, u32[]{:S(2)}, u32[]{:S(2)}) collective-permute-start(f32[10,8,128]{2,1,0:T(8,128)} %get-tuple-element.23), channel_id=1, source_target_pairs={{0,8},{4,12},{8,0},{12,4},{1,9},{5,13},{9,1},{13,5},{2,10},{6,14},... | collective-permute-start | bytes 122888 | tf_op jit(solution)/shard_map/ppermute | solution.py:153
  159.2 24.8 %collective-permute-start.7 = (bf16[128,1280]{1,0:T(8,128)(2,1)}, bf16[128,1280]{1,0:T(8,128)(2,1)}, u32[]{:S(2)}, u32[]{:S(2)}) collective-permute-start(bf16[128,1280]{1,0:T(8,128)(2,1)} %get-tuple-element.24), channel_id=1, source_target_pairs={{0,8},{4,12},{8,0},{12,4},{1,9},{5,13},{9,1},{13,5},{2,10},{6,14},... | collective-permute-start | bytes 983048 | tf_op jit(solution)/shard_map/ppermute | solution.py:153
  173.1 4.4 %copy-start.7 = (f32[128,1280]{1,0:T(8,128)S(1)}, f32[128,1280]{1,0:T(8,128)}, u32[]{:S(2)}) copy-start(f32[128,1280]{1,0:T(8,128)} %get-tuple-element.29) | copy-start | bytes 1966084
  174.7 26.6 %collective-permute-start.22 = (bf16[128,1280]{1,0:T(8,128)(2,1)S(1)}, bf16[128,1280]{1,0:T(8,128)(2,1)S(1)}, u32[]{:S(2)}, u32[]{:S(2)}) collective-permute-start(bf16[128,1280]{1,0:T(8,128)(2,1)S(1)} %divide_convert_fusion), channel_id=1, source_target_pairs={{0,1},{1,2},{2,3},{3,0},{4,5},{5,6},{6,7},{7,4},{8,9},{9,10},{10,1... | collective-permute-start | bytes 983048 | tf_op jit(solution)/shard_map/ppermute | solution.py:164
  177.5 3.2 %copy-start.6 = (f32[128,1280]{1,0:T(8,128)S(1)}, f32[128,1280]{1,0:T(8,128)}, u32[]{:S(2)}) copy-start(f32[128,1280]{1,0:T(8,128)} %get-tuple-element.25) | copy-start | bytes 1966084
  178.7 22.6 %collective-permute-start.17 = (bf16[128,1280]{1,0:T(8,128)(2,1)S(1)}, bf16[128,1280]{1,0:T(8,128)(2,1)S(1)}, u32[]{:S(2)}, u32[]{:S(2)}) collective-permute-start(bf16[128,1280]{1,0:T(8,128)(2,1)S(1)} %divide_convert_fusion.1), channel_id=1, source_target_pairs={{0,2},{1,3},{2,0},{3,1},{4,6},{5,7},{6,4},{7,5},{8,10},{9,11},{10,... | collective-permute-start | bytes 983048 | tf_op jit(solution)/shard_map/ppermute | solution.py:164
  180.7 3.4 %copy-start.8 = (f32[128,1280]{1,0:T(8,128)S(1)}, f32[128,1280]{1,0:T(8,128)}, u32[]{:S(2)}) copy-start(f32[128,1280]{1,0:T(8,128)} %get-tuple-element.21) | copy-start | bytes 1966084
  181.9 19.2 %collective-permute-start.12 = (bf16[128,1280]{1,0:T(8,128)(2,1)S(1)}, bf16[128,1280]{1,0:T(8,128)(2,1)S(1)}, u32[]{:S(2)}, u32[]{:S(2)}) collective-permute-start(bf16[128,1280]{1,0:T(8,128)(2,1)S(1)} %divide_convert_fusion.2), channel_id=1, source_target_pairs={{0,3},{1,0},{2,1},{3,2},{4,7},{5,4},{6,5},{7,6},{8,11},{9,8},{10,9... | collective-permute-start | bytes 983048 | tf_op jit(solution)/shard_map/ppermute | solution.py:164
  (6 other events, 9.9 us)

commit v5 on v3

--- a/solution.py
+++ b/solution.py
@@ -8,7 +8,7 @@
 from jax.sharding import PartitionSpec as P
 
 HEAD_DIM = 128
-ROW_SPLIT = 2
+ROW_SPLIT = 1
 STAT_ROWS = 8
 
 
@@ -16,30 +16,35 @@
     key_refs = refs[:nsrc]
     value_refs = refs[nsrc : 2 * nsrc]
     out_ref, lse_ref = refs[2 * nsrc : 2 * nsrc + 2]
-    score_ref = refs[2 * nsrc + 2]
     score_scale = 1.0 / math.sqrt(HEAD_DIM)
     query = q_ref[...]
+
+    def raw_scores(j):
+        return lax.dot_general(
+            query, key_refs[j][...], (((1,), (1,)), ((), ())), preferred_element_type=jnp.float32
+        )
+
     top = None
     for j in range(nsrc):
-        scores = lax.dot_general(
-            query, key_refs[j][...], (((1,), (1,)), ((), ())), preferred_element_type=jnp.float32
-        ) * score_scale
-        scores = jnp.where(flags_ref[j] > 0, scores, -1e30)
-        score_ref[j] = scores
-        block_top = jnp.max(scores, axis=1, keepdims=True)
+        block_top = jnp.max(raw_scores(j), axis=1, keepdims=True)
+        block_top = jnp.where(flags_ref[j] > 0, block_top, -1e30)
         top = block_top if top is None else jnp.maximum(top, block_top)
+    top = top * score_scale
     total = None
     summed = None
     for j in range(nsrc):
-        weights = jnp.exp(score_ref[j] - top)
+        shift = jnp.where(flags_ref[j] > 0, top, 1e30)
+        weights = jnp.exp(raw_scores(j) * score_scale - shift)
         part_total = jnp.sum(weights, axis=1, keepdims=True)
         product = jnp.dot(
             weights.astype(jnp.bfloat16), value_refs[j][...], preferred_element_type=jnp.float32
         )
         total = part_total if total is None else total + part_total
         summed = product if summed is None else summed + product
-    out_ref[...] = (summed / total).astype(out_ref.dtype)
-    lse = top + jnp.log(total)
+    filled = total > 0
+    safe = jnp.where(filled, total, 1.0)
+    out_ref[...] = (summed / safe).astype(out_ref.dtype)
+    lse = jnp.where(filled, top + jnp.log(safe), -1e30)
     wide = jnp.broadcast_to(lse, (lse.shape[0], 128))
     lse_ref[...] = jnp.transpose(wide)[:STAT_ROWS]
 
@@ -52,19 +57,19 @@
     row_tile = rows // ROW_SPLIT
     q_spec = pl.BlockSpec((row_tile, HEAD_DIM), lambda h, r, f: (r, h))
     kv_spec = pl.BlockSpec((block_rows, HEAD_DIM), lambda h, r, f: (0, h))
+    out_spec = pl.BlockSpec((None, row_tile, HEAD_DIM), lambda h, r, f: (h, r, 0))
     lse_spec = pl.BlockSpec((None, STAT_ROWS, row_tile), lambda h, r, f: (h, 0, r))
     grid_spec = pltpu.PrefetchScalarGridSpec(
         num_scalar_prefetch=1,
         grid=(nheads, ROW_SPLIT),
         in_specs=[q_spec] + [kv_spec] * (2 * nsrc),
-        out_specs=[q_spec, lse_spec],
-        scratch_shapes=[pltpu.VMEM((nsrc, row_tile, block_rows), jnp.float32)],
+        out_specs=[out_spec, lse_spec],
     )
     return pl.pallas_call(
         lambda *a: partial_kernel(nsrc, *a),
         grid_spec=grid_spec,
         out_shape=[
-            jax.ShapeDtypeStruct((rows, width), out_dtype),
+            jax.ShapeDtypeStruct((nheads, rows, HEAD_DIM), out_dtype),
             jax.ShapeDtypeStruct((nheads, STAT_ROWS, rows), jnp.float32),
         ],
         compiler_params=pltpu.CompilerParams(dimension_semantics=("parallel", "arbitrary")),
@@ -152,13 +157,13 @@
     far_out, far_lse = lax.ppermute((far_out, far_lse), "seq", forth)
 
     rows_all = query_block.shape[0]
-    lse_a = local_lse[:, 0, :].T
-    lse_b = far_lse[:, 0, :].T
+    lse_a = local_lse[:, 0, :][:, :, None]
+    lse_b = far_lse[:, 0, :][:, :, None]
     top = jnp.maximum(lse_a, lse_b)
-    weight_a = jnp.repeat(jnp.exp(lse_a - top), HEAD_DIM, axis=1)
-    weight_b = jnp.repeat(jnp.exp(lse_b - top), HEAD_DIM, axis=1)
+    weight_a = jnp.exp(lse_a - top)
+    weight_b = jnp.exp(lse_b - top)
     mixed = (local_out * weight_a + far_out.astype(jnp.float32) * weight_b) / (weight_a + weight_b)
-    heads_out = mixed.astype(jnp.bfloat16)
+    heads_out = jnp.transpose(mixed.astype(jnp.bfloat16), (1, 0, 2)).reshape(rows_all, head_width)
 
     rows = queries.shape[0]
     result = jnp.zeros((rows, queries.shape[1]), jnp.bfloat16)

time: 173 us -> 175 us (1.012)
  Pallas kernels: 53.3 us -> 63.4 us
  waiting for transfers between devices: 76.3 us -> 69.6 us
  local copies, waits for them, and re-layouts: 14.6 us -> 12.3 us
    pallas_call x2, Pallas kernels: 53.3 us -> 63.4 us  [attend_partial(): pl.pallas_call(lambda *a: partial_kernel(nsrc, *a), grid_spec=grid_spec,...]
    reshape x2 -> x0, local copies, waits for them, and re-layouts: 5.4 us -> none  [the longest x1 3.25 us: local(): weight_b = jnp.repeat(jnp.exp(lse_b - top), HEAD_DIM, axis=1)]
    ppermute x2, waiting for transfers between devices: 29.5 us -> 24.9 us  [local(): lax.ppermute((query_block, remote_flags), 'seq', back)]
    transpose x0 -> x1, other arithmetic: none -> 4.58 us  [local(): jnp.transpose(mixed.astype(jnp.bfloat16), (1, 0, 2))]
    unnamed x12 -> x20, local copies, waits for them, and re-layouts: 1.06 us -> 5.25 us
    broadcast_in_dim x2 -> x0, local copies, waits for them, and re-layouts: 3.66 us -> none  [the longest x1 1.86 us: local(): weight_a = jnp.repeat(jnp.exp(lse_a - top), HEAD_DIM, axis=1)]
    convert_element_type x1 -> x0, other arithmetic: 3.58 us -> none  [local(): heads_out = mixed.astype(jnp.bfloat16)]
    ppermute x2, waiting for transfers between devices: 2.54 us -> 0.01 us  [local(): far_out, far_lse = lax.ppermute((far_out, far_lse), 'seq', forth)]
  transfers between devices with their start and end apart: 14 -> 14, of which waited for: 7 -> 5; matrix products, arithmetic and copies ran while one was open for 7% -> 3% of each run, Pallas kernels for 16% -> 18%
where the time goes in v5:
time: 175 us; the launch traced here: 174 us
  waiting for transfers between devices  69.6 us (40%)
  Pallas kernels  63.4 us (36%)
  starting transfers between devices  22 us (13%)
  local copies, waits for them, and re-layouts  12.3 us (7%)
  other arithmetic  6.79 us (4%)
    pallas_call x2, Pallas kernels, attend_partial(): pl.pallas_call(lambda *a: partial_kernel(nsrc, *a), grid_spec=grid_spec,...  63.4 us
    ppermute x3, waiting for transfers between devices, local(): lax.ppermute(piece, 'sp', [(i, (i - d) % sp_count) for i in range(sp_coun...  26.4 us
    ppermute x2, waiting for transfers between devices, local(): lax.ppermute((query_block, remote_flags), 'seq', back)  24.9 us
    ppermute x3, waiting for transfers between devices, local(): lax.ppermute(piece, 'sp', [(i, (i + d) % sp_count) for i in range(sp_coun...  18.4 us
    ppermute x3, starting transfers between devices, local(): lax.ppermute(piece, 'sp', [(i, (i - d) % sp_count) for i in range(sp_coun...  9.28 us
    ppermute x3, starting transfers between devices, local(): lax.ppermute(piece, 'sp', [(i, (i + d) % sp_count) for i in range(sp_coun...  6.98 us
    unnamed x20, local copies, waits for them, and re-layouts  5.25 us
    transpose x1, other arithmetic, local(): jnp.transpose(mixed.astype(jnp.bfloat16), (1, 0, 2))  4.58 us
  transfers between devices with their start and end apart: 14, of which 5 were waited for; matrix products, arithmetic and copies ran while one was open for 3% of the time, Pallas kernels for 18%

profile of v5, /device:TPU:0, one launch (start us, length us, event | category | flops | bytes accessed | tf_op | source)
XLA Modules:
  0.0 174.3 jit_solution(3676121468609306092)
XLA Ops:
  0.0 2.4 %constant_dynamic-slice_fusion.3 = (bf16[128,1280]{1,0:T(8,128)(2,1)S(1)}, bf16[128,1280]{1,0:T(8,128)(2,1)}, bf16[128,1280]{1,0:T(8,128)(2,1)}, bf16[128,1280]{1,0:T(8,128)(2,1)}) fusion(bf16[128,5120]{1,0:T(8,128)(2,1)} %param.6, s32[]{:T(128)S(6)} %select_n.55, s32[]{:T(128)S(6)} %select_n.57, s32[]{:T(128)S(6)} %select_n.61, s32[]{:T(128)S(6)} %select_n.59), kind=kLoop, calls=%fused_computation.15 | loop fusion | bytes 2621456 | tf_op jit(solution)/shard_map/dynamic_slice | solution.py:96
  2.4 3.0 %collective-permute-start = (bf16[128,1280]{1,0:T(8,128)(2,1)}, bf16[128,1280]{1,0:T(8,128)(2,1)S(1)}, u32[]{:S(2)}, u32[]{:S(2)}) collective-permute-start(bf16[128,1280]{1,0:T(8,128)(2,1)} %get-tuple-element.23), channel_id=1, source_target_pairs={{0,1},{1,2},{2,3},{3,0},{4,5},{5,6},{6,7},{7,4},{8,9},{9,10},{10,1... | collective-permute-start | bytes 983048 | tf_op jit(solution)/shard_map/ppermute | solution.py:101
  5.4 2.6 %collective-permute-start.1 = (bf16[128,1280]{1,0:T(8,128)(2,1)}, bf16[128,1280]{1,0:T(8,128)(2,1)}, u32[]{:S(2)}, u32[]{:S(2)}) collective-permute-start(bf16[128,1280]{1,0:T(8,128)(2,1)} %get-tuple-element.25), channel_id=1, source_target_pairs={{0,2},{1,3},{2,0},{3,1},{4,6},{5,7},{6,4},{7,5},{8,10},{9,11},{10,... | collective-permute-start | bytes 983048 | tf_op jit(solution)/shard_map/ppermute | solution.py:101
  8.0 1.3 collective-permute-start.2
  9.7 1.5 collective-permute-start.7
  11.3 5.1 %collective-permute-done = bf16[128,1280]{1,0:T(8,128)(2,1)S(1)} collective-permute-done((bf16[128,1280]{1,0:T(8,128)(2,1)}, bf16[128,1280]{1,0:T(8,128)(2,1)S(1)}, u32[]{:S(2)}, u32[]{:S(2)}) %collective-permute-start) | collective-permute-done | bytes 327712 | tf_op jit(solution)/shard_map/ppermute | solution.py:101
  16.3 13.3 %collective-permute-done.1 = bf16[128,1280]{1,0:T(8,128)(2,1)} collective-permute-done((bf16[128,1280]{1,0:T(8,128)(2,1)}, bf16[128,1280]{1,0:T(8,128)(2,1)}, u32[]{:S(2)}, u32[]{:S(2)}) %collective-permute-start.1) | collective-permute-done | bytes 327712 | tf_op jit(solution)/shard_map/ppermute | solution.py:101
  29.7 0.5 collective-permute-start.6
  30.2 1.2 pad_maximum_fusion.a_1_
  31.4 1.6 collective-permute-start.8
  33.0 1.1 copy-done.2
  34.0 1.1 copy-done.3
  35.1 1.1 copy-done.4
  36.2 1.2 copy-done.5
  37.3 24.9 %collective-permute-done.8.a_1_ = bf16[512,1280]{1,0:T(8,128)(2,1)} collective-permute-done((bf16[512,1280]{1,0:T(8,128)(2,1)S(1)}, bf16[512,1280]{1,0:T(8,128)(2,1)}, u32[]{:S(2)}, u32[]{:S(2)}) %collective-permute-start.8) | collective-permute-done | bytes 1310752 | tf_op jit(solution)/shard_map/ppermute | solution.py:120
  62.2 31.7 %shard_map.65 = (bf16[10,512,128]{2,1,0:T(8,128)(2,1)}, f32[10,8,512]{2,1,0:T(8,128)}) custom-call(s32[4]{0:T(128)} %copy-done.8, bf16[512,1280]{1,0:T(8,128)(2,1)} %collective-permute-done.8.a_1_, bf16[512,1280]{1,0:T(8,128)(2,1)} %a_2_.3, bf16[512,1280]{1,0:T(8,128)(2,1)} %copy-done.2, bf16[512,1280]{1,0:T(8,128)(2,1)} %a_4_.3, ...), custom_call_target="tpu_custom_call" | custom-call | tf_op jit(solution)/shard_map/pallas_call | solution.py:68
  93.9 1.6 collective-permute-start.10
  95.5 0.5 collective-permute-start.9
  96.0 0.7 fusion.3.a_0_
  96.7 31.7 %shard_map.64 = (f32[10,512,128]{2,1,0:T(8,128)}, f32[10,8,512]{2,1,0:T(8,128)}) custom-call(s32[4]{0:T(128)} %fusion.3.a_0_, bf16[512,1280]{1,0:T(8,128)(2,1)} %copy-done.6, bf16[512,1280]{1,0:T(8,128)(2,1)} %a_2_.3, bf16[512,1280]{1,0:T(8,128)(2,1)} %copy-done.2, bf16[512,1280]{1,0:T(8,128)(2,1)} %a_4_.3, bf16[512,1280]{1,0:T(8,128)(2,1)} %copy-done.3, ...), custom_call_target="tpu_custom_call" | custom-call | tf_op jit(solution)/shard_map/pallas_call | solution.py:68
  128.4 1.0 copy.17
  129.5 4.6 %fusion = bf16[512,10,128]{2,0,1:T(8,128)(2,1)S(1)} fusion(f32[10,512]{1,0:T(8,128)S(1)} %get-tuple-element.15, f32[10,512]{1,0:T(8,128)S(1)} %get-tuple-element.16, bf16[10,512,128]{2,1,0:T(8,128)(2,1)S(1)} %collective-permute-done.10, f32[10,512,128]{2,1,0:T(8,128)} %get-tuple-element.9, f32[10,512]{1,0:T(8,128)S(1)} %get-tuple-element.17), kind=kLoop, calls=%fused_computation.2 | loop fusion | flops 3932160 | bytes 5304320 | tf_op jit(solution)/shard_map/transpose | solution.py:166
  134.2 0.2 copy.20
  134.5 8.6 %collective-permute-start.11 = (bf16[128,1280]{0,1:T(8,128)(2,1)S(1)}, bf16[128,1280]{0,1:T(8,128)(2,1)S(1)}, u32[]{:S(2)}, u32[]{:S(2)}) collective-permute-start(bf16[128,1280]{0,1:T(8,128)(2,1)S(1)} %bitcast.33), channel_id=1, source_target_pairs={{0,3},{1,0},{2,1},{3,2},{4,7},{5,4},{6,5},{7,6},{8,11},{9,8},{10,9... | collective-permute-start | bytes 983048 | tf_op jit(solution)/shard_map/ppermute | solution.py:173
  143.4 0.2 copy.22
  143.7 0.5 collective-permute-start.12
  144.4 0.2 collective-permute-start.13
  144.8 6.5 %collective-permute-done.11 = bf16[128,1280]{0,1:T(8,128)(2,1)S(1)} collective-permute-done((bf16[128,1280]{0,1:T(8,128)(2,1)S(1)}, bf16[128,1280]{0,1:T(8,128)(2,1)S(1)}, u32[]{:S(2)}, u32[]{:S(2)}) %collective-permute-start.11) | collective-permute-done | bytes 327712 | tf_op jit(solution)/shard_map/ppermute | solution.py:173
  151.5 19.9 %collective-permute-done.12 = bf16[128,1280]{0,1:T(8,128)(2,1)} collective-permute-done((bf16[128,1280]{0,1:T(8,128)(2,1)S(1)}, bf16[128,1280]{0,1:T(8,128)(2,1)}, u32[]{:S(2)}, u32[]{:S(2)}) %collective-permute-start.12) | collective-permute-done | bytes 327712 | tf_op jit(solution)/shard_map/ppermute | solution.py:173
  171.3 1.1 copy.23
  172.7 0.9 copy-done.7
  173.6 0.7 constant_dynamic-update-slice_fusion
  (42 shorter events, 1.8 us)
Async XLA Ops:
  0.0 9.4 %copy-start.9 = (s32[1,6]{1,0:T(1,128)S(1)}, s32[1,6]{1,0:T(1,128)}, u32[]{:S(2)}) copy-start(s32[1,6]{1,0:T(1,128)} %param.11) | copy-start | bytes 76
  0.0 11.3 %copy-start = (bf16[512,1280]{1,0:T(8,128)(2,1)S(1)}, bf16[512,1280]{1,0:T(8,128)(2,1)}, u32[]{:S(2)}) copy-start(bf16[512,1280]{1,0:T(8,128)(2,1)} %a_2_.3) | copy-start | bytes 3932164
  0.0 16.3 %copy-start.1 = (bf16[512,1280]{1,0:T(8,128)(2,1)S(1)}, bf16[512,1280]{1,0:T(8,128)(2,1)}, u32[]{:S(2)}) copy-start(bf16[512,1280]{1,0:T(8,128)(2,1)} %a_4_.3) | copy-start | bytes 3932164
  2.4 14.0 %collective-permute-start = (bf16[128,1280]{1,0:T(8,128)(2,1)}, bf16[128,1280]{1,0:T(8,128)(2,1)S(1)}, u32[]{:S(2)}, u32[]{:S(2)}) collective-permute-start(bf16[128,1280]{1,0:T(8,128)(2,1)} %get-tuple-element.23), channel_id=1, source_target_pairs={{0,1},{1,2},{2,3},{3,0},{4,5},{5,6},{6,7},{7,4},{8,9},{9,10},{10,1... | collective-permute-start | bytes 983048 | tf_op jit(solution)/shard_map/ppermute | solution.py:101
  5.4 24.2 %collective-permute-start.1 = (bf16[128,1280]{1,0:T(8,128)(2,1)}, bf16[128,1280]{1,0:T(8,128)(2,1)}, u32[]{:S(2)}, u32[]{:S(2)}) collective-permute-start(bf16[128,1280]{1,0:T(8,128)(2,1)} %get-tuple-element.25), channel_id=1, source_target_pairs={{0,2},{1,3},{2,0},{3,1},{4,6},{5,7},{6,4},{7,5},{8,10},{9,11},{10,... | collective-permute-start | bytes 983048 | tf_op jit(solution)/shard_map/ppermute | solution.py:101
  8.0 21.6 %collective-permute-start.2 = (bf16[128,1280]{1,0:T(8,128)(2,1)}, bf16[128,1280]{1,0:T(8,128)(2,1)}, u32[]{:S(2)}, u32[]{:S(2)}) collective-permute-start(bf16[128,1280]{1,0:T(8,128)(2,1)} %get-tuple-element.24), channel_id=1, source_target_pairs={{0,3},{1,0},{2,1},{3,2},{4,7},{5,4},{6,5},{7,6},{8,11},{9,8},{10,9... | collective-permute-start | bytes 983048 | tf_op jit(solution)/shard_map/ppermute | solution.py:101
  9.7 21.6 %collective-permute-start.7 = (s32[4]{0:T(128)S(1)}, s32[4]{0:T(128)S(1)}, u32[]{:S(2)}, u32[]{:S(2)}) collective-permute-start(s32[4]{0:T(128)S(1)} %fusion.4), channel_id=1, source_target_pairs={{0,8},{4,12},{8,0},{12,4},{1,9},{5,13},{9,1},{13,5},{2,10},{6,14},... | collective-permute-start | bytes 56 | tf_op jit(solution)/shard_map/ppermute | solution.py:120
  11.3 21.7 %collective-permute-start.3 = (bf16[512,1280]{1,0:T(8,128)(2,1)S(1)}, bf16[512,1280]{1,0:T(8,128)(2,1)S(1)}, u32[]{:S(2)}, u32[]{:S(2)}) collective-permute-start(bf16[512,1280]{1,0:T(8,128)(2,1)S(1)} %copy-done), channel_id=1, source_target_pairs={{0,4},{4,0},{8,12},{12,8},{1,5},{5,1},{9,13},{13,9},{2,6},{6,2},{1... | collective-permute-start | bytes 3932168 | tf_op jit(solution)/shard_map/ppermute | solution.py:123
  16.3 16.6 %collective-permute-start.4 = (bf16[512,1280]{1,0:T(8,128)(2,1)S(1)}, bf16[512,1280]{1,0:T(8,128)(2,1)S(1)}, u32[]{:S(2)}, u32[]{:S(2)}) collective-permute-start(bf16[512,1280]{1,0:T(8,128)(2,1)S(1)} %copy-done.1), channel_id=1, source_target_pairs={{0,4},{4,0},{8,12},{12,8},{1,5},{5,1},{9,13},{13,9},{2,6},{6,2},{1... | collective-permute-start | bytes 3932168 | tf_op jit(solution)/shard_map/ppermute | solution.py:123
  29.7 4.4 %collective-permute-start.5 = (bf16[512,1280]{1,0:T(8,128)(2,1)}, bf16[512,1280]{1,0:T(8,128)(2,1)S(1)}, u32[]{:S(2)}, u32[]{:S(2)}) collective-permute-start(bf16[512,1280]{1,0:T(8,128)(2,1)} %a_6_.3), channel_id=1, source_target_pairs={{0,4},{4,0},{8,12},{12,8},{1,5},{5,1},{9,13},{13,9},{2,6},{6,2},{1... | collective-permute-start | bytes 3932168 | tf_op jit(solution)/shard_map/ppermute | solution.py:123
  29.7 5.5 %collective-permute-start.6 = (bf16[512,1280]{1,0:T(8,128)(2,1)}, bf16[512,1280]{1,0:T(8,128)(2,1)S(1)}, u32[]{:S(2)}, u32[]{:S(2)}) collective-permute-start(bf16[512,1280]{1,0:T(8,128)(2,1)} %a_8_.3), channel_id=1, source_target_pairs={{0,4},{4,0},{8,12},{12,8},{1,5},{5,1},{9,13},{13,9},{2,6},{6,2},{1... | collective-permute-start | bytes 3932168 | tf_op jit(solution)/shard_map/ppermute | solution.py:123
  31.3 3.8 %copy-start.6 = (bf16[512,1280]{1,0:T(8,128)(2,1)}, bf16[512,1280]{1,0:T(8,128)(2,1)S(1)}, u32[]{:S(2)}) copy-start(bf16[512,1280]{1,0:T(8,128)(2,1)S(1)} %pad_maximum_fusion.a_1_) | copy-start | bytes 3932164
  31.4 30.9 %copy-start.8 = (s32[4]{0:T(128)}, s32[4]{0:T(128)S(1)}, u32[]{:S(2)}) copy-start(s32[4]{0:T(128)S(1)} %collective-permute-done.7.a_0_) | copy-start | bytes 52
  31.4 30.9 %collective-permute-start.8 = (bf16[512,1280]{1,0:T(8,128)(2,1)S(1)}, bf16[512,1280]{1,0:T(8,128)(2,1)}, u32[]{:S(2)}, u32[]{:S(2)}) collective-permute-start(bf16[512,1280]{1,0:T(8,128)(2,1)S(1)} %pad_maximum_fusion.a_1_), channel_id=1, source_target_pairs={{0,8},{4,12},{8,0},{12,4},{1,9},{5,13},{9,1},{13,5},{2,10},{6,14},... | collective-permute-start | bytes 3932168 | tf_op jit(solution)/shard_map/ppermute | solution.py:120
  33.0 1.1 copy-start.2
  34.0 1.1 copy-start.3
  35.1 1.1 copy-start.4
  36.2 1.2 copy-start.5
  93.9 35.6 %collective-permute-start.10 = (bf16[10,512,128]{2,1,0:T(8,128)(2,1)}, bf16[10,512,128]{2,1,0:T(8,128)(2,1)S(1)}, u32[]{:S(2)}, u32[]{:S(2)}) collective-permute-start(bf16[10,512,128]{2,1,0:T(8,128)(2,1)} %get-tuple-element.12), channel_id=1, source_target_pairs={{0,8},{4,12},{8,0},{12,4},{1,9},{5,13},{9,1},{13,5},{2,10},{6,14},... | collective-permute-start | bytes 3932168 | tf_op jit(solution)/shard_map/ppermute | solution.py:157
  95.5 33.9 %collective-permute-start.9 = (f32[10,8,512]{2,1,0:T(8,128)}, f32[10,8,512]{2,1,0:T(8,128)S(1)}, u32[]{:S(2)}, u32[]{:S(2)}) collective-permute-start(f32[10,8,512]{2,1,0:T(8,128)} %get-tuple-element.11), channel_id=1, source_target_pairs={{0,8},{4,12},{8,0},{12,4},{1,9},{5,13},{9,1},{13,5},{2,10},{6,14},... | collective-permute-start | bytes 491528 | tf_op jit(solution)/shard_map/ppermute | solution.py:157
  134.5 16.8 %collective-permute-start.11 = (bf16[128,1280]{0,1:T(8,128)(2,1)S(1)}, bf16[128,1280]{0,1:T(8,128)(2,1)S(1)}, u32[]{:S(2)}, u32[]{:S(2)}) collective-permute-start(bf16[128,1280]{0,1:T(8,128)(2,1)S(1)} %bitcast.33), channel_id=1, source_target_pairs={{0,3},{1,0},{2,1},{3,2},{4,7},{5,4},{6,5},{7,6},{8,11},{9,8},{10,9... | collective-permute-start | bytes 983048 | tf_op jit(solution)/shard_map/ppermute | solution.py:173
  143.7 27.7 %collective-permute-start.12 = (bf16[128,1280]{0,1:T(8,128)(2,1)S(1)}, bf16[128,1280]{0,1:T(8,128)(2,1)}, u32[]{:S(2)}, u32[]{:S(2)}) collective-permute-start(bf16[128,1280]{0,1:T(8,128)(2,1)S(1)} %bitcast.35), channel_id=1, source_target_pairs={{0,2},{1,3},{2,0},{3,1},{4,6},{5,7},{6,4},{7,5},{8,10},{9,11},{10,... | collective-permute-start | bytes 983048 | tf_op jit(solution)/shard_map/ppermute | solution.py:173
  144.4 28.2 %collective-permute-start.13 = (bf16[128,1280]{0,1:T(8,128)(2,1)S(1)}, bf16[128,1280]{0,1:T(8,128)(2,1)S(1)}, u32[]{:S(2)}, u32[]{:S(2)}) collective-permute-start(bf16[128,1280]{0,1:T(8,128)(2,1)S(1)} %bitcast.34), channel_id=1, source_target_pairs={{0,1},{1,2},{2,3},{3,0},{4,5},{5,6},{6,7},{7,4},{8,9},{9,10},{10,1... | collective-permute-start | bytes 983048 | tf_op jit(solution)/shard_map/ppermute | solution.py:173
  172.5 1.1 copy-start.7

commit v6 on v3

--- a/solution.py
+++ b/solution.py
@@ -52,19 +52,20 @@
     row_tile = rows // ROW_SPLIT
     q_spec = pl.BlockSpec((row_tile, HEAD_DIM), lambda h, r, f: (r, h))
     kv_spec = pl.BlockSpec((block_rows, HEAD_DIM), lambda h, r, f: (0, h))
+    out_spec = pl.BlockSpec((None, row_tile, HEAD_DIM), lambda h, r, f: (h, r, 0))
     lse_spec = pl.BlockSpec((None, STAT_ROWS, row_tile), lambda h, r, f: (h, 0, r))
     grid_spec = pltpu.PrefetchScalarGridSpec(
         num_scalar_prefetch=1,
         grid=(nheads, ROW_SPLIT),
         in_specs=[q_spec] + [kv_spec] * (2 * nsrc),
-        out_specs=[q_spec, lse_spec],
+        out_specs=[out_spec, lse_spec],
         scratch_shapes=[pltpu.VMEM((nsrc, row_tile, block_rows), jnp.float32)],
     )
     return pl.pallas_call(
         lambda *a: partial_kernel(nsrc, *a),
         grid_spec=grid_spec,
         out_shape=[
-            jax.ShapeDtypeStruct((rows, width), out_dtype),
+            jax.ShapeDtypeStruct((nheads, rows, HEAD_DIM), out_dtype),
             jax.ShapeDtypeStruct((nheads, STAT_ROWS, rows), jnp.float32),
         ],
         compiler_params=pltpu.CompilerParams(dimension_semantics=("parallel", "arbitrary")),
@@ -152,13 +153,13 @@
     far_out, far_lse = lax.ppermute((far_out, far_lse), "seq", forth)
 
     rows_all = query_block.shape[0]
-    lse_a = local_lse[:, 0, :].T
-    lse_b = far_lse[:, 0, :].T
+    lse_a = local_lse[:, 0, :][:, :, None]
+    lse_b = far_lse[:, 0, :][:, :, None]
     top = jnp.maximum(lse_a, lse_b)
-    weight_a = jnp.repeat(jnp.exp(lse_a - top), HEAD_DIM, axis=1)
-    weight_b = jnp.repeat(jnp.exp(lse_b - top), HEAD_DIM, axis=1)
+    weight_a = jnp.exp(lse_a - top)
+    weight_b = jnp.exp(lse_b - top)
     mixed = (local_out * weight_a + far_out.astype(jnp.float32) * weight_b) / (weight_a + weight_b)
-    heads_out = mixed.astype(jnp.bfloat16)
+    heads_out = jnp.transpose(mixed.astype(jnp.bfloat16), (1, 0, 2)).reshape(rows_all, head_width)
 
     rows = queries.shape[0]
     result = jnp.zeros((rows, queries.shape[1]), jnp.bfloat16)

time: 173 us -> 169 us (0.977)
  waiting for transfers between devices: 76.3 us -> 72.6 us
  local copies, waits for them, and re-layouts: 14.6 us -> 12.3 us
    reshape x2 -> x0, local copies, waits for them, and re-layouts: 5.4 us -> none  [the longest x1 3.25 us: local(): weight_b = jnp.repeat(jnp.exp(lse_b - top), HEAD_DIM, axis=1)]
    ppermute x2, waiting for transfers between devices: 29.5 us -> 24.9 us  [local(): lax.ppermute((query_block, remote_flags), 'seq', back)]
    transpose x0 -> x1, other arithmetic: none -> 4.58 us  [local(): jnp.transpose(mixed.astype(jnp.bfloat16), (1, 0, 2))]
    unnamed x12 -> x20, local copies, waits for them, and re-layouts: 1.06 us -> 5.25 us
    broadcast_in_dim x2 -> x0, local copies, waits for them, and re-layouts: 3.66 us -> none  [the longest x1 1.86 us: local(): weight_a = jnp.repeat(jnp.exp(lse_a - top), HEAD_DIM, axis=1)]
    convert_element_type x1 -> x0, other arithmetic: 3.58 us -> none  [local(): heads_out = mixed.astype(jnp.bfloat16)]
  transfers between devices with their start and end apart: 14 -> 14, of which waited for: 7 -> 6; matrix products, arithmetic and copies ran while one was open for 7% -> 3% of each run, Pallas kernels for 16% -> 16%
where the time goes in v6:
time: 169 us; the launch traced here: 168 us
  waiting for transfers between devices  72.6 us (43%)
  Pallas kernels  53.3 us (32%)
  starting transfers between devices  22.4 us (13%)
  local copies, waits for them, and re-layouts  12.3 us (7%)
  other arithmetic  6.79 us (4%)
    pallas_call x2, Pallas kernels, attend_partial(): pl.pallas_call(lambda *a: partial_kernel(nsrc, *a), grid_spec=grid_spec,...  53.3 us
    ppermute x3, waiting for transfers between devices, local(): lax.ppermute(piece, 'sp', [(i, (i - d) % sp_count) for i in range(sp_coun...  26.2 us
    ppermute x2, waiting for transfers between devices, local(): lax.ppermute((query_block, remote_flags), 'seq', back)  24.9 us
    ppermute x3, waiting for transfers between devices, local(): lax.ppermute(piece, 'sp', [(i, (i + d) % sp_count) for i in range(sp_coun...  18.4 us
    ppermute x3, starting transfers between devices, local(): lax.ppermute(piece, 'sp', [(i, (i - d) % sp_count) for i in range(sp_coun...  9.69 us
    ppermute x3, starting transfers between devices, local(): lax.ppermute(piece, 'sp', [(i, (i + d) % sp_count) for i in range(sp_coun...  6.98 us
    unnamed x20, local copies, waits for them, and re-layouts  5.25 us
    transpose x1, other arithmetic, local(): jnp.transpose(mixed.astype(jnp.bfloat16), (1, 0, 2))  4.58 us
  transfers between devices with their start and end apart: 14, of which 6 were waited for; matrix products, arithmetic and copies ran while one was open for 3% of the time, Pallas kernels for 16%

profile of v6, /device:TPU:0, one launch (start us, length us, event | category | flops | bytes accessed | tf_op | source)
XLA Modules:
  0.0 167.5 jit_solution(11620325390707603296)
XLA Ops:
  0.0 2.4 %constant_dynamic-slice_fusion.3 = (bf16[128,1280]{1,0:T(8,128)(2,1)S(1)}, bf16[128,1280]{1,0:T(8,128)(2,1)}, bf16[128,1280]{1,0:T(8,128)(2,1)}, bf16[128,1280]{1,0:T(8,128)(2,1)}) fusion(bf16[128,5120]{1,0:T(8,128)(2,1)} %param.6, s32[]{:T(128)S(6)} %select_n.55, s32[]{:T(128)S(6)} %select_n.57, s32[]{:T(128)S(6)} %select_n.61, s32[]{:T(128)S(6)} %select_n.59), kind=kLoop, calls=%fused_computation.15 | loop fusion | bytes 2621456 | tf_op jit(solution)/shard_map/dynamic_slice | solution.py:92
  2.4 3.0 %collective-permute-start = (bf16[128,1280]{1,0:T(8,128)(2,1)}, bf16[128,1280]{1,0:T(8,128)(2,1)S(1)}, u32[]{:S(2)}, u32[]{:S(2)}) collective-permute-start(bf16[128,1280]{1,0:T(8,128)(2,1)} %get-tuple-element.23), channel_id=1, source_target_pairs={{0,1},{1,2},{2,3},{3,0},{4,5},{5,6},{6,7},{7,4},{8,9},{9,10},{10,1... | collective-permute-start | bytes 983048 | tf_op jit(solution)/shard_map/ppermute | solution.py:97
  5.4 2.6 %collective-permute-start.1 = (bf16[128,1280]{1,0:T(8,128)(2,1)}, bf16[128,1280]{1,0:T(8,128)(2,1)}, u32[]{:S(2)}, u32[]{:S(2)}) collective-permute-start(bf16[128,1280]{1,0:T(8,128)(2,1)} %get-tuple-element.25), channel_id=1, source_target_pairs={{0,2},{1,3},{2,0},{3,1},{4,6},{5,7},{6,4},{7,5},{8,10},{9,11},{10,... | collective-permute-start | bytes 983048 | tf_op jit(solution)/shard_map/ppermute | solution.py:97
  8.0 1.3 collective-permute-start.2
  9.7 1.5 collective-permute-start.7
  11.3 5.1 %collective-permute-done = bf16[128,1280]{1,0:T(8,128)(2,1)S(1)} collective-permute-done((bf16[128,1280]{1,0:T(8,128)(2,1)}, bf16[128,1280]{1,0:T(8,128)(2,1)S(1)}, u32[]{:S(2)}, u32[]{:S(2)}) %collective-permute-start) | collective-permute-done | bytes 327712 | tf_op jit(solution)/shard_map/ppermute | solution.py:97
  16.3 13.3 %collective-permute-done.1 = bf16[128,1280]{1,0:T(8,128)(2,1)} collective-permute-done((bf16[128,1280]{1,0:T(8,128)(2,1)}, bf16[128,1280]{1,0:T(8,128)(2,1)}, u32[]{:S(2)}, u32[]{:S(2)}) %collective-permute-start.1) | collective-permute-done | bytes 327712 | tf_op jit(solution)/shard_map/ppermute | solution.py:97
  29.7 0.5 collective-permute-start.6
  30.2 1.2 pad_maximum_fusion.a_1_
  31.4 1.6 collective-permute-start.8
  33.0 1.1 copy-done.2
  34.0 1.1 copy-done.3
  35.1 1.1 copy-done.4
  36.2 1.2 copy-done.5
  37.3 24.9 %collective-permute-done.8.a_1_ = bf16[512,1280]{1,0:T(8,128)(2,1)} collective-permute-done((bf16[512,1280]{1,0:T(8,128)(2,1)S(1)}, bf16[512,1280]{1,0:T(8,128)(2,1)}, u32[]{:S(2)}, u32[]{:S(2)}) %collective-permute-start.8) | collective-permute-done | bytes 1310752 | tf_op jit(solution)/shard_map/ppermute | solution.py:116
  62.2 26.5 %shard_map.65 = (bf16[10,512,128]{2,1,0:T(8,128)(2,1)}, f32[10,8,512]{2,1,0:T(8,128)}) custom-call(s32[4]{0:T(128)} %copy-done.8, bf16[512,1280]{1,0:T(8,128)(2,1)} %collective-permute-done.8.a_1_, bf16[512,1280]{1,0:T(8,128)(2,1)} %a_2_.3, bf16[512,1280]{1,0:T(8,128)(2,1)} %copy-done.2, bf16[512,1280]{1,0:T(8,128)(2,1)} %a_4_.3, ...), custom_call_target="tpu_custom_call" | custom-call | tf_op jit(solution)/shard_map/pallas_call | solution.py:64
  88.8 1.6 collective-permute-start.10
  90.3 0.5 collective-permute-start.9
  90.9 0.7 fusion.3.a_0_
  91.5 26.7 %shard_map.64 = (f32[10,512,128]{2,1,0:T(8,128)}, f32[10,8,512]{2,1,0:T(8,128)}) custom-call(s32[4]{0:T(128)} %fusion.3.a_0_, bf16[512,1280]{1,0:T(8,128)(2,1)} %copy-done.6, bf16[512,1280]{1,0:T(8,128)(2,1)} %a_2_.3, bf16[512,1280]{1,0:T(8,128)(2,1)} %copy-done.2, bf16[512,1280]{1,0:T(8,128)(2,1)} %a_4_.3, bf16[512,1280]{1,0:T(8,128)(2,1)} %copy-done.3, ...), custom_call_target="tpu_custom_call" | custom-call | tf_op jit(solution)/shard_map/pallas_call | solution.py:64
  118.3 1.0 copy.17
  119.3 3.1 %collective-permute-done.9 = f32[10,8,512]{2,1,0:T(8,128)S(1)} collective-permute-done((f32[10,8,512]{2,1,0:T(8,128)}, f32[10,8,512]{2,1,0:T(8,128)S(1)}, u32[]{:S(2)}, u32[]{:S(2)}) %collective-permute-start.9) | collective-permute-done | bytes 163872 | tf_op jit(solution)/shard_map/ppermute | solution.py:153
  122.4 4.6 %fusion = bf16[512,10,128]{2,0,1:T(8,128)(2,1)S(1)} fusion(f32[10,512]{1,0:T(8,128)S(1)} %get-tuple-element.15, f32[10,512]{1,0:T(8,128)S(1)} %get-tuple-element.16, bf16[10,512,128]{2,1,0:T(8,128)(2,1)S(1)} %collective-permute-done.10, f32[10,512,128]{2,1,0:T(8,128)} %get-tuple-element.9, f32[10,512]{1,0:T(8,128)S(1)} %get-tuple-element.17), kind=kLoop, calls=%fused_computation.2 | loop fusion | flops 3932160 | bytes 5304320 | tf_op jit(solution)/shard_map/transpose | solution.py:162
  127.2 0.2 copy.20
  127.4 8.6 %collective-permute-start.11 = (bf16[128,1280]{0,1:T(8,128)(2,1)S(1)}, bf16[128,1280]{0,1:T(8,128)(2,1)S(1)}, u32[]{:S(2)}, u32[]{:S(2)}) collective-permute-start(bf16[128,1280]{0,1:T(8,128)(2,1)S(1)} %bitcast.33), channel_id=1, source_target_pairs={{0,3},{1,0},{2,1},{3,2},{4,7},{5,4},{6,5},{7,6},{8,11},{9,8},{10,9... | collective-permute-start | bytes 983048 | tf_op jit(solution)/shard_map/ppermute | solution.py:169
  136.4 0.2 copy.22
  136.6 1.1 collective-permute-start.12
  138.1 6.1 %collective-permute-done.11 = bf16[128,1280]{0,1:T(8,128)(2,1)S(1)} collective-permute-done((bf16[128,1280]{0,1:T(8,128)(2,1)S(1)}, bf16[128,1280]{0,1:T(8,128)(2,1)S(1)}, u32[]{:S(2)}, u32[]{:S(2)}) %collective-permute-start.11) | collective-permute-done | bytes 327712 | tf_op jit(solution)/shard_map/ppermute | solution.py:169
  144.4 20.2 %collective-permute-done.12 = bf16[128,1280]{0,1:T(8,128)(2,1)} collective-permute-done((bf16[128,1280]{0,1:T(8,128)(2,1)S(1)}, bf16[128,1280]{0,1:T(8,128)(2,1)}, u32[]{:S(2)}, u32[]{:S(2)}) %collective-permute-start.12) | collective-permute-done | bytes 327712 | tf_op jit(solution)/shard_map/ppermute | solution.py:169
  164.6 1.1 copy.23
  165.9 0.9 copy-done.7
  166.8 0.7 constant_dynamic-update-slice_fusion
  (42 shorter events, 1.9 us)
Async XLA Ops:
  0.0 9.4 %copy-start.9 = (s32[1,6]{1,0:T(1,128)S(1)}, s32[1,6]{1,0:T(1,128)}, u32[]{:S(2)}) copy-start(s32[1,6]{1,0:T(1,128)} %param.11) | copy-start | bytes 76
  0.0 11.3 %copy-start = (bf16[512,1280]{1,0:T(8,128)(2,1)S(1)}, bf16[512,1280]{1,0:T(8,128)(2,1)}, u32[]{:S(2)}) copy-start(bf16[512,1280]{1,0:T(8,128)(2,1)} %a_2_.3) | copy-start | bytes 3932164
  0.0 16.3 %copy-start.1 = (bf16[512,1280]{1,0:T(8,128)(2,1)S(1)}, bf16[512,1280]{1,0:T(8,128)(2,1)}, u32[]{:S(2)}) copy-start(bf16[512,1280]{1,0:T(8,128)(2,1)} %a_4_.3) | copy-start | bytes 3932164
  2.4 14.0 %collective-permute-start = (bf16[128,1280]{1,0:T(8,128)(2,1)}, bf16[128,1280]{1,0:T(8,128)(2,1)S(1)}, u32[]{:S(2)}, u32[]{:S(2)}) collective-permute-start(bf16[128,1280]{1,0:T(8,128)(2,1)} %get-tuple-element.23), channel_id=1, source_target_pairs={{0,1},{1,2},{2,3},{3,0},{4,5},{5,6},{6,7},{7,4},{8,9},{9,10},{10,1... | collective-permute-start | bytes 983048 | tf_op jit(solution)/shard_map/ppermute | solution.py:97
  5.4 24.2 %collective-permute-start.1 = (bf16[128,1280]{1,0:T(8,128)(2,1)}, bf16[128,1280]{1,0:T(8,128)(2,1)}, u32[]{:S(2)}, u32[]{:S(2)}) collective-permute-start(bf16[128,1280]{1,0:T(8,128)(2,1)} %get-tuple-element.25), channel_id=1, source_target_pairs={{0,2},{1,3},{2,0},{3,1},{4,6},{5,7},{6,4},{7,5},{8,10},{9,11},{10,... | collective-permute-start | bytes 983048 | tf_op jit(solution)/shard_map/ppermute | solution.py:97
  8.0 21.6 %collective-permute-start.2 = (bf16[128,1280]{1,0:T(8,128)(2,1)}, bf16[128,1280]{1,0:T(8,128)(2,1)}, u32[]{:S(2)}, u32[]{:S(2)}) collective-permute-start(bf16[128,1280]{1,0:T(8,128)(2,1)} %get-tuple-element.24), channel_id=1, source_target_pairs={{0,3},{1,0},{2,1},{3,2},{4,7},{5,4},{6,5},{7,6},{8,11},{9,8},{10,9... | collective-permute-start | bytes 983048 | tf_op jit(solution)/shard_map/ppermute | solution.py:97
  9.7 21.6 %collective-permute-start.7 = (s32[4]{0:T(128)S(1)}, s32[4]{0:T(128)S(1)}, u32[]{:S(2)}, u32[]{:S(2)}) collective-permute-start(s32[4]{0:T(128)S(1)} %fusion.4), channel_id=1, source_target_pairs={{0,8},{4,12},{8,0},{12,4},{1,9},{5,13},{9,1},{13,5},{2,10},{6,14},... | collective-permute-start | bytes 56 | tf_op jit(solution)/shard_map/ppermute | solution.py:116
  11.3 21.7 %collective-permute-start.3 = (bf16[512,1280]{1,0:T(8,128)(2,1)S(1)}, bf16[512,1280]{1,0:T(8,128)(2,1)S(1)}, u32[]{:S(2)}, u32[]{:S(2)}) collective-permute-start(bf16[512,1280]{1,0:T(8,128)(2,1)S(1)} %copy-done), channel_id=1, source_target_pairs={{0,4},{4,0},{8,12},{12,8},{1,5},{5,1},{9,13},{13,9},{2,6},{6,2},{1... | collective-permute-start | bytes 3932168 | tf_op jit(solution)/shard_map/ppermute | solution.py:119
  16.3 16.6 %collective-permute-start.4 = (bf16[512,1280]{1,0:T(8,128)(2,1)S(1)}, bf16[512,1280]{1,0:T(8,128)(2,1)S(1)}, u32[]{:S(2)}, u32[]{:S(2)}) collective-permute-start(bf16[512,1280]{1,0:T(8,128)(2,1)S(1)} %copy-done.1), channel_id=1, source_target_pairs={{0,4},{4,0},{8,12},{12,8},{1,5},{5,1},{9,13},{13,9},{2,6},{6,2},{1... | collective-permute-start | bytes 3932168 | tf_op jit(solution)/shard_map/ppermute | solution.py:119
  29.7 4.4 %collective-permute-start.5 = (bf16[512,1280]{1,0:T(8,128)(2,1)}, bf16[512,1280]{1,0:T(8,128)(2,1)S(1)}, u32[]{:S(2)}, u32[]{:S(2)}) collective-permute-start(bf16[512,1280]{1,0:T(8,128)(2,1)} %a_6_.3), channel_id=1, source_target_pairs={{0,4},{4,0},{8,12},{12,8},{1,5},{5,1},{9,13},{13,9},{2,6},{6,2},{1... | collective-permute-start | bytes 3932168 | tf_op jit(solution)/shard_map/ppermute | solution.py:119
  29.7 5.5 %collective-permute-start.6 = (bf16[512,1280]{1,0:T(8,128)(2,1)}, bf16[512,1280]{1,0:T(8,128)(2,1)S(1)}, u32[]{:S(2)}, u32[]{:S(2)}) collective-permute-start(bf16[512,1280]{1,0:T(8,128)(2,1)} %a_8_.3), channel_id=1, source_target_pairs={{0,4},{4,0},{8,12},{12,8},{1,5},{5,1},{9,13},{13,9},{2,6},{6,2},{1... | collective-permute-start | bytes 3932168 | tf_op jit(solution)/shard_map/ppermute | solution.py:119
  31.3 3.8 %copy-start.6 = (bf16[512,1280]{1,0:T(8,128)(2,1)}, bf16[512,1280]{1,0:T(8,128)(2,1)S(1)}, u32[]{:S(2)}) copy-start(bf16[512,1280]{1,0:T(8,128)(2,1)S(1)} %pad_maximum_fusion.a_1_) | copy-start | bytes 3932164
  31.4 30.9 %copy-start.8 = (s32[4]{0:T(128)}, s32[4]{0:T(128)S(1)}, u32[]{:S(2)}) copy-start(s32[4]{0:T(128)S(1)} %collective-permute-done.7.a_0_) | copy-start | bytes 52
  31.4 30.9 %collective-permute-start.8 = (bf16[512,1280]{1,0:T(8,128)(2,1)S(1)}, bf16[512,1280]{1,0:T(8,128)(2,1)}, u32[]{:S(2)}, u32[]{:S(2)}) collective-permute-start(bf16[512,1280]{1,0:T(8,128)(2,1)S(1)} %pad_maximum_fusion.a_1_), channel_id=1, source_target_pairs={{0,8},{4,12},{8,0},{12,4},{1,9},{5,13},{9,1},{13,5},{2,10},{6,14},... | collective-permute-start | bytes 3932168 | tf_op jit(solution)/shard_map/ppermute | solution.py:116
  33.0 1.1 copy-start.2
  34.0 1.1 copy-start.3
  35.1 1.1 copy-start.4
  36.2 1.2 copy-start.5
  88.8 33.7 %collective-permute-start.10 = (bf16[10,512,128]{2,1,0:T(8,128)(2,1)}, bf16[10,512,128]{2,1,0:T(8,128)(2,1)S(1)}, u32[]{:S(2)}, u32[]{:S(2)}) collective-permute-start(bf16[10,512,128]{2,1,0:T(8,128)(2,1)} %get-tuple-element.12), channel_id=1, source_target_pairs={{0,8},{4,12},{8,0},{12,4},{1,9},{5,13},{9,1},{13,5},{2,10},{6,14},... | collective-permute-start | bytes 3932168 | tf_op jit(solution)/shard_map/ppermute | solution.py:153
  90.3 32.0 %collective-permute-start.9 = (f32[10,8,512]{2,1,0:T(8,128)}, f32[10,8,512]{2,1,0:T(8,128)S(1)}, u32[]{:S(2)}, u32[]{:S(2)}) collective-permute-start(f32[10,8,512]{2,1,0:T(8,128)} %get-tuple-element.11), channel_id=1, source_target_pairs={{0,8},{4,12},{8,0},{12,4},{1,9},{5,13},{9,1},{13,5},{2,10},{6,14},... | collective-permute-start | bytes 491528 | tf_op jit(solution)/shard_map/ppermute | solution.py:153
  127.4 16.8 %collective-permute-start.11 = (bf16[128,1280]{0,1:T(8,128)(2,1)S(1)}, bf16[128,1280]{0,1:T(8,128)(2,1)S(1)}, u32[]{:S(2)}, u32[]{:S(2)}) collective-permute-start(bf16[128,1280]{0,1:T(8,128)(2,1)S(1)} %bitcast.33), channel_id=1, source_target_pairs={{0,3},{1,0},{2,1},{3,2},{4,7},{5,4},{6,5},{7,6},{8,11},{9,8},{10,9... | collective-permute-start | bytes 983048 | tf_op jit(solution)/shard_map/ppermute | solution.py:169
  136.6 28.0 %collective-permute-start.12 = (bf16[128,1280]{0,1:T(8,128)(2,1)S(1)}, bf16[128,1280]{0,1:T(8,128)(2,1)}, u32[]{:S(2)}, u32[]{:S(2)}) collective-permute-start(bf16[128,1280]{0,1:T(8,128)(2,1)S(1)} %bitcast.35), channel_id=1, source_target_pairs={{0,2},{1,3},{2,0},{3,1},{4,6},{5,7},{6,4},{7,5},{8,10},{9,11},{10,... | collective-permute-start | bytes 983048 | tf_op jit(solution)/shard_map/ppermute | solution.py:169
  137.9 27.9 %collective-permute-start.13 = (bf16[128,1280]{0,1:T(8,128)(2,1)S(1)}, bf16[128,1280]{0,1:T(8,128)(2,1)S(1)}, u32[]{:S(2)}, u32[]{:S(2)}) collective-permute-start(bf16[128,1280]{0,1:T(8,128)(2,1)S(1)} %bitcast.34), channel_id=1, source_target_pairs={{0,1},{1,2},{2,3},{3,0},{4,5},{5,6},{6,7},{7,4},{8,9},{9,10},{10,1... | collective-permute-start | bytes 983048 | tf_op jit(solution)/shard_map/ppermute | solution.py:169
  165.7 1.1 copy-start.7

commit v7 on v5

--- a/solution.py
+++ b/solution.py
@@ -8,7 +8,7 @@
 from jax.sharding import PartitionSpec as P
 
 HEAD_DIM = 128
-ROW_SPLIT = 1
+ROW_SPLIT = 2
 STAT_ROWS = 8
 
 
@@ -16,37 +16,33 @@
     key_refs = refs[:nsrc]
     value_refs = refs[nsrc : 2 * nsrc]
     out_ref, lse_ref = refs[2 * nsrc : 2 * nsrc + 2]
+    score_ref = refs[2 * nsrc + 2]
     score_scale = 1.0 / math.sqrt(HEAD_DIM)
     query = q_ref[...]
-
-    def raw_scores(j):
-        return lax.dot_general(
+    top = None
+    for j in range(nsrc):
+        raw = lax.dot_general(
             query, key_refs[j][...], (((1,), (1,)), ((), ())), preferred_element_type=jnp.float32
         )
-
-    top = None
-    for j in range(nsrc):
-        block_top = jnp.max(raw_scores(j), axis=1, keepdims=True)
-        block_top = jnp.where(flags_ref[j] > 0, block_top, -1e30)
+        score_ref[j] = raw
+        block_top = jnp.where(flags_ref[j] > 0, jnp.max(raw, axis=1, keepdims=True), -1e30)
         top = block_top if top is None else jnp.maximum(top, block_top)
     top = top * score_scale
+    ones = jnp.ones((score_ref.shape[2], HEAD_DIM), jnp.bfloat16)
     total = None
     summed = None
     for j in range(nsrc):
         shift = jnp.where(flags_ref[j] > 0, top, 1e30)
-        weights = jnp.exp(raw_scores(j) * score_scale - shift)
-        part_total = jnp.sum(weights, axis=1, keepdims=True)
-        product = jnp.dot(
-            weights.astype(jnp.bfloat16), value_refs[j][...], preferred_element_type=jnp.float32
-        )
+        weights = jnp.exp(score_ref[j] * score_scale - shift).astype(jnp.bfloat16)
+        part_total = jnp.dot(weights, ones, preferred_element_type=jnp.float32)
+        product = jnp.dot(weights, value_refs[j][...], preferred_element_type=jnp.float32)
         total = part_total if total is None else total + part_total
         summed = product if summed is None else summed + product
     filled = total > 0
     safe = jnp.where(filled, total, 1.0)
     out_ref[...] = (summed / safe).astype(out_ref.dtype)
     lse = jnp.where(filled, top + jnp.log(safe), -1e30)
-    wide = jnp.broadcast_to(lse, (lse.shape[0], 128))
-    lse_ref[...] = jnp.transpose(wide)[:STAT_ROWS]
+    lse_ref[...] = jnp.transpose(lse)[:STAT_ROWS]
 
 
 def attend_partial(flags, query_block, key_blocks, value_blocks, out_dtype):
@@ -64,6 +60,7 @@
         grid=(nheads, ROW_SPLIT),
         in_specs=[q_spec] + [kv_spec] * (2 * nsrc),
         out_specs=[out_spec, lse_spec],
+        scratch_shapes=[pltpu.VMEM((nsrc, row_tile, block_rows), jnp.float32)],
     )
     return pl.pallas_call(
         lambda *a: partial_kernel(nsrc, *a),

time: 175 us -> 173 us (0.989)
  Pallas kernels: 63.4 us -> 61.3 us
    pallas_call x2, Pallas kernels: 63.4 us -> 61.3 us  [attend_partial(): pl.pallas_call(lambda *a: partial_kernel(nsrc, *a), grid_spec=grid_spec,...]
where the time goes in v7:
time: 173 us; the launch traced here: 172 us
  waiting for transfers between devices  69.6 us (40%)
  Pallas kernels  61.3 us (35%)
  starting transfers between devices  22 us (13%)
  local copies, waits for them, and re-layouts  12.3 us (7%)
  other arithmetic  6.79 us (4%)
    pallas_call x2, Pallas kernels, attend_partial(): pl.pallas_call(lambda *a: partial_kernel(nsrc, *a), grid_spec=grid_spec,...  61.3 us
    ppermute x3, waiting for transfers between devices, local(): lax.ppermute(piece, 'sp', [(i, (i - d) % sp_count) for i in range(sp_coun...  26.4 us
    ppermute x2, waiting for transfers between devices, local(): lax.ppermute((query_block, remote_flags), 'seq', back)  24.9 us
    ppermute x3, waiting for transfers between devices, local(): lax.ppermute(piece, 'sp', [(i, (i + d) % sp_count) for i in range(sp_coun...  18.4 us
    ppermute x3, starting transfers between devices, local(): lax.ppermute(piece, 'sp', [(i, (i - d) % sp_count) for i in range(sp_coun...  9.28 us
    ppermute x3, starting transfers between devices, local(): lax.ppermute(piece, 'sp', [(i, (i + d) % sp_count) for i in range(sp_coun...  6.98 us
    unnamed x20, local copies, waits for them, and re-layouts  5.25 us
    transpose x1, other arithmetic, local(): jnp.transpose(mixed.astype(jnp.bfloat16), (1, 0, 2))  4.58 us
  transfers between devices with their start and end apart: 14, of which 5 were waited for; matrix products, arithmetic and copies ran while one was open for 3% of the time, Pallas kernels for 18%

profile of v7, /device:TPU:0, one launch (start us, length us, event | category | flops | bytes accessed | tf_op | source)
XLA Modules:
  0.0 172.2 jit_solution(1283938829426922727)
XLA Ops:
  0.0 2.4 %constant_dynamic-slice_fusion.3 = (bf16[128,1280]{1,0:T(8,128)(2,1)S(1)}, bf16[128,1280]{1,0:T(8,128)(2,1)}, bf16[128,1280]{1,0:T(8,128)(2,1)}, bf16[128,1280]{1,0:T(8,128)(2,1)}) fusion(bf16[128,5120]{1,0:T(8,128)(2,1)} %param.6, s32[]{:T(128)S(6)} %select_n.55, s32[]{:T(128)S(6)} %select_n.57, s32[]{:T(128)S(6)} %select_n.61, s32[]{:T(128)S(6)} %select_n.59), kind=kLoop, calls=%fused_computation.15 | loop fusion | bytes 2621456 | tf_op jit(solution)/shard_map/dynamic_slice | solution.py:93
  2.4 3.0 %collective-permute-start = (bf16[128,1280]{1,0:T(8,128)(2,1)}, bf16[128,1280]{1,0:T(8,128)(2,1)S(1)}, u32[]{:S(2)}, u32[]{:S(2)}) collective-permute-start(bf16[128,1280]{1,0:T(8,128)(2,1)} %get-tuple-element.23), channel_id=1, source_target_pairs={{0,1},{1,2},{2,3},{3,0},{4,5},{5,6},{6,7},{7,4},{8,9},{9,10},{10,1... | collective-permute-start | bytes 983048 | tf_op jit(solution)/shard_map/ppermute | solution.py:98
  5.4 2.6 %collective-permute-start.1 = (bf16[128,1280]{1,0:T(8,128)(2,1)}, bf16[128,1280]{1,0:T(8,128)(2,1)}, u32[]{:S(2)}, u32[]{:S(2)}) collective-permute-start(bf16[128,1280]{1,0:T(8,128)(2,1)} %get-tuple-element.25), channel_id=1, source_target_pairs={{0,2},{1,3},{2,0},{3,1},{4,6},{5,7},{6,4},{7,5},{8,10},{9,11},{10,... | collective-permute-start | bytes 983048 | tf_op jit(solution)/shard_map/ppermute | solution.py:98
  8.0 1.3 collective-permute-start.2
  9.7 1.5 collective-permute-start.7
  11.3 5.1 %collective-permute-done = bf16[128,1280]{1,0:T(8,128)(2,1)S(1)} collective-permute-done((bf16[128,1280]{1,0:T(8,128)(2,1)}, bf16[128,1280]{1,0:T(8,128)(2,1)S(1)}, u32[]{:S(2)}, u32[]{:S(2)}) %collective-permute-start) | collective-permute-done | bytes 327712 | tf_op jit(solution)/shard_map/ppermute | solution.py:98
  16.3 13.3 %collective-permute-done.1 = bf16[128,1280]{1,0:T(8,128)(2,1)} collective-permute-done((bf16[128,1280]{1,0:T(8,128)(2,1)}, bf16[128,1280]{1,0:T(8,128)(2,1)}, u32[]{:S(2)}, u32[]{:S(2)}) %collective-permute-start.1) | collective-permute-done | bytes 327712 | tf_op jit(solution)/shard_map/ppermute | solution.py:98
  29.7 0.5 collective-permute-start.6
  30.2 1.2 pad_maximum_fusion.a_1_
  31.4 1.6 collective-permute-start.8
  33.0 1.1 copy-done.2
  34.0 1.1 copy-done.3
  35.1 1.1 copy-done.4
  36.2 1.2 copy-done.5
  37.3 24.9 %collective-permute-done.8.a_1_ = bf16[512,1280]{1,0:T(8,128)(2,1)} collective-permute-done((bf16[512,1280]{1,0:T(8,128)(2,1)S(1)}, bf16[512,1280]{1,0:T(8,128)(2,1)}, u32[]{:S(2)}, u32[]{:S(2)}) %collective-permute-start.8) | collective-permute-done | bytes 1310752 | tf_op jit(solution)/shard_map/ppermute | solution.py:117
  62.2 30.6 %shard_map.65 = (bf16[10,512,128]{2,1,0:T(8,128)(2,1)}, f32[10,8,512]{2,1,0:T(8,128)}) custom-call(s32[4]{0:T(128)} %copy-done.8, bf16[512,1280]{1,0:T(8,128)(2,1)} %collective-permute-done.8.a_1_, bf16[512,1280]{1,0:T(8,128)(2,1)} %a_2_.3, bf16[512,1280]{1,0:T(8,128)(2,1)} %copy-done.2, bf16[512,1280]{1,0:T(8,128)(2,1)} %a_4_.3, ...), custom_call_target="tpu_custom_call" | custom-call | tf_op jit(solution)/shard_map/pallas_call | solution.py:65
  92.8 1.6 collective-permute-start.10
  94.4 0.5 collective-permute-start.9
  95.0 0.7 fusion.3.a_0_
  95.6 30.6 %shard_map.64 = (f32[10,512,128]{2,1,0:T(8,128)}, f32[10,8,512]{2,1,0:T(8,128)}) custom-call(s32[4]{0:T(128)} %fusion.3.a_0_, bf16[512,1280]{1,0:T(8,128)(2,1)} %copy-done.6, bf16[512,1280]{1,0:T(8,128)(2,1)} %a_2_.3, bf16[512,1280]{1,0:T(8,128)(2,1)} %copy-done.2, bf16[512,1280]{1,0:T(8,128)(2,1)} %a_4_.3, bf16[512,1280]{1,0:T(8,128)(2,1)} %copy-done.3, ...), custom_call_target="tpu_custom_call" | custom-call | tf_op jit(solution)/shard_map/pallas_call | solution.py:65
  126.2 1.0 copy.17
  127.3 4.6 %fusion = bf16[512,10,128]{2,0,1:T(8,128)(2,1)S(1)} fusion(f32[10,512]{1,0:T(8,128)S(1)} %get-tuple-element.15, f32[10,512]{1,0:T(8,128)S(1)} %get-tuple-element.16, bf16[10,512,128]{2,1,0:T(8,128)(2,1)S(1)} %collective-permute-done.10, f32[10,512,128]{2,1,0:T(8,128)} %get-tuple-element.9, f32[10,512]{1,0:T(8,128)S(1)} %get-tuple-element.17), kind=kLoop, calls=%fused_computation.2 | loop fusion | flops 3932160 | bytes 5304320 | tf_op jit(solution)/shard_map/transpose | solution.py:163
  132.1 0.2 copy.20
  132.3 8.6 %collective-permute-start.11 = (bf16[128,1280]{0,1:T(8,128)(2,1)S(1)}, bf16[128,1280]{0,1:T(8,128)(2,1)S(1)}, u32[]{:S(2)}, u32[]{:S(2)}) collective-permute-start(bf16[128,1280]{0,1:T(8,128)(2,1)S(1)} %bitcast.33), channel_id=1, source_target_pairs={{0,3},{1,0},{2,1},{3,2},{4,7},{5,4},{6,5},{7,6},{8,11},{9,8},{10,9... | collective-permute-start | bytes 983048 | tf_op jit(solution)/shard_map/ppermute | solution.py:170
  141.3 0.2 copy.22
  141.5 0.5 collective-permute-start.12
  142.2 0.2 collective-permute-start.13
  142.6 6.5 %collective-permute-done.11 = bf16[128,1280]{0,1:T(8,128)(2,1)S(1)} collective-permute-done((bf16[128,1280]{0,1:T(8,128)(2,1)S(1)}, bf16[128,1280]{0,1:T(8,128)(2,1)S(1)}, u32[]{:S(2)}, u32[]{:S(2)}) %collective-permute-start.11) | collective-permute-done | bytes 327712 | tf_op jit(solution)/shard_map/ppermute | solution.py:170
  149.3 19.9 %collective-permute-done.12 = bf16[128,1280]{0,1:T(8,128)(2,1)} collective-permute-done((bf16[128,1280]{0,1:T(8,128)(2,1)S(1)}, bf16[128,1280]{0,1:T(8,128)(2,1)}, u32[]{:S(2)}, u32[]{:S(2)}) %collective-permute-start.12) | collective-permute-done | bytes 327712 | tf_op jit(solution)/shard_map/ppermute | solution.py:170
  169.2 1.1 copy.23
  170.6 0.9 copy-done.7
  171.4 0.7 constant_dynamic-update-slice_fusion
  (42 shorter events, 1.8 us)
Async XLA Ops:
  0.0 9.4 %copy-start.9 = (s32[1,6]{1,0:T(1,128)S(1)}, s32[1,6]{1,0:T(1,128)}, u32[]{:S(2)}) copy-start(s32[1,6]{1,0:T(1,128)} %param.11) | copy-start | bytes 76
  0.0 11.3 %copy-start = (bf16[512,1280]{1,0:T(8,128)(2,1)S(1)}, bf16[512,1280]{1,0:T(8,128)(2,1)}, u32[]{:S(2)}) copy-start(bf16[512,1280]{1,0:T(8,128)(2,1)} %a_2_.3) | copy-start | bytes 3932164
  0.0 16.3 %copy-start.1 = (bf16[512,1280]{1,0:T(8,128)(2,1)S(1)}, bf16[512,1280]{1,0:T(8,128)(2,1)}, u32[]{:S(2)}) copy-start(bf16[512,1280]{1,0:T(8,128)(2,1)} %a_4_.3) | copy-start | bytes 3932164
  2.4 14.0 %collective-permute-start = (bf16[128,1280]{1,0:T(8,128)(2,1)}, bf16[128,1280]{1,0:T(8,128)(2,1)S(1)}, u32[]{:S(2)}, u32[]{:S(2)}) collective-permute-start(bf16[128,1280]{1,0:T(8,128)(2,1)} %get-tuple-element.23), channel_id=1, source_target_pairs={{0,1},{1,2},{2,3},{3,0},{4,5},{5,6},{6,7},{7,4},{8,9},{9,10},{10,1... | collective-permute-start | bytes 983048 | tf_op jit(solution)/shard_map/ppermute | solution.py:98
  5.4 24.2 %collective-permute-start.1 = (bf16[128,1280]{1,0:T(8,128)(2,1)}, bf16[128,1280]{1,0:T(8,128)(2,1)}, u32[]{:S(2)}, u32[]{:S(2)}) collective-permute-start(bf16[128,1280]{1,0:T(8,128)(2,1)} %get-tuple-element.25), channel_id=1, source_target_pairs={{0,2},{1,3},{2,0},{3,1},{4,6},{5,7},{6,4},{7,5},{8,10},{9,11},{10,... | collective-permute-start | bytes 983048 | tf_op jit(solution)/shard_map/ppermute | solution.py:98
  8.0 21.6 %collective-permute-start.2 = (bf16[128,1280]{1,0:T(8,128)(2,1)}, bf16[128,1280]{1,0:T(8,128)(2,1)}, u32[]{:S(2)}, u32[]{:S(2)}) collective-permute-start(bf16[128,1280]{1,0:T(8,128)(2,1)} %get-tuple-element.24), channel_id=1, source_target_pairs={{0,3},{1,0},{2,1},{3,2},{4,7},{5,4},{6,5},{7,6},{8,11},{9,8},{10,9... | collective-permute-start | bytes 983048 | tf_op jit(solution)/shard_map/ppermute | solution.py:98
  9.7 21.6 %collective-permute-start.7 = (s32[4]{0:T(128)S(1)}, s32[4]{0:T(128)S(1)}, u32[]{:S(2)}, u32[]{:S(2)}) collective-permute-start(s32[4]{0:T(128)S(1)} %fusion.4), channel_id=1, source_target_pairs={{0,8},{4,12},{8,0},{12,4},{1,9},{5,13},{9,1},{13,5},{2,10},{6,14},... | collective-permute-start | bytes 56 | tf_op jit(solution)/shard_map/ppermute | solution.py:117
  11.3 21.7 %collective-permute-start.3 = (bf16[512,1280]{1,0:T(8,128)(2,1)S(1)}, bf16[512,1280]{1,0:T(8,128)(2,1)S(1)}, u32[]{:S(2)}, u32[]{:S(2)}) collective-permute-start(bf16[512,1280]{1,0:T(8,128)(2,1)S(1)} %copy-done), channel_id=1, source_target_pairs={{0,4},{4,0},{8,12},{12,8},{1,5},{5,1},{9,13},{13,9},{2,6},{6,2},{1... | collective-permute-start | bytes 3932168 | tf_op jit(solution)/shard_map/ppermute | solution.py:120
  16.3 16.6 %collective-permute-start.4 = (bf16[512,1280]{1,0:T(8,128)(2,1)S(1)}, bf16[512,1280]{1,0:T(8,128)(2,1)S(1)}, u32[]{:S(2)}, u32[]{:S(2)}) collective-permute-start(bf16[512,1280]{1,0:T(8,128)(2,1)S(1)} %copy-done.1), channel_id=1, source_target_pairs={{0,4},{4,0},{8,12},{12,8},{1,5},{5,1},{9,13},{13,9},{2,6},{6,2},{1... | collective-permute-start | bytes 3932168 | tf_op jit(solution)/shard_map/ppermute | solution.py:120
  29.7 4.4 %collective-permute-start.5 = (bf16[512,1280]{1,0:T(8,128)(2,1)}, bf16[512,1280]{1,0:T(8,128)(2,1)S(1)}, u32[]{:S(2)}, u32[]{:S(2)}) collective-permute-start(bf16[512,1280]{1,0:T(8,128)(2,1)} %a_6_.3), channel_id=1, source_target_pairs={{0,4},{4,0},{8,12},{12,8},{1,5},{5,1},{9,13},{13,9},{2,6},{6,2},{1... | collective-permute-start | bytes 3932168 | tf_op jit(solution)/shard_map/ppermute | solution.py:120
  29.7 5.5 %collective-permute-start.6 = (bf16[512,1280]{1,0:T(8,128)(2,1)}, bf16[512,1280]{1,0:T(8,128)(2,1)S(1)}, u32[]{:S(2)}, u32[]{:S(2)}) collective-permute-start(bf16[512,1280]{1,0:T(8,128)(2,1)} %a_8_.3), channel_id=1, source_target_pairs={{0,4},{4,0},{8,12},{12,8},{1,5},{5,1},{9,13},{13,9},{2,6},{6,2},{1... | collective-permute-start | bytes 3932168 | tf_op jit(solution)/shard_map/ppermute | solution.py:120
  31.3 3.8 %copy-start.6 = (bf16[512,1280]{1,0:T(8,128)(2,1)}, bf16[512,1280]{1,0:T(8,128)(2,1)S(1)}, u32[]{:S(2)}) copy-start(bf16[512,1280]{1,0:T(8,128)(2,1)S(1)} %pad_maximum_fusion.a_1_) | copy-start | bytes 3932164
  31.4 30.9 %copy-start.8 = (s32[4]{0:T(128)}, s32[4]{0:T(128)S(1)}, u32[]{:S(2)}) copy-start(s32[4]{0:T(128)S(1)} %collective-permute-done.7.a_0_) | copy-start | bytes 52
  31.4 30.9 %collective-permute-start.8 = (bf16[512,1280]{1,0:T(8,128)(2,1)S(1)}, bf16[512,1280]{1,0:T(8,128)(2,1)}, u32[]{:S(2)}, u32[]{:S(2)}) collective-permute-start(bf16[512,1280]{1,0:T(8,128)(2,1)S(1)} %pad_maximum_fusion.a_1_), channel_id=1, source_target_pairs={{0,8},{4,12},{8,0},{12,4},{1,9},{5,13},{9,1},{13,5},{2,10},{6,14},... | collective-permute-start | bytes 3932168 | tf_op jit(solution)/shard_map/ppermute | solution.py:117
  33.0 1.1 copy-start.2
  34.0 1.1 copy-start.3
  35.1 1.1 copy-start.4
  36.2 1.2 copy-start.5
  92.8 34.5 %collective-permute-start.10 = (bf16[10,512,128]{2,1,0:T(8,128)(2,1)}, bf16[10,512,128]{2,1,0:T(8,128)(2,1)S(1)}, u32[]{:S(2)}, u32[]{:S(2)}) collective-permute-start(bf16[10,512,128]{2,1,0:T(8,128)(2,1)} %get-tuple-element.12), channel_id=1, source_target_pairs={{0,8},{4,12},{8,0},{12,4},{1,9},{5,13},{9,1},{13,5},{2,10},{6,14},... | collective-permute-start | bytes 3932168 | tf_op jit(solution)/shard_map/ppermute | solution.py:154
  94.4 32.8 %collective-permute-start.9 = (f32[10,8,512]{2,1,0:T(8,128)}, f32[10,8,512]{2,1,0:T(8,128)S(1)}, u32[]{:S(2)}, u32[]{:S(2)}) collective-permute-start(f32[10,8,512]{2,1,0:T(8,128)} %get-tuple-element.11), channel_id=1, source_target_pairs={{0,8},{4,12},{8,0},{12,4},{1,9},{5,13},{9,1},{13,5},{2,10},{6,14},... | collective-permute-start | bytes 491528 | tf_op jit(solution)/shard_map/ppermute | solution.py:154
  132.3 16.8 %collective-permute-start.11 = (bf16[128,1280]{0,1:T(8,128)(2,1)S(1)}, bf16[128,1280]{0,1:T(8,128)(2,1)S(1)}, u32[]{:S(2)}, u32[]{:S(2)}) collective-permute-start(bf16[128,1280]{0,1:T(8,128)(2,1)S(1)} %bitcast.33), channel_id=1, source_target_pairs={{0,3},{1,0},{2,1},{3,2},{4,7},{5,4},{6,5},{7,6},{8,11},{9,8},{10,9... | collective-permute-start | bytes 983048 | tf_op jit(solution)/shard_map/ppermute | solution.py:170
  141.5 27.7 %collective-permute-start.12 = (bf16[128,1280]{0,1:T(8,128)(2,1)S(1)}, bf16[128,1280]{0,1:T(8,128)(2,1)}, u32[]{:S(2)}, u32[]{:S(2)}) collective-permute-start(bf16[128,1280]{0,1:T(8,128)(2,1)S(1)} %bitcast.35), channel_id=1, source_target_pairs={{0,2},{1,3},{2,0},{3,1},{4,6},{5,7},{6,4},{7,5},{8,10},{9,11},{10,... | collective-permute-start | bytes 983048 | tf_op jit(solution)/shard_map/ppermute | solution.py:170
  142.2 28.2 %collective-permute-start.13 = (bf16[128,1280]{0,1:T(8,128)(2,1)S(1)}, bf16[128,1280]{0,1:T(8,128)(2,1)S(1)}, u32[]{:S(2)}, u32[]{:S(2)}) collective-permute-start(bf16[128,1280]{0,1:T(8,128)(2,1)S(1)} %bitcast.34), channel_id=1, source_target_pairs={{0,1},{1,2},{2,3},{3,0},{4,5},{5,6},{6,7},{7,4},{8,9},{9,10},{10,1... | collective-permute-start | bytes 983048 | tf_op jit(solution)/shard_map/ppermute | solution.py:170
  170.4 1.1 copy-start.7

commit v8 on v6

--- a/solution.py
+++ b/solution.py
@@ -99,7 +99,6 @@
     query_block = jnp.concatenate(query_parts, axis=0)
 
     back = [(i, (i - 2) % seq_count) for i in range(seq_count)]
-    forth = [(i, (i + 2) % seq_count) for i in range(seq_count)]
     t = (s - 2) % seq_count
     t_chip = t // 2
     remote_ids = [seq_count + t, seq_count + (t ^ 1), t, t ^ 1]
@@ -148,25 +147,41 @@
         [s >= 0, s >= 0, chip == 0, chip == 0],
     )
     local_out, local_lse = attend_partial(local_flags, query_block, keys, values, jnp.float32)
+    got_query, local_out, local_lse = lax.optimization_barrier((got_query, local_out, local_lse))
 
     far_out, far_lse = attend_partial(got_flags, got_query, remote_keys, remote_values, jnp.bfloat16)
-    far_out, far_lse = lax.ppermute((far_out, far_lse), "seq", forth)
-
-    rows_all = query_block.shape[0]
-    lse_a = local_lse[:, 0, :][:, :, None]
-    lse_b = far_lse[:, 0, :][:, :, None]
-    top = jnp.maximum(lse_a, lse_b)
-    weight_a = jnp.exp(lse_a - top)
-    weight_b = jnp.exp(lse_b - top)
-    mixed = (local_out * weight_a + far_out.astype(jnp.float32) * weight_b) / (weight_a + weight_b)
-    heads_out = jnp.transpose(mixed.astype(jnp.bfloat16), (1, 0, 2)).reshape(rows_all, head_width)
-
     rows = queries.shape[0]
+    near_lse = local_lse[:, 0, :]
+    far_lse = far_lse[:, 0, :]
     result = jnp.zeros((rows, queries.shape[1]), jnp.bfloat16)
     for d in range(sp_count):
-        piece = heads_out[d * rows : (d + 1) * rows]
+        near_part = local_out[:, d * rows : (d + 1) * rows]
+        near_stat = near_lse[:, d * rows : (d + 1) * rows]
         if d:
-            piece = lax.ppermute(piece, "sp", [(i, (i - d) % sp_count) for i in range(sp_count)])
+            near_part, near_stat = lax.ppermute(
+                (near_part.astype(jnp.bfloat16), near_stat),
+                "sp",
+                [(i, (i - d) % sp_count) for i in range(sp_count)],
+            )
+        diagonal = [
+            (i * sp_count + j, ((i + 2) % seq_count) * sp_count + (j - d) % sp_count)
+            for i in range(seq_count)
+            for j in range(sp_count)
+        ]
+        far_part, far_stat = lax.ppermute(
+            (far_out[:, d * rows : (d + 1) * rows], far_lse[:, d * rows : (d + 1) * rows]),
+            ("seq", "sp"),
+            diagonal,
+        )
+        lse_a = near_stat[:, :, None]
+        lse_b = far_stat[:, :, None]
+        top = jnp.maximum(lse_a, lse_b)
+        weight_a = jnp.exp(lse_a - top)
+        weight_b = jnp.exp(lse_b - top)
+        mixed = (
+            near_part.astype(jnp.float32) * weight_a + far_part.astype(jnp.float32) * weight_b
+        ) / (weight_a + weight_b)
+        piece = jnp.transpose(mixed.astype(jnp.bfloat16), (1, 0, 2)).reshape(rows, head_width)
         columns = ((sp_place + d) % sp_count) * head_width
         result = lax.dynamic_update_slice_in_dim(result, piece, columns, 1)
     return result

time: 169 us -> 180 us (1.065)
  the two profiles are of different devices: /device:TPU:0 before, /device:TPU:27 now
where the time goes in v8:
time: 180 us; the launch traced here: 178 us
  waiting for transfers between devices  75.5 us (42%)
  Pallas kernels  53.3 us (30%)
  starting transfers between devices  23.1 us (13%)
  local copies, waits for them, and re-layouts  18.1 us (10%)
  other arithmetic  8.15 us (5%)
    pallas_call x2, Pallas kernels, attend_partial(): pl.pallas_call(lambda *a: partial_kernel(nsrc, *a), grid_spec=grid_spec,...  53.3 us
    ppermute x6, waiting for transfers between devices, local(): lax.ppermute((near_part.astype(jnp.bfloat16), near_stat), 'sp', [(i, (i -...  40.1 us
    ppermute x3, waiting for transfers between devices, local(): lax.ppermute(piece, 'sp', [(i, (i + d) % sp_count) for i in range(sp_coun...  24.5 us
    ppermute x8, waiting for transfers between devices, local(): lax.ppermute((far_out[:, d * rows:(d + 1) * rows], far_lse[:, d * rows:(d...  9.37 us
    ppermute x8, starting transfers between devices, local(): lax.ppermute((far_out[:, d * rows:(d + 1) * rows], far_lse[:, d * rows:(d...  7.9 us
    ppermute x6, starting transfers between devices, local(): lax.ppermute((near_part.astype(jnp.bfloat16), near_stat), 'sp', [(i, (i -...  7.13 us
    transpose x4, other arithmetic, local(): jnp.transpose(mixed.astype(jnp.bfloat16), (1, 0, 2))  5.79 us
    ppermute x4, starting transfers between devices, local(): lax.ppermute((new_keys, new_values, cache_keys, cache_values), 'seq', swap)  5.06 us
  transfers between devices with their start and end apart: 23, of which 7 were waited for; matrix products, arithmetic and copies ran while one was open for 10% of the time, Pallas kernels for 15%

profile of v8, /device:TPU:27, one launch (start us, length us, event | category | flops | bytes accessed | tf_op | source)
XLA Modules:
  0.0 178.4 jit_solution(9913479323604293803)
XLA Ops:
  0.0 1.5 constant_dynamic-slice_fusion.3
  1.6 1.3 collective-permute-start.1
  3.1 1.5 collective-permute-start.4
  4.7 5.5 %collective-permute-done = bf16[128,1280]{1,0:T(8,128)(2,1)S(1)} collective-permute-done((bf16[128,1280]{1,0:T(8,128)(2,1)S(1)}, bf16[128,1280]{1,0:T(8,128)(2,1)S(1)}, u32[]{:S(2)}, u32[]{:S(2)}) %collective-permute-start) | collective-permute-done | bytes 327712 | tf_op jit(solution)/shard_map/ppermute | solution.py:97
  10.1 1.9 %collective-permute-start.6 = (bf16[512,1280]{1,0:T(8,128)(2,1)}, bf16[512,1280]{1,0:T(8,128)(2,1)}, u32[]{:S(2)}, u32[]{:S(2)}) collective-permute-start(bf16[512,1280]{1,0:T(8,128)(2,1)} %a_6_.3), channel_id=1, source_target_pairs={{0,4},{4,0},{8,12},{12,8},{1,5},{5,1},{9,13},{13,9},{2,6},{6,2},{1... | collective-permute-start | bytes 3932168 | tf_op jit(solution)/shard_map/ppermute | solution.py:118
  12.1 19.0 %collective-permute-done.1 = bf16[128,1280]{1,0:T(8,128)(2,1)S(1)} collective-permute-done((bf16[128,1280]{1,0:T(8,128)(2,1)S(1)}, bf16[128,1280]{1,0:T(8,128)(2,1)S(1)}, u32[]{:S(2)}, u32[]{:S(2)}) %collective-permute-start.1) | collective-permute-done | bytes 327712 | tf_op jit(solution)/shard_map/ppermute | solution.py:97
  31.1 1.5 collective-permute-start.7
  32.7 1.1 pad_maximum_fusion.a_1_
  33.8 1.2 collective-permute-start.3
  36.2 26.7 %shard_map.64 = (f32[10,512,128]{2,1,0:T(8,128)}, f32[10,8,512]{2,1,0:T(8,128)}) custom-call(s32[4]{0:T(128)} %fusion.12.a_0_, bf16[512,1280]{1,0:T(8,128)(2,1)} %pad_maximum_fusion.a_1_, bf16[512,1280]{1,0:T(8,128)(2,1)} %a_2_.3, bf16[512,1280]{1,0:T(8,128)(2,1)} %collective-permute-done.4.a_3_, bf16[512,1280]{1,0:T(8,128)(2,1)} %a_4_.3, ...), custom_call_target="tpu_custom_call" | custom-call | tf_op jit(solution)/shard_map/pallas_call | solution.py:64
  63.0 1.6 collective-permute-done.3.a_1_
  65.1 26.6 %shard_map.65 = (bf16[10,512,128]{2,1,0:T(8,128)(2,1)}, f32[10,8,512]{2,1,0:T(8,128)}) custom-call(s32[4]{0:T(128)} %copy-done.6, bf16[512,1280]{1,0:T(8,128)(2,1)} %collective-permute-done.3.a_1_, bf16[512,1280]{1,0:T(8,128)(2,1)} %a_2_.3, bf16[512,1280]{1,0:T(8,128)(2,1)} %collective-permute-done.4.a_3_, bf16[512,1280]{1,0:T(8,128)(2,1)} %a_4_.3, ...), custom_call_target="tpu_custom_call" | custom-call | tf_op jit(solution)/shard_map/pallas_call | solution.py:64
  91.6 0.9 slice.60
  92.6 1.3 collective-permute-start.9
  94.1 2.4 %fusion.27 = (bf16[10,128,128]{2,1,0:T(8,128)(2,1)S(1)}, bf16[10,128,128]{2,1,0:T(8,128)(2,1)S(1)}, bf16[10,128,128]{2,1,0:T(8,128)(2,1)}, bf16[10,128,128]{2,1,0:T(8,128)(2,1)}) fusion(bf16[10,512,128]{2,1,0:T(8,128)(2,1)} %get-tuple-element.18), kind=kLoop, calls=%fused_computation.48 | loop fusion | bytes 2621440 | tf_op jit(solution)/shard_map/slice | solution.py:172
  96.4 2.1 %collective-permute-start.22 = (bf16[10,128,128]{2,1,0:T(8,128)(2,1)S(1)}, bf16[10,128,128]{2,1,0:T(8,128)(2,1)S(1)}, u32[]{:S(2)}, u32[]{:S(2)}) collective-permute-start(bf16[10,128,128]{2,1,0:T(8,128)(2,1)S(1)} %get-tuple-element.36), channel_id=1, source_target_pairs={{0,9},{1,10},{2,11},{3,8},{4,13},{5,14},{6,15},{7,12},{8,1},{9,2},... | collective-permute-start | bytes 983048 | tf_op jit(solution)/shard_map/ppermute | solution.py:171
  99.6 2.6 %collective-permute-start.19 = (bf16[10,128,128]{2,1,0:T(8,128)(2,1)S(1)}, bf16[10,128,128]{2,1,0:T(8,128)(2,1)S(1)}, u32[]{:S(2)}, u32[]{:S(2)}) collective-permute-start(bf16[10,128,128]{2,1,0:T(8,128)(2,1)S(1)} %get-tuple-element.33), channel_id=1, source_target_pairs={{0,1},{1,2},{2,3},{3,0},{4,5},{5,6},{6,7},{7,4},{8,9},{9,10},{10,1... | collective-permute-start | bytes 983048 | tf_op jit(solution)/shard_map/ppermute | solution.py:161
  102.3 3.3 %collective-permute-start.18 = (bf16[10,128,128]{2,1,0:T(8,128)(2,1)S(1)}, bf16[10,128,128]{2,1,0:T(8,128)(2,1)S(1)}, u32[]{:S(2)}, u32[]{:S(2)}) collective-permute-start(bf16[10,128,128]{2,1,0:T(8,128)(2,1)S(1)} %get-tuple-element.37), channel_id=1, source_target_pairs={{0,10},{1,11},{2,8},{3,9},{4,14},{5,15},{6,12},{7,13},{8,2},{9,3},... | collective-permute-start | bytes 983048 | tf_op jit(solution)/shard_map/ppermute | solution.py:171
  105.8 9.4 %collective-permute-done.17 = f32[10,128]{1,0:T(8,128)S(1)} collective-permute-done((f32[10,128]{1,0:T(8,128)S(1)}, f32[10,128]{1,0:T(8,128)S(1)}, u32[]{:S(2)}, u32[]{:S(2)}) %collective-permute-start.17) | collective-permute-done | bytes 5152 | tf_op jit(solution)/shard_map/ppermute | solution.py:171
  115.1 13.2 %collective-permute-done.16 = f32[10,128]{1,0:T(8,128)S(1)} collective-permute-done((f32[10,128]{1,0:T(8,128)S(1)}, f32[10,128]{1,0:T(8,128)S(1)}, u32[]{:S(2)}, u32[]{:S(2)}) %collective-permute-start.16) | collective-permute-done | bytes 5152 | tf_op jit(solution)/shard_map/ppermute | solution.py:161
  129.1 3.1 %collective-permute-start.15 = (bf16[10,128,128]{2,1,0:T(8,128)(2,1)S(1)}, bf16[10,128,128]{2,1,0:T(8,128)(2,1)S(1)}, u32[]{:S(2)}, u32[]{:S(2)}) collective-permute-start(bf16[10,128,128]{2,1,0:T(8,128)(2,1)S(1)} %get-tuple-element.34), channel_id=1, source_target_pairs={{0,2},{1,3},{2,0},{3,1},{4,6},{5,7},{6,4},{7,5},{8,10},{9,11},{10,... | collective-permute-start | bytes 983048 | tf_op jit(solution)/shard_map/ppermute | solution.py:161
  133.3 1.2 collective-permute-start.10
  135.1 26.2 %collective-permute-done.15 = bf16[10,128,128]{2,1,0:T(8,128)(2,1)S(1)} collective-permute-done((bf16[10,128,128]{2,1,0:T(8,128)(2,1)S(1)}, bf16[10,128,128]{2,1,0:T(8,128)(2,1)S(1)}, u32[]{:S(2)}, u32[]{:S(2)}) %collective-permute-start.15) | collective-permute-done | bytes 327712 | tf_op jit(solution)/shard_map/ppermute | solution.py:161
  162.8 1.1 copy.25
  163.9 0.9 copy.22
  164.8 1.1 copy.23
  166.0 2.4 %fusion = bf16[128,10,128]{2,0,1:T(8,128)(2,1)} fusion(f32[10,128]{1,0:T(8,128)S(1)} %get-tuple-element.27, f32[10,128]{1,0:T(8,128)S(1)} %get-tuple-element.28, bf16[10,128,128]{2,1,0:T(8,128)(2,1)} %collective-permute-done.14, f32[10,128]{1,0:T(8,128)S(1)} %get-tuple-element.29, bf16[10,128,128]{2,1,0:T(8,128)(2,1)} %collective-permute-done.11), kind=kLoop, calls=%fused_computation.5 | loop fusion | flops 1146880 | bytes 998400 | tf_op jit(solution)/shard_map/transpose | solution.py:184
  168.4 1.9 %copy.20 = bf16[128,10,128]{0,2,1:T(8,128)(2,1)} copy(bf16[128,10,128]{2,0,1:T(8,128)(2,1)} %fusion) | data formatting | bytes 655360 | tf_op jit(solution)/shard_map/transpose | solution.py:184
  170.2 1.9 %copy.21 = bf16[128,1280]{1,0:T(8,128)(2,1)} copy(bf16[128,1280]{0,1:T(8,128)(2,1)} %bitcast.32) | data formatting | bytes 655360 | tf_op jit(solution)/shard_map/reshape | solution.py:184
  172.1 2.3 %fusion.3 = bf16[128,10,128]{2,0,1:T(8,128)(2,1)} fusion(f32[10,128]{1,0:T(8,128)S(1)} %get-tuple-element.47, f32[10,128]{1,0:T(8,128)S(1)} %get-tuple-element.48, bf16[10,128,128]{2,1,0:T(8,128)(2,1)} %collective-permute-done.10, f32[10,128]{1,0:T(8,128)S(1)} %get-tuple-element.49, f32[10,512,128]{2,1,0:T(8,128)S(1)} %copy-done.2), kind=kLoop, calls=%fused_computation.8 | loop fusion | flops 983040 | bytes 1326080 | tf_op jit(solution)/shard_map/transpose | solution.py:184
  174.4 1.2 copy.18
  176.6 1.0 copy-done.3
  (67 shorter events, 9.2 us)
Async XLA Ops:
  0.0 3.1 %copy-start = (bf16[512,1280]{1,0:T(8,128)(2,1)S(1)}, bf16[512,1280]{1,0:T(8,128)(2,1)}, u32[]{:S(2)}) copy-start(bf16[512,1280]{1,0:T(8,128)(2,1)} %a_2_.3) | copy-start | bytes 3932164
  0.0 4.6 %copy-start.1 = (bf16[512,1280]{1,0:T(8,128)(2,1)S(1)}, bf16[512,1280]{1,0:T(8,128)(2,1)}, u32[]{:S(2)}) copy-start(bf16[512,1280]{1,0:T(8,128)(2,1)} %a_4_.3) | copy-start | bytes 3932164
  1.5 8.6 %collective-permute-start = (bf16[128,1280]{1,0:T(8,128)(2,1)S(1)}, bf16[128,1280]{1,0:T(8,128)(2,1)S(1)}, u32[]{:S(2)}, u32[]{:S(2)}) collective-permute-start(bf16[128,1280]{1,0:T(8,128)(2,1)S(1)} %get-tuple-element.41), channel_id=1, source_target_pairs={{0,1},{1,2},{2,3},{3,0},{4,5},{5,6},{6,7},{7,4},{8,9},{9,10},{10,1... | collective-permute-start | bytes 983048 | tf_op jit(solution)/shard_map/ppermute | solution.py:97
  1.6 29.5 %collective-permute-start.1 = (bf16[128,1280]{1,0:T(8,128)(2,1)S(1)}, bf16[128,1280]{1,0:T(8,128)(2,1)S(1)}, u32[]{:S(2)}, u32[]{:S(2)}) collective-permute-start(bf16[128,1280]{1,0:T(8,128)(2,1)S(1)} %get-tuple-element.43), channel_id=1, source_target_pairs={{0,2},{1,3},{2,0},{3,1},{4,6},{5,7},{6,4},{7,5},{8,10},{9,11},{10,... | collective-permute-start | bytes 983048 | tf_op jit(solution)/shard_map/ppermute | solution.py:97
  2.9 29.7 %collective-permute-start.2 = (bf16[128,1280]{1,0:T(8,128)(2,1)S(1)}, bf16[128,1280]{1,0:T(8,128)(2,1)S(1)}, u32[]{:S(2)}, u32[]{:S(2)}) collective-permute-start(bf16[128,1280]{1,0:T(8,128)(2,1)S(1)} %get-tuple-element.42), channel_id=1, source_target_pairs={{0,3},{1,0},{2,1},{3,2},{4,7},{5,4},{6,5},{7,6},{8,11},{9,8},{10,9... | collective-permute-start | bytes 983048 | tf_op jit(solution)/shard_map/ppermute | solution.py:97
  3.1 32.9 %collective-permute-start.4 = (bf16[512,1280]{1,0:T(8,128)(2,1)S(1)}, bf16[512,1280]{1,0:T(8,128)(2,1)}, u32[]{:S(2)}, u32[]{:S(2)}) collective-permute-start(bf16[512,1280]{1,0:T(8,128)(2,1)S(1)} %copy-done), channel_id=1, source_target_pairs={{0,4},{4,0},{8,12},{12,8},{1,5},{5,1},{9,13},{13,9},{2,6},{6,2},{1... | collective-permute-start | bytes 3932168 | tf_op jit(solution)/shard_map/ppermute | solution.py:118
  4.6 31.6 %collective-permute-start.5 = (bf16[512,1280]{1,0:T(8,128)(2,1)S(1)}, bf16[512,1280]{1,0:T(8,128)(2,1)}, u32[]{:S(2)}, u32[]{:S(2)}) collective-permute-start(bf16[512,1280]{1,0:T(8,128)(2,1)S(1)} %copy-done.1), channel_id=1, source_target_pairs={{0,4},{4,0},{8,12},{12,8},{1,5},{5,1},{9,13},{13,9},{2,6},{6,2},{1... | collective-permute-start | bytes 3932168 | tf_op jit(solution)/shard_map/ppermute | solution.py:118
  10.1 26.1 %collective-permute-start.6 = (bf16[512,1280]{1,0:T(8,128)(2,1)}, bf16[512,1280]{1,0:T(8,128)(2,1)}, u32[]{:S(2)}, u32[]{:S(2)}) collective-permute-start(bf16[512,1280]{1,0:T(8,128)(2,1)} %a_6_.3), channel_id=1, source_target_pairs={{0,4},{4,0},{8,12},{12,8},{1,5},{5,1},{9,13},{13,9},{2,6},{6,2},{1... | collective-permute-start | bytes 3932168 | tf_op jit(solution)/shard_map/ppermute | solution.py:118
  31.1 5.1 %collective-permute-start.7 = (bf16[512,1280]{1,0:T(8,128)(2,1)}, bf16[512,1280]{1,0:T(8,128)(2,1)}, u32[]{:S(2)}, u32[]{:S(2)}) collective-permute-start(bf16[512,1280]{1,0:T(8,128)(2,1)} %a_8_.3), channel_id=1, source_target_pairs={{0,4},{4,0},{8,12},{12,8},{1,5},{5,1},{9,13},{13,9},{2,6},{6,2},{1... | collective-permute-start | bytes 3932168 | tf_op jit(solution)/shard_map/ppermute | solution.py:118
  32.7 2.5 %copy-start.7 = (s32[1,6]{1,0:T(1,128)S(1)}, s32[1,6]{1,0:T(1,128)}, u32[]{:S(2)}) copy-start(s32[1,6]{1,0:T(1,128)} %param.11) | copy-start | bytes 76
  33.8 30.7 %collective-permute-start.3 = (bf16[512,1280]{1,0:T(8,128)(2,1)}, bf16[512,1280]{1,0:T(8,128)(2,1)}, u32[]{:S(2)}, u32[]{:S(2)}) collective-permute-start(bf16[512,1280]{1,0:T(8,128)(2,1)} %pad_maximum_fusion.a_1_), channel_id=1, source_target_pairs={{0,8},{4,12},{8,0},{12,4},{1,9},{5,13},{9,1},{13,5},{2,10},{6,14},... | collective-permute-start | bytes 3932168 | tf_op jit(solution)/shard_map/ppermute | solution.py:115
  36.0 28.5 %collective-permute-start.8 = (s32[4]{0:T(128)S(1)}, s32[4]{0:T(128)S(1)}, u32[]{:S(2)}, u32[]{:S(2)}) collective-permute-start(s32[4]{0:T(128)S(1)} %fusion.13), channel_id=1, source_target_pairs={{0,8},{4,12},{8,0},{12,4},{1,9},{5,13},{9,1},{13,5},{2,10},{6,14},... | collective-permute-start | bytes 56 | tf_op jit(solution)/shard_map/ppermute | solution.py:115
  64.5 29.4 %copy-start.5 = (f32[10,8,512]{2,1,0:T(8,128)S(1)}, f32[10,8,512]{2,1,0:T(8,128)}, u32[]{:S(2)}) copy-start(f32[10,8,512]{2,1,0:T(8,128)} %get-tuple-element.15) | copy-start | bytes 491524
  64.5 0.5 copy-start.6
  92.6 6.2 %collective-permute-start.9 = (f32[10,128]{1,0:T(8,128)S(1)}, f32[10,128]{1,0:T(8,128)S(1)}, u32[]{:S(2)}, u32[]{:S(2)}) collective-permute-start(f32[10,128]{1,0:T(8,128)S(1)} %get-tuple-element.53), channel_id=1, source_target_pairs={{0,8},{1,9},{2,10},{3,11},{4,12},{5,13},{6,14},{7,15},{8,0},{9,1},... | collective-permute-start | bytes 15368 | tf_op jit(solution)/shard_map/ppermute | solution.py:171
  94.0 8.3 %collective-permute-start.21 = (f32[10,128]{1,0:T(8,128)S(1)}, f32[10,128]{1,0:T(8,128)S(1)}, u32[]{:S(2)}, u32[]{:S(2)}) collective-permute-start(f32[10,128]{1,0:T(8,128)S(1)} %get-tuple-element.50), channel_id=1, source_target_pairs={{0,9},{1,10},{2,11},{3,8},{4,13},{5,14},{6,15},{7,12},{8,1},{9,2},... | collective-permute-start | bytes 15368 | tf_op jit(solution)/shard_map/ppermute | solution.py:171
  94.1 4.5 %copy-start.2 = (f32[10,512,128]{2,1,0:T(8,128)S(1)}, f32[10,512,128]{2,1,0:T(8,128)}, u32[]{:S(2)}) copy-start(f32[10,512,128]{2,1,0:T(8,128)} %get-tuple-element.14) | copy-start | bytes 7864324
  96.4 36.5 %collective-permute-start.22 = (bf16[10,128,128]{2,1,0:T(8,128)(2,1)S(1)}, bf16[10,128,128]{2,1,0:T(8,128)(2,1)S(1)}, u32[]{:S(2)}, u32[]{:S(2)}) collective-permute-start(bf16[10,128,128]{2,1,0:T(8,128)(2,1)S(1)} %get-tuple-element.36), channel_id=1, source_target_pairs={{0,9},{1,10},{2,11},{3,8},{4,13},{5,14},{6,15},{7,12},{8,1},{9,2},... | collective-permute-start | bytes 983048 | tf_op jit(solution)/shard_map/ppermute | solution.py:171
  98.8 6.7 %collective-permute-start.20 = (f32[10,128]{1,0:T(8,128)S(1)}, f32[10,128]{1,0:T(8,128)S(1)}, u32[]{:S(2)}, u32[]{:S(2)}) collective-permute-start(f32[10,128]{1,0:T(8,128)S(1)} %get-tuple-element.44), channel_id=1, source_target_pairs={{0,1},{1,2},{2,3},{3,0},{4,5},{5,6},{6,7},{7,4},{8,9},{9,10},{10,1... | collective-permute-start | bytes 15368 | tf_op jit(solution)/shard_map/ppermute | solution.py:161
  99.6 33.7 %collective-permute-start.19 = (bf16[10,128,128]{2,1,0:T(8,128)(2,1)S(1)}, bf16[10,128,128]{2,1,0:T(8,128)(2,1)S(1)}, u32[]{:S(2)}, u32[]{:S(2)}) collective-permute-start(bf16[10,128,128]{2,1,0:T(8,128)(2,1)S(1)} %get-tuple-element.33), channel_id=1, source_target_pairs={{0,1},{1,2},{2,3},{3,0},{4,5},{5,6},{6,7},{7,4},{8,9},{9,10},{10,1... | collective-permute-start | bytes 983048 | tf_op jit(solution)/shard_map/ppermute | solution.py:161
  102.3 12.9 %collective-permute-start.17 = (f32[10,128]{1,0:T(8,128)S(1)}, f32[10,128]{1,0:T(8,128)S(1)}, u32[]{:S(2)}, u32[]{:S(2)}) collective-permute-start(f32[10,128]{1,0:T(8,128)S(1)} %get-tuple-element.51), channel_id=1, source_target_pairs={{0,10},{1,11},{2,8},{3,9},{4,14},{5,15},{6,12},{7,13},{8,2},{9,3},... | collective-permute-start | bytes 15368 | tf_op jit(solution)/shard_map/ppermute | solution.py:171
  102.3 32.8 %collective-permute-start.18 = (bf16[10,128,128]{2,1,0:T(8,128)(2,1)S(1)}, bf16[10,128,128]{2,1,0:T(8,128)(2,1)S(1)}, u32[]{:S(2)}, u32[]{:S(2)}) collective-permute-start(bf16[10,128,128]{2,1,0:T(8,128)(2,1)S(1)} %get-tuple-element.37), channel_id=1, source_target_pairs={{0,10},{1,11},{2,8},{3,9},{4,14},{5,15},{6,12},{7,13},{8,2},{9,3},... | collective-permute-start | bytes 983048 | tf_op jit(solution)/shard_map/ppermute | solution.py:171
  105.5 22.8 %collective-permute-start.16 = (f32[10,128]{1,0:T(8,128)S(1)}, f32[10,128]{1,0:T(8,128)S(1)}, u32[]{:S(2)}, u32[]{:S(2)}) collective-permute-start(f32[10,128]{1,0:T(8,128)S(1)} %get-tuple-element.45), channel_id=1, source_target_pairs={{0,2},{1,3},{2,0},{3,1},{4,6},{5,7},{6,4},{7,5},{8,10},{9,11},{10,... | collective-permute-start | bytes 15368 | tf_op jit(solution)/shard_map/ppermute | solution.py:161
  115.1 14.0 %collective-permute-start.13 = (f32[10,128]{1,0:T(8,128)S(1)}, f32[10,128]{1,0:T(8,128)S(1)}, u32[]{:S(2)}, u32[]{:S(2)}) collective-permute-start(f32[10,128]{1,0:T(8,128)S(1)} %get-tuple-element.52), channel_id=1, source_target_pairs={{0,11},{1,8},{2,9},{3,10},{4,15},{5,12},{6,13},{7,14},{8,3},{9,0},... | collective-permute-start | bytes 15368 | tf_op jit(solution)/shard_map/ppermute | solution.py:171
  128.4 4.5 %collective-permute-start.12 = (f32[10,128]{1,0:T(8,128)S(1)}, f32[10,128]{1,0:T(8,128)S(1)}, u32[]{:S(2)}, u32[]{:S(2)}) collective-permute-start(f32[10,128]{1,0:T(8,128)S(1)} %get-tuple-element.46), channel_id=1, source_target_pairs={{0,3},{1,0},{2,1},{3,2},{4,7},{5,4},{6,5},{7,6},{8,11},{9,8},{10,9... | collective-permute-start | bytes 15368 | tf_op jit(solution)/shard_map/ppermute | solution.py:161
  129.1 32.2 %collective-permute-start.15 = (bf16[10,128,128]{2,1,0:T(8,128)(2,1)S(1)}, bf16[10,128,128]{2,1,0:T(8,128)(2,1)S(1)}, u32[]{:S(2)}, u32[]{:S(2)}) collective-permute-start(bf16[10,128,128]{2,1,0:T(8,128)(2,1)S(1)} %get-tuple-element.34), channel_id=1, source_target_pairs={{0,2},{1,3},{2,0},{3,1},{4,6},{5,7},{6,4},{7,5},{8,10},{9,11},{10,... | collective-permute-start | bytes 983048 | tf_op jit(solution)/shard_map/ppermute | solution.py:161
  132.9 33.0 %collective-permute-start.14 = (bf16[10,128,128]{2,1,0:T(8,128)(2,1)}, bf16[10,128,128]{2,1,0:T(8,128)(2,1)}, u32[]{:S(2)}, u32[]{:S(2)}) collective-permute-start(bf16[10,128,128]{2,1,0:T(8,128)(2,1)} %get-tuple-element.38), channel_id=1, source_target_pairs={{0,11},{1,8},{2,9},{3,10},{4,15},{5,12},{6,13},{7,14},{8,3},{9,0},... | collective-permute-start | bytes 983048 | tf_op jit(solution)/shard_map/ppermute | solution.py:171
  132.9 33.0 %collective-permute-start.11 = (bf16[10,128,128]{2,1,0:T(8,128)(2,1)}, bf16[10,128,128]{2,1,0:T(8,128)(2,1)}, u32[]{:S(2)}, u32[]{:S(2)}) collective-permute-start(bf16[10,128,128]{2,1,0:T(8,128)(2,1)} %get-tuple-element.35), channel_id=1, source_target_pairs={{0,3},{1,0},{2,1},{3,2},{4,7},{5,4},{6,5},{7,6},{8,11},{9,8},{10,9... | collective-permute-start | bytes 983048 | tf_op jit(solution)/shard_map/ppermute | solution.py:161
  133.3 38.8 %collective-permute-start.10 = (bf16[10,128,128]{2,1,0:T(8,128)(2,1)}, bf16[10,128,128]{2,1,0:T(8,128)(2,1)}, u32[]{:S(2)}, u32[]{:S(2)}) collective-permute-start(bf16[10,128,128]{2,1,0:T(8,128)(2,1)} %get-tuple-element.39), channel_id=1, source_target_pairs={{0,8},{1,9},{2,10},{3,11},{4,12},{5,13},{6,14},{7,15},{8,0},{9,1},... | collective-permute-start | bytes 983048 | tf_op jit(solution)/shard_map/ppermute | solution.py:171
  175.6 1.0 copy-start.4
  176.6 1.1 copy-start.3

commit v9 on v6

--- a/solution.py
+++ b/solution.py
@@ -12,36 +12,41 @@
 STAT_ROWS = 8
 
 
-def partial_kernel(nsrc, flags_ref, q_ref, *refs):
+def partial_kernel(nsrc, group, flags_ref, q_ref, *refs):
     key_refs = refs[:nsrc]
     value_refs = refs[nsrc : 2 * nsrc]
     out_ref, lse_ref = refs[2 * nsrc : 2 * nsrc + 2]
     score_ref = refs[2 * nsrc + 2]
     score_scale = 1.0 / math.sqrt(HEAD_DIM)
-    query = q_ref[...]
-    top = None
-    for j in range(nsrc):
-        scores = lax.dot_general(
-            query, key_refs[j][...], (((1,), (1,)), ((), ())), preferred_element_type=jnp.float32
-        ) * score_scale
-        scores = jnp.where(flags_ref[j] > 0, scores, -1e30)
-        score_ref[j] = scores
-        block_top = jnp.max(scores, axis=1, keepdims=True)
-        top = block_top if top is None else jnp.maximum(top, block_top)
-    total = None
-    summed = None
-    for j in range(nsrc):
-        weights = jnp.exp(score_ref[j] - top)
-        part_total = jnp.sum(weights, axis=1, keepdims=True)
-        product = jnp.dot(
-            weights.astype(jnp.bfloat16), value_refs[j][...], preferred_element_type=jnp.float32
-        )
-        total = part_total if total is None else total + part_total
-        summed = product if summed is None else summed + product
-    out_ref[...] = (summed / total).astype(out_ref.dtype)
-    lse = top + jnp.log(total)
-    wide = jnp.broadcast_to(lse, (lse.shape[0], 128))
-    lse_ref[...] = jnp.transpose(wide)[:STAT_ROWS]
+    for g in range(group):
+        cols = slice(g * HEAD_DIM, (g + 1) * HEAD_DIM)
+        query = q_ref[:, cols]
+        top = None
+        for j in range(nsrc):
+            scores = lax.dot_general(
+                query,
+                key_refs[j][:, cols],
+                (((1,), (1,)), ((), ())),
+                preferred_element_type=jnp.float32,
+            ) * score_scale
+            scores = jnp.where(flags_ref[j] > 0, scores, -1e30)
+            score_ref[j] = scores
+            block_top = jnp.max(scores, axis=1, keepdims=True)
+            top = block_top if top is None else jnp.maximum(top, block_top)
+        total = None
+        summed = None
+        for j in range(nsrc):
+            weights = jnp.exp(score_ref[j] - top)
+            part_total = jnp.sum(weights, axis=1, keepdims=True)
+            product = jnp.dot(
+                weights.astype(jnp.bfloat16), value_refs[j][:, cols], preferred_element_type=jnp.float32
+            )
+            total = part_total if total is None else total + part_total
+            summed = product if summed is None else summed + product
+        out_ref[g] = (summed / total).astype(out_ref.dtype)
+        lse = top + jnp.log(total)
+        wide = jnp.broadcast_to(lse, (lse.shape[0], 128))
+        lse_ref[g] = jnp.transpose(wide)[:STAT_ROWS]
 
 
 def attend_partial(flags, query_block, key_blocks, value_blocks, out_dtype):
@@ -49,20 +54,22 @@
     rows, width = query_block.shape
     block_rows = key_blocks[0].shape[0]
     nheads = width // HEAD_DIM
+    group = 2 if nheads % 2 == 0 else 1
     row_tile = rows // ROW_SPLIT
-    q_spec = pl.BlockSpec((row_tile, HEAD_DIM), lambda h, r, f: (r, h))
-    kv_spec = pl.BlockSpec((block_rows, HEAD_DIM), lambda h, r, f: (0, h))
-    out_spec = pl.BlockSpec((None, row_tile, HEAD_DIM), lambda h, r, f: (h, r, 0))
-    lse_spec = pl.BlockSpec((None, STAT_ROWS, row_tile), lambda h, r, f: (h, 0, r))
+    span = group * HEAD_DIM
+    q_spec = pl.BlockSpec((row_tile, span), lambda h, r, f: (r, h))
+    kv_spec = pl.BlockSpec((block_rows, span), lambda h, r, f: (0, h))
+    out_spec = pl.BlockSpec((group, row_tile, HEAD_DIM), lambda h, r, f: (h, r, 0))
+    lse_spec = pl.BlockSpec((group, STAT_ROWS, row_tile), lambda h, r, f: (h, 0, r))
     grid_spec = pltpu.PrefetchScalarGridSpec(
         num_scalar_prefetch=1,
-        grid=(nheads, ROW_SPLIT),
+        grid=(nheads // group, ROW_SPLIT),
         in_specs=[q_spec] + [kv_spec] * (2 * nsrc),
         out_specs=[out_spec, lse_spec],
         scratch_shapes=[pltpu.VMEM((nsrc, row_tile, block_rows), jnp.float32)],
     )
     return pl.pallas_call(
-        lambda *a: partial_kernel(nsrc, *a),
+        lambda *a: partial_kernel(nsrc, group, *a),
         grid_spec=grid_spec,
         out_shape=[
             jax.ShapeDtypeStruct((nheads, rows, HEAD_DIM), out_dtype),

time: 169 us -> 164 us (0.970)
  Pallas kernels: 53.3 us -> 45.4 us
  waiting for transfers between devices: 72.6 us -> 76.6 us
    pallas_call x2, Pallas kernels: 53.3 us -> 45.4 us  [attend_partial(): pl.pallas_call(lambda *a: partial_kernel(nsrc, group, *a), grid_spec=grid...]
    ppermute x2, waiting for transfers between devices: 3.1 us -> 7.1 us  [local(): far_out, far_lse = lax.ppermute((far_out, far_lse), 'seq', forth)]
  transfers between devices with their start and end apart: 14 -> 14, of which waited for: 6 -> 6; matrix products, arithmetic and copies ran while one was open for 3% -> 3% of each run, Pallas kernels for 16% -> 14%
where the time goes in v9:
time: 164 us
  waiting for transfers between devices  76.6 us (47%)
  Pallas kernels  45.4 us (28%)
  starting transfers between devices  22.4 us (14%)
  local copies, waits for them, and re-layouts  12.3 us (8%)
  other arithmetic  6.79 us (4%)
    pallas_call x2, Pallas kernels, attend_partial(): pl.pallas_call(lambda *a: partial_kernel(nsrc, group, *a), grid_spec=grid...  45.4 us
    ppermute x3, waiting for transfers between devices, local(): lax.ppermute(piece, 'sp', [(i, (i - d) % sp_count) for i in range(sp_coun...  26.2 us
    ppermute x2, waiting for transfers between devices, local(): lax.ppermute((query_block, remote_flags), 'seq', back)  24.9 us
    ppermute x3, waiting for transfers between devices, local(): lax.ppermute(piece, 'sp', [(i, (i + d) % sp_count) for i in range(sp_coun...  18.4 us
    ppermute x3, starting transfers between devices, local(): lax.ppermute(piece, 'sp', [(i, (i - d) % sp_count) for i in range(sp_coun...  9.67 us
    ppermute x2, waiting for transfers between devices, local(): far_out, far_lse = lax.ppermute((far_out, far_lse), 'seq', forth)  7.1 us
    ppermute x3, starting transfers between devices, local(): lax.ppermute(piece, 'sp', [(i, (i + d) % sp_count) for i in range(sp_coun...  6.98 us
    unnamed x20, local copies, waits for them, and re-layouts  5.25 us
  transfers between devices with their start and end apart: 14, of which 6 were waited for; matrix products, arithmetic and copies ran while one was open for 3% of the time, Pallas kernels for 14%

profile of v9, /device:TPU:0, one launch (start us, length us, event | category | flops | bytes accessed | tf_op | source)
XLA Modules:
  0.0 163.6 jit_solution(2704443517889614602)
XLA Ops:
  0.0 2.4 %constant_dynamic-slice_fusion.3 = (bf16[128,1280]{1,0:T(8,128)(2,1)S(1)}, bf16[128,1280]{1,0:T(8,128)(2,1)}, bf16[128,1280]{1,0:T(8,128)(2,1)}, bf16[128,1280]{1,0:T(8,128)(2,1)}) fusion(bf16[128,5120]{1,0:T(8,128)(2,1)} %param.6, s32[]{:T(128)S(6)} %select_n.55, s32[]{:T(128)S(6)} %select_n.57, s32[]{:T(128)S(6)} %select_n.61, s32[]{:T(128)S(6)} %select_n.59), kind=kLoop, calls=%fused_computation.15 | loop fusion | bytes 2621456 | tf_op jit(solution)/shard_map/dynamic_slice | solution.py:99
  2.4 3.0 %collective-permute-start = (bf16[128,1280]{1,0:T(8,128)(2,1)}, bf16[128,1280]{1,0:T(8,128)(2,1)S(1)}, u32[]{:S(2)}, u32[]{:S(2)}) collective-permute-start(bf16[128,1280]{1,0:T(8,128)(2,1)} %get-tuple-element.23), channel_id=1, source_target_pairs={{0,1},{1,2},{2,3},{3,0},{4,5},{5,6},{6,7},{7,4},{8,9},{9,10},{10,1... | collective-permute-start | bytes 983048 | tf_op jit(solution)/shard_map/ppermute | solution.py:104
  5.4 2.6 %collective-permute-start.1 = (bf16[128,1280]{1,0:T(8,128)(2,1)}, bf16[128,1280]{1,0:T(8,128)(2,1)}, u32[]{:S(2)}, u32[]{:S(2)}) collective-permute-start(bf16[128,1280]{1,0:T(8,128)(2,1)} %get-tuple-element.25), channel_id=1, source_target_pairs={{0,2},{1,3},{2,0},{3,1},{4,6},{5,7},{6,4},{7,5},{8,10},{9,11},{10,... | collective-permute-start | bytes 983048 | tf_op jit(solution)/shard_map/ppermute | solution.py:104
  8.0 1.3 collective-permute-start.2
  9.7 1.5 collective-permute-start.7
  11.3 5.1 %collective-permute-done = bf16[128,1280]{1,0:T(8,128)(2,1)S(1)} collective-permute-done((bf16[128,1280]{1,0:T(8,128)(2,1)}, bf16[128,1280]{1,0:T(8,128)(2,1)S(1)}, u32[]{:S(2)}, u32[]{:S(2)}) %collective-permute-start) | collective-permute-done | bytes 327712 | tf_op jit(solution)/shard_map/ppermute | solution.py:104
  16.3 13.3 %collective-permute-done.1 = bf16[128,1280]{1,0:T(8,128)(2,1)} collective-permute-done((bf16[128,1280]{1,0:T(8,128)(2,1)}, bf16[128,1280]{1,0:T(8,128)(2,1)}, u32[]{:S(2)}, u32[]{:S(2)}) %collective-permute-start.1) | collective-permute-done | bytes 327712 | tf_op jit(solution)/shard_map/ppermute | solution.py:104
  29.7 0.5 collective-permute-start.6
  30.2 1.2 pad_maximum_fusion.a_1_
  31.4 1.6 collective-permute-start.8
  33.0 1.1 copy-done.2
  34.0 1.1 copy-done.3
  35.1 1.1 copy-done.4
  36.2 1.2 copy-done.5
  37.3 24.9 %collective-permute-done.8.a_1_ = bf16[512,1280]{1,0:T(8,128)(2,1)} collective-permute-done((bf16[512,1280]{1,0:T(8,128)(2,1)S(1)}, bf16[512,1280]{1,0:T(8,128)(2,1)}, u32[]{:S(2)}, u32[]{:S(2)}) %collective-permute-start.8) | collective-permute-done | bytes 1310752 | tf_op jit(solution)/shard_map/ppermute | solution.py:123
  62.2 22.7 %shard_map.65 = (bf16[10,512,128]{2,1,0:T(8,128)(2,1)}, f32[10,8,512]{2,1,0:T(8,128)}) custom-call(s32[4]{0:T(128)} %copy-done.8, bf16[512,1280]{1,0:T(8,128)(2,1)} %collective-permute-done.8.a_1_, bf16[512,1280]{1,0:T(8,128)(2,1)} %a_2_.3, bf16[512,1280]{1,0:T(8,128)(2,1)} %copy-done.2, bf16[512,1280]{1,0:T(8,128)(2,1)} %a_4_.3, ...), custom_call_target="tpu_custom_call" | custom-call | tf_op jit(solution)/shard_map/pallas_call | solution.py:71
  84.9 1.6 collective-permute-start.10
  86.5 0.5 collective-permute-start.9
  87.0 0.7 fusion.3.a_0_
  87.6 22.7 %shard_map.64 = (f32[10,512,128]{2,1,0:T(8,128)}, f32[10,8,512]{2,1,0:T(8,128)}) custom-call(s32[4]{0:T(128)} %fusion.3.a_0_, bf16[512,1280]{1,0:T(8,128)(2,1)} %copy-done.6, bf16[512,1280]{1,0:T(8,128)(2,1)} %a_2_.3, bf16[512,1280]{1,0:T(8,128)(2,1)} %copy-done.2, bf16[512,1280]{1,0:T(8,128)(2,1)} %a_4_.3, bf16[512,1280]{1,0:T(8,128)(2,1)} %copy-done.3, ...), custom_call_target="tpu_custom_call" | custom-call | tf_op jit(solution)/shard_map/pallas_call | solution.py:71
  110.4 1.0 copy.17
  111.4 7.1 %collective-permute-done.9 = f32[10,8,512]{2,1,0:T(8,128)S(1)} collective-permute-done((f32[10,8,512]{2,1,0:T(8,128)}, f32[10,8,512]{2,1,0:T(8,128)S(1)}, u32[]{:S(2)}, u32[]{:S(2)}) %collective-permute-start.9) | collective-permute-done | bytes 163872 | tf_op jit(solution)/shard_map/ppermute | solution.py:160
  118.5 4.6 %fusion = bf16[512,10,128]{2,0,1:T(8,128)(2,1)S(1)} fusion(f32[10,512]{1,0:T(8,128)S(1)} %get-tuple-element.15, f32[10,512]{1,0:T(8,128)S(1)} %get-tuple-element.16, bf16[10,512,128]{2,1,0:T(8,128)(2,1)S(1)} %collective-permute-done.10, f32[10,512,128]{2,1,0:T(8,128)} %get-tuple-element.9, f32[10,512]{1,0:T(8,128)S(1)} %get-tuple-element.17), kind=kLoop, calls=%fused_computation.2 | loop fusion | flops 3932160 | bytes 5304320 | tf_op jit(solution)/shard_map/transpose | solution.py:169
  123.3 0.2 copy.20
  123.5 8.6 %collective-permute-start.11 = (bf16[128,1280]{0,1:T(8,128)(2,1)S(1)}, bf16[128,1280]{0,1:T(8,128)(2,1)S(1)}, u32[]{:S(2)}, u32[]{:S(2)}) collective-permute-start(bf16[128,1280]{0,1:T(8,128)(2,1)S(1)} %bitcast.33), channel_id=1, source_target_pairs={{0,3},{1,0},{2,1},{3,2},{4,7},{5,4},{6,5},{7,6},{8,11},{9,8},{10,9... | collective-permute-start | bytes 983048 | tf_op jit(solution)/shard_map/ppermute | solution.py:176
  132.5 0.2 copy.22
  132.7 1.0 collective-permute-start.12
  134.2 6.1 %collective-permute-done.11 = bf16[128,1280]{0,1:T(8,128)(2,1)S(1)} collective-permute-done((bf16[128,1280]{0,1:T(8,128)(2,1)S(1)}, bf16[128,1280]{0,1:T(8,128)(2,1)S(1)}, u32[]{:S(2)}, u32[]{:S(2)}) %collective-permute-start.11) | collective-permute-done | bytes 327712 | tf_op jit(solution)/shard_map/ppermute | solution.py:176
  140.5 20.1 %collective-permute-done.12 = bf16[128,1280]{0,1:T(8,128)(2,1)} collective-permute-done((bf16[128,1280]{0,1:T(8,128)(2,1)S(1)}, bf16[128,1280]{0,1:T(8,128)(2,1)}, u32[]{:S(2)}, u32[]{:S(2)}) %collective-permute-start.12) | collective-permute-done | bytes 327712 | tf_op jit(solution)/shard_map/ppermute | solution.py:176
  160.6 1.1 copy.23
  162.0 0.9 copy-done.7
  162.9 0.7 constant_dynamic-update-slice_fusion
  (42 shorter events, 1.9 us)
Async XLA Ops:
  0.0 9.4 %copy-start.9 = (s32[1,6]{1,0:T(1,128)S(1)}, s32[1,6]{1,0:T(1,128)}, u32[]{:S(2)}) copy-start(s32[1,6]{1,0:T(1,128)} %param.11) | copy-start | bytes 76
  0.0 11.3 %copy-start = (bf16[512,1280]{1,0:T(8,128)(2,1)S(1)}, bf16[512,1280]{1,0:T(8,128)(2,1)}, u32[]{:S(2)}) copy-start(bf16[512,1280]{1,0:T(8,128)(2,1)} %a_2_.3) | copy-start | bytes 3932164
  0.0 16.3 %copy-start.1 = (bf16[512,1280]{1,0:T(8,128)(2,1)S(1)}, bf16[512,1280]{1,0:T(8,128)(2,1)}, u32[]{:S(2)}) copy-start(bf16[512,1280]{1,0:T(8,128)(2,1)} %a_4_.3) | copy-start | bytes 3932164
  2.4 14.0 %collective-permute-start = (bf16[128,1280]{1,0:T(8,128)(2,1)}, bf16[128,1280]{1,0:T(8,128)(2,1)S(1)}, u32[]{:S(2)}, u32[]{:S(2)}) collective-permute-start(bf16[128,1280]{1,0:T(8,128)(2,1)} %get-tuple-element.23), channel_id=1, source_target_pairs={{0,1},{1,2},{2,3},{3,0},{4,5},{5,6},{6,7},{7,4},{8,9},{9,10},{10,1... | collective-permute-start | bytes 983048 | tf_op jit(solution)/shard_map/ppermute | solution.py:104
  5.4 24.2 %collective-permute-start.1 = (bf16[128,1280]{1,0:T(8,128)(2,1)}, bf16[128,1280]{1,0:T(8,128)(2,1)}, u32[]{:S(2)}, u32[]{:S(2)}) collective-permute-start(bf16[128,1280]{1,0:T(8,128)(2,1)} %get-tuple-element.25), channel_id=1, source_target_pairs={{0,2},{1,3},{2,0},{3,1},{4,6},{5,7},{6,4},{7,5},{8,10},{9,11},{10,... | collective-permute-start | bytes 983048 | tf_op jit(solution)/shard_map/ppermute | solution.py:104
  8.0 21.6 %collective-permute-start.2 = (bf16[128,1280]{1,0:T(8,128)(2,1)}, bf16[128,1280]{1,0:T(8,128)(2,1)}, u32[]{:S(2)}, u32[]{:S(2)}) collective-permute-start(bf16[128,1280]{1,0:T(8,128)(2,1)} %get-tuple-element.24), channel_id=1, source_target_pairs={{0,3},{1,0},{2,1},{3,2},{4,7},{5,4},{6,5},{7,6},{8,11},{9,8},{10,9... | collective-permute-start | bytes 983048 | tf_op jit(solution)/shard_map/ppermute | solution.py:104
  9.7 21.6 %collective-permute-start.7 = (s32[4]{0:T(128)S(1)}, s32[4]{0:T(128)S(1)}, u32[]{:S(2)}, u32[]{:S(2)}) collective-permute-start(s32[4]{0:T(128)S(1)} %fusion.4), channel_id=1, source_target_pairs={{0,8},{4,12},{8,0},{12,4},{1,9},{5,13},{9,1},{13,5},{2,10},{6,14},... | collective-permute-start | bytes 56 | tf_op jit(solution)/shard_map/ppermute | solution.py:123
  11.3 21.7 %collective-permute-start.3 = (bf16[512,1280]{1,0:T(8,128)(2,1)S(1)}, bf16[512,1280]{1,0:T(8,128)(2,1)S(1)}, u32[]{:S(2)}, u32[]{:S(2)}) collective-permute-start(bf16[512,1280]{1,0:T(8,128)(2,1)S(1)} %copy-done), channel_id=1, source_target_pairs={{0,4},{4,0},{8,12},{12,8},{1,5},{5,1},{9,13},{13,9},{2,6},{6,2},{1... | collective-permute-start | bytes 3932168 | tf_op jit(solution)/shard_map/ppermute | solution.py:126
  16.3 16.6 %collective-permute-start.4 = (bf16[512,1280]{1,0:T(8,128)(2,1)S(1)}, bf16[512,1280]{1,0:T(8,128)(2,1)S(1)}, u32[]{:S(2)}, u32[]{:S(2)}) collective-permute-start(bf16[512,1280]{1,0:T(8,128)(2,1)S(1)} %copy-done.1), channel_id=1, source_target_pairs={{0,4},{4,0},{8,12},{12,8},{1,5},{5,1},{9,13},{13,9},{2,6},{6,2},{1... | collective-permute-start | bytes 3932168 | tf_op jit(solution)/shard_map/ppermute | solution.py:126
  29.7 4.4 %collective-permute-start.5 = (bf16[512,1280]{1,0:T(8,128)(2,1)}, bf16[512,1280]{1,0:T(8,128)(2,1)S(1)}, u32[]{:S(2)}, u32[]{:S(2)}) collective-permute-start(bf16[512,1280]{1,0:T(8,128)(2,1)} %a_6_.3), channel_id=1, source_target_pairs={{0,4},{4,0},{8,12},{12,8},{1,5},{5,1},{9,13},{13,9},{2,6},{6,2},{1... | collective-permute-start | bytes 3932168 | tf_op jit(solution)/shard_map/ppermute | solution.py:126
  29.7 5.5 %collective-permute-start.6 = (bf16[512,1280]{1,0:T(8,128)(2,1)}, bf16[512,1280]{1,0:T(8,128)(2,1)S(1)}, u32[]{:S(2)}, u32[]{:S(2)}) collective-permute-start(bf16[512,1280]{1,0:T(8,128)(2,1)} %a_8_.3), channel_id=1, source_target_pairs={{0,4},{4,0},{8,12},{12,8},{1,5},{5,1},{9,13},{13,9},{2,6},{6,2},{1... | collective-permute-start | bytes 3932168 | tf_op jit(solution)/shard_map/ppermute | solution.py:126
  31.3 3.8 %copy-start.6 = (bf16[512,1280]{1,0:T(8,128)(2,1)}, bf16[512,1280]{1,0:T(8,128)(2,1)S(1)}, u32[]{:S(2)}) copy-start(bf16[512,1280]{1,0:T(8,128)(2,1)S(1)} %pad_maximum_fusion.a_1_) | copy-start | bytes 3932164
  31.4 30.9 %copy-start.8 = (s32[4]{0:T(128)}, s32[4]{0:T(128)S(1)}, u32[]{:S(2)}) copy-start(s32[4]{0:T(128)S(1)} %collective-permute-done.7.a_0_) | copy-start | bytes 52
  31.4 30.9 %collective-permute-start.8 = (bf16[512,1280]{1,0:T(8,128)(2,1)S(1)}, bf16[512,1280]{1,0:T(8,128)(2,1)}, u32[]{:S(2)}, u32[]{:S(2)}) collective-permute-start(bf16[512,1280]{1,0:T(8,128)(2,1)S(1)} %pad_maximum_fusion.a_1_), channel_id=1, source_target_pairs={{0,8},{4,12},{8,0},{12,4},{1,9},{5,13},{9,1},{13,5},{2,10},{6,14},... | collective-permute-start | bytes 3932168 | tf_op jit(solution)/shard_map/ppermute | solution.py:123
  33.0 1.1 copy-start.2
  34.0 1.1 copy-start.3
  35.1 1.1 copy-start.4
  36.2 1.2 copy-start.5
  84.9 33.7 %collective-permute-start.10 = (bf16[10,512,128]{2,1,0:T(8,128)(2,1)}, bf16[10,512,128]{2,1,0:T(8,128)(2,1)S(1)}, u32[]{:S(2)}, u32[]{:S(2)}) collective-permute-start(bf16[10,512,128]{2,1,0:T(8,128)(2,1)} %get-tuple-element.12), channel_id=1, source_target_pairs={{0,8},{4,12},{8,0},{12,4},{1,9},{5,13},{9,1},{13,5},{2,10},{6,14},... | collective-permute-start | bytes 3932168 | tf_op jit(solution)/shard_map/ppermute | solution.py:160
  86.5 32.0 %collective-permute-start.9 = (f32[10,8,512]{2,1,0:T(8,128)}, f32[10,8,512]{2,1,0:T(8,128)S(1)}, u32[]{:S(2)}, u32[]{:S(2)}) collective-permute-start(f32[10,8,512]{2,1,0:T(8,128)} %get-tuple-element.11), channel_id=1, source_target_pairs={{0,8},{4,12},{8,0},{12,4},{1,9},{5,13},{9,1},{13,5},{2,10},{6,14},... | collective-permute-start | bytes 491528 | tf_op jit(solution)/shard_map/ppermute | solution.py:160
  123.5 16.8 %collective-permute-start.11 = (bf16[128,1280]{0,1:T(8,128)(2,1)S(1)}, bf16[128,1280]{0,1:T(8,128)(2,1)S(1)}, u32[]{:S(2)}, u32[]{:S(2)}) collective-permute-start(bf16[128,1280]{0,1:T(8,128)(2,1)S(1)} %bitcast.33), channel_id=1, source_target_pairs={{0,3},{1,0},{2,1},{3,2},{4,7},{5,4},{6,5},{7,6},{8,11},{9,8},{10,9... | collective-permute-start | bytes 983048 | tf_op jit(solution)/shard_map/ppermute | solution.py:176
  132.7 27.9 %collective-permute-start.12 = (bf16[128,1280]{0,1:T(8,128)(2,1)S(1)}, bf16[128,1280]{0,1:T(8,128)(2,1)}, u32[]{:S(2)}, u32[]{:S(2)}) collective-permute-start(bf16[128,1280]{0,1:T(8,128)(2,1)S(1)} %bitcast.35), channel_id=1, source_target_pairs={{0,2},{1,3},{2,0},{3,1},{4,6},{5,7},{6,4},{7,5},{8,10},{9,11},{10,... | collective-permute-start | bytes 983048 | tf_op jit(solution)/shard_map/ppermute | solution.py:176
  134.0 27.8 %collective-permute-start.13 = (bf16[128,1280]{0,1:T(8,128)(2,1)S(1)}, bf16[128,1280]{0,1:T(8,128)(2,1)S(1)}, u32[]{:S(2)}, u32[]{:S(2)}) collective-permute-start(bf16[128,1280]{0,1:T(8,128)(2,1)S(1)} %bitcast.34), channel_id=1, source_target_pairs={{0,1},{1,2},{2,3},{3,0},{4,5},{5,6},{6,7},{7,4},{8,9},{9,10},{10,1... | collective-permute-start | bytes 983048 | tf_op jit(solution)/shard_map/ppermute | solution.py:176
  161.8 1.1 copy-start.7

commit v10 on v9

--- a/solution.py
+++ b/solution.py
@@ -54,7 +54,7 @@
     rows, width = query_block.shape
     block_rows = key_blocks[0].shape[0]
     nheads = width // HEAD_DIM
-    group = 2 if nheads % 2 == 0 else 1
+    group = max(g for g in range(1, 6) if nheads % g == 0)
     row_tile = rows // ROW_SPLIT
     span = group * HEAD_DIM
     q_spec = pl.BlockSpec((row_tile, span), lambda h, r, f: (r, h))

time: 164 us -> 163 us (level)
  no operation moved by 1% of the time
where the time goes in v10:
time: 163 us
  waiting for transfers between devices  77.3 us (47%)
  Pallas kernels  43.9 us (27%)
  starting transfers between devices  22.4 us (14%)
  local copies, waits for them, and re-layouts  12.3 us (8%)
  other arithmetic  6.79 us (4%)
    pallas_call x2, Pallas kernels, attend_partial(): pl.pallas_call(lambda *a: partial_kernel(nsrc, group, *a), grid_spec=grid...  43.9 us
    ppermute x3, waiting for transfers between devices, local(): lax.ppermute(piece, 'sp', [(i, (i - d) % sp_count) for i in range(sp_coun...  26.2 us
    ppermute x2, waiting for transfers between devices, local(): lax.ppermute((query_block, remote_flags), 'seq', back)  24.9 us
    ppermute x3, waiting for transfers between devices, local(): lax.ppermute(piece, 'sp', [(i, (i + d) % sp_count) for i in range(sp_coun...  18.4 us
    ppermute x3, starting transfers between devices, local(): lax.ppermute(piece, 'sp', [(i, (i - d) % sp_count) for i in range(sp_coun...  9.67 us
    ppermute x2, waiting for transfers between devices, local(): far_out, far_lse = lax.ppermute((far_out, far_lse), 'seq', forth)  7.81 us
    ppermute x3, starting transfers between devices, local(): lax.ppermute(piece, 'sp', [(i, (i + d) % sp_count) for i in range(sp_coun...  6.98 us
    unnamed x20, local copies, waits for them, and re-layouts  5.25 us
  transfers between devices with their start and end apart: 14, of which 6 were waited for; matrix products, arithmetic and copies ran while one was open for 3% of the time, Pallas kernels for 14%

profile of v10, /device:TPU:0, one launch (start us, length us, event | category | flops | bytes accessed | tf_op | source)
XLA Modules:
  0.0 162.8 jit_solution(13141768423576817985)
XLA Ops:
  0.0 2.4 %constant_dynamic-slice_fusion.3 = (bf16[128,1280]{1,0:T(8,128)(2,1)S(1)}, bf16[128,1280]{1,0:T(8,128)(2,1)}, bf16[128,1280]{1,0:T(8,128)(2,1)}, bf16[128,1280]{1,0:T(8,128)(2,1)}) fusion(bf16[128,5120]{1,0:T(8,128)(2,1)} %param.6, s32[]{:T(128)S(6)} %select_n.55, s32[]{:T(128)S(6)} %select_n.57, s32[]{:T(128)S(6)} %select_n.61, s32[]{:T(128)S(6)} %select_n.59), kind=kLoop, calls=%fused_computation.15 | loop fusion | bytes 2621456 | tf_op jit(solution)/shard_map/dynamic_slice | solution.py:99
  2.4 3.0 %collective-permute-start = (bf16[128,1280]{1,0:T(8,128)(2,1)}, bf16[128,1280]{1,0:T(8,128)(2,1)S(1)}, u32[]{:S(2)}, u32[]{:S(2)}) collective-permute-start(bf16[128,1280]{1,0:T(8,128)(2,1)} %get-tuple-element.23), channel_id=1, source_target_pairs={{0,1},{1,2},{2,3},{3,0},{4,5},{5,6},{6,7},{7,4},{8,9},{9,10},{10,1... | collective-permute-start | bytes 983048 | tf_op jit(solution)/shard_map/ppermute | solution.py:104
  5.4 2.6 %collective-permute-start.1 = (bf16[128,1280]{1,0:T(8,128)(2,1)}, bf16[128,1280]{1,0:T(8,128)(2,1)}, u32[]{:S(2)}, u32[]{:S(2)}) collective-permute-start(bf16[128,1280]{1,0:T(8,128)(2,1)} %get-tuple-element.25), channel_id=1, source_target_pairs={{0,2},{1,3},{2,0},{3,1},{4,6},{5,7},{6,4},{7,5},{8,10},{9,11},{10,... | collective-permute-start | bytes 983048 | tf_op jit(solution)/shard_map/ppermute | solution.py:104
  8.0 1.3 collective-permute-start.2
  9.7 1.5 collective-permute-start.7
  11.3 5.1 %collective-permute-done = bf16[128,1280]{1,0:T(8,128)(2,1)S(1)} collective-permute-done((bf16[128,1280]{1,0:T(8,128)(2,1)}, bf16[128,1280]{1,0:T(8,128)(2,1)S(1)}, u32[]{:S(2)}, u32[]{:S(2)}) %collective-permute-start) | collective-permute-done | bytes 327712 | tf_op jit(solution)/shard_map/ppermute | solution.py:104
  16.3 13.3 %collective-permute-done.1 = bf16[128,1280]{1,0:T(8,128)(2,1)} collective-permute-done((bf16[128,1280]{1,0:T(8,128)(2,1)}, bf16[128,1280]{1,0:T(8,128)(2,1)}, u32[]{:S(2)}, u32[]{:S(2)}) %collective-permute-start.1) | collective-permute-done | bytes 327712 | tf_op jit(solution)/shard_map/ppermute | solution.py:104
  29.7 0.5 collective-permute-start.6
  30.2 1.2 pad_maximum_fusion.a_1_
  31.4 1.6 collective-permute-start.8
  33.0 1.1 copy-done.2
  34.0 1.1 copy-done.3
  35.1 1.1 copy-done.4
  36.2 1.2 copy-done.5
  37.3 24.9 %collective-permute-done.8.a_1_ = bf16[512,1280]{1,0:T(8,128)(2,1)} collective-permute-done((bf16[512,1280]{1,0:T(8,128)(2,1)S(1)}, bf16[512,1280]{1,0:T(8,128)(2,1)}, u32[]{:S(2)}, u32[]{:S(2)}) %collective-permute-start.8) | collective-permute-done | bytes 1310752 | tf_op jit(solution)/shard_map/ppermute | solution.py:123
  62.2 21.9 %shard_map.65 = (bf16[10,512,128]{2,1,0:T(8,128)(2,1)}, f32[10,8,512]{2,1,0:T(8,128)}) custom-call(s32[4]{0:T(128)} %copy-done.8, bf16[512,1280]{1,0:T(8,128)(2,1)} %collective-permute-done.8.a_1_, bf16[512,1280]{1,0:T(8,128)(2,1)} %a_2_.3, bf16[512,1280]{1,0:T(8,128)(2,1)} %copy-done.2, bf16[512,1280]{1,0:T(8,128)(2,1)} %a_4_.3, ...), custom_call_target="tpu_custom_call" | custom-call | tf_op jit(solution)/shard_map/pallas_call | solution.py:71
  84.1 1.6 collective-permute-start.10
  85.7 0.5 collective-permute-start.9
  86.2 0.7 fusion.3.a_0_
  86.9 22.0 %shard_map.64 = (f32[10,512,128]{2,1,0:T(8,128)}, f32[10,8,512]{2,1,0:T(8,128)}) custom-call(s32[4]{0:T(128)} %fusion.3.a_0_, bf16[512,1280]{1,0:T(8,128)(2,1)} %copy-done.6, bf16[512,1280]{1,0:T(8,128)(2,1)} %a_2_.3, bf16[512,1280]{1,0:T(8,128)(2,1)} %copy-done.2, bf16[512,1280]{1,0:T(8,128)(2,1)} %a_4_.3, bf16[512,1280]{1,0:T(8,128)(2,1)} %copy-done.3, ...), custom_call_target="tpu_custom_call" | custom-call | tf_op jit(solution)/shard_map/pallas_call | solution.py:71
  108.9 1.0 copy.17
  109.9 7.8 %collective-permute-done.9 = f32[10,8,512]{2,1,0:T(8,128)S(1)} collective-permute-done((f32[10,8,512]{2,1,0:T(8,128)}, f32[10,8,512]{2,1,0:T(8,128)S(1)}, u32[]{:S(2)}, u32[]{:S(2)}) %collective-permute-start.9) | collective-permute-done | bytes 163872 | tf_op jit(solution)/shard_map/ppermute | solution.py:160
  117.8 4.6 %fusion = bf16[512,10,128]{2,0,1:T(8,128)(2,1)S(1)} fusion(f32[10,512]{1,0:T(8,128)S(1)} %get-tuple-element.15, f32[10,512]{1,0:T(8,128)S(1)} %get-tuple-element.16, bf16[10,512,128]{2,1,0:T(8,128)(2,1)S(1)} %collective-permute-done.10, f32[10,512,128]{2,1,0:T(8,128)} %get-tuple-element.9, f32[10,512]{1,0:T(8,128)S(1)} %get-tuple-element.17), kind=kLoop, calls=%fused_computation.2 | loop fusion | flops 3932160 | bytes 5304320 | tf_op jit(solution)/shard_map/transpose | solution.py:169
  122.5 0.2 copy.20
  122.7 8.6 %collective-permute-start.11 = (bf16[128,1280]{0,1:T(8,128)(2,1)S(1)}, bf16[128,1280]{0,1:T(8,128)(2,1)S(1)}, u32[]{:S(2)}, u32[]{:S(2)}) collective-permute-start(bf16[128,1280]{0,1:T(8,128)(2,1)S(1)} %bitcast.33), channel_id=1, source_target_pairs={{0,3},{1,0},{2,1},{3,2},{4,7},{5,4},{6,5},{7,6},{8,11},{9,8},{10,9... | collective-permute-start | bytes 983048 | tf_op jit(solution)/shard_map/ppermute | solution.py:176
  131.7 0.2 copy.22
  131.9 1.0 collective-permute-start.12
  133.4 6.1 %collective-permute-done.11 = bf16[128,1280]{0,1:T(8,128)(2,1)S(1)} collective-permute-done((bf16[128,1280]{0,1:T(8,128)(2,1)S(1)}, bf16[128,1280]{0,1:T(8,128)(2,1)S(1)}, u32[]{:S(2)}, u32[]{:S(2)}) %collective-permute-start.11) | collective-permute-done | bytes 327712 | tf_op jit(solution)/shard_map/ppermute | solution.py:176
  139.7 20.1 %collective-permute-done.12 = bf16[128,1280]{0,1:T(8,128)(2,1)} collective-permute-done((bf16[128,1280]{0,1:T(8,128)(2,1)S(1)}, bf16[128,1280]{0,1:T(8,128)(2,1)}, u32[]{:S(2)}, u32[]{:S(2)}) %collective-permute-start.12) | collective-permute-done | bytes 327712 | tf_op jit(solution)/shard_map/ppermute | solution.py:176
  159.8 1.1 copy.23
  161.2 0.9 copy-done.7
  162.1 0.7 constant_dynamic-update-slice_fusion
  (42 shorter events, 1.9 us)
Async XLA Ops:
  0.0 9.4 %copy-start.9 = (s32[1,6]{1,0:T(1,128)S(1)}, s32[1,6]{1,0:T(1,128)}, u32[]{:S(2)}) copy-start(s32[1,6]{1,0:T(1,128)} %param.11) | copy-start | bytes 76
  0.0 11.3 %copy-start = (bf16[512,1280]{1,0:T(8,128)(2,1)S(1)}, bf16[512,1280]{1,0:T(8,128)(2,1)}, u32[]{:S(2)}) copy-start(bf16[512,1280]{1,0:T(8,128)(2,1)} %a_2_.3) | copy-start | bytes 3932164
  0.0 16.3 %copy-start.1 = (bf16[512,1280]{1,0:T(8,128)(2,1)S(1)}, bf16[512,1280]{1,0:T(8,128)(2,1)}, u32[]{:S(2)}) copy-start(bf16[512,1280]{1,0:T(8,128)(2,1)} %a_4_.3) | copy-start | bytes 3932164
  2.4 14.0 %collective-permute-start = (bf16[128,1280]{1,0:T(8,128)(2,1)}, bf16[128,1280]{1,0:T(8,128)(2,1)S(1)}, u32[]{:S(2)}, u32[]{:S(2)}) collective-permute-start(bf16[128,1280]{1,0:T(8,128)(2,1)} %get-tuple-element.23), channel_id=1, source_target_pairs={{0,1},{1,2},{2,3},{3,0},{4,5},{5,6},{6,7},{7,4},{8,9},{9,10},{10,1... | collective-permute-start | bytes 983048 | tf_op jit(solution)/shard_map/ppermute | solution.py:104
  5.4 24.2 %collective-permute-start.1 = (bf16[128,1280]{1,0:T(8,128)(2,1)}, bf16[128,1280]{1,0:T(8,128)(2,1)}, u32[]{:S(2)}, u32[]{:S(2)}) collective-permute-start(bf16[128,1280]{1,0:T(8,128)(2,1)} %get-tuple-element.25), channel_id=1, source_target_pairs={{0,2},{1,3},{2,0},{3,1},{4,6},{5,7},{6,4},{7,5},{8,10},{9,11},{10,... | collective-permute-start | bytes 983048 | tf_op jit(solution)/shard_map/ppermute | solution.py:104
  8.0 21.6 %collective-permute-start.2 = (bf16[128,1280]{1,0:T(8,128)(2,1)}, bf16[128,1280]{1,0:T(8,128)(2,1)}, u32[]{:S(2)}, u32[]{:S(2)}) collective-permute-start(bf16[128,1280]{1,0:T(8,128)(2,1)} %get-tuple-element.24), channel_id=1, source_target_pairs={{0,3},{1,0},{2,1},{3,2},{4,7},{5,4},{6,5},{7,6},{8,11},{9,8},{10,9... | collective-permute-start | bytes 983048 | tf_op jit(solution)/shard_map/ppermute | solution.py:104
  9.7 21.6 %collective-permute-start.7 = (s32[4]{0:T(128)S(1)}, s32[4]{0:T(128)S(1)}, u32[]{:S(2)}, u32[]{:S(2)}) collective-permute-start(s32[4]{0:T(128)S(1)} %fusion.4), channel_id=1, source_target_pairs={{0,8},{4,12},{8,0},{12,4},{1,9},{5,13},{9,1},{13,5},{2,10},{6,14},... | collective-permute-start | bytes 56 | tf_op jit(solution)/shard_map/ppermute | solution.py:123
  11.3 21.7 %collective-permute-start.3 = (bf16[512,1280]{1,0:T(8,128)(2,1)S(1)}, bf16[512,1280]{1,0:T(8,128)(2,1)S(1)}, u32[]{:S(2)}, u32[]{:S(2)}) collective-permute-start(bf16[512,1280]{1,0:T(8,128)(2,1)S(1)} %copy-done), channel_id=1, source_target_pairs={{0,4},{4,0},{8,12},{12,8},{1,5},{5,1},{9,13},{13,9},{2,6},{6,2},{1... | collective-permute-start | bytes 3932168 | tf_op jit(solution)/shard_map/ppermute | solution.py:126
  16.3 16.6 %collective-permute-start.4 = (bf16[512,1280]{1,0:T(8,128)(2,1)S(1)}, bf16[512,1280]{1,0:T(8,128)(2,1)S(1)}, u32[]{:S(2)}, u32[]{:S(2)}) collective-permute-start(bf16[512,1280]{1,0:T(8,128)(2,1)S(1)} %copy-done.1), channel_id=1, source_target_pairs={{0,4},{4,0},{8,12},{12,8},{1,5},{5,1},{9,13},{13,9},{2,6},{6,2},{1... | collective-permute-start | bytes 3932168 | tf_op jit(solution)/shard_map/ppermute | solution.py:126
  29.7 4.4 %collective-permute-start.5 = (bf16[512,1280]{1,0:T(8,128)(2,1)}, bf16[512,1280]{1,0:T(8,128)(2,1)S(1)}, u32[]{:S(2)}, u32[]{:S(2)}) collective-permute-start(bf16[512,1280]{1,0:T(8,128)(2,1)} %a_6_.3), channel_id=1, source_target_pairs={{0,4},{4,0},{8,12},{12,8},{1,5},{5,1},{9,13},{13,9},{2,6},{6,2},{1... | collective-permute-start | bytes 3932168 | tf_op jit(solution)/shard_map/ppermute | solution.py:126
  29.7 5.5 %collective-permute-start.6 = (bf16[512,1280]{1,0:T(8,128)(2,1)}, bf16[512,1280]{1,0:T(8,128)(2,1)S(1)}, u32[]{:S(2)}, u32[]{:S(2)}) collective-permute-start(bf16[512,1280]{1,0:T(8,128)(2,1)} %a_8_.3), channel_id=1, source_target_pairs={{0,4},{4,0},{8,12},{12,8},{1,5},{5,1},{9,13},{13,9},{2,6},{6,2},{1... | collective-permute-start | bytes 3932168 | tf_op jit(solution)/shard_map/ppermute | solution.py:126
  31.3 3.8 %copy-start.6 = (bf16[512,1280]{1,0:T(8,128)(2,1)}, bf16[512,1280]{1,0:T(8,128)(2,1)S(1)}, u32[]{:S(2)}) copy-start(bf16[512,1280]{1,0:T(8,128)(2,1)S(1)} %pad_maximum_fusion.a_1_) | copy-start | bytes 3932164
  31.4 30.9 %copy-start.8 = (s32[4]{0:T(128)}, s32[4]{0:T(128)S(1)}, u32[]{:S(2)}) copy-start(s32[4]{0:T(128)S(1)} %collective-permute-done.7.a_0_) | copy-start | bytes 52
  31.4 30.9 %collective-permute-start.8 = (bf16[512,1280]{1,0:T(8,128)(2,1)S(1)}, bf16[512,1280]{1,0:T(8,128)(2,1)}, u32[]{:S(2)}, u32[]{:S(2)}) collective-permute-start(bf16[512,1280]{1,0:T(8,128)(2,1)S(1)} %pad_maximum_fusion.a_1_), channel_id=1, source_target_pairs={{0,8},{4,12},{8,0},{12,4},{1,9},{5,13},{9,1},{13,5},{2,10},{6,14},... | collective-permute-start | bytes 3932168 | tf_op jit(solution)/shard_map/ppermute | solution.py:123
  33.0 1.1 copy-start.2
  34.0 1.1 copy-start.3
  35.1 1.1 copy-start.4
  36.2 1.2 copy-start.5
  84.1 33.7 %collective-permute-start.10 = (bf16[10,512,128]{2,1,0:T(8,128)(2,1)}, bf16[10,512,128]{2,1,0:T(8,128)(2,1)S(1)}, u32[]{:S(2)}, u32[]{:S(2)}) collective-permute-start(bf16[10,512,128]{2,1,0:T(8,128)(2,1)} %get-tuple-element.12), channel_id=1, source_target_pairs={{0,8},{4,12},{8,0},{12,4},{1,9},{5,13},{9,1},{13,5},{2,10},{6,14},... | collective-permute-start | bytes 3932168 | tf_op jit(solution)/shard_map/ppermute | solution.py:160
  85.7 32.0 %collective-permute-start.9 = (f32[10,8,512]{2,1,0:T(8,128)}, f32[10,8,512]{2,1,0:T(8,128)S(1)}, u32[]{:S(2)}, u32[]{:S(2)}) collective-permute-start(f32[10,8,512]{2,1,0:T(8,128)} %get-tuple-element.11), channel_id=1, source_target_pairs={{0,8},{4,12},{8,0},{12,4},{1,9},{5,13},{9,1},{13,5},{2,10},{6,14},... | collective-permute-start | bytes 491528 | tf_op jit(solution)/shard_map/ppermute | solution.py:160
  122.7 16.8 %collective-permute-start.11 = (bf16[128,1280]{0,1:T(8,128)(2,1)S(1)}, bf16[128,1280]{0,1:T(8,128)(2,1)S(1)}, u32[]{:S(2)}, u32[]{:S(2)}) collective-permute-start(bf16[128,1280]{0,1:T(8,128)(2,1)S(1)} %bitcast.33), channel_id=1, source_target_pairs={{0,3},{1,0},{2,1},{3,2},{4,7},{5,4},{6,5},{7,6},{8,11},{9,8},{10,9... | collective-permute-start | bytes 983048 | tf_op jit(solution)/shard_map/ppermute | solution.py:176
  131.9 27.9 %collective-permute-start.12 = (bf16[128,1280]{0,1:T(8,128)(2,1)S(1)}, bf16[128,1280]{0,1:T(8,128)(2,1)}, u32[]{:S(2)}, u32[]{:S(2)}) collective-permute-start(bf16[128,1280]{0,1:T(8,128)(2,1)S(1)} %bitcast.35), channel_id=1, source_target_pairs={{0,2},{1,3},{2,0},{3,1},{4,6},{5,7},{6,4},{7,5},{8,10},{9,11},{10,... | collective-permute-start | bytes 983048 | tf_op jit(solution)/shard_map/ppermute | solution.py:176
  133.2 27.9 %collective-permute-start.13 = (bf16[128,1280]{0,1:T(8,128)(2,1)S(1)}, bf16[128,1280]{0,1:T(8,128)(2,1)S(1)}, u32[]{:S(2)}, u32[]{:S(2)}) collective-permute-start(bf16[128,1280]{0,1:T(8,128)(2,1)S(1)} %bitcast.34), channel_id=1, source_target_pairs={{0,1},{1,2},{2,3},{3,0},{4,5},{5,6},{6,7},{7,4},{8,9},{9,10},{10,1... | collective-permute-start | bytes 983048 | tf_op jit(solution)/shard_map/ppermute | solution.py:176
  161.0 1.1 copy-start.7

commit v11 on v10

--- a/solution.py
+++ b/solution.py
@@ -120,7 +120,12 @@
         remote_ids += [t % 2, 1 - t % 2]
         remote_valid += [(t_chip >= 1) & (t_chip <= chips - 2)] * 2
     remote_flags = membership(listed, remote_ids, remote_valid)
-    got_query, got_flags = lax.ppermute((query_block, remote_flags), "seq", back)
+    half = query_block.shape[0] // 2
+    got_flags = lax.ppermute(remote_flags, "seq", back)
+    got_halves = [
+        lax.ppermute(query_block[:half], "seq", back),
+        lax.ppermute(query_block[half:], "seq", back),
+    ]
 
     swap = [(i, i ^ 1) for i in range(seq_count)]
     partner_k, partner_v, partner_ck, partner_cv = lax.ppermute(
@@ -156,17 +161,26 @@
     )
     local_out, local_lse = attend_partial(local_flags, query_block, keys, values, jnp.float32)
 
-    far_out, far_lse = attend_partial(got_flags, got_query, remote_keys, remote_values, jnp.bfloat16)
-    far_out, far_lse = lax.ppermute((far_out, far_lse), "seq", forth)
-
+    mixed_halves = []
+    for k, got_query in enumerate(got_halves):
+        far_out, far_lse = attend_partial(
+            got_flags, got_query, remote_keys, remote_values, jnp.bfloat16
+        )
+        far_out, far_lse = lax.ppermute((far_out, far_lse), "seq", forth)
+        near = slice(k * half, (k + 1) * half)
+        lse_a = local_lse[:, 0, near][:, :, None]
+        lse_b = far_lse[:, 0, :][:, :, None]
+        top = jnp.maximum(lse_a, lse_b)
+        weight_a = jnp.exp(lse_a - top)
+        weight_b = jnp.exp(lse_b - top)
+        mixed = (
+            local_out[:, near] * weight_a + far_out.astype(jnp.float32) * weight_b
+        ) / (weight_a + weight_b)
+        mixed_halves.append(mixed.astype(jnp.bfloat16))
     rows_all = query_block.shape[0]
-    lse_a = local_lse[:, 0, :][:, :, None]
-    lse_b = far_lse[:, 0, :][:, :, None]
-    top = jnp.maximum(lse_a, lse_b)
-    weight_a = jnp.exp(lse_a - top)
-    weight_b = jnp.exp(lse_b - top)
-    mixed = (local_out * weight_a + far_out.astype(jnp.float32) * weight_b) / (weight_a + weight_b)
-    heads_out = jnp.transpose(mixed.astype(jnp.bfloat16), (1, 0, 2)).reshape(rows_all, head_width)
+    heads_out = jnp.transpose(jnp.concatenate(mixed_halves, axis=1), (1, 0, 2)).reshape(
+        rows_all, head_width
+    )
 
     rows = queries.shape[0]
     result = jnp.zeros((rows, queries.shape[1]), jnp.bfloat16)

time: 163 us -> 154 us (0.945)
  waiting for transfers between devices: 77.3 us -> 58.3 us
  Pallas kernels: 43.9 us -> 51.9 us
  local copies, waits for them, and re-layouts: 12.3 us -> 7.95 us
  starting transfers between devices: 22.4 us -> 25.6 us
  other arithmetic: 6.79 us -> 9.89 us
    ppermute x2 -> x3, waiting for transfers between devices: 24.9 us -> 16.4 us  [the longest x1 14.3 us: local(): lax.ppermute(query_block[half:], 'seq', back)]
    pallas_call x2 -> x3, Pallas kernels: 43.9 us -> 51.9 us  [attend_partial(): pl.pallas_call(lambda *a: partial_kernel(nsrc, group, *a), grid_spec=grid...]
    ppermute x2 -> x4, waiting for transfers between devices: 7.81 us -> 0.01 us  [local(): far_out, far_lse = lax.ppermute((far_out, far_lse), 'seq', forth)]
    convert_element_type x0 -> x1, other arithmetic: none -> 4.58 us  [local(): mixed_halves.append(mixed.astype(jnp.bfloat16))]
    transpose x1, other arithmetic: 4.58 us -> 0.09 us  [local(): jnp.transpose(jnp.concatenate(mixed_halves, axis=1), (1, 0, 2))]
    unnamed x20 -> x12, local copies, waits for them, and re-layouts: 5.25 us -> 0.87 us
    concatenate x1 -> x3, other arithmetic: 1.16 us -> 4.21 us  [local(): query_block = jnp.concatenate(query_parts, axis=0)]
    ppermute x2 -> x4, starting transfers between devices: 2.11 us -> 4.18 us  [local(): far_out, far_lse = lax.ppermute((far_out, far_lse), 'seq', forth)]
  transfers between devices with their start and end apart: 14 -> 17, of which waited for: 6 -> 5; matrix products, arithmetic and copies ran while one was open for 3% -> 6% of each run, Pallas kernels for 14% -> 34%
where the time goes in v11:
time: 154 us
  waiting for transfers between devices  58.3 us (38%)
  Pallas kernels  51.9 us (34%)
  starting transfers between devices  25.6 us (17%)
  other arithmetic  9.89 us (6%)
  local copies, waits for them, and re-layouts  7.95 us (5%)
    pallas_call x3, Pallas kernels, attend_partial(): pl.pallas_call(lambda *a: partial_kernel(nsrc, group, *a), grid_spec=grid...  51.9 us
    ppermute x3, waiting for transfers between devices, local(): lax.ppermute(piece, 'sp', [(i, (i - d) % sp_count) for i in range(sp_coun...  25.6 us
    ppermute x3, waiting for transfers between devices, local(): lax.ppermute(piece, 'sp', [(i, (i + d) % sp_count) for i in range(sp_coun...  16.4 us
    ppermute x1, waiting for transfers between devices, local(): lax.ppermute(query_block[half:], 'seq', back)  14.3 us
    ppermute x3, starting transfers between devices, local(): lax.ppermute(piece, 'sp', [(i, (i - d) % sp_count) for i in range(sp_coun...  9.28 us
    ppermute x3, starting transfers between devices, local(): lax.ppermute(piece, 'sp', [(i, (i + d) % sp_count) for i in range(sp_coun...  6.98 us
    convert_element_type x1, other arithmetic, local(): mixed_halves.append(mixed.astype(jnp.bfloat16))  4.58 us
    concatenate x3, other arithmetic, local(): query_block = jnp.concatenate(query_parts, axis=0)  4.21 us
  transfers between devices with their start and end apart: 17, of which 5 were waited for; matrix products, arithmetic and copies ran while one was open for 6% of the time, Pallas kernels for 34%

profile of v11, /device:TPU:0, one launch (start us, length us, event | category | flops | bytes accessed | tf_op | source)
XLA Modules:
  0.0 153.9 jit_solution(17014259484348388305)
XLA Ops:
  0.0 2.4 %constant_dynamic-slice_fusion.3 = (bf16[128,1280]{1,0:T(8,128)(2,1)S(1)}, bf16[128,1280]{1,0:T(8,128)(2,1)}, bf16[128,1280]{1,0:T(8,128)(2,1)}, bf16[128,1280]{1,0:T(8,128)(2,1)}) fusion(bf16[128,5120]{1,0:T(8,128)(2,1)} %param.6, s32[]{:T(128)S(6)} %select_n.55, s32[]{:T(128)S(6)} %select_n.57, s32[]{:T(128)S(6)} %select_n.61, s32[]{:T(128)S(6)} %select_n.59), kind=kLoop, calls=%fused_computation.23 | loop fusion | bytes 2621456 | tf_op jit(solution)/shard_map/dynamic_slice | solution.py:99
  2.4 3.0 %collective-permute-start = (bf16[128,1280]{1,0:T(8,128)(2,1)}, bf16[128,1280]{1,0:T(8,128)(2,1)S(1)}, u32[]{:S(2)}, u32[]{:S(2)}) collective-permute-start(bf16[128,1280]{1,0:T(8,128)(2,1)} %get-tuple-element.32), channel_id=1, source_target_pairs={{0,1},{1,2},{2,3},{3,0},{4,5},{5,6},{6,7},{7,4},{8,9},{9,10},{10,1... | collective-permute-start | bytes 983048 | tf_op jit(solution)/shard_map/ppermute | solution.py:104
  5.4 2.6 %collective-permute-start.1 = (bf16[128,1280]{1,0:T(8,128)(2,1)}, bf16[128,1280]{1,0:T(8,128)(2,1)}, u32[]{:S(2)}, u32[]{:S(2)}) collective-permute-start(bf16[128,1280]{1,0:T(8,128)(2,1)} %get-tuple-element.34), channel_id=1, source_target_pairs={{0,2},{1,3},{2,0},{3,1},{4,6},{5,7},{6,4},{7,5},{8,10},{9,11},{10,... | collective-permute-start | bytes 983048 | tf_op jit(solution)/shard_map/ppermute | solution.py:104
  8.0 1.3 collective-permute-start.2
  9.8 1.5 collective-permute-start.7
  11.3 2.0 %collective-permute-done.7.a_0_ = s32[4]{0:T(128)S(1)} collective-permute-done((s32[4]{0:T(128)S(1)}, s32[4]{0:T(128)S(1)}, u32[]{:S(2)}, u32[]{:S(2)}) %collective-permute-start.7) | collective-permute-done | bytes 48 | tf_op jit(solution)/shard_map/ppermute | solution.py:124
  13.3 16.3 %collective-permute-done.1 = bf16[128,1280]{1,0:T(8,128)(2,1)} collective-permute-done((bf16[128,1280]{1,0:T(8,128)(2,1)}, bf16[128,1280]{1,0:T(8,128)(2,1)}, u32[]{:S(2)}, u32[]{:S(2)}) %collective-permute-start.1) | collective-permute-done | bytes 327712 | tf_op jit(solution)/shard_map/ppermute | solution.py:104
  29.7 0.5 collective-permute-start.6
  30.2 1.1 pad_maximum_fusion.2
  31.3 1.6 %collective-permute-start.11 = (bf16[256,1280]{1,0:T(8,128)(2,1)S(1)}, bf16[256,1280]{1,0:T(8,128)(2,1)}, u32[]{:S(2)}, u32[]{:S(2)}) collective-permute-start(bf16[256,1280]{1,0:T(8,128)(2,1)S(1)} %pad_maximum_fusion.2), channel_id=1, source_target_pairs={{0,8},{4,12},{8,0},{12,4},{1,9},{5,13},{9,1},{13,5},{2,10},{6,14},... | collective-permute-start | bytes 1966088 | tf_op jit(solution)/shard_map/ppermute | solution.py:127
  32.9 0.9 pad_maximum_fusion.1
  33.8 14.3 %collective-permute-done.11.a_1_ = bf16[256,1280]{1,0:T(8,128)(2,1)} collective-permute-done((bf16[256,1280]{1,0:T(8,128)(2,1)S(1)}, bf16[256,1280]{1,0:T(8,128)(2,1)}, u32[]{:S(2)}, u32[]{:S(2)}) %collective-permute-start.11) | collective-permute-done | bytes 655392 | tf_op jit(solution)/shard_map/ppermute | solution.py:127
  48.1 1.5 collective-permute-start.8
  49.7 15.0 %shard_map.66 = (bf16[10,256,128]{2,1,0:T(8,128)(2,1)}, f32[10,8,256]{2,1,0:T(8,128)}) custom-call(s32[4]{0:T(128)} %copy-done.3, bf16[256,1280]{1,0:T(8,128)(2,1)} %collective-permute-done.11.a_1_, bf16[512,1280]{1,0:T(8,128)(2,1)} %a_2_.5, bf16[512,1280]{1,0:T(8,128)(2,1)} %collective-permute-done.3.a_3_, bf16[512,1280]{1,0:T(8,128)(2,1)} %a_4_.5, ...), custom_call_target="tpu_custom_call" | custom-call | tf_op jit(solution)/shard_map/pallas_call | solution.py:71
  64.6 0.6 collective-permute-start.13
  65.2 14.9 %shard_map.65 = (bf16[10,256,128]{2,1,0:T(8,128)(2,1)}, f32[10,8,256]{2,1,0:T(8,128)}) custom-call(s32[4]{0:T(128)} %copy-done.3, bf16[256,1280]{1,0:T(8,128)(2,1)} %collective-permute-done.8.a_1_, bf16[512,1280]{1,0:T(8,128)(2,1)} %a_2_.5, bf16[512,1280]{1,0:T(8,128)(2,1)} %collective-permute-done.3.a_3_, bf16[512,1280]{1,0:T(8,128)(2,1)} %a_4_.5, ...), custom_call_target="tpu_custom_call" | custom-call | tf_op jit(solution)/shard_map/pallas_call | solution.py:71
  80.1 1.6 %collective-permute-start.10 = (bf16[10,256,128]{2,1,0:T(8,128)(2,1)}, bf16[10,256,128]{2,1,0:T(8,128)(2,1)S(1)}, u32[]{:S(2)}, u32[]{:S(2)}) collective-permute-start(bf16[10,256,128]{2,1,0:T(8,128)(2,1)} %get-tuple-element.14), channel_id=1, source_target_pairs={{0,8},{4,12},{8,0},{12,4},{1,9},{5,13},{9,1},{13,5},{2,10},{6,14},... | collective-permute-start | bytes 1966088 | tf_op jit(solution)/shard_map/ppermute | solution.py:169
  81.7 0.6 fusion.4.a_0_
  82.3 0.5 collective-permute-start.12
  82.8 1.5 collective-permute-start.9
  84.3 2.2 %pad_maximum_fusion.a_1_ = bf16[512,1280]{1,0:T(8,128)(2,1)} fusion(bf16[128,1280]{1,0:T(8,128)(2,1)} %collective-permute-done.2, bf16[128,1280]{1,0:T(8,128)(2,1)} %collective-permute-done.1, bf16[128,1280]{1,0:T(8,128)(2,1)S(1)} %collective-permute-done, bf16[128,1280]{1,0:T(8,128)(2,1)S(1)} %get-tuple-element.31), kind=kLoop, calls=%fused_computation | loop fusion | flops 5242880 | bytes 2621440 | tf_op jit(solution)/shard_map/concatenate | solution.py:106
  86.5 22.1 %shard_map.64 = (f32[10,512,128]{2,1,0:T(8,128)}, f32[10,8,512]{2,1,0:T(8,128)}) custom-call(s32[4]{0:T(128)} %fusion.4.a_0_, bf16[512,1280]{1,0:T(8,128)(2,1)} %pad_maximum_fusion.a_1_, bf16[512,1280]{1,0:T(8,128)(2,1)} %a_2_.5, bf16[512,1280]{1,0:T(8,128)(2,1)} %collective-permute-done.3.a_3_, bf16[512,1280]{1,0:T(8,128)(2,1)} %a_4_.5, ...), custom_call_target="tpu_custom_call" | custom-call | tf_op jit(solution)/shard_map/pallas_call | solution.py:71
  108.6 1.0 copy.19
  109.7 4.6 %divide_convert_fusion.1 = (bf16[10,256,128]{2,1,0:T(8,128)(2,1)S(1)}, bf16[10,256,128]{2,1,0:T(8,128)(2,1)S(1)}) fusion(bf16[10,256,128]{2,1,0:T(8,128)(2,1)S(1)} %collective-permute-done.10, f32[10,512,128]{2,1,0:T(8,128)} %get-tuple-element.11, f32[10,256]{1,0:T(8,128)S(1)} %get-tuple-element.19, f32[10,256]{1,0:T(8,128)S(1)} %get-tuple-element.20, ...), kind=kLoop, calls=%fused_computation.3 | loop fusion | flops 3932160 | bytes 5304320 | tf_op jit(solution)/shard_map/convert_element_type | solution.py:179
  114.6 0.2 copy.23
  114.8 8.6 %collective-permute-start.14 = (bf16[128,1280]{0,1:T(8,128)(2,1)S(1)}, bf16[128,1280]{0,1:T(8,128)(2,1)S(1)}, u32[]{:S(2)}, u32[]{:S(2)}) collective-permute-start(bf16[128,1280]{0,1:T(8,128)(2,1)S(1)} %bitcast.46), channel_id=1, source_target_pairs={{0,3},{1,0},{2,1},{3,2},{4,7},{5,4},{6,5},{7,6},{8,11},{9,8},{10,9... | collective-permute-start | bytes 983048 | tf_op jit(solution)/shard_map/ppermute | solution.py:190
  124.0 0.5 collective-permute-start.15
  125.1 6.5 %collective-permute-done.14 = bf16[128,1280]{0,1:T(8,128)(2,1)S(1)} collective-permute-done((bf16[128,1280]{0,1:T(8,128)(2,1)S(1)}, bf16[128,1280]{0,1:T(8,128)(2,1)S(1)}, u32[]{:S(2)}, u32[]{:S(2)}) %collective-permute-start.14) | collective-permute-done | bytes 327712 | tf_op jit(solution)/shard_map/ppermute | solution.py:190
  131.8 19.1 %collective-permute-done.15 = bf16[128,1280]{0,1:T(8,128)(2,1)} collective-permute-done((bf16[128,1280]{0,1:T(8,128)(2,1)S(1)}, bf16[128,1280]{0,1:T(8,128)(2,1)}, u32[]{:S(2)}, u32[]{:S(2)}) %collective-permute-start.15) | collective-permute-done | bytes 327712 | tf_op jit(solution)/shard_map/ppermute | solution.py:190
  150.9 1.1 copy.26
  152.3 0.9 copy-done.2
  153.1 0.7 constant_dynamic-update-slice_fusion
  (45 shorter events, 2.3 us)
Async XLA Ops:
  0.0 9.4 %copy-start = (bf16[512,1280]{1,0:T(8,128)(2,1)S(1)}, bf16[512,1280]{1,0:T(8,128)(2,1)}, u32[]{:S(2)}) copy-start(bf16[512,1280]{1,0:T(8,128)(2,1)} %a_2_.5) | copy-start | bytes 3932164
  0.0 9.5 %copy-start.4 = (s32[1,6]{1,0:T(1,128)S(1)}, s32[1,6]{1,0:T(1,128)}, u32[]{:S(2)}) copy-start(s32[1,6]{1,0:T(1,128)} %param.11) | copy-start | bytes 76
  0.0 13.3 %copy-start.1 = (bf16[512,1280]{1,0:T(8,128)(2,1)S(1)}, bf16[512,1280]{1,0:T(8,128)(2,1)}, u32[]{:S(2)}) copy-start(bf16[512,1280]{1,0:T(8,128)(2,1)} %a_4_.5) | copy-start | bytes 3932164
  2.4 28.9 %collective-permute-start = (bf16[128,1280]{1,0:T(8,128)(2,1)}, bf16[128,1280]{1,0:T(8,128)(2,1)S(1)}, u32[]{:S(2)}, u32[]{:S(2)}) collective-permute-start(bf16[128,1280]{1,0:T(8,128)(2,1)} %get-tuple-element.32), channel_id=1, source_target_pairs={{0,1},{1,2},{2,3},{3,0},{4,5},{5,6},{6,7},{7,4},{8,9},{9,10},{10,1... | collective-permute-start | bytes 983048 | tf_op jit(solution)/shard_map/ppermute | solution.py:104
  5.4 24.2 %collective-permute-start.1 = (bf16[128,1280]{1,0:T(8,128)(2,1)}, bf16[128,1280]{1,0:T(8,128)(2,1)}, u32[]{:S(2)}, u32[]{:S(2)}) collective-permute-start(bf16[128,1280]{1,0:T(8,128)(2,1)} %get-tuple-element.34), channel_id=1, source_target_pairs={{0,2},{1,3},{2,0},{3,1},{4,6},{5,7},{6,4},{7,5},{8,10},{9,11},{10,... | collective-permute-start | bytes 983048 | tf_op jit(solution)/shard_map/ppermute | solution.py:104
  8.0 21.6 %collective-permute-start.2 = (bf16[128,1280]{1,0:T(8,128)(2,1)}, bf16[128,1280]{1,0:T(8,128)(2,1)}, u32[]{:S(2)}, u32[]{:S(2)}) collective-permute-start(bf16[128,1280]{1,0:T(8,128)(2,1)} %get-tuple-element.33), channel_id=1, source_target_pairs={{0,3},{1,0},{2,1},{3,2},{4,7},{5,4},{6,5},{7,6},{8,11},{9,8},{10,9... | collective-permute-start | bytes 983048 | tf_op jit(solution)/shard_map/ppermute | solution.py:104
  9.4 40.3 %collective-permute-start.3 = (bf16[512,1280]{1,0:T(8,128)(2,1)S(1)}, bf16[512,1280]{1,0:T(8,128)(2,1)}, u32[]{:S(2)}, u32[]{:S(2)}) collective-permute-start(bf16[512,1280]{1,0:T(8,128)(2,1)S(1)} %copy-done), channel_id=1, source_target_pairs={{0,4},{4,0},{8,12},{12,8},{1,5},{5,1},{9,13},{13,9},{2,6},{6,2},{1... | collective-permute-start | bytes 3932168 | tf_op jit(solution)/shard_map/ppermute | solution.py:131
  9.8 3.6 %collective-permute-start.7 = (s32[4]{0:T(128)S(1)}, s32[4]{0:T(128)S(1)}, u32[]{:S(2)}, u32[]{:S(2)}) collective-permute-start(s32[4]{0:T(128)S(1)} %fusion.5), channel_id=1, source_target_pairs={{0,8},{4,12},{8,0},{12,4},{1,9},{5,13},{9,1},{13,5},{2,10},{6,14},... | collective-permute-start | bytes 56 | tf_op jit(solution)/shard_map/ppermute | solution.py:124
  13.3 20.5 %copy-start.3 = (s32[4]{0:T(128)}, s32[4]{0:T(128)S(1)}, u32[]{:S(2)}) copy-start(s32[4]{0:T(128)S(1)} %collective-permute-done.7.a_0_) | copy-start | bytes 52
  13.3 36.3 %collective-permute-start.4 = (bf16[512,1280]{1,0:T(8,128)(2,1)S(1)}, bf16[512,1280]{1,0:T(8,128)(2,1)}, u32[]{:S(2)}, u32[]{:S(2)}) collective-permute-start(bf16[512,1280]{1,0:T(8,128)(2,1)S(1)} %copy-done.1), channel_id=1, source_target_pairs={{0,4},{4,0},{8,12},{12,8},{1,5},{5,1},{9,13},{13,9},{2,6},{6,2},{1... | collective-permute-start | bytes 3932168 | tf_op jit(solution)/shard_map/ppermute | solution.py:131
  29.7 20.0 %collective-permute-start.5 = (bf16[512,1280]{1,0:T(8,128)(2,1)}, bf16[512,1280]{1,0:T(8,128)(2,1)}, u32[]{:S(2)}, u32[]{:S(2)}) collective-permute-start(bf16[512,1280]{1,0:T(8,128)(2,1)} %a_6_.5), channel_id=1, source_target_pairs={{0,4},{4,0},{8,12},{12,8},{1,5},{5,1},{9,13},{13,9},{2,6},{6,2},{1... | collective-permute-start | bytes 3932168 | tf_op jit(solution)/shard_map/ppermute | solution.py:131
  29.7 20.0 %collective-permute-start.6 = (bf16[512,1280]{1,0:T(8,128)(2,1)}, bf16[512,1280]{1,0:T(8,128)(2,1)}, u32[]{:S(2)}, u32[]{:S(2)}) collective-permute-start(bf16[512,1280]{1,0:T(8,128)(2,1)} %a_8_.5), channel_id=1, source_target_pairs={{0,4},{4,0},{8,12},{12,8},{1,5},{5,1},{9,13},{13,9},{2,6},{6,2},{1... | collective-permute-start | bytes 3932168 | tf_op jit(solution)/shard_map/ppermute | solution.py:131
  31.3 16.8 %collective-permute-start.11 = (bf16[256,1280]{1,0:T(8,128)(2,1)S(1)}, bf16[256,1280]{1,0:T(8,128)(2,1)}, u32[]{:S(2)}, u32[]{:S(2)}) collective-permute-start(bf16[256,1280]{1,0:T(8,128)(2,1)S(1)} %pad_maximum_fusion.2), channel_id=1, source_target_pairs={{0,8},{4,12},{8,0},{12,4},{1,9},{5,13},{9,1},{13,5},{2,10},{6,14},... | collective-permute-start | bytes 1966088 | tf_op jit(solution)/shard_map/ppermute | solution.py:127
  48.1 17.1 %collective-permute-start.8 = (bf16[256,1280]{1,0:T(8,128)(2,1)}, bf16[256,1280]{1,0:T(8,128)(2,1)}, u32[]{:S(2)}, u32[]{:S(2)}) collective-permute-start(bf16[256,1280]{1,0:T(8,128)(2,1)} %pad_maximum_fusion.1), channel_id=1, source_target_pairs={{0,8},{4,12},{8,0},{12,4},{1,9},{5,13},{9,1},{13,5},{2,10},{6,14},... | collective-permute-start | bytes 1966088 | tf_op jit(solution)/shard_map/ppermute | solution.py:126
  64.6 17.7 %copy-start.5 = (f32[10,8,256]{2,1,0:T(8,128)S(1)}, f32[10,8,256]{2,1,0:T(8,128)}, u32[]{:S(2)}) copy-start(f32[10,8,256]{2,1,0:T(8,128)} %get-tuple-element.15) | copy-start | bytes 245764
  64.6 45.1 %collective-permute-start.13 = (bf16[10,256,128]{2,1,0:T(8,128)(2,1)}, bf16[10,256,128]{2,1,0:T(8,128)(2,1)S(1)}, u32[]{:S(2)}, u32[]{:S(2)}) collective-permute-start(bf16[10,256,128]{2,1,0:T(8,128)(2,1)} %get-tuple-element.16), channel_id=1, source_target_pairs={{0,8},{4,12},{8,0},{12,4},{1,9},{5,13},{9,1},{13,5},{2,10},{6,14},... | collective-permute-start | bytes 1966088 | tf_op jit(solution)/shard_map/ppermute | solution.py:169
  80.1 29.6 %collective-permute-start.10 = (bf16[10,256,128]{2,1,0:T(8,128)(2,1)}, bf16[10,256,128]{2,1,0:T(8,128)(2,1)S(1)}, u32[]{:S(2)}, u32[]{:S(2)}) collective-permute-start(bf16[10,256,128]{2,1,0:T(8,128)(2,1)} %get-tuple-element.14), channel_id=1, source_target_pairs={{0,8},{4,12},{8,0},{12,4},{1,9},{5,13},{9,1},{13,5},{2,10},{6,14},... | collective-permute-start | bytes 1966088 | tf_op jit(solution)/shard_map/ppermute | solution.py:169
  82.3 27.4 %collective-permute-start.12 = (f32[10,8,256]{2,1,0:T(8,128)S(1)}, f32[10,8,256]{2,1,0:T(8,128)S(1)}, u32[]{:S(2)}, u32[]{:S(2)}) collective-permute-start(f32[10,8,256]{2,1,0:T(8,128)S(1)} %copy-done.5), channel_id=1, source_target_pairs={{0,8},{4,12},{8,0},{12,4},{1,9},{5,13},{9,1},{13,5},{2,10},{6,14},... | collective-permute-start | bytes 245768 | tf_op jit(solution)/shard_map/ppermute | solution.py:169
  82.8 26.9 %collective-permute-start.9 = (f32[10,8,256]{2,1,0:T(8,128)}, f32[10,8,256]{2,1,0:T(8,128)S(1)}, u32[]{:S(2)}, u32[]{:S(2)}) collective-permute-start(f32[10,8,256]{2,1,0:T(8,128)} %get-tuple-element.13), channel_id=1, source_target_pairs={{0,8},{4,12},{8,0},{12,4},{1,9},{5,13},{9,1},{13,5},{2,10},{6,14},... | collective-permute-start | bytes 245768 | tf_op jit(solution)/shard_map/ppermute | solution.py:169
  114.8 16.8 %collective-permute-start.14 = (bf16[128,1280]{0,1:T(8,128)(2,1)S(1)}, bf16[128,1280]{0,1:T(8,128)(2,1)S(1)}, u32[]{:S(2)}, u32[]{:S(2)}) collective-permute-start(bf16[128,1280]{0,1:T(8,128)(2,1)S(1)} %bitcast.46), channel_id=1, source_target_pairs={{0,3},{1,0},{2,1},{3,2},{4,7},{5,4},{6,5},{7,6},{8,11},{9,8},{10,9... | collective-permute-start | bytes 983048 | tf_op jit(solution)/shard_map/ppermute | solution.py:190
  124.0 26.9 %collective-permute-start.15 = (bf16[128,1280]{0,1:T(8,128)(2,1)S(1)}, bf16[128,1280]{0,1:T(8,128)(2,1)}, u32[]{:S(2)}, u32[]{:S(2)}) collective-permute-start(bf16[128,1280]{0,1:T(8,128)(2,1)S(1)} %bitcast.48), channel_id=1, source_target_pairs={{0,2},{1,3},{2,0},{3,1},{4,6},{5,7},{6,4},{7,5},{8,10},{9,11},{10,... | collective-permute-start | bytes 983048 | tf_op jit(solution)/shard_map/ppermute | solution.py:190
  124.7 27.4 %collective-permute-start.16 = (bf16[128,1280]{0,1:T(8,128)(2,1)S(1)}, bf16[128,1280]{0,1:T(8,128)(2,1)S(1)}, u32[]{:S(2)}, u32[]{:S(2)}) collective-permute-start(bf16[128,1280]{0,1:T(8,128)(2,1)S(1)} %bitcast.47), channel_id=1, source_target_pairs={{0,1},{1,2},{2,3},{3,0},{4,5},{5,6},{6,7},{7,4},{8,9},{9,10},{10,1... | collective-permute-start | bytes 983048 | tf_op jit(solution)/shard_map/ppermute | solution.py:190
  152.0 1.1 copy-start.2

commit v12 on v11

--- a/solution.py
+++ b/solution.py
@@ -49,15 +49,16 @@
         lse_ref[g] = jnp.transpose(wide)[:STAT_ROWS]
 
 
-def attend_partial(flags, query_block, key_blocks, value_blocks, out_dtype):
+def attend_partial(flags, query_block, key_blocks, value_blocks, out_dtype, parts=1, part=0):
     nsrc = len(key_blocks)
     rows, width = query_block.shape
+    rows = rows // parts
     block_rows = key_blocks[0].shape[0]
     nheads = width // HEAD_DIM
     group = max(g for g in range(1, 6) if nheads % g == 0)
     row_tile = rows // ROW_SPLIT
     span = group * HEAD_DIM
-    q_spec = pl.BlockSpec((row_tile, span), lambda h, r, f: (r, h))
+    q_spec = pl.BlockSpec((row_tile, span), lambda h, r, f: (r + part * ROW_SPLIT, h))
     kv_spec = pl.BlockSpec((block_rows, span), lambda h, r, f: (0, h))
     out_spec = pl.BlockSpec((group, row_tile, HEAD_DIM), lambda h, r, f: (h, r, 0))
     lse_spec = pl.BlockSpec((group, STAT_ROWS, row_tile), lambda h, r, f: (h, 0, r))
@@ -159,7 +160,14 @@
         [seq_count + s, seq_count + other, s, other],
         [s >= 0, s >= 0, chip == 0, chip == 0],
     )
-    local_out, local_lse = attend_partial(local_flags, query_block, keys, values, jnp.float32)
+    local_parts = [
+        attend_partial(local_flags, query_block, keys, values, jnp.float32, 2, k) for k in range(2)
+    ]
+    got_first, first_out, first_lse = lax.optimization_barrier(
+        (got_halves[0], local_parts[0][0], local_parts[0][1])
+    )
+    got_halves = [got_first, got_halves[1]]
+    local_parts = [(first_out, first_lse), local_parts[1]]
 
     mixed_halves = []
     for k, got_query in enumerate(got_halves):
@@ -167,25 +175,24 @@
             got_flags, got_query, remote_keys, remote_values, jnp.bfloat16
         )
         far_out, far_lse = lax.ppermute((far_out, far_lse), "seq", forth)
-        near = slice(k * half, (k + 1) * half)
-        lse_a = local_lse[:, 0, near][:, :, None]
+        local_out, local_lse = local_parts[k]
+        lse_a = local_lse[:, 0, :][:, :, None]
         lse_b = far_lse[:, 0, :][:, :, None]
         top = jnp.maximum(lse_a, lse_b)
         weight_a = jnp.exp(lse_a - top)
         weight_b = jnp.exp(lse_b - top)
         mixed = (
-            local_out[:, near] * weight_a + far_out.astype(jnp.float32) * weight_b
+            local_out * weight_a + far_out.astype(jnp.float32) * weight_b
         ) / (weight_a + weight_b)
-        mixed_halves.append(mixed.astype(jnp.bfloat16))
-    rows_all = query_block.shape[0]
-    heads_out = jnp.transpose(jnp.concatenate(mixed_halves, axis=1), (1, 0, 2)).reshape(
-        rows_all, head_width
-    )
+        mixed_halves.append(
+            jnp.transpose(mixed.astype(jnp.bfloat16), (1, 0, 2)).reshape(half, head_width)
+        )
 
     rows = queries.shape[0]
     result = jnp.zeros((rows, queries.shape[1]), jnp.bfloat16)
     for d in range(sp_count):
-        piece = heads_out[d * rows : (d + 1) * rows]
+        start = d * rows
+        piece = mixed_halves[start // half][start % half : start % half + rows]
         if d:
             piece = lax.ppermute(piece, "sp", [(i, (i - d) % sp_count) for i in range(sp_count)])
         columns = ((sp_place + d) % sp_count) * head_width

time: 154 us -> 162 us (1.052)
  Pallas kernels: 51.9 us -> 60.5 us
  waiting for transfers between devices: 58.3 us -> 60.2 us
    ppermute x1, waiting for transfers between devices: 14.3 us -> 0.01 us  [local(): lax.ppermute(query_block[half:], 'seq', back)]
    ppermute x4, waiting for transfers between devices: 0.01 us -> 11.3 us  [local(): far_out, far_lse = lax.ppermute((far_out, far_lse), 'seq', forth)]
    pallas_call x3 -> x4, Pallas kernels: 51.9 us -> 60.5 us  [attend_partial(): pl.pallas_call(lambda *a: partial_kernel(nsrc, group, *a), grid_spec=grid...]
    ppermute x1, waiting for transfers between devices: 0.01 us -> 8.42 us  [local(): lax.ppermute(query_block[:half], 'seq', back)]
    ppermute x3, waiting for transfers between devices: 25.6 us -> 17.3 us  [local(): lax.ppermute(piece, 'sp', [(i, (i - d) % sp_count) for i in range(sp_coun...]
    ppermute x3, waiting for transfers between devices: 16.4 us -> 23.2 us  [local(): lax.ppermute(piece, 'sp', [(i, (i + d) % sp_count) for i in range(sp_coun...]
    ppermute x3, starting transfers between devices: 9.28 us -> 3.54 us  [local(): lax.ppermute(piece, 'sp', [(i, (i - d) % sp_count) for i in range(sp_coun...]
    ppermute x3, starting transfers between devices: 6.98 us -> 12.5 us  [local(): lax.ppermute(piece, 'sp', [(i, (i + d) % sp_count) for i in range(sp_coun...]
  transfers between devices with their start and end apart: 17 -> 17, of which waited for: 5 -> 6; matrix products, arithmetic and copies ran while one was open for 6% -> 8% of each run, Pallas kernels for 34% -> 37%
where the time goes in v12:
time: 162 us
  Pallas kernels  60.5 us (37%)
  waiting for transfers between devices  60.2 us (37%)
  starting transfers between devices  24.8 us (15%)
  other arithmetic  8.34 us (5%)
  local copies, waits for them, and re-layouts  7.79 us (5%)
    pallas_call x4, Pallas kernels, attend_partial(): pl.pallas_call(lambda *a: partial_kernel(nsrc, group, *a), grid_spec=grid...  60.5 us
    ppermute x3, waiting for transfers between devices, local(): lax.ppermute(piece, 'sp', [(i, (i + d) % sp_count) for i in range(sp_coun...  23.2 us
    ppermute x3, waiting for transfers between devices, local(): lax.ppermute(piece, 'sp', [(i, (i - d) % sp_count) for i in range(sp_coun...  17.3 us
    ppermute x3, starting transfers between devices, local(): lax.ppermute(piece, 'sp', [(i, (i + d) % sp_count) for i in range(sp_coun...  12.5 us
    ppermute x4, waiting for transfers between devices, local(): far_out, far_lse = lax.ppermute((far_out, far_lse), 'seq', forth)  11.3 us
    ppermute x1, waiting for transfers between devices, local(): lax.ppermute(query_block[:half], 'seq', back)  8.42 us
    concatenate x3, other arithmetic, local(): query_block = jnp.concatenate(query_parts, axis=0)  5.02 us
    ppermute x4, starting transfers between devices, local(): far_out, far_lse = lax.ppermute((far_out, far_lse), 'seq', forth)  4.23 us
  transfers between devices with their start and end apart: 17, of which 6 were waited for; matrix products, arithmetic and copies ran while one was open for 8% of the time, Pallas kernels for 37%

profile of v12, /device:TPU:0, one launch (start us, length us, event | category | flops | bytes accessed | tf_op | source)
XLA Modules:
  0.0 161.8 jit_solution(15842720471354874936)
XLA Ops:
  0.5 2.4 %constant_dynamic-slice_fusion.1 = (bf16[128,1280]{1,0:T(8,128)(2,1)}, bf16[128,1280]{1,0:T(8,128)(2,1)}, bf16[128,1280]{1,0:T(8,128)(2,1)S(1)}, bf16[128,1280]{1,0:T(8,128)(2,1)}) fusion(bf16[128,5120]{1,0:T(8,128)(2,1)} %param.6, s32[]{:T(128)S(6)} %select_n.59, s32[]{:T(128)S(6)} %select_n.56, s32[]{:T(128)S(6)} %select_n.54, s32[]{:T(128)S(6)} %select_n.61), kind=kLoop, calls=%fused_computation.22 | loop fusion | bytes 2621456 | tf_op jit(solution)/shard_map/dynamic_slice | solution.py:103
  2.8 3.6 %collective-permute-start.2 = (bf16[128,1280]{1,0:T(8,128)(2,1)}, bf16[128,1280]{1,0:T(8,128)(2,1)S(1)}, u32[]{:S(2)}, u32[]{:S(2)}) collective-permute-start(bf16[128,1280]{1,0:T(8,128)(2,1)} %get-tuple-element.35), channel_id=1, source_target_pairs={{0,2},{1,3},{2,0},{3,1},{4,6},{5,7},{6,4},{7,5},{8,10},{9,11},{10,... | collective-permute-start | bytes 983048 | tf_op jit(solution)/shard_map/ppermute | solution.py:105
  6.5 1.3 collective-permute-start.3
  8.4 13.9 %collective-permute-done.2 = bf16[128,1280]{1,0:T(8,128)(2,1)S(1)} collective-permute-done((bf16[128,1280]{1,0:T(8,128)(2,1)}, bf16[128,1280]{1,0:T(8,128)(2,1)S(1)}, u32[]{:S(2)}, u32[]{:S(2)}) %collective-permute-start.2) | collective-permute-done | bytes 327712 | tf_op jit(solution)/shard_map/ppermute | solution.py:105
  22.4 7.5 %collective-permute-start = (bf16[128,1280]{1,0:T(8,128)(2,1)}, bf16[128,1280]{1,0:T(8,128)(2,1)S(1)}, u32[]{:S(2)}, u32[]{:S(2)}) collective-permute-start(bf16[128,1280]{1,0:T(8,128)(2,1)} %get-tuple-element.36), channel_id=1, source_target_pairs={{0,1},{1,2},{2,3},{3,0},{4,5},{5,6},{6,7},{7,4},{8,9},{9,10},{10,1... | collective-permute-start | bytes 983048 | tf_op jit(solution)/shard_map/ppermute | solution.py:105
  30.2 1.9 %pad_maximum_fusion.2 = bf16[256,1280]{1,0:T(8,128)(2,1)} fusion(bf16[128,1280]{1,0:T(8,128)(2,1)} %collective-permute-done.3, bf16[128,1280]{1,0:T(8,128)(2,1)S(1)} %collective-permute-done.2), kind=kLoop, calls=%fused_computation.4 | loop fusion | flops 1310720 | bytes 1310720 | tf_op jit(solution)/shard_map/concatenate | solution.py:107
  32.1 9.2 %collective-permute-done = bf16[128,1280]{1,0:T(8,128)(2,1)S(1)} collective-permute-done((bf16[128,1280]{1,0:T(8,128)(2,1)}, bf16[128,1280]{1,0:T(8,128)(2,1)S(1)}, u32[]{:S(2)}, u32[]{:S(2)}) %collective-permute-start) | collective-permute-done | bytes 327712 | tf_op jit(solution)/shard_map/ppermute | solution.py:105
  41.2 1.5 collective-permute-start.12
  42.7 0.9 pad_maximum_fusion.1
  43.7 0.7 collective-permute-start.1
  44.5 0.6 fusion.6.a_0_
  45.0 2.2 %pad_maximum_fusion.a_1_ = bf16[512,1280]{1,0:T(8,128)(2,1)} fusion(bf16[128,1280]{1,0:T(8,128)(2,1)} %collective-permute-done.3, bf16[128,1280]{1,0:T(8,128)(2,1)S(1)} %collective-permute-done.2, bf16[128,1280]{1,0:T(8,128)(2,1)} %copy-done.2, bf16[128,1280]{1,0:T(8,128)(2,1)S(1)} %get-tuple-element.37), kind=kLoop, calls=%fused_computation | loop fusion | flops 5242880 | bytes 2621440 | tf_op jit(solution)/shard_map/concatenate | solution.py:107
  47.2 1.3 collective-permute-start.8
  48.6 15.1 %shard_map.64 = (f32[10,256,128]{2,1,0:T(8,128)}, f32[10,8,256]{2,1,0:T(8,128)}) custom-call(s32[4]{0:T(128)} %fusion.6.a_0_, bf16[512,1280]{1,0:T(8,128)(2,1)} %pad_maximum_fusion.a_1_, bf16[512,1280]{1,0:T(8,128)(2,1)} %a_2_.7, bf16[512,1280]{1,0:T(8,128)(2,1)} %collective-permute-done.4.a_3_, bf16[512,1280]{1,0:T(8,128)(2,1)} %a_4_.7, ...), custom_call_target="tpu_custom_call" | custom-call | tf_op jit(solution)/shard_map/pallas_call | solution.py:72
  63.7 8.4 %collective-permute-done.1.a_1_ = bf16[256,1280]{1,0:T(8,128)(2,1)} collective-permute-done((bf16[256,1280]{1,0:T(8,128)(2,1)}, bf16[256,1280]{1,0:T(8,128)(2,1)}, u32[]{:S(2)}, u32[]{:S(2)}) %collective-permute-start.1) | collective-permute-done | bytes 655392 | tf_op jit(solution)/shard_map/ppermute | solution.py:127
  72.1 0.5 copy-done.7
  72.6 15.0 %shard_map.65 = (bf16[10,256,128]{2,1,0:T(8,128)(2,1)}, f32[10,8,256]{2,1,0:T(8,128)}) custom-call(s32[4]{0:T(128)} %copy-done.7, bf16[256,1280]{1,0:T(8,128)(2,1)} %collective-permute-done.1.a_1_, bf16[512,1280]{1,0:T(8,128)(2,1)} %a_2_.7, bf16[512,1280]{1,0:T(8,128)(2,1)} %collective-permute-done.4.a_3_, bf16[512,1280]{1,0:T(8,128)(2,1)} %a_4_.7, ...), custom_call_target="tpu_custom_call" | custom-call | tf_op jit(solution)/shard_map/pallas_call | solution.py:72
  87.6 1.6 collective-permute-start.10
  89.2 15.1 %shard_map.67 = (bf16[10,256,128]{2,1,0:T(8,128)(2,1)}, f32[10,8,256]{2,1,0:T(8,128)}) custom-call(s32[4]{0:T(128)} %copy-done.7, bf16[256,1280]{1,0:T(8,128)(2,1)} %collective-permute-done.12.a_1_, bf16[512,1280]{1,0:T(8,128)(2,1)} %a_2_.7, bf16[512,1280]{1,0:T(8,128)(2,1)} %collective-permute-done.4.a_3_, bf16[512,1280]{1,0:T(8,128)(2,1)} %a_4_.7, ...), custom_call_target="tpu_custom_call" | custom-call | tf_op jit(solution)/shard_map/pallas_call | solution.py:72
  104.3 0.6 collective-permute-start.13
  104.8 1.5 collective-permute-start.9
  106.4 15.4 %shard_map.66 = (f32[10,256,128]{2,1,0:T(8,128)}, f32[10,8,256]{2,1,0:T(8,128)}) custom-call(s32[4]{0:T(128)} %fusion.6.a_0_, bf16[512,1280]{1,0:T(8,128)(2,1)} %pad_maximum_fusion.a_1_, bf16[512,1280]{1,0:T(8,128)(2,1)} %a_2_.7, bf16[512,1280]{1,0:T(8,128)(2,1)} %collective-permute-done.4.a_3_, bf16[512,1280]{1,0:T(8,128)(2,1)} %a_4_.7, ...), custom_call_target="tpu_custom_call" | custom-call | tf_op jit(solution)/shard_map/pallas_call | solution.py:72
  121.7 0.9 copy.24
  122.7 0.6 collective-permute-start.14
  123.4 1.2 fusion
  124.9 1.6 collective-permute-start.11
  126.4 11.3 %collective-permute-done.14 = bf16[10,256,128]{2,1,0:T(8,128)(2,1)S(1)} collective-permute-done((bf16[10,256,128]{2,1,0:T(8,128)(2,1)}, bf16[10,256,128]{2,1,0:T(8,128)(2,1)S(1)}, u32[]{:S(2)}, u32[]{:S(2)}) %collective-permute-start.14) | collective-permute-done | bytes 655392 | tf_op jit(solution)/shard_map/ppermute | solution.py:177
  137.7 1.2 fusion.1
  139.9 1.9 %collective-permute-start.16 = (bf16[128,1280]{0,1:T(8,128)(2,1)S(1)}, bf16[128,1280]{0,1:T(8,128)(2,1)}, u32[]{:S(2)}, u32[]{:S(2)}) collective-permute-start(bf16[128,1280]{0,1:T(8,128)(2,1)S(1)} %bitcast.50), channel_id=1, source_target_pairs={{0,1},{1,2},{2,3},{3,0},{4,5},{5,6},{6,7},{7,4},{8,9},{9,10},{10,1... | collective-permute-start | bytes 983048 | tf_op jit(solution)/shard_map/ppermute | solution.py:197
  142.2 17.3 %collective-permute-done.15 = bf16[128,1280]{0,1:T(8,128)(2,1)S(1)} collective-permute-done((bf16[128,1280]{0,1:T(8,128)(2,1)S(1)}, bf16[128,1280]{0,1:T(8,128)(2,1)S(1)}, u32[]{:S(2)}, u32[]{:S(2)}) %collective-permute-start.15) | collective-permute-done | bytes 327712 | tf_op jit(solution)/shard_map/ppermute | solution.py:197
  159.7 1.4 copy.28
  161.1 0.8 constant_dynamic-update-slice_fusion
  (57 shorter events, 3.4 us)
Async XLA Ops:
  0.0 43.7 %collective-permute-start.4 = (bf16[512,1280]{1,0:T(8,128)(2,1)}, bf16[512,1280]{1,0:T(8,128)(2,1)}, u32[]{:S(2)}, u32[]{:S(2)}) collective-permute-start(bf16[512,1280]{1,0:T(8,128)(2,1)} %a_2_.7), channel_id=1, source_target_pairs={{0,4},{4,0},{8,12},{12,8},{1,5},{5,1},{9,13},{13,9},{2,6},{6,2},{1... | collective-permute-start | bytes 3932168 | tf_op jit(solution)/shard_map/ppermute | solution.py:132
  0.5 7.4 %copy-start = (bf16[512,1280]{1,0:T(8,128)(2,1)S(1)}, bf16[512,1280]{1,0:T(8,128)(2,1)}, u32[]{:S(2)}) copy-start(bf16[512,1280]{1,0:T(8,128)(2,1)} %a_4_.7) | copy-start | bytes 3932164
  0.5 7.4 %copy-start.1 = (bf16[512,1280]{1,0:T(8,128)(2,1)S(1)}, bf16[512,1280]{1,0:T(8,128)(2,1)}, u32[]{:S(2)}) copy-start(bf16[512,1280]{1,0:T(8,128)(2,1)} %a_6_.7) | copy-start | bytes 3932164
  0.5 29.5 %copy-start.8 = (s32[1,6]{1,0:T(1,128)S(1)}, s32[1,6]{1,0:T(1,128)}, u32[]{:S(2)}) copy-start(s32[1,6]{1,0:T(1,128)} %param.11) | copy-start | bytes 76
  2.8 19.5 %collective-permute-start.2 = (bf16[128,1280]{1,0:T(8,128)(2,1)}, bf16[128,1280]{1,0:T(8,128)(2,1)S(1)}, u32[]{:S(2)}, u32[]{:S(2)}) collective-permute-start(bf16[128,1280]{1,0:T(8,128)(2,1)} %get-tuple-element.35), channel_id=1, source_target_pairs={{0,2},{1,3},{2,0},{3,1},{4,6},{5,7},{6,4},{7,5},{8,10},{9,11},{10,... | collective-permute-start | bytes 983048 | tf_op jit(solution)/shard_map/ppermute | solution.py:105
  6.5 16.0 %collective-permute-start.3 = (bf16[128,1280]{1,0:T(8,128)(2,1)}, bf16[128,1280]{1,0:T(8,128)(2,1)}, u32[]{:S(2)}, u32[]{:S(2)}) collective-permute-start(bf16[128,1280]{1,0:T(8,128)(2,1)} %get-tuple-element.38), channel_id=1, source_target_pairs={{0,3},{1,0},{2,1},{3,2},{4,7},{5,4},{6,5},{7,6},{8,11},{9,8},{10,9... | collective-permute-start | bytes 983048 | tf_op jit(solution)/shard_map/ppermute | solution.py:105
  7.8 39.4 %collective-permute-start.5 = (bf16[512,1280]{1,0:T(8,128)(2,1)S(1)}, bf16[512,1280]{1,0:T(8,128)(2,1)}, u32[]{:S(2)}, u32[]{:S(2)}) collective-permute-start(bf16[512,1280]{1,0:T(8,128)(2,1)S(1)} %copy-done), channel_id=1, source_target_pairs={{0,4},{4,0},{8,12},{12,8},{1,5},{5,1},{9,13},{13,9},{2,6},{6,2},{1... | collective-permute-start | bytes 3932168 | tf_op jit(solution)/shard_map/ppermute | solution.py:132
  7.8 40.7 %collective-permute-start.6 = (bf16[512,1280]{1,0:T(8,128)(2,1)S(1)}, bf16[512,1280]{1,0:T(8,128)(2,1)}, u32[]{:S(2)}, u32[]{:S(2)}) collective-permute-start(bf16[512,1280]{1,0:T(8,128)(2,1)S(1)} %copy-done.1), channel_id=1, source_target_pairs={{0,4},{4,0},{8,12},{12,8},{1,5},{5,1},{9,13},{13,9},{2,6},{6,2},{1... | collective-permute-start | bytes 3932168 | tf_op jit(solution)/shard_map/ppermute | solution.py:132
  22.3 26.3 %collective-permute-start.7 = (bf16[512,1280]{1,0:T(8,128)(2,1)}, bf16[512,1280]{1,0:T(8,128)(2,1)}, u32[]{:S(2)}, u32[]{:S(2)}) collective-permute-start(bf16[512,1280]{1,0:T(8,128)(2,1)} %a_8_.7), channel_id=1, source_target_pairs={{0,4},{4,0},{8,12},{12,8},{1,5},{5,1},{9,13},{13,9},{2,6},{6,2},{1... | collective-permute-start | bytes 3932168 | tf_op jit(solution)/shard_map/ppermute | solution.py:132
  22.4 18.8 %collective-permute-start = (bf16[128,1280]{1,0:T(8,128)(2,1)}, bf16[128,1280]{1,0:T(8,128)(2,1)S(1)}, u32[]{:S(2)}, u32[]{:S(2)}) collective-permute-start(bf16[128,1280]{1,0:T(8,128)(2,1)} %get-tuple-element.36), channel_id=1, source_target_pairs={{0,1},{1,2},{2,3},{3,0},{4,5},{5,6},{6,7},{7,4},{8,9},{9,10},{10,1... | collective-permute-start | bytes 983048 | tf_op jit(solution)/shard_map/ppermute | solution.py:105
  41.2 1.5 copy-start.2
  41.2 48.0 %collective-permute-start.12 = (bf16[256,1280]{1,0:T(8,128)(2,1)}, bf16[256,1280]{1,0:T(8,128)(2,1)}, u32[]{:S(2)}, u32[]{:S(2)}) collective-permute-start(bf16[256,1280]{1,0:T(8,128)(2,1)} %pad_maximum_fusion.2), channel_id=1, source_target_pairs={{0,8},{4,12},{8,0},{12,4},{1,9},{5,13},{9,1},{13,5},{2,10},{6,14},... | collective-permute-start | bytes 1966088 | tf_op jit(solution)/shard_map/ppermute | solution.py:128
  43.7 28.4 %collective-permute-start.1 = (bf16[256,1280]{1,0:T(8,128)(2,1)}, bf16[256,1280]{1,0:T(8,128)(2,1)}, u32[]{:S(2)}, u32[]{:S(2)}) collective-permute-start(bf16[256,1280]{1,0:T(8,128)(2,1)} %pad_maximum_fusion.1), channel_id=1, source_target_pairs={{0,8},{4,12},{8,0},{12,4},{1,9},{5,13},{9,1},{13,5},{2,10},{6,14},... | collective-permute-start | bytes 1966088 | tf_op jit(solution)/shard_map/ppermute | solution.py:127
  47.2 24.8 %collective-permute-start.8 = (s32[4]{0:T(128)S(1)}, s32[4]{0:T(128)S(1)}, u32[]{:S(2)}, u32[]{:S(2)}) collective-permute-start(s32[4]{0:T(128)S(1)} %fusion.7), channel_id=1, source_target_pairs={{0,8},{4,12},{8,0},{12,4},{1,9},{5,13},{9,1},{13,5},{2,10},{6,14},... | collective-permute-start | bytes 56 | tf_op jit(solution)/shard_map/ppermute | solution.py:125
  72.1 0.5 copy-start.7
  87.6 17.2 %copy-start.9 = (f32[10,8,256]{2,1,0:T(8,128)S(1)}, f32[10,8,256]{2,1,0:T(8,128)}, u32[]{:S(2)}) copy-start(f32[10,8,256]{2,1,0:T(8,128)} %get-tuple-element.21) | copy-start | bytes 245764
  87.6 35.7 %collective-permute-start.10 = (bf16[10,256,128]{2,1,0:T(8,128)(2,1)}, bf16[10,256,128]{2,1,0:T(8,128)(2,1)S(1)}, u32[]{:S(2)}, u32[]{:S(2)}) collective-permute-start(bf16[10,256,128]{2,1,0:T(8,128)(2,1)} %get-tuple-element.22), channel_id=1, source_target_pairs={{0,8},{4,12},{8,0},{12,4},{1,9},{5,13},{9,1},{13,5},{2,10},{6,14},... | collective-permute-start | bytes 1966088 | tf_op jit(solution)/shard_map/ppermute | solution.py:177
  104.3 19.0 %collective-permute-start.13 = (f32[10,8,256]{2,1,0:T(8,128)}, f32[10,8,256]{2,1,0:T(8,128)S(1)}, u32[]{:S(2)}, u32[]{:S(2)}) collective-permute-start(f32[10,8,256]{2,1,0:T(8,128)} %get-tuple-element.25), channel_id=1, source_target_pairs={{0,8},{4,12},{8,0},{12,4},{1,9},{5,13},{9,1},{13,5},{2,10},{6,14},... | collective-permute-start | bytes 245768 | tf_op jit(solution)/shard_map/ppermute | solution.py:177
  104.8 18.4 %collective-permute-start.9 = (f32[10,8,256]{2,1,0:T(8,128)S(1)}, f32[10,8,256]{2,1,0:T(8,128)S(1)}, u32[]{:S(2)}, u32[]{:S(2)}) collective-permute-start(f32[10,8,256]{2,1,0:T(8,128)S(1)} %copy-done.9), channel_id=1, source_target_pairs={{0,8},{4,12},{8,0},{12,4},{1,9},{5,13},{9,1},{13,5},{2,10},{6,14},... | collective-permute-start | bytes 245768 | tf_op jit(solution)/shard_map/ppermute | solution.py:177
  106.4 16.9 %copy-start.6 = (f32[10,8,256]{2,1,0:T(8,128)S(1)}, f32[10,8,256]{2,1,0:T(8,128)}, u32[]{:S(2)}) copy-start(f32[10,8,256]{2,1,0:T(8,128)} %get-tuple-element.19) | copy-start | bytes 245764
  106.4 17.0 %copy-start.3 = (f32[10,256,128]{2,1,0:T(8,128)S(1)}, f32[10,256,128]{2,1,0:T(8,128)}, u32[]{:S(2)}) copy-start(f32[10,256,128]{2,1,0:T(8,128)} %get-tuple-element.18) | copy-start | bytes 3932164
  122.7 15.1 %collective-permute-start.14 = (bf16[10,256,128]{2,1,0:T(8,128)(2,1)}, bf16[10,256,128]{2,1,0:T(8,128)(2,1)S(1)}, u32[]{:S(2)}, u32[]{:S(2)}) collective-permute-start(bf16[10,256,128]{2,1,0:T(8,128)(2,1)} %get-tuple-element.26), channel_id=1, source_target_pairs={{0,8},{4,12},{8,0},{12,4},{1,9},{5,13},{9,1},{13,5},{2,10},{6,14},... | collective-permute-start | bytes 1966088 | tf_op jit(solution)/shard_map/ppermute | solution.py:177
  124.6 13.1 %copy-start.4 = (f32[10,256,128]{2,1,0:T(8,128)S(1)}, f32[10,256,128]{2,1,0:T(8,128)}, u32[]{:S(2)}) copy-start(f32[10,256,128]{2,1,0:T(8,128)} %get-tuple-element.23) | copy-start | bytes 3932164
  124.9 17.1 %collective-permute-start.11 = (bf16[128,1280]{0,1:T(8,128)(2,1)S(1)}, bf16[128,1280]{0,1:T(8,128)(2,1)S(1)}, u32[]{:S(2)}, u32[]{:S(2)}) collective-permute-start(bf16[128,1280]{0,1:T(8,128)(2,1)S(1)} %bitcast.48), channel_id=1, source_target_pairs={{0,3},{1,0},{2,1},{3,2},{4,7},{5,4},{6,5},{7,6},{8,11},{9,8},{10,9... | collective-permute-start | bytes 983048 | tf_op jit(solution)/shard_map/ppermute | solution.py:197
  139.2 20.3 %collective-permute-start.15 = (bf16[128,1280]{0,1:T(8,128)(2,1)S(1)}, bf16[128,1280]{0,1:T(8,128)(2,1)S(1)}, u32[]{:S(2)}, u32[]{:S(2)}) collective-permute-start(bf16[128,1280]{0,1:T(8,128)(2,1)S(1)} %bitcast.49), channel_id=1, source_target_pairs={{0,2},{1,3},{2,0},{3,1},{4,6},{5,7},{6,4},{7,5},{8,10},{9,11},{10,... | collective-permute-start | bytes 983048 | tf_op jit(solution)/shard_map/ppermute | solution.py:197
  139.9 19.8 %collective-permute-start.16 = (bf16[128,1280]{0,1:T(8,128)(2,1)S(1)}, bf16[128,1280]{0,1:T(8,128)(2,1)}, u32[]{:S(2)}, u32[]{:S(2)}) collective-permute-start(bf16[128,1280]{0,1:T(8,128)(2,1)S(1)} %bitcast.50), channel_id=1, source_target_pairs={{0,1},{1,2},{2,3},{3,0},{4,5},{5,6},{6,7},{7,4},{8,9},{9,10},{10,1... | collective-permute-start | bytes 983048 | tf_op jit(solution)/shard_map/ppermute | solution.py:197
  159.7 1.4 copy-start.5

commit v13 on v11

--- a/solution.py
+++ b/solution.py
@@ -55,7 +55,8 @@
     block_rows = key_blocks[0].shape[0]
     nheads = width // HEAD_DIM
     group = max(g for g in range(1, 6) if nheads % g == 0)
-    row_tile = rows // ROW_SPLIT
+    split = ROW_SPLIT if (rows // ROW_SPLIT) % 128 == 0 else 1
+    row_tile = rows // split
     span = group * HEAD_DIM
     q_spec = pl.BlockSpec((row_tile, span), lambda h, r, f: (r, h))
     kv_spec = pl.BlockSpec((block_rows, span), lambda h, r, f: (0, h))
@@ -63,7 +64,7 @@
     lse_spec = pl.BlockSpec((group, STAT_ROWS, row_tile), lambda h, r, f: (h, 0, r))
     grid_spec = pltpu.PrefetchScalarGridSpec(
         num_scalar_prefetch=1,
-        grid=(nheads // group, ROW_SPLIT),
+        grid=(nheads // group, split),
         in_specs=[q_spec] + [kv_spec] * (2 * nsrc),
         out_specs=[out_spec, lse_spec],
         scratch_shapes=[pltpu.VMEM((nsrc, row_tile, block_rows), jnp.float32)],
@@ -120,12 +121,13 @@
         remote_ids += [t % 2, 1 - t % 2]
         remote_valid += [(t_chip >= 1) & (t_chip <= chips - 2)] * 2
     remote_flags = membership(listed, remote_ids, remote_valid)
-    half = query_block.shape[0] // 2
+    rows = queries.shape[0]
     got_flags = lax.ppermute(remote_flags, "seq", back)
     got_halves = [
-        lax.ppermute(query_block[:half], "seq", back),
-        lax.ppermute(query_block[half:], "seq", back),
+        lax.ppermute(query_parts[0], "seq", back),
+        lax.ppermute(jnp.concatenate(query_parts[1:], axis=0), "seq", back),
     ]
+    bounds = [(0, rows), (rows, query_parts[0].shape[0] * sp_count)]
 
     swap = [(i, i ^ 1) for i in range(seq_count)]
     partner_k, partner_v, partner_ck, partner_cv = lax.ppermute(
@@ -167,7 +169,7 @@
             got_flags, got_query, remote_keys, remote_values, jnp.bfloat16
         )
         far_out, far_lse = lax.ppermute((far_out, far_lse), "seq", forth)
-        near = slice(k * half, (k + 1) * half)
+        near = slice(*bounds[k])
         lse_a = local_lse[:, 0, near][:, :, None]
         lse_b = far_lse[:, 0, :][:, :, None]
         top = jnp.maximum(lse_a, lse_b)
@@ -176,16 +178,16 @@
         mixed = (
             local_out[:, near] * weight_a + far_out.astype(jnp.float32) * weight_b
         ) / (weight_a + weight_b)
-        mixed_halves.append(mixed.astype(jnp.bfloat16))
-    rows_all = query_block.shape[0]
-    heads_out = jnp.transpose(jnp.concatenate(mixed_halves, axis=1), (1, 0, 2)).reshape(
-        rows_all, head_width
-    )
-
-    rows = queries.shape[0]
+        mixed_halves.append(
+            jnp.transpose(mixed.astype(jnp.bfloat16), (1, 0, 2)).reshape(-1, head_width)
+        )
+
     result = jnp.zeros((rows, queries.shape[1]), jnp.bfloat16)
     for d in range(sp_count):
-        piece = heads_out[d * rows : (d + 1) * rows]
+        if d:
+            piece = mixed_halves[1][(d - 1) * rows : d * rows]
+        else:
+            piece = mixed_halves[0]
         if d:
             piece = lax.ppermute(piece, "sp", [(i, (i - d) % sp_count) for i in range(sp_count)])
         columns = ((sp_place + d) % sp_count) * head_width

time: 154 us -> 159 us (1.032)
  waiting for transfers between devices: 58.3 us -> 61.5 us
  Pallas kernels: 51.9 us -> 48.8 us
  local copies, waits for them, and re-layouts: 7.95 us -> 10.8 us
  starting transfers between devices: 25.6 us -> 27.8 us
    ppermute x2, waiting for transfers between devices: 14.3 us -> 22.1 us  [the longest x1 22.1 us: local(): lax.ppermute(jnp.concatenate(query_parts[1:], axis=0), 'seq', back)]
    transpose x1 -> x2, other arithmetic: 0.09 us -> 5.17 us  [local(): jnp.transpose(mixed.astype(jnp.bfloat16), (1, 0, 2)).reshape(-1, head_width)]
    ppermute x3, waiting for transfers between devices: 25.6 us -> 20.9 us  [local(): lax.ppermute(piece, 'sp', [(i, (i - d) % sp_count) for i in range(sp_coun...]
    convert_element_type x1 -> x0, other arithmetic: 4.58 us -> none  [local(): mixed_halves.append(mixed.astype(jnp.bfloat16))]
    unnamed x12 -> x22, local copies, waits for them, and re-layouts: 0.87 us -> 4.1 us
    pallas_call x3, Pallas kernels: 51.9 us -> 48.8 us  [attend_partial(): pl.pallas_call(lambda *a: partial_kernel(nsrc, group, *a), grid_spec=grid...]
    ppermute x3, starting transfers between devices: 9.28 us -> 11.5 us  [local(): lax.ppermute(piece, 'sp', [(i, (i - d) % sp_count) for i in range(sp_coun...]
    ppermute x3, waiting for transfers between devices: 16.4 us -> 18.4 us  [local(): lax.ppermute(piece, 'sp', [(i, (i + d) % sp_count) for i in range(sp_coun...]
  transfers between devices with their start and end apart: 17 -> 17, of which waited for: 5 -> 5; matrix products, arithmetic and copies ran while one was open for 6% -> 8% of each run, Pallas kernels for 34% -> 31%
where the time goes in v13:
time: 159 us
  waiting for transfers between devices  61.5 us (39%)
  Pallas kernels  48.8 us (31%)
  starting transfers between devices  27.8 us (17%)
  local copies, waits for them, and re-layouts  10.8 us (7%)
  other arithmetic  9.59 us (6%)
    pallas_call x3, Pallas kernels, attend_partial(): pl.pallas_call(lambda *a: partial_kernel(nsrc, group, *a), grid_spec=grid...  48.8 us
    ppermute x1, waiting for transfers between devices, local(): lax.ppermute(jnp.concatenate(query_parts[1:], axis=0), 'seq', back)  22.1 us
    ppermute x3, waiting for transfers between devices, local(): lax.ppermute(piece, 'sp', [(i, (i - d) % sp_count) for i in range(sp_coun...  20.9 us
    ppermute x3, waiting for transfers between devices, local(): lax.ppermute(piece, 'sp', [(i, (i + d) % sp_count) for i in range(sp_coun...  18.4 us
    ppermute x3, starting transfers between devices, local(): lax.ppermute(piece, 'sp', [(i, (i - d) % sp_count) for i in range(sp_coun...  11.5 us
    ppermute x3, starting transfers between devices, local(): lax.ppermute(piece, 'sp', [(i, (i + d) % sp_count) for i in range(sp_coun...  6.98 us
    transpose x2, other arithmetic, local(): jnp.transpose(mixed.astype(jnp.bfloat16), (1, 0, 2)).reshape(-1, head_width)  5.17 us
    ppermute x4, starting transfers between devices, local(): far_out, far_lse = lax.ppermute((far_out, far_lse), 'seq', forth)  4.24 us
  transfers between devices with their start and end apart: 17, of which 5 were waited for; matrix products, arithmetic and copies ran while one was open for 8% of the time, Pallas kernels for 31%

profile of v13, /device:TPU:0, one launch (start us, length us, event | category | flops | bytes accessed | tf_op | source)
XLA Modules:
  0.0 158.7 jit_solution(15657169993180955896)
XLA Ops:
  0.0 2.4 %constant_dynamic-slice_fusion.3 = (bf16[128,1280]{1,0:T(8,128)(2,1)S(1)}, bf16[128,1280]{1,0:T(8,128)(2,1)}, bf16[128,1280]{1,0:T(8,128)(2,1)}, bf16[128,1280]{1,0:T(8,128)(2,1)}) fusion(bf16[128,5120]{1,0:T(8,128)(2,1)} %param.6, s32[]{:T(128)S(6)} %select_n.55, s32[]{:T(128)S(6)} %select_n.57, s32[]{:T(128)S(6)} %select_n.61, s32[]{:T(128)S(6)} %select_n.59), kind=kLoop, calls=%fused_computation.23 | loop fusion | bytes 2621456 | tf_op jit(solution)/shard_map/dynamic_slice | solution.py:100
  2.4 3.0 %collective-permute-start = (bf16[128,1280]{1,0:T(8,128)(2,1)}, bf16[128,1280]{1,0:T(8,128)(2,1)S(1)}, u32[]{:S(2)}, u32[]{:S(2)}) collective-permute-start(bf16[128,1280]{1,0:T(8,128)(2,1)} %get-tuple-element.26), channel_id=1, source_target_pairs={{0,1},{1,2},{2,3},{3,0},{4,5},{5,6},{6,7},{7,4},{8,9},{9,10},{10,1... | collective-permute-start | bytes 983048 | tf_op jit(solution)/shard_map/ppermute | solution.py:105
  5.4 2.6 %collective-permute-start.1 = (bf16[128,1280]{1,0:T(8,128)(2,1)}, bf16[128,1280]{1,0:T(8,128)(2,1)}, u32[]{:S(2)}, u32[]{:S(2)}) collective-permute-start(bf16[128,1280]{1,0:T(8,128)(2,1)} %get-tuple-element.28), channel_id=1, source_target_pairs={{0,2},{1,3},{2,0},{3,1},{4,6},{5,7},{6,4},{7,5},{8,10},{9,11},{10,... | collective-permute-start | bytes 983048 | tf_op jit(solution)/shard_map/ppermute | solution.py:105
  8.0 1.3 collective-permute-start.2
  9.7 1.5 collective-permute-start.7
  11.3 5.1 %collective-permute-done = bf16[128,1280]{1,0:T(8,128)(2,1)S(1)} collective-permute-done((bf16[128,1280]{1,0:T(8,128)(2,1)}, bf16[128,1280]{1,0:T(8,128)(2,1)S(1)}, u32[]{:S(2)}, u32[]{:S(2)}) %collective-permute-start) | collective-permute-done | bytes 327712 | tf_op jit(solution)/shard_map/ppermute | solution.py:105
  16.4 13.3 %collective-permute-done.1 = bf16[128,1280]{1,0:T(8,128)(2,1)} collective-permute-done((bf16[128,1280]{1,0:T(8,128)(2,1)}, bf16[128,1280]{1,0:T(8,128)(2,1)}, u32[]{:S(2)}, u32[]{:S(2)}) %collective-permute-start.1) | collective-permute-done | bytes 327712 | tf_op jit(solution)/shard_map/ppermute | solution.py:105
  30.2 1.1 pad_maximum_fusion.1
  31.3 1.6 collective-permute-start.11
  32.9 22.1 %collective-permute-done.11.a_1_ = bf16[384,1280]{1,0:T(8,128)(2,1)S(1)} collective-permute-done((bf16[384,1280]{1,0:T(8,128)(2,1)S(1)}, bf16[384,1280]{1,0:T(8,128)(2,1)S(1)}, u32[]{:S(2)}, u32[]{:S(2)}) %collective-permute-start.11) | collective-permute-done | bytes 983072 | tf_op jit(solution)/shard_map/ppermute | solution.py:128
  55.1 1.5 collective-permute-start.8
  56.6 1.1 copy-done.2
  57.7 1.1 copy-done.3
  58.8 1.1 copy-done.4
  59.8 17.1 %shard_map.66 = (bf16[10,384,128]{2,1,0:T(8,128)(2,1)}, f32[10,8,384]{2,1,0:T(8,128)}) custom-call(s32[4]{0:T(128)} %copy-done.7, bf16[384,1280]{1,0:T(8,128)(2,1)} %copy-done.6, bf16[512,1280]{1,0:T(8,128)(2,1)} %a_2_.5, bf16[512,1280]{1,0:T(8,128)(2,1)} %copy-done.2, bf16[512,1280]{1,0:T(8,128)(2,1)} %a_4_.5, bf16[512,1280]{1,0:T(8,128)(2,1)} %copy-done.3, ...), custom_call_target="tpu_custom_call" | custom-call | tf_op jit(solution)/shard_map/pallas_call | solution.py:72
  77.5 0.7 fusion.6.a_0_
  78.2 9.4 %shard_map.65 = (bf16[10,128,128]{2,1,0:T(8,128)(2,1)}, f32[10,8,128]{2,1,0:T(8,128)}) custom-call(s32[4]{0:T(128)} %copy-done.7, bf16[128,1280]{1,0:T(8,128)(2,1)} %collective-permute-done.8.a_1_, bf16[512,1280]{1,0:T(8,128)(2,1)} %a_2_.5, bf16[512,1280]{1,0:T(8,128)(2,1)} %copy-done.2, bf16[512,1280]{1,0:T(8,128)(2,1)} %a_4_.5, ...), custom_call_target="tpu_custom_call" | custom-call | tf_op jit(solution)/shard_map/pallas_call | solution.py:72
  87.6 1.6 collective-permute-start.9
  89.2 2.2 %pad_maximum_fusion.a_1_ = bf16[512,1280]{1,0:T(8,128)(2,1)} fusion(bf16[128,1280]{1,0:T(8,128)(2,1)} %collective-permute-done.2, bf16[128,1280]{1,0:T(8,128)(2,1)} %collective-permute-done.1, bf16[128,1280]{1,0:T(8,128)(2,1)S(1)} %collective-permute-done, bf16[128,1280]{1,0:T(8,128)(2,1)S(1)} %get-tuple-element.25), kind=kLoop, calls=%fused_computation.1 | loop fusion | flops 5242880 | bytes 2621440 | tf_op jit(solution)/shard_map/concatenate | solution.py:107
  91.9 22.2 %shard_map.64 = (f32[10,512,128]{2,1,0:T(8,128)}, f32[10,8,512]{2,1,0:T(8,128)}) custom-call(s32[4]{0:T(128)} %fusion.6.a_0_, bf16[512,1280]{1,0:T(8,128)(2,1)} %pad_maximum_fusion.a_1_, bf16[512,1280]{1,0:T(8,128)(2,1)} %a_2_.5, bf16[512,1280]{1,0:T(8,128)(2,1)} %copy-done.2, bf16[512,1280]{1,0:T(8,128)(2,1)} %a_4_.5, bf16[512,1280]{1,0:T(8,128)(2,1)} %copy-done.3, ...), custom_call_target="tpu_custom_call" | custom-call | tf_op jit(solution)/shard_map/pallas_call | solution.py:72
  114.2 1.0 copy.19
  115.2 1.6 collective-permute-start.10
  116.9 3.5 %fusion = bf16[384,10,128]{2,0,1:T(8,128)(2,1)S(1)} fusion(f32[10,384]{1,0:T(8,128)S(1)} %get-tuple-element.19, f32[10,384]{1,0:T(8,128)S(1)} %get-tuple-element.20, bf16[10,384,128]{2,1,0:T(8,128)(2,1)S(1)} %collective-permute-done.13, f32[10,384]{1,0:T(8,128)S(1)} %get-tuple-element.21, f32[10,512,128]{2,1,0:T(8,128)} %get-tuple-element.11), kind=kLoop, calls=%fused_computation.3 | loop fusion | flops 2949120 | bytes 3978240 | tf_op jit(solution)/shard_map/transpose | solution.py:182
  120.7 8.6 %collective-permute-start.14 = (bf16[128,1280]{0,1:T(8,128)(2,1)S(1)}, bf16[128,1280]{0,1:T(8,128)(2,1)S(1)}, u32[]{:S(2)}, u32[]{:S(2)}) collective-permute-start(bf16[128,1280]{0,1:T(8,128)(2,1)S(1)} %bitcast.48), channel_id=1, source_target_pairs={{0,3},{1,0},{2,1},{3,2},{4,7},{5,4},{6,5},{7,6},{8,11},{9,8},{10,9... | collective-permute-start | bytes 983048 | tf_op jit(solution)/shard_map/ppermute | solution.py:192
  129.3 1.7 %fusion.1 = bf16[128,10,128]{2,0,1:T(8,128)(2,1)S(1)} fusion(f32[10,128]{1,0:T(8,128)S(1)} %get-tuple-element.22, f32[10,128]{1,0:T(8,128)S(1)} %get-tuple-element.23, bf16[10,128,128]{2,1,0:T(8,128)(2,1)S(1)} %collective-permute-done.10, f32[10,128]{1,0:T(8,128)S(1)} %get-tuple-element.24, f32[10,512,128]{2,1,0:T(8,128)} %get-tuple-element.11), kind=kLoop, calls=%fused_computation.5 | loop fusion | flops 983040 | bytes 1326080 | tf_op jit(solution)/shard_map/transpose | solution.py:182
  131.6 0.8 collective-permute-start.15
  132.6 0.9 copy.27
  133.5 2.1 %collective-permute-start.16 = (bf16[128,1280]{0,1:T(8,128)(2,1)}, bf16[128,1280]{0,1:T(8,128)(2,1)S(1)}, u32[]{:S(2)}, u32[]{:S(2)}) collective-permute-start(bf16[128,1280]{0,1:T(8,128)(2,1)} %bitcast.20), channel_id=1, source_target_pairs={{0,1},{1,2},{2,3},{3,0},{4,5},{5,6},{6,7},{7,4},{8,9},{9,10},{10,1... | collective-permute-start | bytes 983048 | tf_op jit(solution)/shard_map/ppermute | solution.py:192
  135.5 1.9 %collective-permute-done.14 = bf16[128,1280]{0,1:T(8,128)(2,1)S(1)} collective-permute-done((bf16[128,1280]{0,1:T(8,128)(2,1)S(1)}, bf16[128,1280]{0,1:T(8,128)(2,1)S(1)}, u32[]{:S(2)}, u32[]{:S(2)}) %collective-permute-start.14) | collective-permute-done | bytes 327712 | tf_op jit(solution)/shard_map/ppermute | solution.py:192
  137.7 19.0 %collective-permute-done.15 = bf16[128,1280]{0,1:T(8,128)(2,1)S(1)} collective-permute-done((bf16[128,1280]{0,1:T(8,128)(2,1)S(1)}, bf16[128,1280]{0,1:T(8,128)(2,1)S(1)}, u32[]{:S(2)}, u32[]{:S(2)}) %collective-permute-start.15) | collective-permute-done | bytes 327712 | tf_op jit(solution)/shard_map/ppermute | solution.py:192
  157.1 0.9 copy-done.5
  158.0 0.7 constant_dynamic-update-slice_fusion
  (55 shorter events, 3.7 us)
Async XLA Ops:
  0.0 9.5 %copy-start.8 = (s32[1,6]{1,0:T(1,128)S(1)}, s32[1,6]{1,0:T(1,128)}, u32[]{:S(2)}) copy-start(s32[1,6]{1,0:T(1,128)} %param.11) | copy-start | bytes 76
  0.0 11.3 %copy-start = (bf16[512,1280]{1,0:T(8,128)(2,1)S(1)}, bf16[512,1280]{1,0:T(8,128)(2,1)}, u32[]{:S(2)}) copy-start(bf16[512,1280]{1,0:T(8,128)(2,1)} %a_2_.5) | copy-start | bytes 3932164
  0.0 16.3 %copy-start.1 = (bf16[512,1280]{1,0:T(8,128)(2,1)S(1)}, bf16[512,1280]{1,0:T(8,128)(2,1)}, u32[]{:S(2)}) copy-start(bf16[512,1280]{1,0:T(8,128)(2,1)} %a_4_.5) | copy-start | bytes 3932164
  2.4 14.0 %collective-permute-start = (bf16[128,1280]{1,0:T(8,128)(2,1)}, bf16[128,1280]{1,0:T(8,128)(2,1)S(1)}, u32[]{:S(2)}, u32[]{:S(2)}) collective-permute-start(bf16[128,1280]{1,0:T(8,128)(2,1)} %get-tuple-element.26), channel_id=1, source_target_pairs={{0,1},{1,2},{2,3},{3,0},{4,5},{5,6},{6,7},{7,4},{8,9},{9,10},{10,1... | collective-permute-start | bytes 983048 | tf_op jit(solution)/shard_map/ppermute | solution.py:105
  5.4 24.2 %collective-permute-start.1 = (bf16[128,1280]{1,0:T(8,128)(2,1)}, bf16[128,1280]{1,0:T(8,128)(2,1)}, u32[]{:S(2)}, u32[]{:S(2)}) collective-permute-start(bf16[128,1280]{1,0:T(8,128)(2,1)} %get-tuple-element.28), channel_id=1, source_target_pairs={{0,2},{1,3},{2,0},{3,1},{4,6},{5,7},{6,4},{7,5},{8,10},{9,11},{10,... | collective-permute-start | bytes 983048 | tf_op jit(solution)/shard_map/ppermute | solution.py:105
  8.0 21.6 %collective-permute-start.2 = (bf16[128,1280]{1,0:T(8,128)(2,1)}, bf16[128,1280]{1,0:T(8,128)(2,1)}, u32[]{:S(2)}, u32[]{:S(2)}) collective-permute-start(bf16[128,1280]{1,0:T(8,128)(2,1)} %get-tuple-element.27), channel_id=1, source_target_pairs={{0,3},{1,0},{2,1},{3,2},{4,7},{5,4},{6,5},{7,6},{8,11},{9,8},{10,9... | collective-permute-start | bytes 983048 | tf_op jit(solution)/shard_map/ppermute | solution.py:105
  9.7 21.6 %collective-permute-start.7 = (s32[4]{0:T(128)S(1)}, s32[4]{0:T(128)S(1)}, u32[]{:S(2)}, u32[]{:S(2)}) collective-permute-start(s32[4]{0:T(128)S(1)} %fusion.7), channel_id=1, source_target_pairs={{0,8},{4,12},{8,0},{12,4},{1,9},{5,13},{9,1},{13,5},{2,10},{6,14},... | collective-permute-start | bytes 56 | tf_op jit(solution)/shard_map/ppermute | solution.py:125
  11.3 45.3 %collective-permute-start.3 = (bf16[512,1280]{1,0:T(8,128)(2,1)S(1)}, bf16[512,1280]{1,0:T(8,128)(2,1)S(1)}, u32[]{:S(2)}, u32[]{:S(2)}) collective-permute-start(bf16[512,1280]{1,0:T(8,128)(2,1)S(1)} %copy-done), channel_id=1, source_target_pairs={{0,4},{4,0},{8,12},{12,8},{1,5},{5,1},{9,13},{13,9},{2,6},{6,2},{1... | collective-permute-start | bytes 3932168 | tf_op jit(solution)/shard_map/ppermute | solution.py:133
  16.4 40.2 %collective-permute-start.4 = (bf16[512,1280]{1,0:T(8,128)(2,1)S(1)}, bf16[512,1280]{1,0:T(8,128)(2,1)S(1)}, u32[]{:S(2)}, u32[]{:S(2)}) collective-permute-start(bf16[512,1280]{1,0:T(8,128)(2,1)S(1)} %copy-done.1), channel_id=1, source_target_pairs={{0,4},{4,0},{8,12},{12,8},{1,5},{5,1},{9,13},{13,9},{2,6},{6,2},{1... | collective-permute-start | bytes 3932168 | tf_op jit(solution)/shard_map/ppermute | solution.py:133
  29.7 28.0 %collective-permute-start.5 = (bf16[512,1280]{1,0:T(8,128)(2,1)}, bf16[512,1280]{1,0:T(8,128)(2,1)S(1)}, u32[]{:S(2)}, u32[]{:S(2)}) collective-permute-start(bf16[512,1280]{1,0:T(8,128)(2,1)} %a_6_.5), channel_id=1, source_target_pairs={{0,4},{4,0},{8,12},{12,8},{1,5},{5,1},{9,13},{13,9},{2,6},{6,2},{1... | collective-permute-start | bytes 3932168 | tf_op jit(solution)/shard_map/ppermute | solution.py:133
  29.7 30.2 %collective-permute-start.6 = (bf16[512,1280]{1,0:T(8,128)(2,1)}, bf16[512,1280]{1,0:T(8,128)(2,1)}, u32[]{:S(2)}, u32[]{:S(2)}) collective-permute-start(bf16[512,1280]{1,0:T(8,128)(2,1)} %a_8_.5), channel_id=1, source_target_pairs={{0,4},{4,0},{8,12},{12,8},{1,5},{5,1},{9,13},{13,9},{2,6},{6,2},{1... | collective-permute-start | bytes 3932168 | tf_op jit(solution)/shard_map/ppermute | solution.py:133
  31.3 28.5 %copy-start.7 = (s32[4]{0:T(128)}, s32[4]{0:T(128)S(1)}, u32[]{:S(2)}) copy-start(s32[4]{0:T(128)S(1)} %collective-permute-done.7.a_0_) | copy-start | bytes 52
  31.3 23.7 %collective-permute-start.11 = (bf16[384,1280]{1,0:T(8,128)(2,1)S(1)}, bf16[384,1280]{1,0:T(8,128)(2,1)S(1)}, u32[]{:S(2)}, u32[]{:S(2)}) collective-permute-start(bf16[384,1280]{1,0:T(8,128)(2,1)S(1)} %pad_maximum_fusion.1), channel_id=1, source_target_pairs={{0,8},{4,12},{8,0},{12,4},{1,9},{5,13},{9,1},{13,5},{2,10},{6,14},... | collective-permute-start | bytes 2949128 | tf_op jit(solution)/shard_map/ppermute | solution.py:128
  55.1 2.6 %copy-start.6 = (bf16[384,1280]{1,0:T(8,128)(2,1)}, bf16[384,1280]{1,0:T(8,128)(2,1)S(1)}, u32[]{:S(2)}) copy-start(bf16[384,1280]{1,0:T(8,128)(2,1)S(1)} %collective-permute-done.11.a_1_) | copy-start | bytes 2949124
  55.1 23.1 %collective-permute-start.8 = (bf16[128,1280]{1,0:T(8,128)(2,1)S(1)}, bf16[128,1280]{1,0:T(8,128)(2,1)}, u32[]{:S(2)}, u32[]{:S(2)}) collective-permute-start(bf16[128,1280]{1,0:T(8,128)(2,1)S(1)} %get-tuple-element.25), channel_id=1, source_target_pairs={{0,8},{4,12},{8,0},{12,4},{1,9},{5,13},{9,1},{13,5},{2,10},{6,14},... | collective-permute-start | bytes 983048 | tf_op jit(solution)/shard_map/ppermute | solution.py:127
  56.6 1.1 copy-start.2
  57.7 1.1 copy-start.3
  58.8 1.1 copy-start.4
  76.9 39.9 %collective-permute-start.13 = (bf16[10,384,128]{2,1,0:T(8,128)(2,1)}, bf16[10,384,128]{2,1,0:T(8,128)(2,1)S(1)}, u32[]{:S(2)}, u32[]{:S(2)}) collective-permute-start(bf16[10,384,128]{2,1,0:T(8,128)(2,1)} %get-tuple-element.16), channel_id=1, source_target_pairs={{0,8},{4,12},{8,0},{12,4},{1,9},{5,13},{9,1},{13,5},{2,10},{6,14},... | collective-permute-start | bytes 2949128 | tf_op jit(solution)/shard_map/ppermute | solution.py:171
  87.6 3.8 %copy-start.10 = (f32[10,8,384]{2,1,0:T(8,128)S(1)}, f32[10,8,384]{2,1,0:T(8,128)}, u32[]{:S(2)}) copy-start(f32[10,8,384]{2,1,0:T(8,128)} %get-tuple-element.15) | copy-start | bytes 368644
  87.6 29.2 %collective-permute-start.9 = (f32[10,8,128]{2,1,0:T(8,128)}, f32[10,8,128]{2,1,0:T(8,128)S(1)}, u32[]{:S(2)}, u32[]{:S(2)}) collective-permute-start(f32[10,8,128]{2,1,0:T(8,128)} %get-tuple-element.13), channel_id=1, source_target_pairs={{0,8},{4,12},{8,0},{12,4},{1,9},{5,13},{9,1},{13,5},{2,10},{6,14},... | collective-permute-start | bytes 122888 | tf_op jit(solution)/shard_map/ppermute | solution.py:171
  91.4 23.8 %copy-start.9 = (bf16[10,128,128]{2,1,0:T(8,128)(2,1)S(1)}, bf16[10,128,128]{2,1,0:T(8,128)(2,1)}, u32[]{:S(2)}) copy-start(bf16[10,128,128]{2,1,0:T(8,128)(2,1)} %get-tuple-element.14) | copy-start | bytes 983044
  91.4 25.4 %collective-permute-start.12 = (f32[10,8,384]{2,1,0:T(8,128)S(1)}, f32[10,8,384]{2,1,0:T(8,128)S(1)}, u32[]{:S(2)}, u32[]{:S(2)}) collective-permute-start(f32[10,8,384]{2,1,0:T(8,128)S(1)} %copy-done.10), channel_id=1, source_target_pairs={{0,8},{4,12},{8,0},{12,4},{1,9},{5,13},{9,1},{13,5},{2,10},{6,14},... | collective-permute-start | bytes 368648 | tf_op jit(solution)/shard_map/ppermute | solution.py:171
  115.2 14.1 %collective-permute-start.10 = (bf16[10,128,128]{2,1,0:T(8,128)(2,1)S(1)}, bf16[10,128,128]{2,1,0:T(8,128)(2,1)S(1)}, u32[]{:S(2)}, u32[]{:S(2)}) collective-permute-start(bf16[10,128,128]{2,1,0:T(8,128)(2,1)S(1)} %copy-done.9), channel_id=1, source_target_pairs={{0,8},{4,12},{8,0},{12,4},{1,9},{5,13},{9,1},{13,5},{2,10},{6,14},... | collective-permute-start | bytes 983048 | tf_op jit(solution)/shard_map/ppermute | solution.py:171
  120.7 16.8 %collective-permute-start.14 = (bf16[128,1280]{0,1:T(8,128)(2,1)S(1)}, bf16[128,1280]{0,1:T(8,128)(2,1)S(1)}, u32[]{:S(2)}, u32[]{:S(2)}) collective-permute-start(bf16[128,1280]{0,1:T(8,128)(2,1)S(1)} %bitcast.48), channel_id=1, source_target_pairs={{0,3},{1,0},{2,1},{3,2},{4,7},{5,4},{6,5},{7,6},{8,11},{9,8},{10,9... | collective-permute-start | bytes 983048 | tf_op jit(solution)/shard_map/ppermute | solution.py:192
  131.6 25.1 %collective-permute-start.15 = (bf16[128,1280]{0,1:T(8,128)(2,1)S(1)}, bf16[128,1280]{0,1:T(8,128)(2,1)S(1)}, u32[]{:S(2)}, u32[]{:S(2)}) collective-permute-start(bf16[128,1280]{0,1:T(8,128)(2,1)S(1)} %bitcast.49), channel_id=1, source_target_pairs={{0,2},{1,3},{2,0},{3,1},{4,6},{5,7},{6,4},{7,5},{8,10},{9,11},{10,... | collective-permute-start | bytes 983048 | tf_op jit(solution)/shard_map/ppermute | solution.py:192
  133.5 23.4 %collective-permute-start.16 = (bf16[128,1280]{0,1:T(8,128)(2,1)}, bf16[128,1280]{0,1:T(8,128)(2,1)S(1)}, u32[]{:S(2)}, u32[]{:S(2)}) collective-permute-start(bf16[128,1280]{0,1:T(8,128)(2,1)} %bitcast.20), channel_id=1, source_target_pairs={{0,1},{1,2},{2,3},{3,0},{4,5},{5,6},{6,7},{7,4},{8,9},{9,10},{10,1... | collective-permute-start | bytes 983048 | tf_op jit(solution)/shard_map/ppermute | solution.py:192
  156.9 1.1 copy-start.5

commit v14 on v13

--- a/solution.py
+++ b/solution.py
@@ -123,10 +123,11 @@
     remote_flags = membership(listed, remote_ids, remote_valid)
     rows = queries.shape[0]
     got_flags = lax.ppermute(remote_flags, "seq", back)
-    got_halves = [
-        lax.ppermute(query_parts[0], "seq", back),
-        lax.ppermute(jnp.concatenate(query_parts[1:], axis=0), "seq", back),
-    ]
+    got_first = lax.ppermute(query_parts[0], "seq", back)
+    got_first, rest = lax.optimization_barrier(
+        (got_first, jnp.concatenate(query_parts[1:], axis=0))
+    )
+    got_halves = [got_first, lax.ppermute(rest, "seq", back)]
     bounds = [(0, rows), (rows, query_parts[0].shape[0] * sp_count)]
 
     swap = [(i, i ^ 1) for i in range(seq_count)]

time: 159 us -> 158 us (level)
    ppermute x1, waiting for transfers between devices: 0.01 us -> 2.02 us  [local(): got_flags = lax.ppermute(remote_flags, 'seq', back)]
    unnamed x22 -> x20, local copies, waits for them, and re-layouts: 4.1 us -> 3.3 us
  transfers between devices with their start and end apart: 17 -> 17, of which waited for: 5 -> 6; matrix products, arithmetic and copies ran while one was open for 8% -> 8% of each run, Pallas kernels for 31% -> 20%
where the time goes in v14:
time: 158 us
  waiting for transfers between devices  61.2 us (39%)
  Pallas kernels  48.5 us (31%)
  starting transfers between devices  28.2 us (18%)
  local copies, waits for them, and re-layouts  10 us (6%)
  other arithmetic  9.51 us (6%)
    pallas_call x3, Pallas kernels, attend_partial(): pl.pallas_call(lambda *a: partial_kernel(nsrc, group, *a), grid_spec=grid...  48.5 us
    ppermute x1, waiting for transfers between devices, local(): got_halves = [got_first, lax.ppermute(rest, 'seq', back)]  21 us
    ppermute x3, waiting for transfers between devices, local(): lax.ppermute(piece, 'sp', [(i, (i - d) % sp_count) for i in range(sp_coun...  19.7 us
    ppermute x3, waiting for transfers between devices, local(): lax.ppermute(piece, 'sp', [(i, (i + d) % sp_count) for i in range(sp_coun...  18.5 us
    ppermute x3, starting transfers between devices, local(): lax.ppermute(piece, 'sp', [(i, (i - d) % sp_count) for i in range(sp_coun...  11.8 us
    ppermute x3, starting transfers between devices, local(): lax.ppermute(piece, 'sp', [(i, (i + d) % sp_count) for i in range(sp_coun...  6.98 us
    transpose x2, other arithmetic, local(): jnp.transpose(mixed.astype(jnp.bfloat16), (1, 0, 2)).reshape(-1, head_width)  5.17 us
    ppermute x4, starting transfers between devices, local(): far_out, far_lse = lax.ppermute((far_out, far_lse), 'seq', forth)  4.23 us
  transfers between devices with their start and end apart: 17, of which 6 were waited for; matrix products, arithmetic and copies ran while one was open for 8% of the time, Pallas kernels for 20%

profile of v14, /device:TPU:0, one launch (start us, length us, event | category | flops | bytes accessed | tf_op | source)
XLA Modules:
  0.0 157.6 jit_solution(17519544862814794308)
XLA Ops:
  0.0 2.4 %constant_dynamic-slice_fusion.3 = (bf16[128,1280]{1,0:T(8,128)(2,1)S(1)}, bf16[128,1280]{1,0:T(8,128)(2,1)}, bf16[128,1280]{1,0:T(8,128)(2,1)}, bf16[128,1280]{1,0:T(8,128)(2,1)}) fusion(bf16[128,5120]{1,0:T(8,128)(2,1)} %param.6, s32[]{:T(128)S(6)} %select_n.55, s32[]{:T(128)S(6)} %select_n.57, s32[]{:T(128)S(6)} %select_n.61, s32[]{:T(128)S(6)} %select_n.59), kind=kLoop, calls=%fused_computation.23 | loop fusion | bytes 2621456 | tf_op jit(solution)/shard_map/dynamic_slice | solution.py:100
  2.4 3.0 %collective-permute-start = (bf16[128,1280]{1,0:T(8,128)(2,1)}, bf16[128,1280]{1,0:T(8,128)(2,1)S(1)}, u32[]{:S(2)}, u32[]{:S(2)}) collective-permute-start(bf16[128,1280]{1,0:T(8,128)(2,1)} %get-tuple-element.30), channel_id=1, source_target_pairs={{0,1},{1,2},{2,3},{3,0},{4,5},{5,6},{6,7},{7,4},{8,9},{9,10},{10,1... | collective-permute-start | bytes 983048 | tf_op jit(solution)/shard_map/ppermute | solution.py:105
  5.4 2.6 %collective-permute-start.1 = (bf16[128,1280]{1,0:T(8,128)(2,1)}, bf16[128,1280]{1,0:T(8,128)(2,1)}, u32[]{:S(2)}, u32[]{:S(2)}) collective-permute-start(bf16[128,1280]{1,0:T(8,128)(2,1)} %get-tuple-element.32), channel_id=1, source_target_pairs={{0,2},{1,3},{2,0},{3,1},{4,6},{5,7},{6,4},{7,5},{8,10},{9,11},{10,... | collective-permute-start | bytes 983048 | tf_op jit(solution)/shard_map/ppermute | solution.py:105
  8.0 1.3 collective-permute-start.2
  9.4 1.5 collective-permute-start.8
  11.2 5.2 %collective-permute-done = bf16[128,1280]{1,0:T(8,128)(2,1)S(1)} collective-permute-done((bf16[128,1280]{1,0:T(8,128)(2,1)}, bf16[128,1280]{1,0:T(8,128)(2,1)S(1)}, u32[]{:S(2)}, u32[]{:S(2)}) %collective-permute-start) | collective-permute-done | bytes 327712 | tf_op jit(solution)/shard_map/ppermute | solution.py:105
  16.3 13.3 %collective-permute-done.1 = bf16[128,1280]{1,0:T(8,128)(2,1)} collective-permute-done((bf16[128,1280]{1,0:T(8,128)(2,1)}, bf16[128,1280]{1,0:T(8,128)(2,1)}, u32[]{:S(2)}, u32[]{:S(2)}) %collective-permute-start.1) | collective-permute-done | bytes 327712 | tf_op jit(solution)/shard_map/ppermute | solution.py:105
  30.2 1.1 pad_maximum_fusion.1
  31.4 1.6 %collective-permute-start.7 = (s32[4]{0:T(128)S(1)}, s32[4]{0:T(128)S(1)}, u32[]{:S(2)}, u32[]{:S(2)}) collective-permute-start(s32[4]{0:T(128)S(1)} %fusion.7), channel_id=1, source_target_pairs={{0,8},{4,12},{8,0},{12,4},{1,9},{5,13},{9,1},{13,5},{2,10},{6,14},... | collective-permute-start | bytes 56 | tf_op jit(solution)/shard_map/ppermute | solution.py:125
  33.0 2.0 %collective-permute-done.7.a_0_ = s32[4]{0:T(128)S(1)} collective-permute-done((s32[4]{0:T(128)S(1)}, s32[4]{0:T(128)S(1)}, u32[]{:S(2)}, u32[]{:S(2)}) %collective-permute-start.7) | collective-permute-done | bytes 48 | tf_op jit(solution)/shard_map/ppermute | solution.py:125
  35.0 1.5 collective-permute-start.11
  36.5 21.0 %collective-permute-done.11.a_1_ = bf16[384,1280]{1,0:T(8,128)(2,1)S(1)} collective-permute-done((bf16[384,1280]{1,0:T(8,128)(2,1)S(1)}, bf16[384,1280]{1,0:T(8,128)(2,1)S(1)}, u32[]{:S(2)}, u32[]{:S(2)}) %collective-permute-start.11) | collective-permute-done | bytes 983072 | tf_op jit(solution)/shard_map/ppermute | solution.py:130
  57.5 1.1 copy-done.2
  58.9 1.1 copy-done.3
  60.0 17.0 %shard_map.66 = (bf16[10,384,128]{2,1,0:T(8,128)(2,1)}, f32[10,8,384]{2,1,0:T(8,128)}) custom-call(s32[4]{0:T(128)} %copy-done.6, bf16[384,1280]{1,0:T(8,128)(2,1)} %copy-done.5, bf16[512,1280]{1,0:T(8,128)(2,1)} %a_2_.5, bf16[512,1280]{1,0:T(8,128)(2,1)} %collective-permute-done.3.a_3_, bf16[512,1280]{1,0:T(8,128)(2,1)} %a_4_.5, ...), custom_call_target="tpu_custom_call" | custom-call | tf_op jit(solution)/shard_map/pallas_call | solution.py:72
  76.9 1.6 %collective-permute-start.13 = (bf16[10,384,128]{2,1,0:T(8,128)(2,1)}, bf16[10,384,128]{2,1,0:T(8,128)(2,1)S(1)}, u32[]{:S(2)}, u32[]{:S(2)}) collective-permute-start(bf16[10,384,128]{2,1,0:T(8,128)(2,1)} %get-tuple-element.20), channel_id=1, source_target_pairs={{0,8},{4,12},{8,0},{12,4},{1,9},{5,13},{9,1},{13,5},{2,10},{6,14},... | collective-permute-start | bytes 2949128 | tf_op jit(solution)/shard_map/ppermute | solution.py:172
  78.5 0.6 fusion.6.a_0_
  79.1 9.3 %shard_map.65 = (bf16[10,128,128]{2,1,0:T(8,128)(2,1)}, f32[10,8,128]{2,1,0:T(8,128)}) custom-call(s32[4]{0:T(128)} %copy-done.6, bf16[128,1280]{1,0:T(8,128)(2,1)} %collective-permute-done.8.a_1_, bf16[512,1280]{1,0:T(8,128)(2,1)} %a_2_.5, bf16[512,1280]{1,0:T(8,128)(2,1)} %collective-permute-done.3.a_3_, bf16[512,1280]{1,0:T(8,128)(2,1)} %a_4_.5, ...), custom_call_target="tpu_custom_call" | custom-call | tf_op jit(solution)/shard_map/pallas_call | solution.py:72
  89.0 2.2 %pad_maximum_fusion.a_1_ = bf16[512,1280]{1,0:T(8,128)(2,1)} fusion(bf16[128,1280]{1,0:T(8,128)(2,1)} %collective-permute-done.2, bf16[128,1280]{1,0:T(8,128)(2,1)} %collective-permute-done.1, bf16[128,1280]{1,0:T(8,128)(2,1)S(1)} %collective-permute-done, bf16[128,1280]{1,0:T(8,128)(2,1)S(1)} %get-tuple-element.29), kind=kLoop, calls=%fused_computation.1 | loop fusion | flops 5242880 | bytes 2621440 | tf_op jit(solution)/shard_map/concatenate | solution.py:107
  91.2 1.5 collective-permute-start.12
  92.7 22.2 %shard_map.64 = (f32[10,512,128]{2,1,0:T(8,128)}, f32[10,8,512]{2,1,0:T(8,128)}) custom-call(s32[4]{0:T(128)} %fusion.6.a_0_, bf16[512,1280]{1,0:T(8,128)(2,1)} %pad_maximum_fusion.a_1_, bf16[512,1280]{1,0:T(8,128)(2,1)} %a_2_.5, bf16[512,1280]{1,0:T(8,128)(2,1)} %collective-permute-done.3.a_3_, bf16[512,1280]{1,0:T(8,128)(2,1)} %a_4_.5, ...), custom_call_target="tpu_custom_call" | custom-call | tf_op jit(solution)/shard_map/pallas_call | solution.py:72
  114.9 1.0 copy.19
  116.6 3.5 %fusion = bf16[384,10,128]{2,0,1:T(8,128)(2,1)S(1)} fusion(f32[10,384]{1,0:T(8,128)S(1)} %get-tuple-element.23, f32[10,384]{1,0:T(8,128)S(1)} %get-tuple-element.24, bf16[10,384,128]{2,1,0:T(8,128)(2,1)S(1)} %collective-permute-done.13, f32[10,384]{1,0:T(8,128)S(1)} %get-tuple-element.25, f32[10,512,128]{2,1,0:T(8,128)} %get-tuple-element.13), kind=kLoop, calls=%fused_computation.3 | loop fusion | flops 2949120 | bytes 3978240 | tf_op jit(solution)/shard_map/transpose | solution.py:183
  120.4 8.6 %collective-permute-start.14 = (bf16[128,1280]{0,1:T(8,128)(2,1)S(1)}, bf16[128,1280]{0,1:T(8,128)(2,1)S(1)}, u32[]{:S(2)}, u32[]{:S(2)}) collective-permute-start(bf16[128,1280]{0,1:T(8,128)(2,1)S(1)} %bitcast.48), channel_id=1, source_target_pairs={{0,3},{1,0},{2,1},{3,2},{4,7},{5,4},{6,5},{7,6},{8,11},{9,8},{10,9... | collective-permute-start | bytes 983048 | tf_op jit(solution)/shard_map/ppermute | solution.py:193
  129.0 1.7 %fusion.1 = bf16[128,10,128]{2,0,1:T(8,128)(2,1)S(1)} fusion(f32[10,128]{1,0:T(8,128)S(1)} %get-tuple-element.26, f32[10,128]{1,0:T(8,128)S(1)} %get-tuple-element.27, bf16[10,128,128]{2,1,0:T(8,128)(2,1)S(1)} %collective-permute-done.10, f32[10,128]{1,0:T(8,128)S(1)} %get-tuple-element.28, f32[10,512,128]{2,1,0:T(8,128)} %get-tuple-element.13), kind=kLoop, calls=%fused_computation.5 | loop fusion | flops 983040 | bytes 1326080 | tf_op jit(solution)/shard_map/transpose | solution.py:183
  131.3 0.7 collective-permute-start.15
  132.2 0.9 copy.27
  133.1 2.5 %collective-permute-start.16 = (bf16[128,1280]{0,1:T(8,128)(2,1)}, bf16[128,1280]{0,1:T(8,128)(2,1)S(1)}, u32[]{:S(2)}, u32[]{:S(2)}) collective-permute-start(bf16[128,1280]{0,1:T(8,128)(2,1)} %bitcast.20), channel_id=1, source_target_pairs={{0,1},{1,2},{2,3},{3,0},{4,5},{5,6},{6,7},{7,4},{8,9},{9,10},{10,1... | collective-permute-start | bytes 983048 | tf_op jit(solution)/shard_map/ppermute | solution.py:193
  135.6 1.6 %collective-permute-done.14 = bf16[128,1280]{0,1:T(8,128)(2,1)S(1)} collective-permute-done((bf16[128,1280]{0,1:T(8,128)(2,1)S(1)}, bf16[128,1280]{0,1:T(8,128)(2,1)S(1)}, u32[]{:S(2)}, u32[]{:S(2)}) %collective-permute-start.14) | collective-permute-done | bytes 327712 | tf_op jit(solution)/shard_map/ppermute | solution.py:193
  137.4 18.1 %collective-permute-done.15 = bf16[128,1280]{0,1:T(8,128)(2,1)S(1)} collective-permute-done((bf16[128,1280]{0,1:T(8,128)(2,1)S(1)}, bf16[128,1280]{0,1:T(8,128)(2,1)S(1)}, u32[]{:S(2)}, u32[]{:S(2)}) %collective-permute-start.15) | collective-permute-done | bytes 327712 | tf_op jit(solution)/shard_map/ppermute | solution.py:193
  156.0 0.9 copy-done.4
  156.8 0.7 constant_dynamic-update-slice_fusion
  (53 shorter events, 4.0 us)
Async XLA Ops:
  0.0 10.9 %copy-start = (bf16[512,1280]{1,0:T(8,128)(2,1)S(1)}, bf16[512,1280]{1,0:T(8,128)(2,1)}, u32[]{:S(2)}) copy-start(bf16[512,1280]{1,0:T(8,128)(2,1)} %a_2_.5) | copy-start | bytes 3932164
  0.0 11.0 %copy-start.7 = (s32[1,6]{1,0:T(1,128)S(1)}, s32[1,6]{1,0:T(1,128)}, u32[]{:S(2)}) copy-start(s32[1,6]{1,0:T(1,128)} %param.11) | copy-start | bytes 76
  0.0 16.3 %copy-start.1 = (bf16[512,1280]{1,0:T(8,128)(2,1)S(1)}, bf16[512,1280]{1,0:T(8,128)(2,1)}, u32[]{:S(2)}) copy-start(bf16[512,1280]{1,0:T(8,128)(2,1)} %a_4_.5) | copy-start | bytes 3932164
  2.4 14.0 %collective-permute-start = (bf16[128,1280]{1,0:T(8,128)(2,1)}, bf16[128,1280]{1,0:T(8,128)(2,1)S(1)}, u32[]{:S(2)}, u32[]{:S(2)}) collective-permute-start(bf16[128,1280]{1,0:T(8,128)(2,1)} %get-tuple-element.30), channel_id=1, source_target_pairs={{0,1},{1,2},{2,3},{3,0},{4,5},{5,6},{6,7},{7,4},{8,9},{9,10},{10,1... | collective-permute-start | bytes 983048 | tf_op jit(solution)/shard_map/ppermute | solution.py:105
  5.4 24.2 %collective-permute-start.1 = (bf16[128,1280]{1,0:T(8,128)(2,1)}, bf16[128,1280]{1,0:T(8,128)(2,1)}, u32[]{:S(2)}, u32[]{:S(2)}) collective-permute-start(bf16[128,1280]{1,0:T(8,128)(2,1)} %get-tuple-element.32), channel_id=1, source_target_pairs={{0,2},{1,3},{2,0},{3,1},{4,6},{5,7},{6,4},{7,5},{8,10},{9,11},{10,... | collective-permute-start | bytes 983048 | tf_op jit(solution)/shard_map/ppermute | solution.py:105
  8.0 21.6 %collective-permute-start.2 = (bf16[128,1280]{1,0:T(8,128)(2,1)}, bf16[128,1280]{1,0:T(8,128)(2,1)}, u32[]{:S(2)}, u32[]{:S(2)}) collective-permute-start(bf16[128,1280]{1,0:T(8,128)(2,1)} %get-tuple-element.31), channel_id=1, source_target_pairs={{0,3},{1,0},{2,1},{3,2},{4,7},{5,4},{6,5},{7,6},{8,11},{9,8},{10,9... | collective-permute-start | bytes 983048 | tf_op jit(solution)/shard_map/ppermute | solution.py:105
  9.4 22.0 %collective-permute-start.8 = (bf16[128,1280]{1,0:T(8,128)(2,1)S(1)}, bf16[128,1280]{1,0:T(8,128)(2,1)}, u32[]{:S(2)}, u32[]{:S(2)}) collective-permute-start(bf16[128,1280]{1,0:T(8,128)(2,1)S(1)} %get-tuple-element.29), channel_id=1, source_target_pairs={{0,8},{4,12},{8,0},{12,4},{1,9},{5,13},{9,1},{13,5},{2,10},{6,14},... | collective-permute-start | bytes 983048 | tf_op jit(solution)/shard_map/ppermute | solution.py:126
  10.9 46.6 %collective-permute-start.3 = (bf16[512,1280]{1,0:T(8,128)(2,1)S(1)}, bf16[512,1280]{1,0:T(8,128)(2,1)}, u32[]{:S(2)}, u32[]{:S(2)}) collective-permute-start(bf16[512,1280]{1,0:T(8,128)(2,1)S(1)} %copy-done), channel_id=1, source_target_pairs={{0,4},{4,0},{8,12},{12,8},{1,5},{5,1},{9,13},{13,9},{2,6},{6,2},{1... | collective-permute-start | bytes 3932168 | tf_op jit(solution)/shard_map/ppermute | solution.py:134
  16.3 41.2 %collective-permute-start.4 = (bf16[512,1280]{1,0:T(8,128)(2,1)S(1)}, bf16[512,1280]{1,0:T(8,128)(2,1)S(1)}, u32[]{:S(2)}, u32[]{:S(2)}) collective-permute-start(bf16[512,1280]{1,0:T(8,128)(2,1)S(1)} %copy-done.1), channel_id=1, source_target_pairs={{0,4},{4,0},{8,12},{12,8},{1,5},{5,1},{9,13},{13,9},{2,6},{6,2},{1... | collective-permute-start | bytes 3932168 | tf_op jit(solution)/shard_map/ppermute | solution.py:134
  29.7 29.0 %collective-permute-start.5 = (bf16[512,1280]{1,0:T(8,128)(2,1)}, bf16[512,1280]{1,0:T(8,128)(2,1)S(1)}, u32[]{:S(2)}, u32[]{:S(2)}) collective-permute-start(bf16[512,1280]{1,0:T(8,128)(2,1)} %a_6_.5), channel_id=1, source_target_pairs={{0,4},{4,0},{8,12},{12,8},{1,5},{5,1},{9,13},{13,9},{2,6},{6,2},{1... | collective-permute-start | bytes 3932168 | tf_op jit(solution)/shard_map/ppermute | solution.py:134
  29.7 30.3 %collective-permute-start.6 = (bf16[512,1280]{1,0:T(8,128)(2,1)}, bf16[512,1280]{1,0:T(8,128)(2,1)}, u32[]{:S(2)}, u32[]{:S(2)}) collective-permute-start(bf16[512,1280]{1,0:T(8,128)(2,1)} %a_8_.5), channel_id=1, source_target_pairs={{0,4},{4,0},{8,12},{12,8},{1,5},{5,1},{9,13},{13,9},{2,6},{6,2},{1... | collective-permute-start | bytes 3932168 | tf_op jit(solution)/shard_map/ppermute | solution.py:134
  31.4 3.6 %collective-permute-start.7 = (s32[4]{0:T(128)S(1)}, s32[4]{0:T(128)S(1)}, u32[]{:S(2)}, u32[]{:S(2)}) collective-permute-start(s32[4]{0:T(128)S(1)} %fusion.7), channel_id=1, source_target_pairs={{0,8},{4,12},{8,0},{12,4},{1,9},{5,13},{9,1},{13,5},{2,10},{6,14},... | collective-permute-start | bytes 56 | tf_op jit(solution)/shard_map/ppermute | solution.py:125
  35.0 25.0 %copy-start.6 = (s32[4]{0:T(128)}, s32[4]{0:T(128)S(1)}, u32[]{:S(2)}) copy-start(s32[4]{0:T(128)S(1)} %collective-permute-done.7.a_0_) | copy-start | bytes 52
  35.0 22.5 %collective-permute-start.11 = (bf16[384,1280]{1,0:T(8,128)(2,1)S(1)}, bf16[384,1280]{1,0:T(8,128)(2,1)S(1)}, u32[]{:S(2)}, u32[]{:S(2)}) collective-permute-start(bf16[384,1280]{1,0:T(8,128)(2,1)S(1)} %pad_maximum_fusion.1), channel_id=1, source_target_pairs={{0,8},{4,12},{8,0},{12,4},{1,9},{5,13},{9,1},{13,5},{2,10},{6,14},... | collective-permute-start | bytes 2949128 | tf_op jit(solution)/shard_map/ppermute | solution.py:130
  57.5 1.4 copy-start.5
  57.5 1.1 copy-start.2
  58.9 1.1 copy-start.3
  76.9 39.7 %collective-permute-start.13 = (bf16[10,384,128]{2,1,0:T(8,128)(2,1)}, bf16[10,384,128]{2,1,0:T(8,128)(2,1)S(1)}, u32[]{:S(2)}, u32[]{:S(2)}) collective-permute-start(bf16[10,384,128]{2,1,0:T(8,128)(2,1)} %get-tuple-element.20), channel_id=1, source_target_pairs={{0,8},{4,12},{8,0},{12,4},{1,9},{5,13},{9,1},{13,5},{2,10},{6,14},... | collective-permute-start | bytes 2949128 | tf_op jit(solution)/shard_map/ppermute | solution.py:172
  88.4 2.8 %copy-start.9 = (f32[10,8,384]{2,1,0:T(8,128)S(1)}, f32[10,8,384]{2,1,0:T(8,128)}, u32[]{:S(2)}) copy-start(f32[10,8,384]{2,1,0:T(8,128)} %get-tuple-element.19) | copy-start | bytes 368644
  88.4 28.1 %collective-permute-start.9 = (f32[10,8,128]{2,1,0:T(8,128)}, f32[10,8,128]{2,1,0:T(8,128)S(1)}, u32[]{:S(2)}, u32[]{:S(2)}) collective-permute-start(f32[10,8,128]{2,1,0:T(8,128)} %get-tuple-element.16), channel_id=1, source_target_pairs={{0,8},{4,12},{8,0},{12,4},{1,9},{5,13},{9,1},{13,5},{2,10},{6,14},... | collective-permute-start | bytes 122888 | tf_op jit(solution)/shard_map/ppermute | solution.py:172
  91.2 24.8 %copy-start.8 = (bf16[10,128,128]{2,1,0:T(8,128)(2,1)S(1)}, bf16[10,128,128]{2,1,0:T(8,128)(2,1)}, u32[]{:S(2)}) copy-start(bf16[10,128,128]{2,1,0:T(8,128)(2,1)} %get-tuple-element.17) | copy-start | bytes 983044
  91.2 25.4 %collective-permute-start.12 = (f32[10,8,384]{2,1,0:T(8,128)S(1)}, f32[10,8,384]{2,1,0:T(8,128)S(1)}, u32[]{:S(2)}, u32[]{:S(2)}) collective-permute-start(f32[10,8,384]{2,1,0:T(8,128)S(1)} %copy-done.9), channel_id=1, source_target_pairs={{0,8},{4,12},{8,0},{12,4},{1,9},{5,13},{9,1},{13,5},{2,10},{6,14},... | collective-permute-start | bytes 368648 | tf_op jit(solution)/shard_map/ppermute | solution.py:172
  116.0 13.0 %collective-permute-start.10 = (bf16[10,128,128]{2,1,0:T(8,128)(2,1)S(1)}, bf16[10,128,128]{2,1,0:T(8,128)(2,1)S(1)}, u32[]{:S(2)}, u32[]{:S(2)}) collective-permute-start(bf16[10,128,128]{2,1,0:T(8,128)(2,1)S(1)} %copy-done.8), channel_id=1, source_target_pairs={{0,8},{4,12},{8,0},{12,4},{1,9},{5,13},{9,1},{13,5},{2,10},{6,14},... | collective-permute-start | bytes 983048 | tf_op jit(solution)/shard_map/ppermute | solution.py:172
  120.4 16.8 %collective-permute-start.14 = (bf16[128,1280]{0,1:T(8,128)(2,1)S(1)}, bf16[128,1280]{0,1:T(8,128)(2,1)S(1)}, u32[]{:S(2)}, u32[]{:S(2)}) collective-permute-start(bf16[128,1280]{0,1:T(8,128)(2,1)S(1)} %bitcast.48), channel_id=1, source_target_pairs={{0,3},{1,0},{2,1},{3,2},{4,7},{5,4},{6,5},{7,6},{8,11},{9,8},{10,9... | collective-permute-start | bytes 983048 | tf_op jit(solution)/shard_map/ppermute | solution.py:193
  131.3 24.3 %collective-permute-start.15 = (bf16[128,1280]{0,1:T(8,128)(2,1)S(1)}, bf16[128,1280]{0,1:T(8,128)(2,1)S(1)}, u32[]{:S(2)}, u32[]{:S(2)}) collective-permute-start(bf16[128,1280]{0,1:T(8,128)(2,1)S(1)} %bitcast.49), channel_id=1, source_target_pairs={{0,2},{1,3},{2,0},{3,1},{4,6},{5,7},{6,4},{7,5},{8,10},{9,11},{10,... | collective-permute-start | bytes 983048 | tf_op jit(solution)/shard_map/ppermute | solution.py:193
  133.1 22.7 %collective-permute-start.16 = (bf16[128,1280]{0,1:T(8,128)(2,1)}, bf16[128,1280]{0,1:T(8,128)(2,1)S(1)}, u32[]{:S(2)}, u32[]{:S(2)}) collective-permute-start(bf16[128,1280]{0,1:T(8,128)(2,1)} %bitcast.20), channel_id=1, source_target_pairs={{0,1},{1,2},{2,3},{3,0},{4,5},{5,6},{6,7},{7,4},{8,9},{9,10},{10,1... | collective-permute-start | bytes 983048 | tf_op jit(solution)/shard_map/ppermute | solution.py:193
  155.8 1.1 copy-start.4

commit v15 on v11

--- a/solution.py
+++ b/solution.py
@@ -121,11 +121,8 @@
         remote_valid += [(t_chip >= 1) & (t_chip <= chips - 2)] * 2
     remote_flags = membership(listed, remote_ids, remote_valid)
     half = query_block.shape[0] // 2
-    got_flags = lax.ppermute(remote_flags, "seq", back)
-    got_halves = [
-        lax.ppermute(query_block[:half], "seq", back),
-        lax.ppermute(query_block[half:], "seq", back),
-    ]
+    got_first, got_flags = lax.ppermute((query_block[:half], remote_flags), "seq", back)
+    got_halves = [got_first, lax.ppermute(query_block[half:], "seq", back)]
 
     swap = [(i, i ^ 1) for i in range(seq_count)]
     partner_k, partner_v, partner_ck, partner_cv = lax.ppermute(
@@ -160,6 +157,8 @@
         [s >= 0, s >= 0, chip == 0, chip == 0],
     )
     local_out, local_lse = attend_partial(local_flags, query_block, keys, values, jnp.float32)
+    got_first, local_out, local_lse = lax.optimization_barrier((got_halves[0], local_out, local_lse))
+    got_halves = [got_first, got_halves[1]]
 
     mixed_halves = []
     for k, got_query in enumerate(got_halves):

time: 154 us -> 155 us (level)
  waiting for transfers between devices: 58.3 us -> 61.1 us
  starting transfers between devices: 25.6 us -> 24 us
    ppermute x4, waiting for transfers between devices: 0.01 us -> 17.2 us  [local(): far_out, far_lse = lax.ppermute((far_out, far_lse), 'seq', forth)]
    ppermute x3, waiting for transfers between devices: 16.4 us -> 0.02 us  [the longest x2 0.01 us: local(): lax.ppermute((query_block[:half], remote_flags), 'seq', back)]
    ppermute x3, waiting for transfers between devices: 16.4 us -> 20.8 us  [local(): lax.ppermute(piece, 'sp', [(i, (i + d) % sp_count) for i in range(sp_coun...]
    ppermute x3, waiting for transfers between devices: 25.6 us -> 23.1 us  [local(): lax.ppermute(piece, 'sp', [(i, (i - d) % sp_count) for i in range(sp_coun...]
    convert_element_type x1, other arithmetic: 4.58 us -> 2.44 us  [local(): mixed_halves.append(mixed.astype(jnp.bfloat16))]
    unnamed x12 -> x18, local copies, waits for them, and re-layouts: 0.87 us -> 2.5 us
  transfers between devices with their start and end apart: 17 -> 17, of which waited for: 5 -> 6; matrix products, arithmetic and copies ran while one was open for 6% -> 7% of each run, Pallas kernels for 34% -> 34%
where the time goes in v15:
time: 155 us; the launch traced here: 154 us
  waiting for transfers between devices  61.1 us (39%)
  Pallas kernels  51.7 us (33%)
  starting transfers between devices  24 us (15%)
  local copies, waits for them, and re-layouts  8.66 us (6%)
  other arithmetic  8.63 us (6%)
    pallas_call x3, Pallas kernels, attend_partial(): pl.pallas_call(lambda *a: partial_kernel(nsrc, group, *a), grid_spec=grid...  51.7 us
    ppermute x3, waiting for transfers between devices, local(): lax.ppermute(piece, 'sp', [(i, (i - d) % sp_count) for i in range(sp_coun...  23.1 us
    ppermute x3, waiting for transfers between devices, local(): lax.ppermute(piece, 'sp', [(i, (i + d) % sp_count) for i in range(sp_coun...  20.8 us
    ppermute x4, waiting for transfers between devices, local(): far_out, far_lse = lax.ppermute((far_out, far_lse), 'seq', forth)  17.2 us
    ppermute x3, starting transfers between devices, local(): lax.ppermute(piece, 'sp', [(i, (i - d) % sp_count) for i in range(sp_coun...  9.3 us
    ppermute x3, starting transfers between devices, local(): lax.ppermute(piece, 'sp', [(i, (i + d) % sp_count) for i in range(sp_coun...  6.54 us
    concatenate x3, other arithmetic, local(): query_block = jnp.concatenate(query_parts, axis=0)  5.1 us
    ppermute x4, starting transfers between devices, local(): far_out, far_lse = lax.ppermute((far_out, far_lse), 'seq', forth)  4.17 us
  transfers between devices with their start and end apart: 17, of which 6 were waited for; matrix products, arithmetic and copies ran while one was open for 7% of the time, Pallas kernels for 34%

profile of v15, /device:TPU:0, one launch (start us, length us, event | category | flops | bytes accessed | tf_op | source)
XLA Modules:
  0.0 154.3 jit_solution(4529470497334215859)
XLA Ops:
  0.5 2.4 %constant_dynamic-slice_fusion.3 = (bf16[128,1280]{1,0:T(8,128)(2,1)S(1)}, bf16[128,1280]{1,0:T(8,128)(2,1)}, bf16[128,1280]{1,0:T(8,128)(2,1)}, bf16[128,1280]{1,0:T(8,128)(2,1)}) fusion(bf16[128,5120]{1,0:T(8,128)(2,1)} %param.6, s32[]{:T(128)S(6)} %select_n.54, s32[]{:T(128)S(6)} %select_n.56, s32[]{:T(128)S(6)} %select_n.61, s32[]{:T(128)S(6)} %select_n.59), kind=kLoop, calls=%fused_computation.23 | loop fusion | bytes 2621456 | tf_op jit(solution)/shard_map/dynamic_slice | solution.py:99
  2.9 2.6 %collective-permute-start = (bf16[128,1280]{1,0:T(8,128)(2,1)}, bf16[128,1280]{1,0:T(8,128)(2,1)S(1)}, u32[]{:S(2)}, u32[]{:S(2)}) collective-permute-start(bf16[128,1280]{1,0:T(8,128)(2,1)} %get-tuple-element.38), channel_id=1, source_target_pairs={{0,1},{1,2},{2,3},{3,0},{4,5},{5,6},{6,7},{7,4},{8,9},{9,10},{10,1... | collective-permute-start | bytes 983048 | tf_op jit(solution)/shard_map/ppermute | solution.py:104
  5.5 2.6 %collective-permute-start.2 = (bf16[128,1280]{1,0:T(8,128)(2,1)}, bf16[128,1280]{1,0:T(8,128)(2,1)}, u32[]{:S(2)}, u32[]{:S(2)}) collective-permute-start(bf16[128,1280]{1,0:T(8,128)(2,1)} %get-tuple-element.40), channel_id=1, source_target_pairs={{0,2},{1,3},{2,0},{3,1},{4,6},{5,7},{6,4},{7,5},{8,10},{9,11},{10,... | collective-permute-start | bytes 983048 | tf_op jit(solution)/shard_map/ppermute | solution.py:104
  8.0 1.3 collective-permute-start.3
  9.5 6.9 %collective-permute-done = bf16[128,1280]{1,0:T(8,128)(2,1)S(1)} collective-permute-done((bf16[128,1280]{1,0:T(8,128)(2,1)}, bf16[128,1280]{1,0:T(8,128)(2,1)S(1)}, u32[]{:S(2)}, u32[]{:S(2)}) %collective-permute-start) | collective-permute-done | bytes 327712 | tf_op jit(solution)/shard_map/ppermute | solution.py:104
  16.4 13.9 %collective-permute-done.2 = bf16[128,1280]{1,0:T(8,128)(2,1)} collective-permute-done((bf16[128,1280]{1,0:T(8,128)(2,1)}, bf16[128,1280]{1,0:T(8,128)(2,1)}, u32[]{:S(2)}, u32[]{:S(2)}) %collective-permute-start.2) | collective-permute-done | bytes 327712 | tf_op jit(solution)/shard_map/ppermute | solution.py:104
  30.5 0.9 pad_maximum_fusion.1
  31.4 1.5 collective-permute-start.1
  33.0 1.9 %pad_maximum_fusion.2 = bf16[256,1280]{1,0:T(8,128)(2,1)} fusion(bf16[128,1280]{1,0:T(8,128)(2,1)} %collective-permute-done.3, bf16[128,1280]{1,0:T(8,128)(2,1)} %collective-permute-done.2), kind=kLoop, calls=%fused_computation.5 | loop fusion | flops 1310720 | bytes 1310720 | tf_op jit(solution)/shard_map/concatenate | solution.py:106
  34.9 0.5 collective-permute-start.11
  35.4 0.6 fusion.4.a_0_
  36.1 2.2 %pad_maximum_fusion.a_1_ = bf16[512,1280]{1,0:T(8,128)(2,1)} fusion(bf16[128,1280]{1,0:T(8,128)(2,1)} %collective-permute-done.3, bf16[128,1280]{1,0:T(8,128)(2,1)} %collective-permute-done.2, bf16[128,1280]{1,0:T(8,128)(2,1)S(1)} %collective-permute-done, bf16[128,1280]{1,0:T(8,128)(2,1)S(1)} %get-tuple-element.37), kind=kLoop, calls=%fused_computation | loop fusion | flops 5242880 | bytes 2621440 | tf_op jit(solution)/shard_map/concatenate | solution.py:106
  38.4 1.5 collective-permute-start.8
  39.9 1.1 copy-done.2
  40.9 22.0 %shard_map.64 = (f32[10,512,128]{2,1,0:T(8,128)}, f32[10,8,512]{2,1,0:T(8,128)}) custom-call(s32[4]{0:T(128)} %fusion.4.a_0_, bf16[512,1280]{1,0:T(8,128)(2,1)} %pad_maximum_fusion.a_1_, bf16[512,1280]{1,0:T(8,128)(2,1)} %a_2_.5, bf16[512,1280]{1,0:T(8,128)(2,1)} %collective-permute-done.4.a_3_, bf16[512,1280]{1,0:T(8,128)(2,1)} %a_4_.5, ...), custom_call_target="tpu_custom_call" | custom-call | tf_op jit(solution)/shard_map/pallas_call | solution.py:71
  63.0 0.6 copy-done.6
  63.5 14.8 %shard_map.65 = (bf16[10,256,128]{2,1,0:T(8,128)(2,1)}, f32[10,8,256]{2,1,0:T(8,128)}) custom-call(s32[4]{0:T(128)} %copy-done.6, bf16[256,1280]{1,0:T(8,128)(2,1)} %collective-permute-done.1.a_1_, bf16[512,1280]{1,0:T(8,128)(2,1)} %a_2_.5, bf16[512,1280]{1,0:T(8,128)(2,1)} %collective-permute-done.4.a_3_, bf16[512,1280]{1,0:T(8,128)(2,1)} %a_4_.5, ...), custom_call_target="tpu_custom_call" | custom-call | tf_op jit(solution)/shard_map/pallas_call | solution.py:71
  78.3 1.6 %collective-permute-start.10 = (bf16[10,256,128]{2,1,0:T(8,128)(2,1)}, bf16[10,256,128]{2,1,0:T(8,128)(2,1)S(1)}, u32[]{:S(2)}, u32[]{:S(2)}) collective-permute-start(bf16[10,256,128]{2,1,0:T(8,128)(2,1)} %get-tuple-element.20), channel_id=1, source_target_pairs={{0,8},{4,12},{8,0},{12,4},{1,9},{5,13},{9,1},{13,5},{2,10},{6,14},... | collective-permute-start | bytes 1966088 | tf_op jit(solution)/shard_map/ppermute | solution.py:168
  79.9 14.9 %shard_map.66 = (bf16[10,256,128]{2,1,0:T(8,128)(2,1)}, f32[10,8,256]{2,1,0:T(8,128)}) custom-call(s32[4]{0:T(128)} %copy-done.6, bf16[256,1280]{1,0:T(8,128)(2,1)} %collective-permute-done.11.a_1_, bf16[512,1280]{1,0:T(8,128)(2,1)} %a_2_.5, bf16[512,1280]{1,0:T(8,128)(2,1)} %collective-permute-done.4.a_3_, bf16[512,1280]{1,0:T(8,128)(2,1)} %a_4_.5, ...), custom_call_target="tpu_custom_call" | custom-call | tf_op jit(solution)/shard_map/pallas_call | solution.py:71
  94.9 0.6 collective-permute-start.13
  95.4 1.5 collective-permute-start.9
  97.0 0.5 collective-permute-start.12
  97.6 16.3 %collective-permute-done.9 = f32[10,8,256]{2,1,0:T(8,128)S(1)} collective-permute-done((f32[10,8,256]{2,1,0:T(8,128)S(1)}, f32[10,8,256]{2,1,0:T(8,128)S(1)}, u32[]{:S(2)}, u32[]{:S(2)}) %collective-permute-start.9) | collective-permute-done | bytes 81952 | tf_op jit(solution)/shard_map/ppermute | solution.py:168
  113.8 0.9 collective-permute-done.12
  114.8 2.4 %divide_convert_fusion.1 = (bf16[10,256,128]{2,1,0:T(8,128)(2,1)S(1)}, bf16[10,256,128]{2,1,0:T(8,128)(2,1)S(1)}) fusion(bf16[10,256,128]{2,1,0:T(8,128)(2,1)S(1)} %collective-permute-done.10, f32[10,512,128]{2,1,0:T(8,128)S(1)} %copy-done.3, f32[10,256]{1,0:T(8,128)S(1)} %get-tuple-element.25, f32[10,256]{1,0:T(8,128)S(1)} %get-tuple-element.26, ...), kind=kLoop, calls=%fused_computation.3 | loop fusion | flops 3932160 | bytes 5304320 | tf_op jit(solution)/shard_map/convert_element_type | solution.py:178
  117.7 8.6 %collective-permute-start.14 = (bf16[128,1280]{0,1:T(8,128)(2,1)S(1)}, bf16[128,1280]{0,1:T(8,128)(2,1)S(1)}, u32[]{:S(2)}, u32[]{:S(2)}) collective-permute-start(bf16[128,1280]{0,1:T(8,128)(2,1)S(1)} %bitcast.46), channel_id=1, source_target_pairs={{0,3},{1,0},{2,1},{3,2},{4,7},{5,4},{6,5},{7,6},{8,11},{9,8},{10,9... | collective-permute-start | bytes 983048 | tf_op jit(solution)/shard_map/ppermute | solution.py:189
  127.2 0.6 collective-permute-start.16
  128.0 6.5 %collective-permute-done.14 = bf16[128,1280]{0,1:T(8,128)(2,1)S(1)} collective-permute-done((bf16[128,1280]{0,1:T(8,128)(2,1)S(1)}, bf16[128,1280]{0,1:T(8,128)(2,1)S(1)}, u32[]{:S(2)}, u32[]{:S(2)}) %collective-permute-start.14) | collective-permute-done | bytes 327712 | tf_op jit(solution)/shard_map/ppermute | solution.py:189
  134.7 16.6 %collective-permute-done.15 = bf16[128,1280]{0,1:T(8,128)(2,1)} collective-permute-done((bf16[128,1280]{0,1:T(8,128)(2,1)S(1)}, bf16[128,1280]{0,1:T(8,128)(2,1)}, u32[]{:S(2)}, u32[]{:S(2)}) %collective-permute-start.15) | collective-permute-done | bytes 327712 | tf_op jit(solution)/shard_map/ppermute | solution.py:189
  151.3 1.1 copy.26
  152.7 0.9 copy-done.4
  153.6 0.7 constant_dynamic-update-slice_fusion
  (51 shorter events, 3.0 us)
Async XLA Ops:
  0.0 34.9 %collective-permute-start.4 = (bf16[512,1280]{1,0:T(8,128)(2,1)}, bf16[512,1280]{1,0:T(8,128)(2,1)}, u32[]{:S(2)}, u32[]{:S(2)}) collective-permute-start(bf16[512,1280]{1,0:T(8,128)(2,1)} %a_2_.5), channel_id=1, source_target_pairs={{0,4},{4,0},{8,12},{12,8},{1,5},{5,1},{9,13},{13,9},{2,6},{6,2},{1... | collective-permute-start | bytes 3932168 | tf_op jit(solution)/shard_map/ppermute | solution.py:128
  0.5 8.9 %copy-start = (bf16[512,1280]{1,0:T(8,128)(2,1)S(1)}, bf16[512,1280]{1,0:T(8,128)(2,1)}, u32[]{:S(2)}) copy-start(bf16[512,1280]{1,0:T(8,128)(2,1)} %a_4_.5) | copy-start | bytes 3932164
  0.5 15.9 %copy-start.1 = (bf16[512,1280]{1,0:T(8,128)(2,1)S(1)}, bf16[512,1280]{1,0:T(8,128)(2,1)}, u32[]{:S(2)}) copy-start(bf16[512,1280]{1,0:T(8,128)(2,1)} %a_6_.5) | copy-start | bytes 3932164
  0.5 29.8 %copy-start.7 = (s32[1,6]{1,0:T(1,128)S(1)}, s32[1,6]{1,0:T(1,128)}, u32[]{:S(2)}) copy-start(s32[1,6]{1,0:T(1,128)} %param.11) | copy-start | bytes 76
  2.9 13.5 %collective-permute-start = (bf16[128,1280]{1,0:T(8,128)(2,1)}, bf16[128,1280]{1,0:T(8,128)(2,1)S(1)}, u32[]{:S(2)}, u32[]{:S(2)}) collective-permute-start(bf16[128,1280]{1,0:T(8,128)(2,1)} %get-tuple-element.38), channel_id=1, source_target_pairs={{0,1},{1,2},{2,3},{3,0},{4,5},{5,6},{6,7},{7,4},{8,9},{9,10},{10,1... | collective-permute-start | bytes 983048 | tf_op jit(solution)/shard_map/ppermute | solution.py:104
  5.5 24.8 %collective-permute-start.2 = (bf16[128,1280]{1,0:T(8,128)(2,1)}, bf16[128,1280]{1,0:T(8,128)(2,1)}, u32[]{:S(2)}, u32[]{:S(2)}) collective-permute-start(bf16[128,1280]{1,0:T(8,128)(2,1)} %get-tuple-element.40), channel_id=1, source_target_pairs={{0,2},{1,3},{2,0},{3,1},{4,6},{5,7},{6,4},{7,5},{8,10},{9,11},{10,... | collective-permute-start | bytes 983048 | tf_op jit(solution)/shard_map/ppermute | solution.py:104
  8.0 23.4 %collective-permute-start.3 = (bf16[128,1280]{1,0:T(8,128)(2,1)}, bf16[128,1280]{1,0:T(8,128)(2,1)}, u32[]{:S(2)}, u32[]{:S(2)}) collective-permute-start(bf16[128,1280]{1,0:T(8,128)(2,1)} %get-tuple-element.39), channel_id=1, source_target_pairs={{0,3},{1,0},{2,1},{3,2},{4,7},{5,4},{6,5},{7,6},{8,11},{9,8},{10,9... | collective-permute-start | bytes 983048 | tf_op jit(solution)/shard_map/ppermute | solution.py:104
  9.4 29.0 %collective-permute-start.5 = (bf16[512,1280]{1,0:T(8,128)(2,1)S(1)}, bf16[512,1280]{1,0:T(8,128)(2,1)}, u32[]{:S(2)}, u32[]{:S(2)}) collective-permute-start(bf16[512,1280]{1,0:T(8,128)(2,1)S(1)} %copy-done), channel_id=1, source_target_pairs={{0,4},{4,0},{8,12},{12,8},{1,5},{5,1},{9,13},{13,9},{2,6},{6,2},{1... | collective-permute-start | bytes 3932168 | tf_op jit(solution)/shard_map/ppermute | solution.py:128
  16.4 23.5 %collective-permute-start.6 = (bf16[512,1280]{1,0:T(8,128)(2,1)S(1)}, bf16[512,1280]{1,0:T(8,128)(2,1)S(1)}, u32[]{:S(2)}, u32[]{:S(2)}) collective-permute-start(bf16[512,1280]{1,0:T(8,128)(2,1)S(1)} %copy-done.1), channel_id=1, source_target_pairs={{0,4},{4,0},{8,12},{12,8},{1,5},{5,1},{9,13},{13,9},{2,6},{6,2},{1... | collective-permute-start | bytes 3932168 | tf_op jit(solution)/shard_map/ppermute | solution.py:128
  30.3 10.6 %collective-permute-start.7 = (bf16[512,1280]{1,0:T(8,128)(2,1)}, bf16[512,1280]{1,0:T(8,128)(2,1)}, u32[]{:S(2)}, u32[]{:S(2)}) collective-permute-start(bf16[512,1280]{1,0:T(8,128)(2,1)} %a_8_.5), channel_id=1, source_target_pairs={{0,4},{4,0},{8,12},{12,8},{1,5},{5,1},{9,13},{13,9},{2,6},{6,2},{1... | collective-permute-start | bytes 3932168 | tf_op jit(solution)/shard_map/ppermute | solution.py:128
  31.4 31.5 %collective-permute-start.1 = (bf16[256,1280]{1,0:T(8,128)(2,1)}, bf16[256,1280]{1,0:T(8,128)(2,1)}, u32[]{:S(2)}, u32[]{:S(2)}) collective-permute-start(bf16[256,1280]{1,0:T(8,128)(2,1)} %pad_maximum_fusion.1), channel_id=1, source_target_pairs={{0,8},{4,12},{8,0},{12,4},{1,9},{5,13},{9,1},{13,5},{2,10},{6,14},... | collective-permute-start | bytes 1966088 | tf_op jit(solution)/shard_map/ppermute | solution.py:124
  34.9 45.0 %collective-permute-start.11 = (bf16[256,1280]{1,0:T(8,128)(2,1)}, bf16[256,1280]{1,0:T(8,128)(2,1)}, u32[]{:S(2)}, u32[]{:S(2)}) collective-permute-start(bf16[256,1280]{1,0:T(8,128)(2,1)} %pad_maximum_fusion.2), channel_id=1, source_target_pairs={{0,8},{4,12},{8,0},{12,4},{1,9},{5,13},{9,1},{13,5},{2,10},{6,14},... | collective-permute-start | bytes 1966088 | tf_op jit(solution)/shard_map/ppermute | solution.py:125
  38.4 24.6 %collective-permute-start.8 = (s32[4]{0:T(128)S(1)}, s32[4]{0:T(128)S(1)}, u32[]{:S(2)}, u32[]{:S(2)}) collective-permute-start(s32[4]{0:T(128)S(1)} %fusion.5), channel_id=1, source_target_pairs={{0,8},{4,12},{8,0},{12,4},{1,9},{5,13},{9,1},{13,5},{2,10},{6,14},... | collective-permute-start | bytes 56 | tf_op jit(solution)/shard_map/ppermute | solution.py:124
  39.9 1.1 copy-start.2
  63.0 0.6 copy-start.6
  78.3 17.1 %copy-start.8 = (f32[10,8,256]{2,1,0:T(8,128)S(1)}, f32[10,8,256]{2,1,0:T(8,128)}, u32[]{:S(2)}) copy-start(f32[10,8,256]{2,1,0:T(8,128)} %get-tuple-element.19) | copy-start | bytes 245764
  78.3 19.1 %copy-start.5 = (f32[10,8,512]{2,1,0:T(8,128)S(1)}, f32[10,8,512]{2,1,0:T(8,128)}, u32[]{:S(2)}) copy-start(f32[10,8,512]{2,1,0:T(8,128)} %get-tuple-element.17) | copy-start | bytes 491524
  78.3 36.4 %collective-permute-start.10 = (bf16[10,256,128]{2,1,0:T(8,128)(2,1)}, bf16[10,256,128]{2,1,0:T(8,128)(2,1)S(1)}, u32[]{:S(2)}, u32[]{:S(2)}) collective-permute-start(bf16[10,256,128]{2,1,0:T(8,128)(2,1)} %get-tuple-element.20), channel_id=1, source_target_pairs={{0,8},{4,12},{8,0},{12,4},{1,9},{5,13},{9,1},{13,5},{2,10},{6,14},... | collective-permute-start | bytes 1966088 | tf_op jit(solution)/shard_map/ppermute | solution.py:168
  79.9 34.8 %copy-start.3 = (f32[10,512,128]{2,1,0:T(8,128)S(1)}, f32[10,512,128]{2,1,0:T(8,128)}, u32[]{:S(2)}) copy-start(f32[10,512,128]{2,1,0:T(8,128)} %get-tuple-element.16) | copy-start | bytes 7864324
  94.9 19.9 %collective-permute-start.13 = (bf16[10,256,128]{2,1,0:T(8,128)(2,1)}, bf16[10,256,128]{2,1,0:T(8,128)(2,1)S(1)}, u32[]{:S(2)}, u32[]{:S(2)}) collective-permute-start(bf16[10,256,128]{2,1,0:T(8,128)(2,1)} %get-tuple-element.22), channel_id=1, source_target_pairs={{0,8},{4,12},{8,0},{12,4},{1,9},{5,13},{9,1},{13,5},{2,10},{6,14},... | collective-permute-start | bytes 1966088 | tf_op jit(solution)/shard_map/ppermute | solution.py:168
  95.4 18.4 %collective-permute-start.9 = (f32[10,8,256]{2,1,0:T(8,128)S(1)}, f32[10,8,256]{2,1,0:T(8,128)S(1)}, u32[]{:S(2)}, u32[]{:S(2)}) collective-permute-start(f32[10,8,256]{2,1,0:T(8,128)S(1)} %copy-done.8), channel_id=1, source_target_pairs={{0,8},{4,12},{8,0},{12,4},{1,9},{5,13},{9,1},{13,5},{2,10},{6,14},... | collective-permute-start | bytes 245768 | tf_op jit(solution)/shard_map/ppermute | solution.py:168
  97.0 17.8 %collective-permute-start.12 = (f32[10,8,256]{2,1,0:T(8,128)}, f32[10,8,256]{2,1,0:T(8,128)S(1)}, u32[]{:S(2)}, u32[]{:S(2)}) collective-permute-start(f32[10,8,256]{2,1,0:T(8,128)} %get-tuple-element.21), channel_id=1, source_target_pairs={{0,8},{4,12},{8,0},{12,4},{1,9},{5,13},{9,1},{13,5},{2,10},{6,14},... | collective-permute-start | bytes 245768 | tf_op jit(solution)/shard_map/ppermute | solution.py:168
  117.7 16.8 %collective-permute-start.14 = (bf16[128,1280]{0,1:T(8,128)(2,1)S(1)}, bf16[128,1280]{0,1:T(8,128)(2,1)S(1)}, u32[]{:S(2)}, u32[]{:S(2)}) collective-permute-start(bf16[128,1280]{0,1:T(8,128)(2,1)S(1)} %bitcast.46), channel_id=1, source_target_pairs={{0,3},{1,0},{2,1},{3,2},{4,7},{5,4},{6,5},{7,6},{8,11},{9,8},{10,9... | collective-permute-start | bytes 983048 | tf_op jit(solution)/shard_map/ppermute | solution.py:189
  126.9 24.4 %collective-permute-start.15 = (bf16[128,1280]{0,1:T(8,128)(2,1)S(1)}, bf16[128,1280]{0,1:T(8,128)(2,1)}, u32[]{:S(2)}, u32[]{:S(2)}) collective-permute-start(bf16[128,1280]{0,1:T(8,128)(2,1)S(1)} %bitcast.48), channel_id=1, source_target_pairs={{0,2},{1,3},{2,0},{3,1},{4,6},{5,7},{6,4},{7,5},{8,10},{9,11},{10,... | collective-permute-start | bytes 983048 | tf_op jit(solution)/shard_map/ppermute | solution.py:189
  127.2 25.3 %collective-permute-start.16 = (bf16[128,1280]{0,1:T(8,128)(2,1)S(1)}, bf16[128,1280]{0,1:T(8,128)(2,1)S(1)}, u32[]{:S(2)}, u32[]{:S(2)}) collective-permute-start(bf16[128,1280]{0,1:T(8,128)(2,1)S(1)} %bitcast.47), channel_id=1, source_target_pairs={{0,1},{1,2},{2,3},{3,0},{4,5},{5,6},{6,7},{7,4},{8,9},{9,10},{10,1... | collective-permute-start | bytes 983048 | tf_op jit(solution)/shard_map/ppermute | solution.py:189
  152.5 1.1 copy-start.4

commit v16 on v15

--- a/solution.py
+++ b/solution.py
@@ -103,7 +103,8 @@
         query_parts.append(
             lax.ppermute(piece, "sp", [(i, (i + d) % sp_count) for i in range(sp_count)])
         )
-    query_block = jnp.concatenate(query_parts, axis=0)
+    order = [0] + sorted(range(1, sp_count), key=lambda d: -min(d, sp_count - d))
+    query_block = jnp.concatenate([query_parts[d] for d in order], axis=0)
 
     back = [(i, (i - 2) % seq_count) for i in range(seq_count)]
     forth = [(i, (i + 2) % seq_count) for i in range(seq_count)]
@@ -175,16 +176,15 @@
         mixed = (
             local_out[:, near] * weight_a + far_out.astype(jnp.float32) * weight_b
         ) / (weight_a + weight_b)
-        mixed_halves.append(mixed.astype(jnp.bfloat16))
-    rows_all = query_block.shape[0]
-    heads_out = jnp.transpose(jnp.concatenate(mixed_halves, axis=1), (1, 0, 2)).reshape(
-        rows_all, head_width
-    )
+        mixed_halves.append(
+            jnp.transpose(mixed.astype(jnp.bfloat16), (1, 0, 2)).reshape(half, head_width)
+        )
 
     rows = queries.shape[0]
     result = jnp.zeros((rows, queries.shape[1]), jnp.bfloat16)
     for d in range(sp_count):
-        piece = heads_out[d * rows : (d + 1) * rows]
+        start = order.index(d) * rows
+        piece = mixed_halves[start // half][start % half : start % half + rows]
         if d:
             piece = lax.ppermute(piece, "sp", [(i, (i - d) % sp_count) for i in range(sp_count)])
         columns = ((sp_place + d) % sp_count) * head_width

time: 155 us -> 160 us (1.032)
  starting transfers between devices: 24 us -> 28.2 us
  waiting for transfers between devices: 61.1 us -> 58.3 us
  other arithmetic: 8.63 us -> 10.5 us
  local copies, waits for them, and re-layouts: 8.66 us -> 10.3 us
    transpose x1, other arithmetic: 0.09 us -> 4.36 us  [local(): jnp.transpose(mixed.astype(jnp.bfloat16), (1, 0, 2))]
    ppermute x3, starting transfers between devices: 9.3 us -> 11.8 us  [local(): lax.ppermute(piece, 'sp', [(i, (i - d) % sp_count) for i in range(sp_coun...]
    convert_element_type x1 -> x0, other arithmetic: 2.44 us -> none  [local(): mixed_halves.append(mixed.astype(jnp.bfloat16))]
    ppermute x3, waiting for transfers between devices: 20.8 us -> 19 us  [local(): lax.ppermute(piece, 'sp', [(i, (i + d) % sp_count) for i in range(sp_coun...]
    ppermute x4, waiting for transfers between devices: 17.2 us -> 15.3 us  [local(): far_out, far_lse = lax.ppermute((far_out, far_lse), 'seq', forth)]
  transfers between devices with their start and end apart: 17 -> 17, of which waited for: 6 -> 4; matrix products, arithmetic and copies ran while one was open for 7% -> 8% of each run, Pallas kernels for 34% -> 32%
where the time goes in v16:
time: 160 us; the launch traced here: 159 us
  waiting for transfers between devices  58.3 us (36%)
  Pallas kernels  51.8 us (32%)
  starting transfers between devices  28.2 us (18%)
  other arithmetic  10.5 us (7%)
  local copies, waits for them, and re-layouts  10.3 us (6%)
    pallas_call x3, Pallas kernels, attend_partial(): pl.pallas_call(lambda *a: partial_kernel(nsrc, group, *a), grid_spec=grid...  51.8 us
    ppermute x3, waiting for transfers between devices, local(): lax.ppermute(piece, 'sp', [(i, (i - d) % sp_count) for i in range(sp_coun...  24 us
    ppermute x3, waiting for transfers between devices, local(): lax.ppermute(piece, 'sp', [(i, (i + d) % sp_count) for i in range(sp_coun...  19 us
    ppermute x4, waiting for transfers between devices, local(): far_out, far_lse = lax.ppermute((far_out, far_lse), 'seq', forth)  15.3 us
    ppermute x3, starting transfers between devices, local(): lax.ppermute(piece, 'sp', [(i, (i - d) % sp_count) for i in range(sp_coun...  11.8 us
    ppermute x3, starting transfers between devices, local(): lax.ppermute(piece, 'sp', [(i, (i + d) % sp_count) for i in range(sp_coun...  7.44 us
    concatenate x3, other arithmetic, local(): query_block = jnp.concatenate([query_parts[d] for d in order], axis=0)  5.15 us
    transpose x1, other arithmetic, local(): jnp.transpose(mixed.astype(jnp.bfloat16), (1, 0, 2))  4.36 us
  transfers between devices with their start and end apart: 17, of which 4 were waited for; matrix products, arithmetic and copies ran while one was open for 8% of the time, Pallas kernels for 32%

profile of v16, /device:TPU:0, one launch (start us, length us, event | category | flops | bytes accessed | tf_op | source)
XLA Modules:
  0.0 159.3 jit_solution(4021726033390460223)
XLA Ops:
  0.5 2.4 %constant_dynamic-slice_fusion.1 = (bf16[128,1280]{1,0:T(8,128)(2,1)}, bf16[128,1280]{1,0:T(8,128)(2,1)}, bf16[128,1280]{1,0:T(8,128)(2,1)S(1)}, bf16[128,1280]{1,0:T(8,128)(2,1)}) fusion(bf16[128,5120]{1,0:T(8,128)(2,1)} %param.6, s32[]{:T(128)S(6)} %select_n.59, s32[]{:T(128)S(6)} %select_n.56, s32[]{:T(128)S(6)} %select_n.54, s32[]{:T(128)S(6)} %select_n.61), kind=kLoop, calls=%fused_computation.22 | loop fusion | bytes 2621456 | tf_op jit(solution)/shard_map/dynamic_slice | solution.py:102
  2.8 3.6 %collective-permute-start = (bf16[128,1280]{1,0:T(8,128)(2,1)}, bf16[128,1280]{1,0:T(8,128)(2,1)S(1)}, u32[]{:S(2)}, u32[]{:S(2)}) collective-permute-start(bf16[128,1280]{1,0:T(8,128)(2,1)} %get-tuple-element.34), channel_id=1, source_target_pairs={{0,2},{1,3},{2,0},{3,1},{4,6},{5,7},{6,4},{7,5},{8,10},{9,11},{10,... | collective-permute-start | bytes 983048 | tf_op jit(solution)/shard_map/ppermute | solution.py:104
  6.5 1.6 collective-permute-start.2
  8.0 2.2 %collective-permute-start.3 = (bf16[128,1280]{1,0:T(8,128)(2,1)}, bf16[128,1280]{1,0:T(8,128)(2,1)}, u32[]{:S(2)}, u32[]{:S(2)}) collective-permute-start(bf16[128,1280]{1,0:T(8,128)(2,1)} %get-tuple-element.36), channel_id=1, source_target_pairs={{0,3},{1,0},{2,1},{3,2},{4,7},{5,4},{6,5},{7,6},{8,11},{9,8},{10,9... | collective-permute-start | bytes 983048 | tf_op jit(solution)/shard_map/ppermute | solution.py:104
  10.4 19.0 %collective-permute-done = bf16[128,1280]{1,0:T(8,128)(2,1)S(1)} collective-permute-done((bf16[128,1280]{1,0:T(8,128)(2,1)}, bf16[128,1280]{1,0:T(8,128)(2,1)S(1)}, u32[]{:S(2)}, u32[]{:S(2)}) %collective-permute-start) | collective-permute-done | bytes 327712 | tf_op jit(solution)/shard_map/ppermute | solution.py:104
  30.1 0.9 pad_maximum_fusion.1
  31.0 1.8 %collective-permute-start.1 = (bf16[256,1280]{1,0:T(8,128)(2,1)}, bf16[256,1280]{1,0:T(8,128)(2,1)}, u32[]{:S(2)}, u32[]{:S(2)}) collective-permute-start(bf16[256,1280]{1,0:T(8,128)(2,1)} %pad_maximum_fusion.1), channel_id=1, source_target_pairs={{0,8},{4,12},{8,0},{12,4},{1,9},{5,13},{9,1},{13,5},{2,10},{6,14},... | collective-permute-start | bytes 1966088 | tf_op jit(solution)/shard_map/ppermute | solution.py:125
  32.8 2.0 %pad_maximum_fusion.2 = bf16[256,1280]{1,0:T(8,128)(2,1)} fusion(bf16[128,1280]{1,0:T(8,128)(2,1)} %collective-permute-done.3, bf16[128,1280]{1,0:T(8,128)(2,1)} %collective-permute-done.2), kind=kLoop, calls=%fused_computation.4 | loop fusion | flops 1310720 | bytes 1310720 | tf_op jit(solution)/shard_map/concatenate | solution.py:107
  35.0 0.7 fusion.6.a_0_
  35.8 2.2 %pad_maximum_fusion.a_1_ = bf16[512,1280]{1,0:T(8,128)(2,1)} fusion(bf16[128,1280]{1,0:T(8,128)(2,1)} %collective-permute-done.3, bf16[128,1280]{1,0:T(8,128)(2,1)} %collective-permute-done.2, bf16[128,1280]{1,0:T(8,128)(2,1)S(1)} %collective-permute-done, bf16[128,1280]{1,0:T(8,128)(2,1)S(1)} %get-tuple-element.35), kind=kLoop, calls=%fused_computation | loop fusion | flops 5242880 | bytes 2621440 | tf_op jit(solution)/shard_map/concatenate | solution.py:107
  38.0 1.8 %collective-permute-start.8 = (s32[4]{0:T(128)S(1)}, s32[4]{0:T(128)S(1)}, u32[]{:S(2)}, u32[]{:S(2)}) collective-permute-start(s32[4]{0:T(128)S(1)} %fusion.7), channel_id=1, source_target_pairs={{0,8},{4,12},{8,0},{12,4},{1,9},{5,13},{9,1},{13,5},{2,10},{6,14},... | collective-permute-start | bytes 56 | tf_op jit(solution)/shard_map/ppermute | solution.py:125
  39.8 1.1 copy-done.2
  40.8 22.0 %shard_map.64 = (f32[10,512,128]{2,1,0:T(8,128)}, f32[10,8,512]{2,1,0:T(8,128)}) custom-call(s32[4]{0:T(128)} %fusion.6.a_0_, bf16[512,1280]{1,0:T(8,128)(2,1)} %pad_maximum_fusion.a_1_, bf16[512,1280]{1,0:T(8,128)(2,1)} %a_2_.5, bf16[512,1280]{1,0:T(8,128)(2,1)} %collective-permute-done.4.a_3_, bf16[512,1280]{1,0:T(8,128)(2,1)} %a_4_.5, ...), custom_call_target="tpu_custom_call" | custom-call | tf_op jit(solution)/shard_map/pallas_call | solution.py:71
  62.9 0.5 copy-done.7
  63.4 14.8 %shard_map.65 = (bf16[10,256,128]{2,1,0:T(8,128)(2,1)}, f32[10,8,256]{2,1,0:T(8,128)}) custom-call(s32[4]{0:T(128)} %copy-done.7, bf16[256,1280]{1,0:T(8,128)(2,1)} %collective-permute-done.1.a_1_, bf16[512,1280]{1,0:T(8,128)(2,1)} %a_2_.5, bf16[512,1280]{1,0:T(8,128)(2,1)} %collective-permute-done.4.a_3_, bf16[512,1280]{1,0:T(8,128)(2,1)} %a_4_.5, ...), custom_call_target="tpu_custom_call" | custom-call | tf_op jit(solution)/shard_map/pallas_call | solution.py:71
  78.2 1.0 collective-permute-start.10
  79.3 14.9 %shard_map.66 = (bf16[10,256,128]{2,1,0:T(8,128)(2,1)}, f32[10,8,256]{2,1,0:T(8,128)}) custom-call(s32[4]{0:T(128)} %copy-done.7, bf16[256,1280]{1,0:T(8,128)(2,1)} %collective-permute-done.11.a_1_, bf16[512,1280]{1,0:T(8,128)(2,1)} %a_2_.5, bf16[512,1280]{1,0:T(8,128)(2,1)} %collective-permute-done.4.a_3_, bf16[512,1280]{1,0:T(8,128)(2,1)} %a_4_.5, ...), custom_call_target="tpu_custom_call" | custom-call | tf_op jit(solution)/shard_map/pallas_call | solution.py:71
  94.2 1.1 collective-permute-start.13
  95.3 1.0 collective-permute-start.9
  96.3 1.1 collective-permute-start.12
  97.5 15.3 %collective-permute-done.9 = f32[10,8,256]{2,1,0:T(8,128)} collective-permute-done((f32[10,8,256]{2,1,0:T(8,128)}, f32[10,8,256]{2,1,0:T(8,128)}, u32[]{:S(2)}, u32[]{:S(2)}) %collective-permute-start.9) | collective-permute-done | bytes 81952 | tf_op jit(solution)/shard_map/ppermute | solution.py:169
  112.8 0.9 slice.61
  113.8 0.8 copy-done.5
  114.6 4.4 %fusion.1 = (bf16[256,10,128]{2,0,1:T(8,128)(2,1)S(1)}, bf16[256,10,128]{2,0,1:T(8,128)(2,1)S(1)}) fusion(f32[10,256]{1,0:T(8,128)S(1)} %get-tuple-element.25, f32[10,256]{1,0:T(8,128)S(1)} %get-tuple-element.26, bf16[10,256,128]{2,1,0:T(8,128)(2,1)} %collective-permute-done.13, f32[10,256]{1,0:T(8,128)S(1)} %get-tuple-element.27, ...), kind=kLoop, calls=%fused_computation.6 | loop fusion | flops 3932160 | bytes 5304320 | tf_op jit(solution)/shard_map/transpose | solution.py:180
  119.2 0.8 collective-permute-start.14
  120.7 9.0 %collective-permute-start.15 = (bf16[128,1280]{0,1:T(8,128)(2,1)S(1)}, bf16[128,1280]{0,1:T(8,128)(2,1)}, u32[]{:S(2)}, u32[]{:S(2)}) collective-permute-start(bf16[128,1280]{0,1:T(8,128)(2,1)S(1)} %bitcast.50), channel_id=1, source_target_pairs={{0,2},{1,3},{2,0},{3,1},{4,6},{5,7},{6,4},{7,5},{8,10},{9,11},{10,... | collective-permute-start | bytes 983048 | tf_op jit(solution)/shard_map/ppermute | solution.py:189
  129.9 2.1 %collective-permute-start.16 = (bf16[128,1280]{0,1:T(8,128)(2,1)S(1)}, bf16[128,1280]{0,1:T(8,128)(2,1)S(1)}, u32[]{:S(2)}, u32[]{:S(2)}) collective-permute-start(bf16[128,1280]{0,1:T(8,128)(2,1)S(1)} %bitcast.49), channel_id=1, source_target_pairs={{0,1},{1,2},{2,3},{3,0},{4,5},{5,6},{6,7},{7,4},{8,9},{9,10},{10,1... | collective-permute-start | bytes 983048 | tf_op jit(solution)/shard_map/ppermute | solution.py:189
  132.1 1.6 collective-permute-done.14
  133.9 22.4 %collective-permute-done.15 = bf16[128,1280]{0,1:T(8,128)(2,1)} collective-permute-done((bf16[128,1280]{0,1:T(8,128)(2,1)S(1)}, bf16[128,1280]{0,1:T(8,128)(2,1)}, u32[]{:S(2)}, u32[]{:S(2)}) %collective-permute-start.15) | collective-permute-done | bytes 327712 | tf_op jit(solution)/shard_map/ppermute | solution.py:189
  156.3 1.1 copy.26
  157.7 0.9 copy-done.4
  158.6 0.7 constant_dynamic-update-slice_fusion
  (51 shorter events, 3.5 us)
Async XLA Ops:
  0.0 34.8 %collective-permute-start.4 = (bf16[512,1280]{1,0:T(8,128)(2,1)}, bf16[512,1280]{1,0:T(8,128)(2,1)}, u32[]{:S(2)}, u32[]{:S(2)}) collective-permute-start(bf16[512,1280]{1,0:T(8,128)(2,1)} %a_2_.5), channel_id=1, source_target_pairs={{0,4},{4,0},{8,12},{12,8},{1,5},{5,1},{9,13},{13,9},{2,6},{6,2},{1... | collective-permute-start | bytes 3932168 | tf_op jit(solution)/shard_map/ppermute | solution.py:129
  0.5 9.8 %copy-start = (bf16[512,1280]{1,0:T(8,128)(2,1)S(1)}, bf16[512,1280]{1,0:T(8,128)(2,1)}, u32[]{:S(2)}) copy-start(bf16[512,1280]{1,0:T(8,128)(2,1)} %a_4_.5) | copy-start | bytes 3932164
  0.5 28.9 %copy-start.1 = (bf16[512,1280]{1,0:T(8,128)(2,1)S(1)}, bf16[512,1280]{1,0:T(8,128)(2,1)}, u32[]{:S(2)}) copy-start(bf16[512,1280]{1,0:T(8,128)(2,1)} %a_6_.5) | copy-start | bytes 3932164
  0.5 29.4 %copy-start.8 = (s32[1,6]{1,0:T(1,128)S(1)}, s32[1,6]{1,0:T(1,128)}, u32[]{:S(2)}) copy-start(s32[1,6]{1,0:T(1,128)} %param.11) | copy-start | bytes 76
  2.8 26.5 %collective-permute-start = (bf16[128,1280]{1,0:T(8,128)(2,1)}, bf16[128,1280]{1,0:T(8,128)(2,1)S(1)}, u32[]{:S(2)}, u32[]{:S(2)}) collective-permute-start(bf16[128,1280]{1,0:T(8,128)(2,1)} %get-tuple-element.34), channel_id=1, source_target_pairs={{0,2},{1,3},{2,0},{3,1},{4,6},{5,7},{6,4},{7,5},{8,10},{9,11},{10,... | collective-permute-start | bytes 983048 | tf_op jit(solution)/shard_map/ppermute | solution.py:104
  6.5 22.9 %collective-permute-start.2 = (bf16[128,1280]{1,0:T(8,128)(2,1)}, bf16[128,1280]{1,0:T(8,128)(2,1)}, u32[]{:S(2)}, u32[]{:S(2)}) collective-permute-start(bf16[128,1280]{1,0:T(8,128)(2,1)} %get-tuple-element.33), channel_id=1, source_target_pairs={{0,1},{1,2},{2,3},{3,0},{4,5},{5,6},{6,7},{7,4},{8,9},{9,10},{10,1... | collective-permute-start | bytes 983048 | tf_op jit(solution)/shard_map/ppermute | solution.py:104
  8.0 22.9 %collective-permute-start.3 = (bf16[128,1280]{1,0:T(8,128)(2,1)}, bf16[128,1280]{1,0:T(8,128)(2,1)}, u32[]{:S(2)}, u32[]{:S(2)}) collective-permute-start(bf16[128,1280]{1,0:T(8,128)(2,1)} %get-tuple-element.36), channel_id=1, source_target_pairs={{0,3},{1,0},{2,1},{3,2},{4,7},{5,4},{6,5},{7,6},{8,11},{9,8},{10,9... | collective-permute-start | bytes 983048 | tf_op jit(solution)/shard_map/ppermute | solution.py:104
  10.3 27.7 %collective-permute-start.5 = (bf16[512,1280]{1,0:T(8,128)(2,1)S(1)}, bf16[512,1280]{1,0:T(8,128)(2,1)}, u32[]{:S(2)}, u32[]{:S(2)}) collective-permute-start(bf16[512,1280]{1,0:T(8,128)(2,1)S(1)} %copy-done), channel_id=1, source_target_pairs={{0,4},{4,0},{8,12},{12,8},{1,5},{5,1},{9,13},{13,9},{2,6},{6,2},{1... | collective-permute-start | bytes 3932168 | tf_op jit(solution)/shard_map/ppermute | solution.py:129
  29.3 10.4 %collective-permute-start.6 = (bf16[512,1280]{1,0:T(8,128)(2,1)S(1)}, bf16[512,1280]{1,0:T(8,128)(2,1)S(1)}, u32[]{:S(2)}, u32[]{:S(2)}) collective-permute-start(bf16[512,1280]{1,0:T(8,128)(2,1)S(1)} %copy-done.1), channel_id=1, source_target_pairs={{0,4},{4,0},{8,12},{12,8},{1,5},{5,1},{9,13},{13,9},{2,6},{6,2},{1... | collective-permute-start | bytes 3932168 | tf_op jit(solution)/shard_map/ppermute | solution.py:129
  29.3 11.5 %collective-permute-start.7 = (bf16[512,1280]{1,0:T(8,128)(2,1)}, bf16[512,1280]{1,0:T(8,128)(2,1)}, u32[]{:S(2)}, u32[]{:S(2)}) collective-permute-start(bf16[512,1280]{1,0:T(8,128)(2,1)} %a_8_.5), channel_id=1, source_target_pairs={{0,4},{4,0},{8,12},{12,8},{1,5},{5,1},{9,13},{13,9},{2,6},{6,2},{1... | collective-permute-start | bytes 3932168 | tf_op jit(solution)/shard_map/ppermute | solution.py:129
  31.0 31.9 %collective-permute-start.1 = (bf16[256,1280]{1,0:T(8,128)(2,1)}, bf16[256,1280]{1,0:T(8,128)(2,1)}, u32[]{:S(2)}, u32[]{:S(2)}) collective-permute-start(bf16[256,1280]{1,0:T(8,128)(2,1)} %pad_maximum_fusion.1), channel_id=1, source_target_pairs={{0,8},{4,12},{8,0},{12,4},{1,9},{5,13},{9,1},{13,5},{2,10},{6,14},... | collective-permute-start | bytes 1966088 | tf_op jit(solution)/shard_map/ppermute | solution.py:125
  34.8 44.5 %collective-permute-start.11 = (bf16[256,1280]{1,0:T(8,128)(2,1)}, bf16[256,1280]{1,0:T(8,128)(2,1)}, u32[]{:S(2)}, u32[]{:S(2)}) collective-permute-start(bf16[256,1280]{1,0:T(8,128)(2,1)} %pad_maximum_fusion.2), channel_id=1, source_target_pairs={{0,8},{4,12},{8,0},{12,4},{1,9},{5,13},{9,1},{13,5},{2,10},{6,14},... | collective-permute-start | bytes 1966088 | tf_op jit(solution)/shard_map/ppermute | solution.py:126
  38.0 24.9 %collective-permute-start.8 = (s32[4]{0:T(128)S(1)}, s32[4]{0:T(128)S(1)}, u32[]{:S(2)}, u32[]{:S(2)}) collective-permute-start(s32[4]{0:T(128)S(1)} %fusion.7), channel_id=1, source_target_pairs={{0,8},{4,12},{8,0},{12,4},{1,9},{5,13},{9,1},{13,5},{2,10},{6,14},... | collective-permute-start | bytes 56 | tf_op jit(solution)/shard_map/ppermute | solution.py:125
  39.8 1.1 copy-start.2
  62.9 0.5 copy-start.7
  78.2 19.1 %copy-start.6 = (f32[10,8,512]{2,1,0:T(8,128)S(1)}, f32[10,8,512]{2,1,0:T(8,128)}, u32[]{:S(2)}) copy-start(f32[10,8,512]{2,1,0:T(8,128)} %get-tuple-element.17) | copy-start | bytes 491524
  78.2 35.5 %collective-permute-start.10 = (bf16[10,256,128]{2,1,0:T(8,128)(2,1)}, bf16[10,256,128]{2,1,0:T(8,128)(2,1)S(1)}, u32[]{:S(2)}, u32[]{:S(2)}) collective-permute-start(bf16[10,256,128]{2,1,0:T(8,128)(2,1)} %get-tuple-element.20), channel_id=1, source_target_pairs={{0,8},{4,12},{8,0},{12,4},{1,9},{5,13},{9,1},{13,5},{2,10},{6,14},... | collective-permute-start | bytes 1966088 | tf_op jit(solution)/shard_map/ppermute | solution.py:169
  79.3 35.3 %copy-start.3 = (f32[10,512,128]{2,1,0:T(8,128)S(1)}, f32[10,512,128]{2,1,0:T(8,128)}, u32[]{:S(2)}) copy-start(f32[10,512,128]{2,1,0:T(8,128)} %get-tuple-element.16) | copy-start | bytes 7864324
  94.2 19.6 %collective-permute-start.13 = (bf16[10,256,128]{2,1,0:T(8,128)(2,1)}, bf16[10,256,128]{2,1,0:T(8,128)(2,1)}, u32[]{:S(2)}, u32[]{:S(2)}) collective-permute-start(bf16[10,256,128]{2,1,0:T(8,128)(2,1)} %get-tuple-element.22), channel_id=1, source_target_pairs={{0,8},{4,12},{8,0},{12,4},{1,9},{5,13},{9,1},{13,5},{2,10},{6,14},... | collective-permute-start | bytes 1966088 | tf_op jit(solution)/shard_map/ppermute | solution.py:169
  95.3 17.5 %collective-permute-start.9 = (f32[10,8,256]{2,1,0:T(8,128)}, f32[10,8,256]{2,1,0:T(8,128)}, u32[]{:S(2)}, u32[]{:S(2)}) collective-permute-start(f32[10,8,256]{2,1,0:T(8,128)} %get-tuple-element.19), channel_id=1, source_target_pairs={{0,8},{4,12},{8,0},{12,4},{1,9},{5,13},{9,1},{13,5},{2,10},{6,14},... | collective-permute-start | bytes 245768 | tf_op jit(solution)/shard_map/ppermute | solution.py:169
  96.3 17.4 %collective-permute-start.12 = (f32[10,8,256]{2,1,0:T(8,128)}, f32[10,8,256]{2,1,0:T(8,128)S(1)}, u32[]{:S(2)}, u32[]{:S(2)}) collective-permute-start(f32[10,8,256]{2,1,0:T(8,128)} %get-tuple-element.21), channel_id=1, source_target_pairs={{0,8},{4,12},{8,0},{12,4},{1,9},{5,13},{9,1},{13,5},{2,10},{6,14},... | collective-permute-start | bytes 245768 | tf_op jit(solution)/shard_map/ppermute | solution.py:169
  113.7 0.8 copy-start.5
  119.2 14.4 %collective-permute-start.14 = (bf16[128,1280]{0,1:T(8,128)(2,1)S(1)}, bf16[128,1280]{0,1:T(8,128)(2,1)S(1)}, u32[]{:S(2)}, u32[]{:S(2)}) collective-permute-start(bf16[128,1280]{0,1:T(8,128)(2,1)S(1)} %bitcast.48), channel_id=1, source_target_pairs={{0,3},{1,0},{2,1},{3,2},{4,7},{5,4},{6,5},{7,6},{8,11},{9,8},{10,9... | collective-permute-start | bytes 983048 | tf_op jit(solution)/shard_map/ppermute | solution.py:189
  120.7 35.6 %collective-permute-start.15 = (bf16[128,1280]{0,1:T(8,128)(2,1)S(1)}, bf16[128,1280]{0,1:T(8,128)(2,1)}, u32[]{:S(2)}, u32[]{:S(2)}) collective-permute-start(bf16[128,1280]{0,1:T(8,128)(2,1)S(1)} %bitcast.50), channel_id=1, source_target_pairs={{0,2},{1,3},{2,0},{3,1},{4,6},{5,7},{6,4},{7,5},{8,10},{9,11},{10,... | collective-permute-start | bytes 983048 | tf_op jit(solution)/shard_map/ppermute | solution.py:189
  129.9 27.6 %collective-permute-start.16 = (bf16[128,1280]{0,1:T(8,128)(2,1)S(1)}, bf16[128,1280]{0,1:T(8,128)(2,1)S(1)}, u32[]{:S(2)}, u32[]{:S(2)}) collective-permute-start(bf16[128,1280]{0,1:T(8,128)(2,1)S(1)} %bitcast.49), channel_id=1, source_target_pairs={{0,1},{1,2},{2,3},{3,0},{4,5},{5,6},{6,7},{7,4},{8,9},{9,10},{10,1... | collective-permute-start | bytes 983048 | tf_op jit(solution)/shard_map/ppermute | solution.py:189
  157.5 1.1 copy-start.4

commit v17 on v11

--- a/solution.py
+++ b/solution.py
@@ -8,7 +8,7 @@
 from jax.sharding import PartitionSpec as P
 
 HEAD_DIM = 128
-ROW_SPLIT = 2
+ROW_SPLIT = 1
 STAT_ROWS = 8
 
 

time: 154 us -> 151 us (0.981)
  Pallas kernels: 51.9 us -> 47.9 us
    pallas_call x3, Pallas kernels: 51.9 us -> 47.9 us  [attend_partial(): pl.pallas_call(lambda *a: partial_kernel(nsrc, group, *a), grid_spec=grid...]
  transfers between devices with their start and end apart: 17 -> 17, of which waited for: 5 -> 6; matrix products, arithmetic and copies ran while one was open for 6% -> 6% of each run, Pallas kernels for 34% -> 32%
where the time goes in v17:
time: 151 us
  waiting for transfers between devices  58.4 us (39%)
  Pallas kernels  47.9 us (32%)
  starting transfers between devices  26.5 us (18%)
  other arithmetic  9.89 us (7%)
  local copies, waits for them, and re-layouts  7.95 us (5%)
    pallas_call x3, Pallas kernels, attend_partial(): pl.pallas_call(lambda *a: partial_kernel(nsrc, group, *a), grid_spec=grid...  47.9 us
    ppermute x3, waiting for transfers between devices, local(): lax.ppermute(piece, 'sp', [(i, (i - d) % sp_count) for i in range(sp_coun...  24.8 us
    ppermute x3, waiting for transfers between devices, local(): lax.ppermute(piece, 'sp', [(i, (i + d) % sp_count) for i in range(sp_coun...  16.4 us
    ppermute x1, waiting for transfers between devices, local(): lax.ppermute(query_block[half:], 'seq', back)  14.3 us
    ppermute x3, starting transfers between devices, local(): lax.ppermute(piece, 'sp', [(i, (i - d) % sp_count) for i in range(sp_coun...  9.7 us
    ppermute x3, starting transfers between devices, local(): lax.ppermute(piece, 'sp', [(i, (i + d) % sp_count) for i in range(sp_coun...  6.98 us
    ppermute x4, starting transfers between devices, local(): far_out, far_lse = lax.ppermute((far_out, far_lse), 'seq', forth)  4.71 us
    convert_element_type x1, other arithmetic, local(): mixed_halves.append(mixed.astype(jnp.bfloat16))  4.58 us
  transfers between devices with their start and end apart: 17, of which 6 were waited for; matrix products, arithmetic and copies ran while one was open for 6% of the time, Pallas kernels for 32%

profile of v17, /device:TPU:0, one launch (start us, length us, event | category | flops | bytes accessed | tf_op | source)
XLA Modules:
  0.0 150.9 jit_solution(17430564019001308393)
XLA Ops:
  0.0 2.4 %constant_dynamic-slice_fusion.3 = (bf16[128,1280]{1,0:T(8,128)(2,1)S(1)}, bf16[128,1280]{1,0:T(8,128)(2,1)}, bf16[128,1280]{1,0:T(8,128)(2,1)}, bf16[128,1280]{1,0:T(8,128)(2,1)}) fusion(bf16[128,5120]{1,0:T(8,128)(2,1)} %param.6, s32[]{:T(128)S(6)} %select_n.55, s32[]{:T(128)S(6)} %select_n.57, s32[]{:T(128)S(6)} %select_n.61, s32[]{:T(128)S(6)} %select_n.59), kind=kLoop, calls=%fused_computation.23 | loop fusion | bytes 2621456 | tf_op jit(solution)/shard_map/dynamic_slice | solution.py:99
  2.4 3.0 %collective-permute-start = (bf16[128,1280]{1,0:T(8,128)(2,1)}, bf16[128,1280]{1,0:T(8,128)(2,1)S(1)}, u32[]{:S(2)}, u32[]{:S(2)}) collective-permute-start(bf16[128,1280]{1,0:T(8,128)(2,1)} %get-tuple-element.32), channel_id=1, source_target_pairs={{0,1},{1,2},{2,3},{3,0},{4,5},{5,6},{6,7},{7,4},{8,9},{9,10},{10,1... | collective-permute-start | bytes 983048 | tf_op jit(solution)/shard_map/ppermute | solution.py:104
  5.4 2.6 %collective-permute-start.1 = (bf16[128,1280]{1,0:T(8,128)(2,1)}, bf16[128,1280]{1,0:T(8,128)(2,1)}, u32[]{:S(2)}, u32[]{:S(2)}) collective-permute-start(bf16[128,1280]{1,0:T(8,128)(2,1)} %get-tuple-element.34), channel_id=1, source_target_pairs={{0,2},{1,3},{2,0},{3,1},{4,6},{5,7},{6,4},{7,5},{8,10},{9,11},{10,... | collective-permute-start | bytes 983048 | tf_op jit(solution)/shard_map/ppermute | solution.py:104
  8.0 1.3 collective-permute-start.2
  9.8 1.5 %collective-permute-start.7 = (s32[4]{0:T(128)S(1)}, s32[4]{0:T(128)S(1)}, u32[]{:S(2)}, u32[]{:S(2)}) collective-permute-start(s32[4]{0:T(128)S(1)} %fusion.5), channel_id=1, source_target_pairs={{0,8},{4,12},{8,0},{12,4},{1,9},{5,13},{9,1},{13,5},{2,10},{6,14},... | collective-permute-start | bytes 56 | tf_op jit(solution)/shard_map/ppermute | solution.py:124
  11.3 2.0 %collective-permute-done.7.a_0_ = s32[4]{0:T(128)S(1)} collective-permute-done((s32[4]{0:T(128)S(1)}, s32[4]{0:T(128)S(1)}, u32[]{:S(2)}, u32[]{:S(2)}) %collective-permute-start.7) | collective-permute-done | bytes 48 | tf_op jit(solution)/shard_map/ppermute | solution.py:124
  13.3 16.3 %collective-permute-done.1 = bf16[128,1280]{1,0:T(8,128)(2,1)} collective-permute-done((bf16[128,1280]{1,0:T(8,128)(2,1)}, bf16[128,1280]{1,0:T(8,128)(2,1)}, u32[]{:S(2)}, u32[]{:S(2)}) %collective-permute-start.1) | collective-permute-done | bytes 327712 | tf_op jit(solution)/shard_map/ppermute | solution.py:104
  29.7 0.5 collective-permute-start.6
  30.2 1.1 pad_maximum_fusion.2
  31.3 1.6 %collective-permute-start.11 = (bf16[256,1280]{1,0:T(8,128)(2,1)S(1)}, bf16[256,1280]{1,0:T(8,128)(2,1)}, u32[]{:S(2)}, u32[]{:S(2)}) collective-permute-start(bf16[256,1280]{1,0:T(8,128)(2,1)S(1)} %pad_maximum_fusion.2), channel_id=1, source_target_pairs={{0,8},{4,12},{8,0},{12,4},{1,9},{5,13},{9,1},{13,5},{2,10},{6,14},... | collective-permute-start | bytes 1966088 | tf_op jit(solution)/shard_map/ppermute | solution.py:127
  32.9 0.9 pad_maximum_fusion.1
  33.8 14.3 %collective-permute-done.11.a_1_ = bf16[256,1280]{1,0:T(8,128)(2,1)} collective-permute-done((bf16[256,1280]{1,0:T(8,128)(2,1)S(1)}, bf16[256,1280]{1,0:T(8,128)(2,1)}, u32[]{:S(2)}, u32[]{:S(2)}) %collective-permute-start.11) | collective-permute-done | bytes 655392 | tf_op jit(solution)/shard_map/ppermute | solution.py:127
  48.1 1.5 %collective-permute-start.8 = (bf16[256,1280]{1,0:T(8,128)(2,1)}, bf16[256,1280]{1,0:T(8,128)(2,1)}, u32[]{:S(2)}, u32[]{:S(2)}) collective-permute-start(bf16[256,1280]{1,0:T(8,128)(2,1)} %pad_maximum_fusion.1), channel_id=1, source_target_pairs={{0,8},{4,12},{8,0},{12,4},{1,9},{5,13},{9,1},{13,5},{2,10},{6,14},... | collective-permute-start | bytes 1966088 | tf_op jit(solution)/shard_map/ppermute | solution.py:126
  49.7 13.1 %shard_map.66 = (bf16[10,256,128]{2,1,0:T(8,128)(2,1)}, f32[10,8,256]{2,1,0:T(8,128)}) custom-call(s32[4]{0:T(128)} %copy-done.3, bf16[256,1280]{1,0:T(8,128)(2,1)} %collective-permute-done.11.a_1_, bf16[512,1280]{1,0:T(8,128)(2,1)} %a_2_.5, bf16[512,1280]{1,0:T(8,128)(2,1)} %collective-permute-done.3.a_3_, bf16[512,1280]{1,0:T(8,128)(2,1)} %a_4_.5, ...), custom_call_target="tpu_custom_call" | custom-call | tf_op jit(solution)/shard_map/pallas_call | solution.py:71
  62.8 0.6 collective-permute-start.13
  63.4 0.9 collective-permute-done.8.a_1_
  64.2 13.0 %shard_map.65 = (bf16[10,256,128]{2,1,0:T(8,128)(2,1)}, f32[10,8,256]{2,1,0:T(8,128)}) custom-call(s32[4]{0:T(128)} %copy-done.3, bf16[256,1280]{1,0:T(8,128)(2,1)} %collective-permute-done.8.a_1_, bf16[512,1280]{1,0:T(8,128)(2,1)} %a_2_.5, bf16[512,1280]{1,0:T(8,128)(2,1)} %collective-permute-done.3.a_3_, bf16[512,1280]{1,0:T(8,128)(2,1)} %a_4_.5, ...), custom_call_target="tpu_custom_call" | custom-call | tf_op jit(solution)/shard_map/pallas_call | solution.py:71
  77.2 2.1 %collective-permute-start.10 = (bf16[10,256,128]{2,1,0:T(8,128)(2,1)}, bf16[10,256,128]{2,1,0:T(8,128)(2,1)S(1)}, u32[]{:S(2)}, u32[]{:S(2)}) collective-permute-start(bf16[10,256,128]{2,1,0:T(8,128)(2,1)} %get-tuple-element.14), channel_id=1, source_target_pairs={{0,8},{4,12},{8,0},{12,4},{1,9},{5,13},{9,1},{13,5},{2,10},{6,14},... | collective-permute-start | bytes 1966088 | tf_op jit(solution)/shard_map/ppermute | solution.py:169
  79.3 0.6 fusion.4.a_0_
  80.0 2.0 %collective-permute-start.9 = (f32[10,8,256]{2,1,0:T(8,128)}, f32[10,8,256]{2,1,0:T(8,128)S(1)}, u32[]{:S(2)}, u32[]{:S(2)}) collective-permute-start(f32[10,8,256]{2,1,0:T(8,128)} %get-tuple-element.13), channel_id=1, source_target_pairs={{0,8},{4,12},{8,0},{12,4},{1,9},{5,13},{9,1},{13,5},{2,10},{6,14},... | collective-permute-start | bytes 245768 | tf_op jit(solution)/shard_map/ppermute | solution.py:169
  82.0 2.2 %pad_maximum_fusion.a_1_ = bf16[512,1280]{1,0:T(8,128)(2,1)} fusion(bf16[128,1280]{1,0:T(8,128)(2,1)} %collective-permute-done.2, bf16[128,1280]{1,0:T(8,128)(2,1)} %collective-permute-done.1, bf16[128,1280]{1,0:T(8,128)(2,1)S(1)} %collective-permute-done, bf16[128,1280]{1,0:T(8,128)(2,1)S(1)} %get-tuple-element.31), kind=kLoop, calls=%fused_computation | loop fusion | flops 5242880 | bytes 2621440 | tf_op jit(solution)/shard_map/concatenate | solution.py:106
  84.2 21.8 %shard_map.64 = (f32[10,512,128]{2,1,0:T(8,128)}, f32[10,8,512]{2,1,0:T(8,128)}) custom-call(s32[4]{0:T(128)} %fusion.4.a_0_, bf16[512,1280]{1,0:T(8,128)(2,1)} %pad_maximum_fusion.a_1_, bf16[512,1280]{1,0:T(8,128)(2,1)} %a_2_.5, bf16[512,1280]{1,0:T(8,128)(2,1)} %collective-permute-done.3.a_3_, bf16[512,1280]{1,0:T(8,128)(2,1)} %a_4_.5, ...), custom_call_target="tpu_custom_call" | custom-call | tf_op jit(solution)/shard_map/pallas_call | solution.py:71
  106.0 1.0 copy.19
  107.1 4.6 %divide_convert_fusion.1 = (bf16[10,256,128]{2,1,0:T(8,128)(2,1)S(1)}, bf16[10,256,128]{2,1,0:T(8,128)(2,1)S(1)}) fusion(bf16[10,256,128]{2,1,0:T(8,128)(2,1)S(1)} %collective-permute-done.10, f32[10,512,128]{2,1,0:T(8,128)} %get-tuple-element.11, f32[10,256]{1,0:T(8,128)S(1)} %get-tuple-element.19, f32[10,256]{1,0:T(8,128)S(1)} %get-tuple-element.20, ...), kind=kLoop, calls=%fused_computation.3 | loop fusion | flops 3932160 | bytes 5304320 | tf_op jit(solution)/shard_map/convert_element_type | solution.py:179
  111.9 0.2 copy.23
  112.2 8.6 %collective-permute-start.14 = (bf16[128,1280]{0,1:T(8,128)(2,1)S(1)}, bf16[128,1280]{0,1:T(8,128)(2,1)S(1)}, u32[]{:S(2)}, u32[]{:S(2)}) collective-permute-start(bf16[128,1280]{0,1:T(8,128)(2,1)S(1)} %bitcast.46), channel_id=1, source_target_pairs={{0,3},{1,0},{2,1},{3,2},{4,7},{5,4},{6,5},{7,6},{8,11},{9,8},{10,9... | collective-permute-start | bytes 983048 | tf_op jit(solution)/shard_map/ppermute | solution.py:190
  121.4 1.1 collective-permute-start.15
  122.9 6.0 %collective-permute-done.14 = bf16[128,1280]{0,1:T(8,128)(2,1)S(1)} collective-permute-done((bf16[128,1280]{0,1:T(8,128)(2,1)S(1)}, bf16[128,1280]{0,1:T(8,128)(2,1)S(1)}, u32[]{:S(2)}, u32[]{:S(2)}) %collective-permute-start.14) | collective-permute-done | bytes 327712 | tf_op jit(solution)/shard_map/ppermute | solution.py:190
  129.1 18.8 %collective-permute-done.15 = bf16[128,1280]{0,1:T(8,128)(2,1)} collective-permute-done((bf16[128,1280]{0,1:T(8,128)(2,1)S(1)}, bf16[128,1280]{0,1:T(8,128)(2,1)}, u32[]{:S(2)}, u32[]{:S(2)}) %collective-permute-start.15) | collective-permute-done | bytes 327712 | tf_op jit(solution)/shard_map/ppermute | solution.py:190
  147.9 1.1 copy.26
  149.3 0.9 copy-done.2
  150.2 0.7 constant_dynamic-update-slice_fusion
  (45 shorter events, 2.2 us)
Async XLA Ops:
  0.0 9.4 %copy-start = (bf16[512,1280]{1,0:T(8,128)(2,1)S(1)}, bf16[512,1280]{1,0:T(8,128)(2,1)}, u32[]{:S(2)}) copy-start(bf16[512,1280]{1,0:T(8,128)(2,1)} %a_2_.5) | copy-start | bytes 3932164
  0.0 9.5 %copy-start.4 = (s32[1,6]{1,0:T(1,128)S(1)}, s32[1,6]{1,0:T(1,128)}, u32[]{:S(2)}) copy-start(s32[1,6]{1,0:T(1,128)} %param.11) | copy-start | bytes 76
  0.0 13.3 %copy-start.1 = (bf16[512,1280]{1,0:T(8,128)(2,1)S(1)}, bf16[512,1280]{1,0:T(8,128)(2,1)}, u32[]{:S(2)}) copy-start(bf16[512,1280]{1,0:T(8,128)(2,1)} %a_4_.5) | copy-start | bytes 3932164
  2.4 28.9 %collective-permute-start = (bf16[128,1280]{1,0:T(8,128)(2,1)}, bf16[128,1280]{1,0:T(8,128)(2,1)S(1)}, u32[]{:S(2)}, u32[]{:S(2)}) collective-permute-start(bf16[128,1280]{1,0:T(8,128)(2,1)} %get-tuple-element.32), channel_id=1, source_target_pairs={{0,1},{1,2},{2,3},{3,0},{4,5},{5,6},{6,7},{7,4},{8,9},{9,10},{10,1... | collective-permute-start | bytes 983048 | tf_op jit(solution)/shard_map/ppermute | solution.py:104
  5.4 24.2 %collective-permute-start.1 = (bf16[128,1280]{1,0:T(8,128)(2,1)}, bf16[128,1280]{1,0:T(8,128)(2,1)}, u32[]{:S(2)}, u32[]{:S(2)}) collective-permute-start(bf16[128,1280]{1,0:T(8,128)(2,1)} %get-tuple-element.34), channel_id=1, source_target_pairs={{0,2},{1,3},{2,0},{3,1},{4,6},{5,7},{6,4},{7,5},{8,10},{9,11},{10,... | collective-permute-start | bytes 983048 | tf_op jit(solution)/shard_map/ppermute | solution.py:104
  8.0 21.6 %collective-permute-start.2 = (bf16[128,1280]{1,0:T(8,128)(2,1)}, bf16[128,1280]{1,0:T(8,128)(2,1)}, u32[]{:S(2)}, u32[]{:S(2)}) collective-permute-start(bf16[128,1280]{1,0:T(8,128)(2,1)} %get-tuple-element.33), channel_id=1, source_target_pairs={{0,3},{1,0},{2,1},{3,2},{4,7},{5,4},{6,5},{7,6},{8,11},{9,8},{10,9... | collective-permute-start | bytes 983048 | tf_op jit(solution)/shard_map/ppermute | solution.py:104
  9.4 40.3 %collective-permute-start.3 = (bf16[512,1280]{1,0:T(8,128)(2,1)S(1)}, bf16[512,1280]{1,0:T(8,128)(2,1)}, u32[]{:S(2)}, u32[]{:S(2)}) collective-permute-start(bf16[512,1280]{1,0:T(8,128)(2,1)S(1)} %copy-done), channel_id=1, source_target_pairs={{0,4},{4,0},{8,12},{12,8},{1,5},{5,1},{9,13},{13,9},{2,6},{6,2},{1... | collective-permute-start | bytes 3932168 | tf_op jit(solution)/shard_map/ppermute | solution.py:131
  9.8 3.6 %collective-permute-start.7 = (s32[4]{0:T(128)S(1)}, s32[4]{0:T(128)S(1)}, u32[]{:S(2)}, u32[]{:S(2)}) collective-permute-start(s32[4]{0:T(128)S(1)} %fusion.5), channel_id=1, source_target_pairs={{0,8},{4,12},{8,0},{12,4},{1,9},{5,13},{9,1},{13,5},{2,10},{6,14},... | collective-permute-start | bytes 56 | tf_op jit(solution)/shard_map/ppermute | solution.py:124
  13.3 20.5 %copy-start.3 = (s32[4]{0:T(128)}, s32[4]{0:T(128)S(1)}, u32[]{:S(2)}) copy-start(s32[4]{0:T(128)S(1)} %collective-permute-done.7.a_0_) | copy-start | bytes 52
  13.3 36.3 %collective-permute-start.4 = (bf16[512,1280]{1,0:T(8,128)(2,1)S(1)}, bf16[512,1280]{1,0:T(8,128)(2,1)}, u32[]{:S(2)}, u32[]{:S(2)}) collective-permute-start(bf16[512,1280]{1,0:T(8,128)(2,1)S(1)} %copy-done.1), channel_id=1, source_target_pairs={{0,4},{4,0},{8,12},{12,8},{1,5},{5,1},{9,13},{13,9},{2,6},{6,2},{1... | collective-permute-start | bytes 3932168 | tf_op jit(solution)/shard_map/ppermute | solution.py:131
  29.7 20.0 %collective-permute-start.5 = (bf16[512,1280]{1,0:T(8,128)(2,1)}, bf16[512,1280]{1,0:T(8,128)(2,1)}, u32[]{:S(2)}, u32[]{:S(2)}) collective-permute-start(bf16[512,1280]{1,0:T(8,128)(2,1)} %a_6_.5), channel_id=1, source_target_pairs={{0,4},{4,0},{8,12},{12,8},{1,5},{5,1},{9,13},{13,9},{2,6},{6,2},{1... | collective-permute-start | bytes 3932168 | tf_op jit(solution)/shard_map/ppermute | solution.py:131
  29.7 20.0 %collective-permute-start.6 = (bf16[512,1280]{1,0:T(8,128)(2,1)}, bf16[512,1280]{1,0:T(8,128)(2,1)}, u32[]{:S(2)}, u32[]{:S(2)}) collective-permute-start(bf16[512,1280]{1,0:T(8,128)(2,1)} %a_8_.5), channel_id=1, source_target_pairs={{0,4},{4,0},{8,12},{12,8},{1,5},{5,1},{9,13},{13,9},{2,6},{6,2},{1... | collective-permute-start | bytes 3932168 | tf_op jit(solution)/shard_map/ppermute | solution.py:131
  31.3 16.8 %collective-permute-start.11 = (bf16[256,1280]{1,0:T(8,128)(2,1)S(1)}, bf16[256,1280]{1,0:T(8,128)(2,1)}, u32[]{:S(2)}, u32[]{:S(2)}) collective-permute-start(bf16[256,1280]{1,0:T(8,128)(2,1)S(1)} %pad_maximum_fusion.2), channel_id=1, source_target_pairs={{0,8},{4,12},{8,0},{12,4},{1,9},{5,13},{9,1},{13,5},{2,10},{6,14},... | collective-permute-start | bytes 1966088 | tf_op jit(solution)/shard_map/ppermute | solution.py:127
  48.1 16.1 %collective-permute-start.8 = (bf16[256,1280]{1,0:T(8,128)(2,1)}, bf16[256,1280]{1,0:T(8,128)(2,1)}, u32[]{:S(2)}, u32[]{:S(2)}) collective-permute-start(bf16[256,1280]{1,0:T(8,128)(2,1)} %pad_maximum_fusion.1), channel_id=1, source_target_pairs={{0,8},{4,12},{8,0},{12,4},{1,9},{5,13},{9,1},{13,5},{2,10},{6,14},... | collective-permute-start | bytes 1966088 | tf_op jit(solution)/shard_map/ppermute | solution.py:126
  62.8 17.2 %copy-start.5 = (f32[10,8,256]{2,1,0:T(8,128)S(1)}, f32[10,8,256]{2,1,0:T(8,128)}, u32[]{:S(2)}) copy-start(f32[10,8,256]{2,1,0:T(8,128)} %get-tuple-element.15) | copy-start | bytes 245764
  62.8 44.3 %collective-permute-start.13 = (bf16[10,256,128]{2,1,0:T(8,128)(2,1)}, bf16[10,256,128]{2,1,0:T(8,128)(2,1)S(1)}, u32[]{:S(2)}, u32[]{:S(2)}) collective-permute-start(bf16[10,256,128]{2,1,0:T(8,128)(2,1)} %get-tuple-element.16), channel_id=1, source_target_pairs={{0,8},{4,12},{8,0},{12,4},{1,9},{5,13},{9,1},{13,5},{2,10},{6,14},... | collective-permute-start | bytes 1966088 | tf_op jit(solution)/shard_map/ppermute | solution.py:169
  77.2 29.9 %collective-permute-start.10 = (bf16[10,256,128]{2,1,0:T(8,128)(2,1)}, bf16[10,256,128]{2,1,0:T(8,128)(2,1)S(1)}, u32[]{:S(2)}, u32[]{:S(2)}) collective-permute-start(bf16[10,256,128]{2,1,0:T(8,128)(2,1)} %get-tuple-element.14), channel_id=1, source_target_pairs={{0,8},{4,12},{8,0},{12,4},{1,9},{5,13},{9,1},{13,5},{2,10},{6,14},... | collective-permute-start | bytes 1966088 | tf_op jit(solution)/shard_map/ppermute | solution.py:169
  80.0 27.1 %collective-permute-start.12 = (f32[10,8,256]{2,1,0:T(8,128)S(1)}, f32[10,8,256]{2,1,0:T(8,128)S(1)}, u32[]{:S(2)}, u32[]{:S(2)}) collective-permute-start(f32[10,8,256]{2,1,0:T(8,128)S(1)} %copy-done.5), channel_id=1, source_target_pairs={{0,8},{4,12},{8,0},{12,4},{1,9},{5,13},{9,1},{13,5},{2,10},{6,14},... | collective-permute-start | bytes 245768 | tf_op jit(solution)/shard_map/ppermute | solution.py:169
  80.0 27.1 %collective-permute-start.9 = (f32[10,8,256]{2,1,0:T(8,128)}, f32[10,8,256]{2,1,0:T(8,128)S(1)}, u32[]{:S(2)}, u32[]{:S(2)}) collective-permute-start(f32[10,8,256]{2,1,0:T(8,128)} %get-tuple-element.13), channel_id=1, source_target_pairs={{0,8},{4,12},{8,0},{12,4},{1,9},{5,13},{9,1},{13,5},{2,10},{6,14},... | collective-permute-start | bytes 245768 | tf_op jit(solution)/shard_map/ppermute | solution.py:169
  112.2 16.7 %collective-permute-start.14 = (bf16[128,1280]{0,1:T(8,128)(2,1)S(1)}, bf16[128,1280]{0,1:T(8,128)(2,1)S(1)}, u32[]{:S(2)}, u32[]{:S(2)}) collective-permute-start(bf16[128,1280]{0,1:T(8,128)(2,1)S(1)} %bitcast.46), channel_id=1, source_target_pairs={{0,3},{1,0},{2,1},{3,2},{4,7},{5,4},{6,5},{7,6},{8,11},{9,8},{10,9... | collective-permute-start | bytes 983048 | tf_op jit(solution)/shard_map/ppermute | solution.py:190
  121.4 26.6 %collective-permute-start.15 = (bf16[128,1280]{0,1:T(8,128)(2,1)S(1)}, bf16[128,1280]{0,1:T(8,128)(2,1)}, u32[]{:S(2)}, u32[]{:S(2)}) collective-permute-start(bf16[128,1280]{0,1:T(8,128)(2,1)S(1)} %bitcast.48), channel_id=1, source_target_pairs={{0,2},{1,3},{2,0},{3,1},{4,6},{5,7},{6,4},{7,5},{8,10},{9,11},{10,... | collective-permute-start | bytes 983048 | tf_op jit(solution)/shard_map/ppermute | solution.py:190
  122.7 26.5 %collective-permute-start.16 = (bf16[128,1280]{0,1:T(8,128)(2,1)S(1)}, bf16[128,1280]{0,1:T(8,128)(2,1)S(1)}, u32[]{:S(2)}, u32[]{:S(2)}) collective-permute-start(bf16[128,1280]{0,1:T(8,128)(2,1)S(1)} %bitcast.47), channel_id=1, source_target_pairs={{0,1},{1,2},{2,3},{3,0},{4,5},{5,6},{6,7},{7,4},{8,9},{9,10},{10,1... | collective-permute-start | bytes 983048 | tf_op jit(solution)/shard_map/ppermute | solution.py:190
  149.1 1.1 copy-start.2

commit v18 on v17

--- a/solution.py
+++ b/solution.py
@@ -160,6 +160,8 @@
         [s >= 0, s >= 0, chip == 0, chip == 0],
     )
     local_out, local_lse = attend_partial(local_flags, query_block, keys, values, jnp.float32)
+    got_first, local_out, local_lse = lax.optimization_barrier((got_halves[0], local_out, local_lse))
+    got_halves = [got_first, got_halves[1]]
 
     mixed_halves = []
     for k, got_query in enumerate(got_halves):

time: 151 us -> 151 us (level)
  waiting for transfers between devices: 58.4 us -> 61.6 us
  starting transfers between devices: 26.5 us -> 24 us
    ppermute x4, waiting for transfers between devices: 0.01 us -> 17.2 us  [local(): far_out, far_lse = lax.ppermute((far_out, far_lse), 'seq', forth)]
    ppermute x1, waiting for transfers between devices: 14.3 us -> 0.01 us  [local(): lax.ppermute(query_block[half:], 'seq', back)]
    ppermute x3, waiting for transfers between devices: 16.4 us -> 20.8 us  [local(): lax.ppermute(piece, 'sp', [(i, (i + d) % sp_count) for i in range(sp_coun...]
    convert_element_type x1, other arithmetic: 4.58 us -> 2.44 us  [local(): mixed_halves.append(mixed.astype(jnp.bfloat16))]
    ppermute x3, waiting for transfers between devices: 24.8 us -> 23.1 us  [local(): lax.ppermute(piece, 'sp', [(i, (i - d) % sp_count) for i in range(sp_coun...]
    unnamed x12 -> x18, local copies, waits for them, and re-layouts: 0.87 us -> 2.51 us
  transfers between devices with their start and end apart: 17 -> 17, of which waited for: 6 -> 7; matrix products, arithmetic and copies ran while one was open for 6% -> 7% of each run, Pallas kernels for 32% -> 32%
where the time goes in v18:
time: 151 us
  waiting for transfers between devices  61.6 us (41%)
  Pallas kernels  47.6 us (32%)
  starting transfers between devices  24 us (16%)
  local copies, waits for them, and re-layouts  8.67 us (6%)
  other arithmetic  8.63 us (6%)
    pallas_call x3, Pallas kernels, attend_partial(): pl.pallas_call(lambda *a: partial_kernel(nsrc, group, *a), grid_spec=grid...  47.6 us
    ppermute x3, waiting for transfers between devices, local(): lax.ppermute(piece, 'sp', [(i, (i - d) % sp_count) for i in range(sp_coun...  23.1 us
    ppermute x3, waiting for transfers between devices, local(): lax.ppermute(piece, 'sp', [(i, (i + d) % sp_count) for i in range(sp_coun...  20.8 us
    ppermute x4, waiting for transfers between devices, local(): far_out, far_lse = lax.ppermute((far_out, far_lse), 'seq', forth)  17.2 us
    ppermute x3, starting transfers between devices, local(): lax.ppermute(piece, 'sp', [(i, (i - d) % sp_count) for i in range(sp_coun...  9.3 us
    ppermute x3, starting transfers between devices, local(): lax.ppermute(piece, 'sp', [(i, (i + d) % sp_count) for i in range(sp_coun...  6.54 us
    concatenate x3, other arithmetic, local(): query_block = jnp.concatenate(query_parts, axis=0)  5.1 us
    ppermute x4, starting transfers between devices, local(): far_out, far_lse = lax.ppermute((far_out, far_lse), 'seq', forth)  4.18 us
  transfers between devices with their start and end apart: 17, of which 7 were waited for; matrix products, arithmetic and copies ran while one was open for 7% of the time, Pallas kernels for 32%

profile of v18, /device:TPU:0, one launch (start us, length us, event | category | flops | bytes accessed | tf_op | source)
XLA Modules:
  0.0 150.7 jit_solution(2731997415757203447)
XLA Ops:
  0.5 2.4 %constant_dynamic-slice_fusion.3 = (bf16[128,1280]{1,0:T(8,128)(2,1)S(1)}, bf16[128,1280]{1,0:T(8,128)(2,1)}, bf16[128,1280]{1,0:T(8,128)(2,1)}, bf16[128,1280]{1,0:T(8,128)(2,1)}) fusion(bf16[128,5120]{1,0:T(8,128)(2,1)} %param.6, s32[]{:T(128)S(6)} %select_n.54, s32[]{:T(128)S(6)} %select_n.56, s32[]{:T(128)S(6)} %select_n.61, s32[]{:T(128)S(6)} %select_n.59), kind=kLoop, calls=%fused_computation.23 | loop fusion | bytes 2621456 | tf_op jit(solution)/shard_map/dynamic_slice | solution.py:99
  2.9 2.6 %collective-permute-start = (bf16[128,1280]{1,0:T(8,128)(2,1)}, bf16[128,1280]{1,0:T(8,128)(2,1)S(1)}, u32[]{:S(2)}, u32[]{:S(2)}) collective-permute-start(bf16[128,1280]{1,0:T(8,128)(2,1)} %get-tuple-element.38), channel_id=1, source_target_pairs={{0,1},{1,2},{2,3},{3,0},{4,5},{5,6},{6,7},{7,4},{8,9},{9,10},{10,1... | collective-permute-start | bytes 983048 | tf_op jit(solution)/shard_map/ppermute | solution.py:104
  5.5 2.6 %collective-permute-start.2 = (bf16[128,1280]{1,0:T(8,128)(2,1)}, bf16[128,1280]{1,0:T(8,128)(2,1)}, u32[]{:S(2)}, u32[]{:S(2)}) collective-permute-start(bf16[128,1280]{1,0:T(8,128)(2,1)} %get-tuple-element.40), channel_id=1, source_target_pairs={{0,2},{1,3},{2,0},{3,1},{4,6},{5,7},{6,4},{7,5},{8,10},{9,11},{10,... | collective-permute-start | bytes 983048 | tf_op jit(solution)/shard_map/ppermute | solution.py:104
  8.0 1.3 collective-permute-start.3
  9.5 6.9 %collective-permute-done = bf16[128,1280]{1,0:T(8,128)(2,1)S(1)} collective-permute-done((bf16[128,1280]{1,0:T(8,128)(2,1)}, bf16[128,1280]{1,0:T(8,128)(2,1)S(1)}, u32[]{:S(2)}, u32[]{:S(2)}) %collective-permute-start) | collective-permute-done | bytes 327712 | tf_op jit(solution)/shard_map/ppermute | solution.py:104
  16.4 13.9 %collective-permute-done.2 = bf16[128,1280]{1,0:T(8,128)(2,1)} collective-permute-done((bf16[128,1280]{1,0:T(8,128)(2,1)}, bf16[128,1280]{1,0:T(8,128)(2,1)}, u32[]{:S(2)}, u32[]{:S(2)}) %collective-permute-start.2) | collective-permute-done | bytes 327712 | tf_op jit(solution)/shard_map/ppermute | solution.py:104
  30.5 0.9 pad_maximum_fusion.1
  31.4 1.5 %collective-permute-start.1 = (bf16[256,1280]{1,0:T(8,128)(2,1)}, bf16[256,1280]{1,0:T(8,128)(2,1)}, u32[]{:S(2)}, u32[]{:S(2)}) collective-permute-start(bf16[256,1280]{1,0:T(8,128)(2,1)} %pad_maximum_fusion.1), channel_id=1, source_target_pairs={{0,8},{4,12},{8,0},{12,4},{1,9},{5,13},{9,1},{13,5},{2,10},{6,14},... | collective-permute-start | bytes 1966088 | tf_op jit(solution)/shard_map/ppermute | solution.py:126
  33.0 1.9 %pad_maximum_fusion.2 = bf16[256,1280]{1,0:T(8,128)(2,1)} fusion(bf16[128,1280]{1,0:T(8,128)(2,1)} %collective-permute-done.3, bf16[128,1280]{1,0:T(8,128)(2,1)} %collective-permute-done.2), kind=kLoop, calls=%fused_computation.5 | loop fusion | flops 1310720 | bytes 1310720 | tf_op jit(solution)/shard_map/concatenate | solution.py:106
  35.4 0.6 fusion.4.a_0_
  36.1 2.2 %pad_maximum_fusion.a_1_ = bf16[512,1280]{1,0:T(8,128)(2,1)} fusion(bf16[128,1280]{1,0:T(8,128)(2,1)} %collective-permute-done.3, bf16[128,1280]{1,0:T(8,128)(2,1)} %collective-permute-done.2, bf16[128,1280]{1,0:T(8,128)(2,1)S(1)} %collective-permute-done, bf16[128,1280]{1,0:T(8,128)(2,1)S(1)} %get-tuple-element.37), kind=kLoop, calls=%fused_computation | loop fusion | flops 5242880 | bytes 2621440 | tf_op jit(solution)/shard_map/concatenate | solution.py:106
  38.4 1.5 %collective-permute-start.8 = (s32[4]{0:T(128)S(1)}, s32[4]{0:T(128)S(1)}, u32[]{:S(2)}, u32[]{:S(2)}) collective-permute-start(s32[4]{0:T(128)S(1)} %fusion.5), channel_id=1, source_target_pairs={{0,8},{4,12},{8,0},{12,4},{1,9},{5,13},{9,1},{13,5},{2,10},{6,14},... | collective-permute-start | bytes 56 | tf_op jit(solution)/shard_map/ppermute | solution.py:124
  39.9 1.1 copy-done.2
  40.9 21.5 %shard_map.64 = (f32[10,512,128]{2,1,0:T(8,128)}, f32[10,8,512]{2,1,0:T(8,128)}) custom-call(s32[4]{0:T(128)} %fusion.4.a_0_, bf16[512,1280]{1,0:T(8,128)(2,1)} %pad_maximum_fusion.a_1_, bf16[512,1280]{1,0:T(8,128)(2,1)} %a_2_.5, bf16[512,1280]{1,0:T(8,128)(2,1)} %collective-permute-done.4.a_3_, bf16[512,1280]{1,0:T(8,128)(2,1)} %a_4_.5, ...), custom_call_target="tpu_custom_call" | custom-call | tf_op jit(solution)/shard_map/pallas_call | solution.py:71
  62.4 0.5 collective-permute-done.8.a_0_
  63.0 0.6 copy-done.6
  63.5 13.1 %shard_map.65 = (bf16[10,256,128]{2,1,0:T(8,128)(2,1)}, f32[10,8,256]{2,1,0:T(8,128)}) custom-call(s32[4]{0:T(128)} %copy-done.6, bf16[256,1280]{1,0:T(8,128)(2,1)} %collective-permute-done.1.a_1_, bf16[512,1280]{1,0:T(8,128)(2,1)} %a_2_.5, bf16[512,1280]{1,0:T(8,128)(2,1)} %collective-permute-done.4.a_3_, bf16[512,1280]{1,0:T(8,128)(2,1)} %a_4_.5, ...), custom_call_target="tpu_custom_call" | custom-call | tf_op jit(solution)/shard_map/pallas_call | solution.py:71
  76.6 1.6 %collective-permute-start.10 = (bf16[10,256,128]{2,1,0:T(8,128)(2,1)}, bf16[10,256,128]{2,1,0:T(8,128)(2,1)S(1)}, u32[]{:S(2)}, u32[]{:S(2)}) collective-permute-start(bf16[10,256,128]{2,1,0:T(8,128)(2,1)} %get-tuple-element.20), channel_id=1, source_target_pairs={{0,8},{4,12},{8,0},{12,4},{1,9},{5,13},{9,1},{13,5},{2,10},{6,14},... | collective-permute-start | bytes 1966088 | tf_op jit(solution)/shard_map/ppermute | solution.py:171
  78.2 13.0 %shard_map.66 = (bf16[10,256,128]{2,1,0:T(8,128)(2,1)}, f32[10,8,256]{2,1,0:T(8,128)}) custom-call(s32[4]{0:T(128)} %copy-done.6, bf16[256,1280]{1,0:T(8,128)(2,1)} %collective-permute-done.11.a_1_, bf16[512,1280]{1,0:T(8,128)(2,1)} %a_2_.5, bf16[512,1280]{1,0:T(8,128)(2,1)} %collective-permute-done.4.a_3_, bf16[512,1280]{1,0:T(8,128)(2,1)} %a_4_.5, ...), custom_call_target="tpu_custom_call" | custom-call | tf_op jit(solution)/shard_map/pallas_call | solution.py:71
  91.3 0.6 collective-permute-start.13
  91.8 1.5 %collective-permute-start.9 = (f32[10,8,256]{2,1,0:T(8,128)S(1)}, f32[10,8,256]{2,1,0:T(8,128)S(1)}, u32[]{:S(2)}, u32[]{:S(2)}) collective-permute-start(f32[10,8,256]{2,1,0:T(8,128)S(1)} %copy-done.8), channel_id=1, source_target_pairs={{0,8},{4,12},{8,0},{12,4},{1,9},{5,13},{9,1},{13,5},{2,10},{6,14},... | collective-permute-start | bytes 245768 | tf_op jit(solution)/shard_map/ppermute | solution.py:171
  93.3 0.5 collective-permute-start.12
  94.0 16.3 %collective-permute-done.9 = f32[10,8,256]{2,1,0:T(8,128)S(1)} collective-permute-done((f32[10,8,256]{2,1,0:T(8,128)S(1)}, f32[10,8,256]{2,1,0:T(8,128)S(1)}, u32[]{:S(2)}, u32[]{:S(2)}) %collective-permute-start.9) | collective-permute-done | bytes 81952 | tf_op jit(solution)/shard_map/ppermute | solution.py:171
  110.2 0.9 collective-permute-done.12
  111.2 2.4 %divide_convert_fusion.1 = (bf16[10,256,128]{2,1,0:T(8,128)(2,1)S(1)}, bf16[10,256,128]{2,1,0:T(8,128)(2,1)S(1)}) fusion(bf16[10,256,128]{2,1,0:T(8,128)(2,1)S(1)} %collective-permute-done.10, f32[10,512,128]{2,1,0:T(8,128)S(1)} %copy-done.3, f32[10,256]{1,0:T(8,128)S(1)} %get-tuple-element.25, f32[10,256]{1,0:T(8,128)S(1)} %get-tuple-element.26, ...), kind=kLoop, calls=%fused_computation.3 | loop fusion | flops 3932160 | bytes 5304320 | tf_op jit(solution)/shard_map/convert_element_type | solution.py:181
  114.1 8.6 %collective-permute-start.14 = (bf16[128,1280]{0,1:T(8,128)(2,1)S(1)}, bf16[128,1280]{0,1:T(8,128)(2,1)S(1)}, u32[]{:S(2)}, u32[]{:S(2)}) collective-permute-start(bf16[128,1280]{0,1:T(8,128)(2,1)S(1)} %bitcast.46), channel_id=1, source_target_pairs={{0,3},{1,0},{2,1},{3,2},{4,7},{5,4},{6,5},{7,6},{8,11},{9,8},{10,9... | collective-permute-start | bytes 983048 | tf_op jit(solution)/shard_map/ppermute | solution.py:192
  123.6 0.6 collective-permute-start.16
  124.4 6.5 %collective-permute-done.14 = bf16[128,1280]{0,1:T(8,128)(2,1)S(1)} collective-permute-done((bf16[128,1280]{0,1:T(8,128)(2,1)S(1)}, bf16[128,1280]{0,1:T(8,128)(2,1)S(1)}, u32[]{:S(2)}, u32[]{:S(2)}) %collective-permute-start.14) | collective-permute-done | bytes 327712 | tf_op jit(solution)/shard_map/ppermute | solution.py:192
  131.1 16.6 %collective-permute-done.15 = bf16[128,1280]{0,1:T(8,128)(2,1)} collective-permute-done((bf16[128,1280]{0,1:T(8,128)(2,1)S(1)}, bf16[128,1280]{0,1:T(8,128)(2,1)}, u32[]{:S(2)}, u32[]{:S(2)}) %collective-permute-start.15) | collective-permute-done | bytes 327712 | tf_op jit(solution)/shard_map/ppermute | solution.py:192
  147.7 1.1 copy.26
  149.1 0.9 copy-done.4
  149.9 0.7 constant_dynamic-update-slice_fusion
  (51 shorter events, 3.5 us)
Async XLA Ops:
  0.0 34.9 %collective-permute-start.4 = (bf16[512,1280]{1,0:T(8,128)(2,1)}, bf16[512,1280]{1,0:T(8,128)(2,1)}, u32[]{:S(2)}, u32[]{:S(2)}) collective-permute-start(bf16[512,1280]{1,0:T(8,128)(2,1)} %a_2_.5), channel_id=1, source_target_pairs={{0,4},{4,0},{8,12},{12,8},{1,5},{5,1},{9,13},{13,9},{2,6},{6,2},{1... | collective-permute-start | bytes 3932168 | tf_op jit(solution)/shard_map/ppermute | solution.py:131
  0.5 8.9 %copy-start = (bf16[512,1280]{1,0:T(8,128)(2,1)S(1)}, bf16[512,1280]{1,0:T(8,128)(2,1)}, u32[]{:S(2)}) copy-start(bf16[512,1280]{1,0:T(8,128)(2,1)} %a_4_.5) | copy-start | bytes 3932164
  0.5 15.9 %copy-start.1 = (bf16[512,1280]{1,0:T(8,128)(2,1)S(1)}, bf16[512,1280]{1,0:T(8,128)(2,1)}, u32[]{:S(2)}) copy-start(bf16[512,1280]{1,0:T(8,128)(2,1)} %a_6_.5) | copy-start | bytes 3932164
  0.5 29.8 %copy-start.7 = (s32[1,6]{1,0:T(1,128)S(1)}, s32[1,6]{1,0:T(1,128)}, u32[]{:S(2)}) copy-start(s32[1,6]{1,0:T(1,128)} %param.11) | copy-start | bytes 76
  2.9 13.5 %collective-permute-start = (bf16[128,1280]{1,0:T(8,128)(2,1)}, bf16[128,1280]{1,0:T(8,128)(2,1)S(1)}, u32[]{:S(2)}, u32[]{:S(2)}) collective-permute-start(bf16[128,1280]{1,0:T(8,128)(2,1)} %get-tuple-element.38), channel_id=1, source_target_pairs={{0,1},{1,2},{2,3},{3,0},{4,5},{5,6},{6,7},{7,4},{8,9},{9,10},{10,1... | collective-permute-start | bytes 983048 | tf_op jit(solution)/shard_map/ppermute | solution.py:104
  5.5 24.8 %collective-permute-start.2 = (bf16[128,1280]{1,0:T(8,128)(2,1)}, bf16[128,1280]{1,0:T(8,128)(2,1)}, u32[]{:S(2)}, u32[]{:S(2)}) collective-permute-start(bf16[128,1280]{1,0:T(8,128)(2,1)} %get-tuple-element.40), channel_id=1, source_target_pairs={{0,2},{1,3},{2,0},{3,1},{4,6},{5,7},{6,4},{7,5},{8,10},{9,11},{10,... | collective-permute-start | bytes 983048 | tf_op jit(solution)/shard_map/ppermute | solution.py:104
  8.0 23.4 %collective-permute-start.3 = (bf16[128,1280]{1,0:T(8,128)(2,1)}, bf16[128,1280]{1,0:T(8,128)(2,1)}, u32[]{:S(2)}, u32[]{:S(2)}) collective-permute-start(bf16[128,1280]{1,0:T(8,128)(2,1)} %get-tuple-element.39), channel_id=1, source_target_pairs={{0,3},{1,0},{2,1},{3,2},{4,7},{5,4},{6,5},{7,6},{8,11},{9,8},{10,9... | collective-permute-start | bytes 983048 | tf_op jit(solution)/shard_map/ppermute | solution.py:104
  9.4 29.0 %collective-permute-start.5 = (bf16[512,1280]{1,0:T(8,128)(2,1)S(1)}, bf16[512,1280]{1,0:T(8,128)(2,1)}, u32[]{:S(2)}, u32[]{:S(2)}) collective-permute-start(bf16[512,1280]{1,0:T(8,128)(2,1)S(1)} %copy-done), channel_id=1, source_target_pairs={{0,4},{4,0},{8,12},{12,8},{1,5},{5,1},{9,13},{13,9},{2,6},{6,2},{1... | collective-permute-start | bytes 3932168 | tf_op jit(solution)/shard_map/ppermute | solution.py:131
  16.4 23.5 %collective-permute-start.6 = (bf16[512,1280]{1,0:T(8,128)(2,1)S(1)}, bf16[512,1280]{1,0:T(8,128)(2,1)S(1)}, u32[]{:S(2)}, u32[]{:S(2)}) collective-permute-start(bf16[512,1280]{1,0:T(8,128)(2,1)S(1)} %copy-done.1), channel_id=1, source_target_pairs={{0,4},{4,0},{8,12},{12,8},{1,5},{5,1},{9,13},{13,9},{2,6},{6,2},{1... | collective-permute-start | bytes 3932168 | tf_op jit(solution)/shard_map/ppermute | solution.py:131
  30.3 10.6 %collective-permute-start.7 = (bf16[512,1280]{1,0:T(8,128)(2,1)}, bf16[512,1280]{1,0:T(8,128)(2,1)}, u32[]{:S(2)}, u32[]{:S(2)}) collective-permute-start(bf16[512,1280]{1,0:T(8,128)(2,1)} %a_8_.5), channel_id=1, source_target_pairs={{0,4},{4,0},{8,12},{12,8},{1,5},{5,1},{9,13},{13,9},{2,6},{6,2},{1... | collective-permute-start | bytes 3932168 | tf_op jit(solution)/shard_map/ppermute | solution.py:131
  31.4 31.0 %collective-permute-start.1 = (bf16[256,1280]{1,0:T(8,128)(2,1)}, bf16[256,1280]{1,0:T(8,128)(2,1)}, u32[]{:S(2)}, u32[]{:S(2)}) collective-permute-start(bf16[256,1280]{1,0:T(8,128)(2,1)} %pad_maximum_fusion.1), channel_id=1, source_target_pairs={{0,8},{4,12},{8,0},{12,4},{1,9},{5,13},{9,1},{13,5},{2,10},{6,14},... | collective-permute-start | bytes 1966088 | tf_op jit(solution)/shard_map/ppermute | solution.py:126
  34.9 43.3 %collective-permute-start.11 = (bf16[256,1280]{1,0:T(8,128)(2,1)}, bf16[256,1280]{1,0:T(8,128)(2,1)}, u32[]{:S(2)}, u32[]{:S(2)}) collective-permute-start(bf16[256,1280]{1,0:T(8,128)(2,1)} %pad_maximum_fusion.2), channel_id=1, source_target_pairs={{0,8},{4,12},{8,0},{12,4},{1,9},{5,13},{9,1},{13,5},{2,10},{6,14},... | collective-permute-start | bytes 1966088 | tf_op jit(solution)/shard_map/ppermute | solution.py:127
  38.4 24.6 %collective-permute-start.8 = (s32[4]{0:T(128)S(1)}, s32[4]{0:T(128)S(1)}, u32[]{:S(2)}, u32[]{:S(2)}) collective-permute-start(s32[4]{0:T(128)S(1)} %fusion.5), channel_id=1, source_target_pairs={{0,8},{4,12},{8,0},{12,4},{1,9},{5,13},{9,1},{13,5},{2,10},{6,14},... | collective-permute-start | bytes 56 | tf_op jit(solution)/shard_map/ppermute | solution.py:124
  39.9 1.1 copy-start.2
  63.0 0.6 copy-start.6
  76.6 15.2 %copy-start.8 = (f32[10,8,256]{2,1,0:T(8,128)S(1)}, f32[10,8,256]{2,1,0:T(8,128)}, u32[]{:S(2)}) copy-start(f32[10,8,256]{2,1,0:T(8,128)} %get-tuple-element.19) | copy-start | bytes 245764
  76.6 17.2 %copy-start.5 = (f32[10,8,512]{2,1,0:T(8,128)S(1)}, f32[10,8,512]{2,1,0:T(8,128)}, u32[]{:S(2)}) copy-start(f32[10,8,512]{2,1,0:T(8,128)} %get-tuple-element.17) | copy-start | bytes 491524
  76.6 34.5 %collective-permute-start.10 = (bf16[10,256,128]{2,1,0:T(8,128)(2,1)}, bf16[10,256,128]{2,1,0:T(8,128)(2,1)S(1)}, u32[]{:S(2)}, u32[]{:S(2)}) collective-permute-start(bf16[10,256,128]{2,1,0:T(8,128)(2,1)} %get-tuple-element.20), channel_id=1, source_target_pairs={{0,8},{4,12},{8,0},{12,4},{1,9},{5,13},{9,1},{13,5},{2,10},{6,14},... | collective-permute-start | bytes 1966088 | tf_op jit(solution)/shard_map/ppermute | solution.py:171
  78.2 33.0 %copy-start.3 = (f32[10,512,128]{2,1,0:T(8,128)S(1)}, f32[10,512,128]{2,1,0:T(8,128)}, u32[]{:S(2)}) copy-start(f32[10,512,128]{2,1,0:T(8,128)} %get-tuple-element.16) | copy-start | bytes 7864324
  91.3 19.9 %collective-permute-start.13 = (bf16[10,256,128]{2,1,0:T(8,128)(2,1)}, bf16[10,256,128]{2,1,0:T(8,128)(2,1)S(1)}, u32[]{:S(2)}, u32[]{:S(2)}) collective-permute-start(bf16[10,256,128]{2,1,0:T(8,128)(2,1)} %get-tuple-element.22), channel_id=1, source_target_pairs={{0,8},{4,12},{8,0},{12,4},{1,9},{5,13},{9,1},{13,5},{2,10},{6,14},... | collective-permute-start | bytes 1966088 | tf_op jit(solution)/shard_map/ppermute | solution.py:171
  91.8 18.4 %collective-permute-start.9 = (f32[10,8,256]{2,1,0:T(8,128)S(1)}, f32[10,8,256]{2,1,0:T(8,128)S(1)}, u32[]{:S(2)}, u32[]{:S(2)}) collective-permute-start(f32[10,8,256]{2,1,0:T(8,128)S(1)} %copy-done.8), channel_id=1, source_target_pairs={{0,8},{4,12},{8,0},{12,4},{1,9},{5,13},{9,1},{13,5},{2,10},{6,14},... | collective-permute-start | bytes 245768 | tf_op jit(solution)/shard_map/ppermute | solution.py:171
  93.3 17.8 %collective-permute-start.12 = (f32[10,8,256]{2,1,0:T(8,128)}, f32[10,8,256]{2,1,0:T(8,128)S(1)}, u32[]{:S(2)}, u32[]{:S(2)}) collective-permute-start(f32[10,8,256]{2,1,0:T(8,128)} %get-tuple-element.21), channel_id=1, source_target_pairs={{0,8},{4,12},{8,0},{12,4},{1,9},{5,13},{9,1},{13,5},{2,10},{6,14},... | collective-permute-start | bytes 245768 | tf_op jit(solution)/shard_map/ppermute | solution.py:171
  114.1 16.8 %collective-permute-start.14 = (bf16[128,1280]{0,1:T(8,128)(2,1)S(1)}, bf16[128,1280]{0,1:T(8,128)(2,1)S(1)}, u32[]{:S(2)}, u32[]{:S(2)}) collective-permute-start(bf16[128,1280]{0,1:T(8,128)(2,1)S(1)} %bitcast.46), channel_id=1, source_target_pairs={{0,3},{1,0},{2,1},{3,2},{4,7},{5,4},{6,5},{7,6},{8,11},{9,8},{10,9... | collective-permute-start | bytes 983048 | tf_op jit(solution)/shard_map/ppermute | solution.py:192
  123.3 24.4 %collective-permute-start.15 = (bf16[128,1280]{0,1:T(8,128)(2,1)S(1)}, bf16[128,1280]{0,1:T(8,128)(2,1)}, u32[]{:S(2)}, u32[]{:S(2)}) collective-permute-start(bf16[128,1280]{0,1:T(8,128)(2,1)S(1)} %bitcast.48), channel_id=1, source_target_pairs={{0,2},{1,3},{2,0},{3,1},{4,6},{5,7},{6,4},{7,5},{8,10},{9,11},{10,... | collective-permute-start | bytes 983048 | tf_op jit(solution)/shard_map/ppermute | solution.py:192
  123.6 25.3 %collective-permute-start.16 = (bf16[128,1280]{0,1:T(8,128)(2,1)S(1)}, bf16[128,1280]{0,1:T(8,128)(2,1)S(1)}, u32[]{:S(2)}, u32[]{:S(2)}) collective-permute-start(bf16[128,1280]{0,1:T(8,128)(2,1)S(1)} %bitcast.47), channel_id=1, source_target_pairs={{0,1},{1,2},{2,3},{3,0},{4,5},{5,6},{6,7},{7,4},{8,9},{9,10},{10,1... | collective-permute-start | bytes 983048 | tf_op jit(solution)/shard_map/ppermute | solution.py:192
  148.9 1.1 copy-start.4

commit v19 on v17

--- a/solution.py
+++ b/solution.py
@@ -177,17 +177,15 @@
             local_out[:, near] * weight_a + far_out.astype(jnp.float32) * weight_b
         ) / (weight_a + weight_b)
         mixed_halves.append(mixed.astype(jnp.bfloat16))
-    rows_all = query_block.shape[0]
-    heads_out = jnp.transpose(jnp.concatenate(mixed_halves, axis=1), (1, 0, 2)).reshape(
-        rows_all, head_width
-    )
 
     rows = queries.shape[0]
     result = jnp.zeros((rows, queries.shape[1]), jnp.bfloat16)
     for d in range(sp_count):
-        piece = heads_out[d * rows : (d + 1) * rows]
+        start = d * rows
+        piece = mixed_halves[start // half][:, start % half : start % half + rows]
         if d:
             piece = lax.ppermute(piece, "sp", [(i, (i - d) % sp_count) for i in range(sp_count)])
+        piece = jnp.transpose(piece, (1, 0, 2)).reshape(rows, head_width)
         columns = ((sp_place + d) % sp_count) * head_width
         result = lax.dynamic_update_slice_in_dim(result, piece, columns, 1)
     return result

time: 151 us -> 149 us (0.987)
    ppermute x1, waiting for transfers between devices: 0.87 us -> 13.8 us  [local(): lax.ppermute(query_block[:half], 'seq', back)]
    ppermute x1, waiting for transfers between devices: 14.3 us -> 1.59 us  [local(): lax.ppermute(query_block[half:], 'seq', back)]
    transpose x0 -> x4, local copies, waits for them, and re-layouts: none -> 1.84 us  [local(): piece = jnp.transpose(piece, (1, 0, 2)).reshape(rows, head_width)]
  transfers between devices with their start and end apart: 17 -> 17, of which waited for: 6 -> 7; matrix products, arithmetic and copies ran while one was open for 6% -> 6% of each run, Pallas kernels for 32% -> 32%
where the time goes in v19:
time: 149 us
  waiting for transfers between devices  57.4 us (39%)
  Pallas kernels  47.5 us (32%)
  starting transfers between devices  25.7 us (17%)
  other arithmetic  9.85 us (7%)
  local copies, waits for them, and re-layouts  8.11 us (5%)
    pallas_call x3, Pallas kernels, attend_partial(): pl.pallas_call(lambda *a: partial_kernel(nsrc, group, *a), grid_spec=grid...  47.5 us
    ppermute x3, waiting for transfers between devices, local(): lax.ppermute(piece, 'sp', [(i, (i - d) % sp_count) for i in range(sp_coun...  23.6 us
    ppermute x3, waiting for transfers between devices, local(): lax.ppermute(piece, 'sp', [(i, (i + d) % sp_count) for i in range(sp_coun...  16.3 us
    ppermute x1, waiting for transfers between devices, local(): lax.ppermute(query_block[:half], 'seq', back)  13.8 us
    ppermute x3, starting transfers between devices, local(): lax.ppermute(piece, 'sp', [(i, (i - d) % sp_count) for i in range(sp_coun...  9.21 us
    ppermute x3, starting transfers between devices, local(): lax.ppermute(piece, 'sp', [(i, (i + d) % sp_count) for i in range(sp_coun...  6.98 us
    ppermute x4, starting transfers between devices, local(): far_out, far_lse = lax.ppermute((far_out, far_lse), 'seq', forth)  4.83 us
    convert_element_type x1, other arithmetic, local(): mixed_halves.append(mixed.astype(jnp.bfloat16))  4.58 us
  transfers between devices with their start and end apart: 17, of which 7 were waited for; matrix products, arithmetic and copies ran while one was open for 6% of the time, Pallas kernels for 32%

profile of v19, /device:TPU:0, one launch (start us, length us, event | category | flops | bytes accessed | tf_op | source)
XLA Modules:
  0.0 148.8 jit_solution(6111301015109908197)
XLA Ops:
  0.0 2.4 %constant_dynamic-slice_fusion.1 = (bf16[128,1280]{1,0:T(8,128)(2,1)}, bf16[128,1280]{1,0:T(8,128)(2,1)}, bf16[128,1280]{1,0:T(8,128)(2,1)S(1)}, bf16[128,1280]{1,0:T(8,128)(2,1)}) fusion(bf16[128,5120]{1,0:T(8,128)(2,1)} %param.6, s32[]{:T(128)S(6)} %select_n.59, s32[]{:T(128)S(6)} %select_n.57, s32[]{:T(128)S(6)} %select_n.55, s32[]{:T(128)S(6)} %select_n.61), kind=kLoop, calls=%fused_computation.21 | loop fusion | bytes 2621456 | tf_op jit(solution)/shard_map/dynamic_slice | solution.py:102
  2.4 3.0 %collective-permute-start = (bf16[128,1280]{1,0:T(8,128)(2,1)}, bf16[128,1280]{1,0:T(8,128)(2,1)S(1)}, u32[]{:S(2)}, u32[]{:S(2)}) collective-permute-start(bf16[128,1280]{1,0:T(8,128)(2,1)} %get-tuple-element.28), channel_id=1, source_target_pairs={{0,1},{1,2},{2,3},{3,0},{4,5},{5,6},{6,7},{7,4},{8,9},{9,10},{10,1... | collective-permute-start | bytes 983048 | tf_op jit(solution)/shard_map/ppermute | solution.py:104
  5.4 2.6 %collective-permute-start.1 = (bf16[128,1280]{1,0:T(8,128)(2,1)}, bf16[128,1280]{1,0:T(8,128)(2,1)}, u32[]{:S(2)}, u32[]{:S(2)}) collective-permute-start(bf16[128,1280]{1,0:T(8,128)(2,1)} %get-tuple-element.27), channel_id=1, source_target_pairs={{0,2},{1,3},{2,0},{3,1},{4,6},{5,7},{6,4},{7,5},{8,10},{9,11},{10,... | collective-permute-start | bytes 983048 | tf_op jit(solution)/shard_map/ppermute | solution.py:104
  8.0 1.3 collective-permute-start.2
  9.8 1.5 %collective-permute-start.7 = (s32[4]{0:T(128)S(1)}, s32[4]{0:T(128)S(1)}, u32[]{:S(2)}, u32[]{:S(2)}) collective-permute-start(s32[4]{0:T(128)S(1)} %fusion.5), channel_id=1, source_target_pairs={{0,8},{4,12},{8,0},{12,4},{1,9},{5,13},{9,1},{13,5},{2,10},{6,14},... | collective-permute-start | bytes 56 | tf_op jit(solution)/shard_map/ppermute | solution.py:124
  11.3 2.0 %collective-permute-done.7.a_0_ = s32[4]{0:T(128)S(1)} collective-permute-done((s32[4]{0:T(128)S(1)}, s32[4]{0:T(128)S(1)}, u32[]{:S(2)}, u32[]{:S(2)}) %collective-permute-start.7) | collective-permute-done | bytes 48 | tf_op jit(solution)/shard_map/ppermute | solution.py:124
  13.3 3.0 %collective-permute-done = bf16[128,1280]{1,0:T(8,128)(2,1)S(1)} collective-permute-done((bf16[128,1280]{1,0:T(8,128)(2,1)}, bf16[128,1280]{1,0:T(8,128)(2,1)S(1)}, u32[]{:S(2)}, u32[]{:S(2)}) %collective-permute-start) | collective-permute-done | bytes 327712 | tf_op jit(solution)/shard_map/ppermute | solution.py:104
  16.4 13.3 %collective-permute-done.1 = bf16[128,1280]{1,0:T(8,128)(2,1)} collective-permute-done((bf16[128,1280]{1,0:T(8,128)(2,1)}, bf16[128,1280]{1,0:T(8,128)(2,1)}, u32[]{:S(2)}, u32[]{:S(2)}) %collective-permute-start.1) | collective-permute-done | bytes 327712 | tf_op jit(solution)/shard_map/ppermute | solution.py:104
  29.7 1.6 %collective-permute-start.8 = (bf16[256,1280]{1,0:T(8,128)(2,1)S(1)}, bf16[256,1280]{1,0:T(8,128)(2,1)}, u32[]{:S(2)}, u32[]{:S(2)}) collective-permute-start(bf16[256,1280]{1,0:T(8,128)(2,1)S(1)} %pad_maximum_fusion.1), channel_id=1, source_target_pairs={{0,8},{4,12},{8,0},{12,4},{1,9},{5,13},{9,1},{13,5},{2,10},{6,14},... | collective-permute-start | bytes 1966088 | tf_op jit(solution)/shard_map/ppermute | solution.py:126
  31.3 1.9 %pad_maximum_fusion.2 = bf16[256,1280]{1,0:T(8,128)(2,1)} fusion(bf16[128,1280]{1,0:T(8,128)(2,1)} %collective-permute-done.2, bf16[128,1280]{1,0:T(8,128)(2,1)} %collective-permute-done.1), kind=kLoop, calls=%fused_computation.4 | loop fusion | flops 1310720 | bytes 1310720 | tf_op jit(solution)/shard_map/concatenate | solution.py:106
  33.3 13.8 %collective-permute-done.8.a_1_ = bf16[256,1280]{1,0:T(8,128)(2,1)} collective-permute-done((bf16[256,1280]{1,0:T(8,128)(2,1)S(1)}, bf16[256,1280]{1,0:T(8,128)(2,1)}, u32[]{:S(2)}, u32[]{:S(2)}) %collective-permute-start.8) | collective-permute-done | bytes 655392 | tf_op jit(solution)/shard_map/ppermute | solution.py:126
  47.0 1.5 %collective-permute-start.12 = (bf16[256,1280]{1,0:T(8,128)(2,1)}, bf16[256,1280]{1,0:T(8,128)(2,1)}, u32[]{:S(2)}, u32[]{:S(2)}) collective-permute-start(bf16[256,1280]{1,0:T(8,128)(2,1)} %pad_maximum_fusion.2), channel_id=1, source_target_pairs={{0,8},{4,12},{8,0},{12,4},{1,9},{5,13},{9,1},{13,5},{2,10},{6,14},... | collective-permute-start | bytes 1966088 | tf_op jit(solution)/shard_map/ppermute | solution.py:127
  48.6 13.0 %shard_map.65 = (bf16[10,256,128]{2,1,0:T(8,128)(2,1)}, f32[10,8,256]{2,1,0:T(8,128)}) custom-call(s32[4]{0:T(128)} %copy-done.3, bf16[256,1280]{1,0:T(8,128)(2,1)} %collective-permute-done.8.a_1_, bf16[512,1280]{1,0:T(8,128)(2,1)} %a_2_.5, bf16[512,1280]{1,0:T(8,128)(2,1)} %collective-permute-done.3.a_3_, bf16[512,1280]{1,0:T(8,128)(2,1)} %a_4_.5, ...), custom_call_target="tpu_custom_call" | custom-call | tf_op jit(solution)/shard_map/pallas_call | solution.py:71
  61.6 0.6 collective-permute-start.10
  62.1 1.6 %collective-permute-done.12.a_1_ = bf16[256,1280]{1,0:T(8,128)(2,1)} collective-permute-done((bf16[256,1280]{1,0:T(8,128)(2,1)}, bf16[256,1280]{1,0:T(8,128)(2,1)}, u32[]{:S(2)}, u32[]{:S(2)}) %collective-permute-start.12) | collective-permute-done | bytes 655392 | tf_op jit(solution)/shard_map/ppermute | solution.py:127
  63.7 12.9 %shard_map.66 = (bf16[10,256,128]{2,1,0:T(8,128)(2,1)}, f32[10,8,256]{2,1,0:T(8,128)}) custom-call(s32[4]{0:T(128)} %copy-done.3, bf16[256,1280]{1,0:T(8,128)(2,1)} %collective-permute-done.12.a_1_, bf16[512,1280]{1,0:T(8,128)(2,1)} %a_2_.5, bf16[512,1280]{1,0:T(8,128)(2,1)} %collective-permute-done.3.a_3_, bf16[512,1280]{1,0:T(8,128)(2,1)} %a_4_.5, ...), custom_call_target="tpu_custom_call" | custom-call | tf_op jit(solution)/shard_map/pallas_call | solution.py:71
  76.6 2.3 %collective-permute-start.14 = (bf16[10,256,128]{2,1,0:T(8,128)(2,1)}, bf16[10,256,128]{2,1,0:T(8,128)(2,1)S(1)}, u32[]{:S(2)}, u32[]{:S(2)}) collective-permute-start(bf16[10,256,128]{2,1,0:T(8,128)(2,1)} %get-tuple-element.16), channel_id=1, source_target_pairs={{0,8},{4,12},{8,0},{12,4},{1,9},{5,13},{9,1},{13,5},{2,10},{6,14},... | collective-permute-start | bytes 1966088 | tf_op jit(solution)/shard_map/ppermute | solution.py:169
  78.9 0.7 fusion.4.a_0_
  79.6 2.0 %collective-permute-start.13 = (f32[10,8,256]{2,1,0:T(8,128)}, f32[10,8,256]{2,1,0:T(8,128)S(1)}, u32[]{:S(2)}, u32[]{:S(2)}) collective-permute-start(f32[10,8,256]{2,1,0:T(8,128)} %get-tuple-element.15), channel_id=1, source_target_pairs={{0,8},{4,12},{8,0},{12,4},{1,9},{5,13},{9,1},{13,5},{2,10},{6,14},... | collective-permute-start | bytes 245768 | tf_op jit(solution)/shard_map/ppermute | solution.py:169
  81.6 2.2 %pad_maximum_fusion.a_1_ = bf16[512,1280]{1,0:T(8,128)(2,1)} fusion(bf16[128,1280]{1,0:T(8,128)(2,1)} %collective-permute-done.2, bf16[128,1280]{1,0:T(8,128)(2,1)} %collective-permute-done.1, bf16[128,1280]{1,0:T(8,128)(2,1)S(1)} %collective-permute-done, bf16[128,1280]{1,0:T(8,128)(2,1)S(1)} %get-tuple-element.29), kind=kLoop, calls=%fused_computation | loop fusion | flops 5242880 | bytes 2621440 | tf_op jit(solution)/shard_map/concatenate | solution.py:106
  83.8 21.6 %shard_map.64 = (f32[10,512,128]{2,1,0:T(8,128)}, f32[10,8,512]{2,1,0:T(8,128)}) custom-call(s32[4]{0:T(128)} %fusion.4.a_0_, bf16[512,1280]{1,0:T(8,128)(2,1)} %pad_maximum_fusion.a_1_, bf16[512,1280]{1,0:T(8,128)(2,1)} %a_2_.5, bf16[512,1280]{1,0:T(8,128)(2,1)} %collective-permute-done.3.a_3_, bf16[512,1280]{1,0:T(8,128)(2,1)} %a_4_.5, ...), custom_call_target="tpu_custom_call" | custom-call | tf_op jit(solution)/shard_map/pallas_call | solution.py:71
  105.4 1.0 copy.19
  106.6 4.6 %divide_convert_fusion = (bf16[10,256,128]{2,1,0:T(8,128)(2,1)S(1)}, bf16[10,256,128]{2,1,0:T(8,128)(2,1)S(1)}) fusion(bf16[10,256,128]{2,1,0:T(8,128)(2,1)S(1)} %collective-permute-done.14, f32[10,512,128]{2,1,0:T(8,128)} %get-tuple-element.11, f32[10,256]{1,0:T(8,128)S(1)} %get-tuple-element.19, f32[10,256]{1,0:T(8,128)S(1)} %get-tuple-element.20, ...), kind=kLoop, calls=%fused_computation.1 | loop fusion | flops 3932160 | bytes 5304320 | tf_op jit(solution)/shard_map/convert_element_type | solution.py:179
  111.2 8.6 %collective-permute-start.11 = (bf16[10,128,128]{2,1,0:T(8,128)(2,1)S(1)}, bf16[10,128,128]{2,1,0:T(8,128)(2,1)S(1)}, u32[]{:S(2)}, u32[]{:S(2)}) collective-permute-start(bf16[10,128,128]{2,1,0:T(8,128)(2,1)S(1)} %get-tuple-element.33), channel_id=1, source_target_pairs={{0,3},{1,0},{2,1},{3,2},{4,7},{5,4},{6,5},{7,6},{8,11},{9,8},{10,9... | collective-permute-start | bytes 983048 | tf_op jit(solution)/shard_map/ppermute | solution.py:187
  119.9 0.6 collective-permute-start.16
  120.5 0.2 copy.20
  121.0 6.9 %collective-permute-done.11 = bf16[10,128,128]{2,1,0:T(8,128)(2,1)S(1)} collective-permute-done((bf16[10,128,128]{2,1,0:T(8,128)(2,1)S(1)}, bf16[10,128,128]{2,1,0:T(8,128)(2,1)S(1)}, u32[]{:S(2)}, u32[]{:S(2)}) %collective-permute-start.11) | collective-permute-done | bytes 327712 | tf_op jit(solution)/shard_map/ppermute | solution.py:187
  128.3 16.8 %collective-permute-done.15 = bf16[10,128,128]{2,1,0:T(8,128)(2,1)} collective-permute-done((bf16[10,128,128]{2,1,0:T(8,128)(2,1)S(1)}, bf16[10,128,128]{2,1,0:T(8,128)(2,1)}, u32[]{:S(2)}, u32[]{:S(2)}) %collective-permute-start.15) | collective-permute-done | bytes 327712 | tf_op jit(solution)/shard_map/ppermute | solution.py:187
  145.1 1.2 copy.25
  146.5 0.2 copy.27
  147.0 1.0 copy-done.2
  148.0 0.7 constant_dynamic-update-slice_fusion
  (45 shorter events, 1.9 us)
Async XLA Ops:
  0.0 9.4 %copy-start = (bf16[512,1280]{1,0:T(8,128)(2,1)S(1)}, bf16[512,1280]{1,0:T(8,128)(2,1)}, u32[]{:S(2)}) copy-start(bf16[512,1280]{1,0:T(8,128)(2,1)} %a_2_.5) | copy-start | bytes 3932164
  0.0 9.5 %copy-start.4 = (s32[1,6]{1,0:T(1,128)S(1)}, s32[1,6]{1,0:T(1,128)}, u32[]{:S(2)}) copy-start(s32[1,6]{1,0:T(1,128)} %param.11) | copy-start | bytes 76
  0.0 13.3 %copy-start.1 = (bf16[512,1280]{1,0:T(8,128)(2,1)S(1)}, bf16[512,1280]{1,0:T(8,128)(2,1)}, u32[]{:S(2)}) copy-start(bf16[512,1280]{1,0:T(8,128)(2,1)} %a_4_.5) | copy-start | bytes 3932164
  2.4 14.0 %collective-permute-start = (bf16[128,1280]{1,0:T(8,128)(2,1)}, bf16[128,1280]{1,0:T(8,128)(2,1)S(1)}, u32[]{:S(2)}, u32[]{:S(2)}) collective-permute-start(bf16[128,1280]{1,0:T(8,128)(2,1)} %get-tuple-element.28), channel_id=1, source_target_pairs={{0,1},{1,2},{2,3},{3,0},{4,5},{5,6},{6,7},{7,4},{8,9},{9,10},{10,1... | collective-permute-start | bytes 983048 | tf_op jit(solution)/shard_map/ppermute | solution.py:104
  5.4 24.2 %collective-permute-start.1 = (bf16[128,1280]{1,0:T(8,128)(2,1)}, bf16[128,1280]{1,0:T(8,128)(2,1)}, u32[]{:S(2)}, u32[]{:S(2)}) collective-permute-start(bf16[128,1280]{1,0:T(8,128)(2,1)} %get-tuple-element.27), channel_id=1, source_target_pairs={{0,2},{1,3},{2,0},{3,1},{4,6},{5,7},{6,4},{7,5},{8,10},{9,11},{10,... | collective-permute-start | bytes 983048 | tf_op jit(solution)/shard_map/ppermute | solution.py:104
  8.0 21.7 %collective-permute-start.2 = (bf16[128,1280]{1,0:T(8,128)(2,1)}, bf16[128,1280]{1,0:T(8,128)(2,1)}, u32[]{:S(2)}, u32[]{:S(2)}) collective-permute-start(bf16[128,1280]{1,0:T(8,128)(2,1)} %get-tuple-element.30), channel_id=1, source_target_pairs={{0,3},{1,0},{2,1},{3,2},{4,7},{5,4},{6,5},{7,6},{8,11},{9,8},{10,9... | collective-permute-start | bytes 983048 | tf_op jit(solution)/shard_map/ppermute | solution.py:104
  9.4 39.2 %collective-permute-start.3 = (bf16[512,1280]{1,0:T(8,128)(2,1)S(1)}, bf16[512,1280]{1,0:T(8,128)(2,1)}, u32[]{:S(2)}, u32[]{:S(2)}) collective-permute-start(bf16[512,1280]{1,0:T(8,128)(2,1)S(1)} %copy-done), channel_id=1, source_target_pairs={{0,4},{4,0},{8,12},{12,8},{1,5},{5,1},{9,13},{13,9},{2,6},{6,2},{1... | collective-permute-start | bytes 3932168 | tf_op jit(solution)/shard_map/ppermute | solution.py:131
  9.8 3.6 %collective-permute-start.7 = (s32[4]{0:T(128)S(1)}, s32[4]{0:T(128)S(1)}, u32[]{:S(2)}, u32[]{:S(2)}) collective-permute-start(s32[4]{0:T(128)S(1)} %fusion.5), channel_id=1, source_target_pairs={{0,8},{4,12},{8,0},{12,4},{1,9},{5,13},{9,1},{13,5},{2,10},{6,14},... | collective-permute-start | bytes 56 | tf_op jit(solution)/shard_map/ppermute | solution.py:124
  13.3 20.0 %copy-start.3 = (s32[4]{0:T(128)}, s32[4]{0:T(128)S(1)}, u32[]{:S(2)}) copy-start(s32[4]{0:T(128)S(1)} %collective-permute-done.7.a_0_) | copy-start | bytes 52
  13.3 35.3 %collective-permute-start.4 = (bf16[512,1280]{1,0:T(8,128)(2,1)S(1)}, bf16[512,1280]{1,0:T(8,128)(2,1)}, u32[]{:S(2)}, u32[]{:S(2)}) collective-permute-start(bf16[512,1280]{1,0:T(8,128)(2,1)S(1)} %copy-done.1), channel_id=1, source_target_pairs={{0,4},{4,0},{8,12},{12,8},{1,5},{5,1},{9,13},{13,9},{2,6},{6,2},{1... | collective-permute-start | bytes 3932168 | tf_op jit(solution)/shard_map/ppermute | solution.py:131
  16.3 32.2 %collective-permute-start.5 = (bf16[512,1280]{1,0:T(8,128)(2,1)}, bf16[512,1280]{1,0:T(8,128)(2,1)}, u32[]{:S(2)}, u32[]{:S(2)}) collective-permute-start(bf16[512,1280]{1,0:T(8,128)(2,1)} %a_6_.5), channel_id=1, source_target_pairs={{0,4},{4,0},{8,12},{12,8},{1,5},{5,1},{9,13},{13,9},{2,6},{6,2},{1... | collective-permute-start | bytes 3932168 | tf_op jit(solution)/shard_map/ppermute | solution.py:131
  29.7 18.9 %collective-permute-start.6 = (bf16[512,1280]{1,0:T(8,128)(2,1)}, bf16[512,1280]{1,0:T(8,128)(2,1)}, u32[]{:S(2)}, u32[]{:S(2)}) collective-permute-start(bf16[512,1280]{1,0:T(8,128)(2,1)} %a_8_.5), channel_id=1, source_target_pairs={{0,4},{4,0},{8,12},{12,8},{1,5},{5,1},{9,13},{13,9},{2,6},{6,2},{1... | collective-permute-start | bytes 3932168 | tf_op jit(solution)/shard_map/ppermute | solution.py:131
  29.7 17.3 %collective-permute-start.8 = (bf16[256,1280]{1,0:T(8,128)(2,1)S(1)}, bf16[256,1280]{1,0:T(8,128)(2,1)}, u32[]{:S(2)}, u32[]{:S(2)}) collective-permute-start(bf16[256,1280]{1,0:T(8,128)(2,1)S(1)} %pad_maximum_fusion.1), channel_id=1, source_target_pairs={{0,8},{4,12},{8,0},{12,4},{1,9},{5,13},{9,1},{13,5},{2,10},{6,14},... | collective-permute-start | bytes 1966088 | tf_op jit(solution)/shard_map/ppermute | solution.py:126
  47.0 16.7 %collective-permute-start.12 = (bf16[256,1280]{1,0:T(8,128)(2,1)}, bf16[256,1280]{1,0:T(8,128)(2,1)}, u32[]{:S(2)}, u32[]{:S(2)}) collective-permute-start(bf16[256,1280]{1,0:T(8,128)(2,1)} %pad_maximum_fusion.2), channel_id=1, source_target_pairs={{0,8},{4,12},{8,0},{12,4},{1,9},{5,13},{9,1},{13,5},{2,10},{6,14},... | collective-permute-start | bytes 1966088 | tf_op jit(solution)/shard_map/ppermute | solution.py:127
  61.6 18.0 %copy-start.5 = (f32[10,8,256]{2,1,0:T(8,128)S(1)}, f32[10,8,256]{2,1,0:T(8,128)}, u32[]{:S(2)}) copy-start(f32[10,8,256]{2,1,0:T(8,128)} %get-tuple-element.13) | copy-start | bytes 245764
  61.6 45.0 %collective-permute-start.10 = (bf16[10,256,128]{2,1,0:T(8,128)(2,1)}, bf16[10,256,128]{2,1,0:T(8,128)(2,1)S(1)}, u32[]{:S(2)}, u32[]{:S(2)}) collective-permute-start(bf16[10,256,128]{2,1,0:T(8,128)(2,1)} %get-tuple-element.14), channel_id=1, source_target_pairs={{0,8},{4,12},{8,0},{12,4},{1,9},{5,13},{9,1},{13,5},{2,10},{6,14},... | collective-permute-start | bytes 1966088 | tf_op jit(solution)/shard_map/ppermute | solution.py:169
  76.6 29.9 %collective-permute-start.14 = (bf16[10,256,128]{2,1,0:T(8,128)(2,1)}, bf16[10,256,128]{2,1,0:T(8,128)(2,1)S(1)}, u32[]{:S(2)}, u32[]{:S(2)}) collective-permute-start(bf16[10,256,128]{2,1,0:T(8,128)(2,1)} %get-tuple-element.16), channel_id=1, source_target_pairs={{0,8},{4,12},{8,0},{12,4},{1,9},{5,13},{9,1},{13,5},{2,10},{6,14},... | collective-permute-start | bytes 1966088 | tf_op jit(solution)/shard_map/ppermute | solution.py:169
  79.6 26.9 %collective-permute-start.9 = (f32[10,8,256]{2,1,0:T(8,128)S(1)}, f32[10,8,256]{2,1,0:T(8,128)S(1)}, u32[]{:S(2)}, u32[]{:S(2)}) collective-permute-start(f32[10,8,256]{2,1,0:T(8,128)S(1)} %copy-done.5), channel_id=1, source_target_pairs={{0,8},{4,12},{8,0},{12,4},{1,9},{5,13},{9,1},{13,5},{2,10},{6,14},... | collective-permute-start | bytes 245768 | tf_op jit(solution)/shard_map/ppermute | solution.py:169
  79.6 26.9 %collective-permute-start.13 = (f32[10,8,256]{2,1,0:T(8,128)}, f32[10,8,256]{2,1,0:T(8,128)S(1)}, u32[]{:S(2)}, u32[]{:S(2)}) collective-permute-start(f32[10,8,256]{2,1,0:T(8,128)} %get-tuple-element.15), channel_id=1, source_target_pairs={{0,8},{4,12},{8,0},{12,4},{1,9},{5,13},{9,1},{13,5},{2,10},{6,14},... | collective-permute-start | bytes 245768 | tf_op jit(solution)/shard_map/ppermute | solution.py:169
  111.2 16.7 %collective-permute-start.11 = (bf16[10,128,128]{2,1,0:T(8,128)(2,1)S(1)}, bf16[10,128,128]{2,1,0:T(8,128)(2,1)S(1)}, u32[]{:S(2)}, u32[]{:S(2)}) collective-permute-start(bf16[10,128,128]{2,1,0:T(8,128)(2,1)S(1)} %get-tuple-element.33), channel_id=1, source_target_pairs={{0,3},{1,0},{2,1},{3,2},{4,7},{5,4},{6,5},{7,6},{8,11},{9,8},{10,9... | collective-permute-start | bytes 983048 | tf_op jit(solution)/shard_map/ppermute | solution.py:187
  119.8 25.3 %collective-permute-start.15 = (bf16[10,128,128]{2,1,0:T(8,128)(2,1)S(1)}, bf16[10,128,128]{2,1,0:T(8,128)(2,1)}, u32[]{:S(2)}, u32[]{:S(2)}) collective-permute-start(bf16[10,128,128]{2,1,0:T(8,128)(2,1)S(1)} %get-tuple-element.32), channel_id=1, source_target_pairs={{0,2},{1,3},{2,0},{3,1},{4,6},{5,7},{6,4},{7,5},{8,10},{9,11},{10,... | collective-permute-start | bytes 983048 | tf_op jit(solution)/shard_map/ppermute | solution.py:187
  119.9 26.6 %collective-permute-start.16 = (bf16[10,128,128]{2,1,0:T(8,128)(2,1)S(1)}, bf16[10,128,128]{2,1,0:T(8,128)(2,1)S(1)}, u32[]{:S(2)}, u32[]{:S(2)}) collective-permute-start(bf16[10,128,128]{2,1,0:T(8,128)(2,1)S(1)} %get-tuple-element.31), channel_id=1, source_target_pairs={{0,1},{1,2},{2,3},{3,0},{4,5},{5,6},{6,7},{7,4},{8,9},{9,10},{10,1... | collective-permute-start | bytes 983048 | tf_op jit(solution)/shard_map/ppermute | solution.py:187
  147.0 1.1 copy-start.2

commit v20 on v19

--- a/solution.py
+++ b/solution.py
@@ -166,10 +166,10 @@
         far_out, far_lse = attend_partial(
             got_flags, got_query, remote_keys, remote_values, jnp.bfloat16
         )
-        far_out, far_lse = lax.ppermute((far_out, far_lse), "seq", forth)
+        far_out, far_lse = lax.ppermute((far_out, far_lse[:, 0, :]), "seq", forth)
         near = slice(k * half, (k + 1) * half)
         lse_a = local_lse[:, 0, near][:, :, None]
-        lse_b = far_lse[:, 0, :][:, :, None]
+        lse_b = far_lse[:, :, None]
         top = jnp.maximum(lse_a, lse_b)
         weight_a = jnp.exp(lse_a - top)
         weight_b = jnp.exp(lse_b - top)

time: 149 us -> 151 us (1.013)
  local copies, waits for them, and re-layouts: 8.11 us -> 9.89 us
    slice x2, local copies, waits for them, and re-layouts: 0.01 us -> 1.79 us  [local(): far_out, far_lse = lax.ppermute((far_out, far_lse[:, 0, :]), 'seq', forth)]
  transfers between devices with their start and end apart: 17 -> 17, of which waited for: 7 -> 7; matrix products, arithmetic and copies ran while one was open for 6% -> 7% of each run, Pallas kernels for 32% -> 32%
where the time goes in v20:
time: 151 us
  waiting for transfers between devices  57.4 us (38%)
  Pallas kernels  47.8 us (32%)
  starting transfers between devices  25.7 us (17%)
  local copies, waits for them, and re-layouts  9.89 us (7%)
  other arithmetic  9.78 us (6%)
    pallas_call x3, Pallas kernels, attend_partial(): pl.pallas_call(lambda *a: partial_kernel(nsrc, group, *a), grid_spec=grid...  47.8 us
    ppermute x3, waiting for transfers between devices, local(): lax.ppermute(piece, 'sp', [(i, (i - d) % sp_count) for i in range(sp_coun...  23.8 us
    ppermute x3, waiting for transfers between devices, local(): lax.ppermute(piece, 'sp', [(i, (i + d) % sp_count) for i in range(sp_coun...  16.3 us
    ppermute x1, waiting for transfers between devices, local(): lax.ppermute(query_block[:half], 'seq', back)  13.8 us
    ppermute x3, starting transfers between devices, local(): lax.ppermute(piece, 'sp', [(i, (i - d) % sp_count) for i in range(sp_coun...  9.21 us
    ppermute x3, starting transfers between devices, local(): lax.ppermute(piece, 'sp', [(i, (i + d) % sp_count) for i in range(sp_coun...  6.98 us
    ppermute x4, starting transfers between devices, local(): far_out, far_lse = lax.ppermute((far_out, far_lse[:, 0, :]), 'seq', forth)  4.87 us
    convert_element_type x1, other arithmetic, local(): mixed_halves.append(mixed.astype(jnp.bfloat16))  4.58 us
  transfers between devices with their start and end apart: 17, of which 7 were waited for; matrix products, arithmetic and copies ran while one was open for 7% of the time, Pallas kernels for 32%

profile of v20, /device:TPU:0, one launch (start us, length us, event | category | flops | bytes accessed | tf_op | source)
XLA Modules:
  0.0 150.8 jit_solution(5416047157592212630)
XLA Ops:
  0.0 2.4 %constant_dynamic-slice_fusion.1 = (bf16[128,1280]{1,0:T(8,128)(2,1)}, bf16[128,1280]{1,0:T(8,128)(2,1)}, bf16[128,1280]{1,0:T(8,128)(2,1)S(1)}, bf16[128,1280]{1,0:T(8,128)(2,1)}) fusion(bf16[128,5120]{1,0:T(8,128)(2,1)} %param.6, s32[]{:T(128)S(6)} %select_n.59, s32[]{:T(128)S(6)} %select_n.57, s32[]{:T(128)S(6)} %select_n.55, s32[]{:T(128)S(6)} %select_n.61), kind=kLoop, calls=%fused_computation.23 | loop fusion | bytes 2621456 | tf_op jit(solution)/shard_map/dynamic_slice | solution.py:102
  2.4 3.0 %collective-permute-start = (bf16[128,1280]{1,0:T(8,128)(2,1)}, bf16[128,1280]{1,0:T(8,128)(2,1)S(1)}, u32[]{:S(2)}, u32[]{:S(2)}) collective-permute-start(bf16[128,1280]{1,0:T(8,128)(2,1)} %get-tuple-element.28), channel_id=1, source_target_pairs={{0,1},{1,2},{2,3},{3,0},{4,5},{5,6},{6,7},{7,4},{8,9},{9,10},{10,1... | collective-permute-start | bytes 983048 | tf_op jit(solution)/shard_map/ppermute | solution.py:104
  5.4 2.6 %collective-permute-start.1 = (bf16[128,1280]{1,0:T(8,128)(2,1)}, bf16[128,1280]{1,0:T(8,128)(2,1)}, u32[]{:S(2)}, u32[]{:S(2)}) collective-permute-start(bf16[128,1280]{1,0:T(8,128)(2,1)} %get-tuple-element.27), channel_id=1, source_target_pairs={{0,2},{1,3},{2,0},{3,1},{4,6},{5,7},{6,4},{7,5},{8,10},{9,11},{10,... | collective-permute-start | bytes 983048 | tf_op jit(solution)/shard_map/ppermute | solution.py:104
  8.0 1.3 collective-permute-start.2
  9.8 1.5 %collective-permute-start.7 = (s32[4]{0:T(128)S(1)}, s32[4]{0:T(128)S(1)}, u32[]{:S(2)}, u32[]{:S(2)}) collective-permute-start(s32[4]{0:T(128)S(1)} %fusion.5), channel_id=1, source_target_pairs={{0,8},{4,12},{8,0},{12,4},{1,9},{5,13},{9,1},{13,5},{2,10},{6,14},... | collective-permute-start | bytes 56 | tf_op jit(solution)/shard_map/ppermute | solution.py:124
  11.3 2.0 %collective-permute-done.7.a_0_ = s32[4]{0:T(128)S(1)} collective-permute-done((s32[4]{0:T(128)S(1)}, s32[4]{0:T(128)S(1)}, u32[]{:S(2)}, u32[]{:S(2)}) %collective-permute-start.7) | collective-permute-done | bytes 48 | tf_op jit(solution)/shard_map/ppermute | solution.py:124
  13.3 3.0 %collective-permute-done = bf16[128,1280]{1,0:T(8,128)(2,1)S(1)} collective-permute-done((bf16[128,1280]{1,0:T(8,128)(2,1)}, bf16[128,1280]{1,0:T(8,128)(2,1)S(1)}, u32[]{:S(2)}, u32[]{:S(2)}) %collective-permute-start) | collective-permute-done | bytes 327712 | tf_op jit(solution)/shard_map/ppermute | solution.py:104
  16.4 13.3 %collective-permute-done.1 = bf16[128,1280]{1,0:T(8,128)(2,1)} collective-permute-done((bf16[128,1280]{1,0:T(8,128)(2,1)}, bf16[128,1280]{1,0:T(8,128)(2,1)}, u32[]{:S(2)}, u32[]{:S(2)}) %collective-permute-start.1) | collective-permute-done | bytes 327712 | tf_op jit(solution)/shard_map/ppermute | solution.py:104
  29.7 1.6 %collective-permute-start.8 = (bf16[256,1280]{1,0:T(8,128)(2,1)S(1)}, bf16[256,1280]{1,0:T(8,128)(2,1)}, u32[]{:S(2)}, u32[]{:S(2)}) collective-permute-start(bf16[256,1280]{1,0:T(8,128)(2,1)S(1)} %pad_maximum_fusion.1), channel_id=1, source_target_pairs={{0,8},{4,12},{8,0},{12,4},{1,9},{5,13},{9,1},{13,5},{2,10},{6,14},... | collective-permute-start | bytes 1966088 | tf_op jit(solution)/shard_map/ppermute | solution.py:126
  31.3 1.9 %pad_maximum_fusion.2 = bf16[256,1280]{1,0:T(8,128)(2,1)} fusion(bf16[128,1280]{1,0:T(8,128)(2,1)} %collective-permute-done.2, bf16[128,1280]{1,0:T(8,128)(2,1)} %collective-permute-done.1), kind=kLoop, calls=%fused_computation.4 | loop fusion | flops 1310720 | bytes 1310720 | tf_op jit(solution)/shard_map/concatenate | solution.py:106
  33.3 13.8 %collective-permute-done.8.a_1_ = bf16[256,1280]{1,0:T(8,128)(2,1)} collective-permute-done((bf16[256,1280]{1,0:T(8,128)(2,1)S(1)}, bf16[256,1280]{1,0:T(8,128)(2,1)}, u32[]{:S(2)}, u32[]{:S(2)}) %collective-permute-start.8) | collective-permute-done | bytes 655392 | tf_op jit(solution)/shard_map/ppermute | solution.py:126
  47.0 1.5 %collective-permute-start.12 = (bf16[256,1280]{1,0:T(8,128)(2,1)}, bf16[256,1280]{1,0:T(8,128)(2,1)}, u32[]{:S(2)}, u32[]{:S(2)}) collective-permute-start(bf16[256,1280]{1,0:T(8,128)(2,1)} %pad_maximum_fusion.2), channel_id=1, source_target_pairs={{0,8},{4,12},{8,0},{12,4},{1,9},{5,13},{9,1},{13,5},{2,10},{6,14},... | collective-permute-start | bytes 1966088 | tf_op jit(solution)/shard_map/ppermute | solution.py:127
  48.6 13.1 %shard_map.65 = (bf16[10,256,128]{2,1,0:T(8,128)(2,1)}, f32[10,8,256]{2,1,0:T(8,128)}) custom-call(s32[4]{0:T(128)} %copy-done.3, bf16[256,1280]{1,0:T(8,128)(2,1)} %collective-permute-done.8.a_1_, bf16[512,1280]{1,0:T(8,128)(2,1)} %a_2_.5, bf16[512,1280]{1,0:T(8,128)(2,1)} %collective-permute-done.3.a_3_, bf16[512,1280]{1,0:T(8,128)(2,1)} %a_4_.5, ...), custom_call_target="tpu_custom_call" | custom-call | tf_op jit(solution)/shard_map/pallas_call | solution.py:71
  61.7 0.6 collective-permute-start.10
  62.2 1.5 collective-permute-done.12.a_1_
  63.7 13.0 %shard_map.66 = (bf16[10,256,128]{2,1,0:T(8,128)(2,1)}, f32[10,8,256]{2,1,0:T(8,128)}) custom-call(s32[4]{0:T(128)} %copy-done.3, bf16[256,1280]{1,0:T(8,128)(2,1)} %collective-permute-done.12.a_1_, bf16[512,1280]{1,0:T(8,128)(2,1)} %a_2_.5, bf16[512,1280]{1,0:T(8,128)(2,1)} %collective-permute-done.3.a_3_, bf16[512,1280]{1,0:T(8,128)(2,1)} %a_4_.5, ...), custom_call_target="tpu_custom_call" | custom-call | tf_op jit(solution)/shard_map/pallas_call | solution.py:71
  76.7 2.2 %collective-permute-start.14 = (bf16[10,256,128]{2,1,0:T(8,128)(2,1)}, bf16[10,256,128]{2,1,0:T(8,128)(2,1)S(1)}, u32[]{:S(2)}, u32[]{:S(2)}) collective-permute-start(bf16[10,256,128]{2,1,0:T(8,128)(2,1)} %get-tuple-element.16), channel_id=1, source_target_pairs={{0,8},{4,12},{8,0},{12,4},{1,9},{5,13},{9,1},{13,5},{2,10},{6,14},... | collective-permute-start | bytes 1966088 | tf_op jit(solution)/shard_map/ppermute | solution.py:169
  78.8 0.6 fusion.4.a_0_
  79.4 0.9 slice.36
  80.4 0.9 slice.41
  81.3 2.1 %collective-permute-start.13 = (f32[10,256]{1,0:T(8,128)S(1)}, f32[10,256]{1,0:T(8,128)S(1)}, u32[]{:S(2)}, u32[]{:S(2)}) collective-permute-start(f32[10,256]{1,0:T(8,128)S(1)} %bitcast.51), channel_id=1, source_target_pairs={{0,8},{4,12},{8,0},{12,4},{1,9},{5,13},{9,1},{13,5},{2,10},{6,14},... | collective-permute-start | bytes 30728 | tf_op jit(solution)/shard_map/ppermute | solution.py:169
  83.4 2.2 %pad_maximum_fusion.a_1_ = bf16[512,1280]{1,0:T(8,128)(2,1)} fusion(bf16[128,1280]{1,0:T(8,128)(2,1)} %collective-permute-done.2, bf16[128,1280]{1,0:T(8,128)(2,1)} %collective-permute-done.1, bf16[128,1280]{1,0:T(8,128)(2,1)S(1)} %collective-permute-done, bf16[128,1280]{1,0:T(8,128)(2,1)S(1)} %get-tuple-element.29), kind=kLoop, calls=%fused_computation | loop fusion | flops 5242880 | bytes 2621440 | tf_op jit(solution)/shard_map/concatenate | solution.py:106
  85.6 21.8 %shard_map.64 = (f32[10,512,128]{2,1,0:T(8,128)}, f32[10,8,512]{2,1,0:T(8,128)}) custom-call(s32[4]{0:T(128)} %fusion.4.a_0_, bf16[512,1280]{1,0:T(8,128)(2,1)} %pad_maximum_fusion.a_1_, bf16[512,1280]{1,0:T(8,128)(2,1)} %a_2_.5, bf16[512,1280]{1,0:T(8,128)(2,1)} %collective-permute-done.3.a_3_, bf16[512,1280]{1,0:T(8,128)(2,1)} %a_4_.5, ...), custom_call_target="tpu_custom_call" | custom-call | tf_op jit(solution)/shard_map/pallas_call | solution.py:71
  107.4 1.0 copy.19
  108.5 4.6 %divide_convert_fusion = (bf16[10,256,128]{2,1,0:T(8,128)(2,1)S(1)}, bf16[10,256,128]{2,1,0:T(8,128)(2,1)S(1)}) fusion(bf16[10,256,128]{2,1,0:T(8,128)(2,1)S(1)} %collective-permute-done.14, f32[10,512,128]{2,1,0:T(8,128)} %get-tuple-element.11, f32[10,256]{1,0:T(8,128)S(1)} %get-tuple-element.19, f32[10,256]{1,0:T(8,128)S(1)} %get-tuple-element.20, ...), kind=kLoop, calls=%fused_computation.1 | loop fusion | flops 3932160 | bytes 5304320 | tf_op jit(solution)/shard_map/convert_element_type | solution.py:179
  113.1 8.6 %collective-permute-start.11 = (bf16[10,128,128]{2,1,0:T(8,128)(2,1)S(1)}, bf16[10,128,128]{2,1,0:T(8,128)(2,1)S(1)}, u32[]{:S(2)}, u32[]{:S(2)}) collective-permute-start(bf16[10,128,128]{2,1,0:T(8,128)(2,1)S(1)} %get-tuple-element.33), channel_id=1, source_target_pairs={{0,3},{1,0},{2,1},{3,2},{4,7},{5,4},{6,5},{7,6},{8,11},{9,8},{10,9... | collective-permute-start | bytes 983048 | tf_op jit(solution)/shard_map/ppermute | solution.py:187
  121.8 0.6 collective-permute-start.16
  123.0 6.9 %collective-permute-done.11 = bf16[10,128,128]{2,1,0:T(8,128)(2,1)S(1)} collective-permute-done((bf16[10,128,128]{2,1,0:T(8,128)(2,1)S(1)}, bf16[10,128,128]{2,1,0:T(8,128)(2,1)S(1)}, u32[]{:S(2)}, u32[]{:S(2)}) %collective-permute-start.11) | collective-permute-done | bytes 327712 | tf_op jit(solution)/shard_map/ppermute | solution.py:187
  130.3 16.9 %collective-permute-done.15 = bf16[10,128,128]{2,1,0:T(8,128)(2,1)} collective-permute-done((bf16[10,128,128]{2,1,0:T(8,128)(2,1)S(1)}, bf16[10,128,128]{2,1,0:T(8,128)(2,1)}, u32[]{:S(2)}, u32[]{:S(2)}) %collective-permute-start.15) | collective-permute-done | bytes 327712 | tf_op jit(solution)/shard_map/ppermute | solution.py:187
  147.1 1.2 copy.25
  149.0 1.0 copy-done.2
  150.1 0.7 constant_dynamic-update-slice_fusion
  (45 shorter events, 2.3 us)
Async XLA Ops:
  0.0 9.4 %copy-start = (bf16[512,1280]{1,0:T(8,128)(2,1)S(1)}, bf16[512,1280]{1,0:T(8,128)(2,1)}, u32[]{:S(2)}) copy-start(bf16[512,1280]{1,0:T(8,128)(2,1)} %a_2_.5) | copy-start | bytes 3932164
  0.0 9.5 %copy-start.4 = (s32[1,6]{1,0:T(1,128)S(1)}, s32[1,6]{1,0:T(1,128)}, u32[]{:S(2)}) copy-start(s32[1,6]{1,0:T(1,128)} %param.11) | copy-start | bytes 76
  0.0 13.3 %copy-start.1 = (bf16[512,1280]{1,0:T(8,128)(2,1)S(1)}, bf16[512,1280]{1,0:T(8,128)(2,1)}, u32[]{:S(2)}) copy-start(bf16[512,1280]{1,0:T(8,128)(2,1)} %a_4_.5) | copy-start | bytes 3932164
  2.4 14.0 %collective-permute-start = (bf16[128,1280]{1,0:T(8,128)(2,1)}, bf16[128,1280]{1,0:T(8,128)(2,1)S(1)}, u32[]{:S(2)}, u32[]{:S(2)}) collective-permute-start(bf16[128,1280]{1,0:T(8,128)(2,1)} %get-tuple-element.28), channel_id=1, source_target_pairs={{0,1},{1,2},{2,3},{3,0},{4,5},{5,6},{6,7},{7,4},{8,9},{9,10},{10,1... | collective-permute-start | bytes 983048 | tf_op jit(solution)/shard_map/ppermute | solution.py:104
  5.4 24.2 %collective-permute-start.1 = (bf16[128,1280]{1,0:T(8,128)(2,1)}, bf16[128,1280]{1,0:T(8,128)(2,1)}, u32[]{:S(2)}, u32[]{:S(2)}) collective-permute-start(bf16[128,1280]{1,0:T(8,128)(2,1)} %get-tuple-element.27), channel_id=1, source_target_pairs={{0,2},{1,3},{2,0},{3,1},{4,6},{5,7},{6,4},{7,5},{8,10},{9,11},{10,... | collective-permute-start | bytes 983048 | tf_op jit(solution)/shard_map/ppermute | solution.py:104
  8.0 21.7 %collective-permute-start.2 = (bf16[128,1280]{1,0:T(8,128)(2,1)}, bf16[128,1280]{1,0:T(8,128)(2,1)}, u32[]{:S(2)}, u32[]{:S(2)}) collective-permute-start(bf16[128,1280]{1,0:T(8,128)(2,1)} %get-tuple-element.30), channel_id=1, source_target_pairs={{0,3},{1,0},{2,1},{3,2},{4,7},{5,4},{6,5},{7,6},{8,11},{9,8},{10,9... | collective-permute-start | bytes 983048 | tf_op jit(solution)/shard_map/ppermute | solution.py:104
  9.4 39.2 %collective-permute-start.3 = (bf16[512,1280]{1,0:T(8,128)(2,1)S(1)}, bf16[512,1280]{1,0:T(8,128)(2,1)}, u32[]{:S(2)}, u32[]{:S(2)}) collective-permute-start(bf16[512,1280]{1,0:T(8,128)(2,1)S(1)} %copy-done), channel_id=1, source_target_pairs={{0,4},{4,0},{8,12},{12,8},{1,5},{5,1},{9,13},{13,9},{2,6},{6,2},{1... | collective-permute-start | bytes 3932168 | tf_op jit(solution)/shard_map/ppermute | solution.py:131
  9.8 3.6 %collective-permute-start.7 = (s32[4]{0:T(128)S(1)}, s32[4]{0:T(128)S(1)}, u32[]{:S(2)}, u32[]{:S(2)}) collective-permute-start(s32[4]{0:T(128)S(1)} %fusion.5), channel_id=1, source_target_pairs={{0,8},{4,12},{8,0},{12,4},{1,9},{5,13},{9,1},{13,5},{2,10},{6,14},... | collective-permute-start | bytes 56 | tf_op jit(solution)/shard_map/ppermute | solution.py:124
  13.3 20.0 %copy-start.3 = (s32[4]{0:T(128)}, s32[4]{0:T(128)S(1)}, u32[]{:S(2)}) copy-start(s32[4]{0:T(128)S(1)} %collective-permute-done.7.a_0_) | copy-start | bytes 52
  13.3 35.3 %collective-permute-start.4 = (bf16[512,1280]{1,0:T(8,128)(2,1)S(1)}, bf16[512,1280]{1,0:T(8,128)(2,1)}, u32[]{:S(2)}, u32[]{:S(2)}) collective-permute-start(bf16[512,1280]{1,0:T(8,128)(2,1)S(1)} %copy-done.1), channel_id=1, source_target_pairs={{0,4},{4,0},{8,12},{12,8},{1,5},{5,1},{9,13},{13,9},{2,6},{6,2},{1... | collective-permute-start | bytes 3932168 | tf_op jit(solution)/shard_map/ppermute | solution.py:131
  16.3 32.2 %collective-permute-start.5 = (bf16[512,1280]{1,0:T(8,128)(2,1)}, bf16[512,1280]{1,0:T(8,128)(2,1)}, u32[]{:S(2)}, u32[]{:S(2)}) collective-permute-start(bf16[512,1280]{1,0:T(8,128)(2,1)} %a_6_.5), channel_id=1, source_target_pairs={{0,4},{4,0},{8,12},{12,8},{1,5},{5,1},{9,13},{13,9},{2,6},{6,2},{1... | collective-permute-start | bytes 3932168 | tf_op jit(solution)/shard_map/ppermute | solution.py:131
  29.7 18.9 %collective-permute-start.6 = (bf16[512,1280]{1,0:T(8,128)(2,1)}, bf16[512,1280]{1,0:T(8,128)(2,1)}, u32[]{:S(2)}, u32[]{:S(2)}) collective-permute-start(bf16[512,1280]{1,0:T(8,128)(2,1)} %a_8_.5), channel_id=1, source_target_pairs={{0,4},{4,0},{8,12},{12,8},{1,5},{5,1},{9,13},{13,9},{2,6},{6,2},{1... | collective-permute-start | bytes 3932168 | tf_op jit(solution)/shard_map/ppermute | solution.py:131
  29.7 17.3 %collective-permute-start.8 = (bf16[256,1280]{1,0:T(8,128)(2,1)S(1)}, bf16[256,1280]{1,0:T(8,128)(2,1)}, u32[]{:S(2)}, u32[]{:S(2)}) collective-permute-start(bf16[256,1280]{1,0:T(8,128)(2,1)S(1)} %pad_maximum_fusion.1), channel_id=1, source_target_pairs={{0,8},{4,12},{8,0},{12,4},{1,9},{5,13},{9,1},{13,5},{2,10},{6,14},... | collective-permute-start | bytes 1966088 | tf_op jit(solution)/shard_map/ppermute | solution.py:126
  47.0 16.7 %collective-permute-start.12 = (bf16[256,1280]{1,0:T(8,128)(2,1)}, bf16[256,1280]{1,0:T(8,128)(2,1)}, u32[]{:S(2)}, u32[]{:S(2)}) collective-permute-start(bf16[256,1280]{1,0:T(8,128)(2,1)} %pad_maximum_fusion.2), channel_id=1, source_target_pairs={{0,8},{4,12},{8,0},{12,4},{1,9},{5,13},{9,1},{13,5},{2,10},{6,14},... | collective-permute-start | bytes 1966088 | tf_op jit(solution)/shard_map/ppermute | solution.py:127
  61.7 46.8 %collective-permute-start.10 = (bf16[10,256,128]{2,1,0:T(8,128)(2,1)}, bf16[10,256,128]{2,1,0:T(8,128)(2,1)S(1)}, u32[]{:S(2)}, u32[]{:S(2)}) collective-permute-start(bf16[10,256,128]{2,1,0:T(8,128)(2,1)} %get-tuple-element.14), channel_id=1, source_target_pairs={{0,8},{4,12},{8,0},{12,4},{1,9},{5,13},{9,1},{13,5},{2,10},{6,14},... | collective-permute-start | bytes 1966088 | tf_op jit(solution)/shard_map/ppermute | solution.py:169
  76.7 31.8 %collective-permute-start.14 = (bf16[10,256,128]{2,1,0:T(8,128)(2,1)}, bf16[10,256,128]{2,1,0:T(8,128)(2,1)S(1)}, u32[]{:S(2)}, u32[]{:S(2)}) collective-permute-start(bf16[10,256,128]{2,1,0:T(8,128)(2,1)} %get-tuple-element.16), channel_id=1, source_target_pairs={{0,8},{4,12},{8,0},{12,4},{1,9},{5,13},{9,1},{13,5},{2,10},{6,14},... | collective-permute-start | bytes 1966088 | tf_op jit(solution)/shard_map/ppermute | solution.py:169
  80.3 28.1 %collective-permute-start.9 = (f32[10,256]{1,0:T(8,128)S(1)}, f32[10,256]{1,0:T(8,128)S(1)}, u32[]{:S(2)}, u32[]{:S(2)}) collective-permute-start(f32[10,256]{1,0:T(8,128)S(1)} %bitcast.50), channel_id=1, source_target_pairs={{0,8},{4,12},{8,0},{12,4},{1,9},{5,13},{9,1},{13,5},{2,10},{6,14},... | collective-permute-start | bytes 30728 | tf_op jit(solution)/shard_map/ppermute | solution.py:169
  81.3 27.1 %collective-permute-start.13 = (f32[10,256]{1,0:T(8,128)S(1)}, f32[10,256]{1,0:T(8,128)S(1)}, u32[]{:S(2)}, u32[]{:S(2)}) collective-permute-start(f32[10,256]{1,0:T(8,128)S(1)} %bitcast.51), channel_id=1, source_target_pairs={{0,8},{4,12},{8,0},{12,4},{1,9},{5,13},{9,1},{13,5},{2,10},{6,14},... | collective-permute-start | bytes 30728 | tf_op jit(solution)/shard_map/ppermute | solution.py:169
  113.1 16.7 %collective-permute-start.11 = (bf16[10,128,128]{2,1,0:T(8,128)(2,1)S(1)}, bf16[10,128,128]{2,1,0:T(8,128)(2,1)S(1)}, u32[]{:S(2)}, u32[]{:S(2)}) collective-permute-start(bf16[10,128,128]{2,1,0:T(8,128)(2,1)S(1)} %get-tuple-element.33), channel_id=1, source_target_pairs={{0,3},{1,0},{2,1},{3,2},{4,7},{5,4},{6,5},{7,6},{8,11},{9,8},{10,9... | collective-permute-start | bytes 983048 | tf_op jit(solution)/shard_map/ppermute | solution.py:187
  121.7 25.4 %collective-permute-start.15 = (bf16[10,128,128]{2,1,0:T(8,128)(2,1)S(1)}, bf16[10,128,128]{2,1,0:T(8,128)(2,1)}, u32[]{:S(2)}, u32[]{:S(2)}) collective-permute-start(bf16[10,128,128]{2,1,0:T(8,128)(2,1)S(1)} %get-tuple-element.32), channel_id=1, source_target_pairs={{0,2},{1,3},{2,0},{3,1},{4,6},{5,7},{6,4},{7,5},{8,10},{9,11},{10,... | collective-permute-start | bytes 983048 | tf_op jit(solution)/shard_map/ppermute | solution.py:187
  121.8 26.7 %collective-permute-start.16 = (bf16[10,128,128]{2,1,0:T(8,128)(2,1)S(1)}, bf16[10,128,128]{2,1,0:T(8,128)(2,1)S(1)}, u32[]{:S(2)}, u32[]{:S(2)}) collective-permute-start(bf16[10,128,128]{2,1,0:T(8,128)(2,1)S(1)} %get-tuple-element.31), channel_id=1, source_target_pairs={{0,1},{1,2},{2,3},{3,0},{4,5},{5,6},{6,7},{7,4},{8,9},{9,10},{10,1... | collective-permute-start | bytes 983048 | tf_op jit(solution)/shard_map/ppermute | solution.py:187
  149.0 1.1 copy-start.2

commit v21 on v19

--- a/solution.py
+++ b/solution.py
@@ -96,13 +96,14 @@
     other = s ^ 1
     listed = sources[0]
 
-    query_parts = [lax.dynamic_slice_in_dim(queries, sp_place * head_width, head_width, 1)]
-    for d in range(1, sp_count):
+    issue = sorted(range(1, sp_count), key=lambda d: -min(d, sp_count - d))
+    received = {}
+    for d in issue:
         columns = ((sp_place + d) % sp_count) * head_width
         piece = lax.dynamic_slice_in_dim(queries, columns, head_width, 1)
-        query_parts.append(
-            lax.ppermute(piece, "sp", [(i, (i + d) % sp_count) for i in range(sp_count)])
-        )
+        received[d] = lax.ppermute(piece, "sp", [(i, (i + d) % sp_count) for i in range(sp_count)])
+    query_parts = [lax.dynamic_slice_in_dim(queries, sp_place * head_width, head_width, 1)]
+    query_parts += [received[d] for d in range(1, sp_count)]
     query_block = jnp.concatenate(query_parts, axis=0)
 
     back = [(i, (i - 2) % seq_count) for i in range(seq_count)]
@@ -180,7 +181,7 @@
 
     rows = queries.shape[0]
     result = jnp.zeros((rows, queries.shape[1]), jnp.bfloat16)
-    for d in range(sp_count):
+    for d in issue + [0]:
         start = d * rows
         piece = mixed_halves[start // half][:, start % half : start % half + rows]
         if d:

time: 149 us -> 147 us (0.987); the launches traced: 149 us -> 145 us
  waiting for transfers between devices: 57.4 us -> 52.3 us
  starting transfers between devices: 25.7 us -> 27.5 us
    ppermute x1, waiting for transfers between devices: 13.8 us -> 1 us  [local(): lax.ppermute(query_block[:half], 'seq', back)]
    ppermute x1, waiting for transfers between devices: 1.59 us -> 14.3 us  [local(): lax.ppermute(query_block[half:], 'seq', back)]
    ppermute x3, waiting for transfers between devices: 23.6 us -> 18.6 us  [local(): lax.ppermute(piece, 'sp', [(i, (i - d) % sp_count) for i in range(sp_coun...]
  transfers between devices with their start and end apart: 17 -> 17, of which waited for: 7 -> 5; matrix products, arithmetic and copies ran while one was open for 6% -> 5% of each run, Pallas kernels for 32% -> 33%
where the time goes in v21:
time: 147 us; the launch traced here: 145 us
  waiting for transfers between devices  52.3 us (36%)
  Pallas kernels  47.5 us (32%)
  starting transfers between devices  27.5 us (19%)
  other arithmetic  9.85 us (7%)
  local copies, waits for them, and re-layouts  7.16 us (5%)
    pallas_call x3, Pallas kernels, attend_partial(): pl.pallas_call(lambda *a: partial_kernel(nsrc, group, *a), grid_spec=grid...  47.5 us
    ppermute x3, waiting for transfers between devices, local(): lax.ppermute(piece, 'sp', [(i, (i - d) % sp_count) for i in range(sp_coun...  18.6 us
    ppermute x3, waiting for transfers between devices, local(): lax.ppermute(piece, 'sp', [(i, (i + d) % sp_count) for i in range(sp_coun...  16.4 us
    ppermute x1, waiting for transfers between devices, local(): lax.ppermute(query_block[half:], 'seq', back)  14.3 us
    ppermute x3, starting transfers between devices, local(): lax.ppermute(piece, 'sp', [(i, (i - d) % sp_count) for i in range(sp_coun...  10.5 us
    ppermute x3, starting transfers between devices, local(): lax.ppermute(piece, 'sp', [(i, (i + d) % sp_count) for i in range(sp_coun...  6.98 us
    ppermute x4, starting transfers between devices, local(): far_out, far_lse = lax.ppermute((far_out, far_lse), 'seq', forth)  4.86 us
    convert_element_type x1, other arithmetic, local(): mixed_halves.append(mixed.astype(jnp.bfloat16))  4.58 us
  transfers between devices with their start and end apart: 17, of which 5 were waited for; matrix products, arithmetic and copies ran while one was open for 5% of the time, Pallas kernels for 33%

profile of v21, /device:TPU:0, one launch (start us, length us, event | category | flops | bytes accessed | tf_op | source)
XLA Modules:
  0.0 144.6 jit_solution(13200387252119310138)
XLA Ops:
  0.0 2.4 %constant_dynamic-slice_fusion.3 = (bf16[128,1280]{1,0:T(8,128)(2,1)S(1)}, bf16[128,1280]{1,0:T(8,128)(2,1)}, bf16[128,1280]{1,0:T(8,128)(2,1)}, bf16[128,1280]{1,0:T(8,128)(2,1)}) fusion(bf16[128,5120]{1,0:T(8,128)(2,1)} %param.6, s32[]{:T(128)S(6)} %select_n.55, s32[]{:T(128)S(6)} %select_n.57, s32[]{:T(128)S(6)} %select_n.61, s32[]{:T(128)S(6)} %select_n.59), kind=kLoop, calls=%fused_computation.23 | loop fusion | bytes 2621456 | tf_op jit(solution)/shard_map/dynamic_slice | solution.py:105
  2.4 3.0 %collective-permute-start = (bf16[128,1280]{1,0:T(8,128)(2,1)}, bf16[128,1280]{1,0:T(8,128)(2,1)S(1)}, u32[]{:S(2)}, u32[]{:S(2)}) collective-permute-start(bf16[128,1280]{1,0:T(8,128)(2,1)} %get-tuple-element.28), channel_id=1, source_target_pairs={{0,1},{1,2},{2,3},{3,0},{4,5},{5,6},{6,7},{7,4},{8,9},{9,10},{10,1... | collective-permute-start | bytes 983048 | tf_op jit(solution)/shard_map/ppermute | solution.py:104
  5.4 2.6 %collective-permute-start.1 = (bf16[128,1280]{1,0:T(8,128)(2,1)}, bf16[128,1280]{1,0:T(8,128)(2,1)}, u32[]{:S(2)}, u32[]{:S(2)}) collective-permute-start(bf16[128,1280]{1,0:T(8,128)(2,1)} %get-tuple-element.30), channel_id=1, source_target_pairs={{0,2},{1,3},{2,0},{3,1},{4,6},{5,7},{6,4},{7,5},{8,10},{9,11},{10,... | collective-permute-start | bytes 983048 | tf_op jit(solution)/shard_map/ppermute | solution.py:104
  8.0 1.3 collective-permute-start.2
  9.8 1.5 %collective-permute-start.7 = (s32[4]{0:T(128)S(1)}, s32[4]{0:T(128)S(1)}, u32[]{:S(2)}, u32[]{:S(2)}) collective-permute-start(s32[4]{0:T(128)S(1)} %fusion.5), channel_id=1, source_target_pairs={{0,8},{4,12},{8,0},{12,4},{1,9},{5,13},{9,1},{13,5},{2,10},{6,14},... | collective-permute-start | bytes 56 | tf_op jit(solution)/shard_map/ppermute | solution.py:125
  11.3 2.0 %collective-permute-done.7.a_0_ = s32[4]{0:T(128)S(1)} collective-permute-done((s32[4]{0:T(128)S(1)}, s32[4]{0:T(128)S(1)}, u32[]{:S(2)}, u32[]{:S(2)}) %collective-permute-start.7) | collective-permute-done | bytes 48 | tf_op jit(solution)/shard_map/ppermute | solution.py:125
  13.3 16.3 %collective-permute-done.1 = bf16[128,1280]{1,0:T(8,128)(2,1)} collective-permute-done((bf16[128,1280]{1,0:T(8,128)(2,1)}, bf16[128,1280]{1,0:T(8,128)(2,1)}, u32[]{:S(2)}, u32[]{:S(2)}) %collective-permute-start.1) | collective-permute-done | bytes 327712 | tf_op jit(solution)/shard_map/ppermute | solution.py:104
  29.7 0.5 collective-permute-start.6
  30.2 1.1 pad_maximum_fusion.1
  31.3 1.6 %collective-permute-start.8 = (bf16[256,1280]{1,0:T(8,128)(2,1)S(1)}, bf16[256,1280]{1,0:T(8,128)(2,1)}, u32[]{:S(2)}, u32[]{:S(2)}) collective-permute-start(bf16[256,1280]{1,0:T(8,128)(2,1)S(1)} %pad_maximum_fusion.1), channel_id=1, source_target_pairs={{0,8},{4,12},{8,0},{12,4},{1,9},{5,13},{9,1},{13,5},{2,10},{6,14},... | collective-permute-start | bytes 1966088 | tf_op jit(solution)/shard_map/ppermute | solution.py:128
  32.9 0.9 pad_maximum_fusion.2
  33.8 14.3 %collective-permute-done.8.a_1_ = bf16[256,1280]{1,0:T(8,128)(2,1)} collective-permute-done((bf16[256,1280]{1,0:T(8,128)(2,1)S(1)}, bf16[256,1280]{1,0:T(8,128)(2,1)}, u32[]{:S(2)}, u32[]{:S(2)}) %collective-permute-start.8) | collective-permute-done | bytes 655392 | tf_op jit(solution)/shard_map/ppermute | solution.py:128
  48.1 1.5 %collective-permute-start.12 = (bf16[256,1280]{1,0:T(8,128)(2,1)}, bf16[256,1280]{1,0:T(8,128)(2,1)}, u32[]{:S(2)}, u32[]{:S(2)}) collective-permute-start(bf16[256,1280]{1,0:T(8,128)(2,1)} %pad_maximum_fusion.2), channel_id=1, source_target_pairs={{0,8},{4,12},{8,0},{12,4},{1,9},{5,13},{9,1},{13,5},{2,10},{6,14},... | collective-permute-start | bytes 1966088 | tf_op jit(solution)/shard_map/ppermute | solution.py:127
  49.7 13.0 %shard_map.65 = (bf16[10,256,128]{2,1,0:T(8,128)(2,1)}, f32[10,8,256]{2,1,0:T(8,128)}) custom-call(s32[4]{0:T(128)} %copy-done.3, bf16[256,1280]{1,0:T(8,128)(2,1)} %collective-permute-done.8.a_1_, bf16[512,1280]{1,0:T(8,128)(2,1)} %a_2_.5, bf16[512,1280]{1,0:T(8,128)(2,1)} %collective-permute-done.3.a_3_, bf16[512,1280]{1,0:T(8,128)(2,1)} %a_4_.5, ...), custom_call_target="tpu_custom_call" | custom-call | tf_op jit(solution)/shard_map/pallas_call | solution.py:71
  62.6 0.6 collective-permute-start.10
  63.2 1.0 collective-permute-done.12.a_1_
  64.2 12.9 %shard_map.66 = (bf16[10,256,128]{2,1,0:T(8,128)(2,1)}, f32[10,8,256]{2,1,0:T(8,128)}) custom-call(s32[4]{0:T(128)} %copy-done.3, bf16[256,1280]{1,0:T(8,128)(2,1)} %collective-permute-done.12.a_1_, bf16[512,1280]{1,0:T(8,128)(2,1)} %a_2_.5, bf16[512,1280]{1,0:T(8,128)(2,1)} %collective-permute-done.3.a_3_, bf16[512,1280]{1,0:T(8,128)(2,1)} %a_4_.5, ...), custom_call_target="tpu_custom_call" | custom-call | tf_op jit(solution)/shard_map/pallas_call | solution.py:71
  77.2 2.3 %collective-permute-start.14 = (bf16[10,256,128]{2,1,0:T(8,128)(2,1)}, bf16[10,256,128]{2,1,0:T(8,128)(2,1)S(1)}, u32[]{:S(2)}, u32[]{:S(2)}) collective-permute-start(bf16[10,256,128]{2,1,0:T(8,128)(2,1)} %get-tuple-element.16), channel_id=1, source_target_pairs={{0,8},{4,12},{8,0},{12,4},{1,9},{5,13},{9,1},{13,5},{2,10},{6,14},... | collective-permute-start | bytes 1966088 | tf_op jit(solution)/shard_map/ppermute | solution.py:170
  79.4 0.7 fusion.4.a_0_
  80.1 2.0 %collective-permute-start.13 = (f32[10,8,256]{2,1,0:T(8,128)}, f32[10,8,256]{2,1,0:T(8,128)S(1)}, u32[]{:S(2)}, u32[]{:S(2)}) collective-permute-start(f32[10,8,256]{2,1,0:T(8,128)} %get-tuple-element.15), channel_id=1, source_target_pairs={{0,8},{4,12},{8,0},{12,4},{1,9},{5,13},{9,1},{13,5},{2,10},{6,14},... | collective-permute-start | bytes 245768 | tf_op jit(solution)/shard_map/ppermute | solution.py:170
  82.1 2.2 %pad_maximum_fusion.a_1_ = bf16[512,1280]{1,0:T(8,128)(2,1)} fusion(bf16[128,1280]{1,0:T(8,128)(2,1)} %collective-permute-done.2, bf16[128,1280]{1,0:T(8,128)(2,1)} %collective-permute-done.1, bf16[128,1280]{1,0:T(8,128)(2,1)S(1)} %collective-permute-done, bf16[128,1280]{1,0:T(8,128)(2,1)S(1)} %get-tuple-element.27), kind=kLoop, calls=%fused_computation | loop fusion | flops 5242880 | bytes 2621440 | tf_op jit(solution)/shard_map/concatenate | solution.py:107
  84.3 21.6 %shard_map.64 = (f32[10,512,128]{2,1,0:T(8,128)}, f32[10,8,512]{2,1,0:T(8,128)}) custom-call(s32[4]{0:T(128)} %fusion.4.a_0_, bf16[512,1280]{1,0:T(8,128)(2,1)} %pad_maximum_fusion.a_1_, bf16[512,1280]{1,0:T(8,128)(2,1)} %a_2_.5, bf16[512,1280]{1,0:T(8,128)(2,1)} %collective-permute-done.3.a_3_, bf16[512,1280]{1,0:T(8,128)(2,1)} %a_4_.5, ...), custom_call_target="tpu_custom_call" | custom-call | tf_op jit(solution)/shard_map/pallas_call | solution.py:71
  106.0 1.0 copy.19
  107.1 4.6 %divide_convert_fusion = (bf16[10,256,128]{2,1,0:T(8,128)(2,1)S(1)}, bf16[10,256,128]{2,1,0:T(8,128)(2,1)S(1)}) fusion(bf16[10,256,128]{2,1,0:T(8,128)(2,1)S(1)} %collective-permute-done.14, f32[10,512,128]{2,1,0:T(8,128)} %get-tuple-element.11, f32[10,256]{1,0:T(8,128)S(1)} %get-tuple-element.19, f32[10,256]{1,0:T(8,128)S(1)} %get-tuple-element.20, ...), kind=kLoop, calls=%fused_computation.1 | loop fusion | flops 3932160 | bytes 5304320 | tf_op jit(solution)/shard_map/convert_element_type | solution.py:180
  111.7 7.1 %collective-permute-start.11 = (bf16[10,128,128]{2,1,0:T(8,128)(2,1)S(1)}, bf16[10,128,128]{2,1,0:T(8,128)(2,1)S(1)}, u32[]{:S(2)}, u32[]{:S(2)}) collective-permute-start(bf16[10,128,128]{2,1,0:T(8,128)(2,1)S(1)} %get-tuple-element.34), channel_id=1, source_target_pairs={{0,2},{1,3},{2,0},{3,1},{4,6},{5,7},{6,4},{7,5},{8,10},{9,11},{10,... | collective-permute-start | bytes 983048 | tf_op jit(solution)/shard_map/ppermute | solution.py:188
  118.8 3.4 %collective-permute-start.15 = (bf16[10,128,128]{2,1,0:T(8,128)(2,1)S(1)}, bf16[10,128,128]{2,1,0:T(8,128)(2,1)S(1)}, u32[]{:S(2)}, u32[]{:S(2)}) collective-permute-start(bf16[10,128,128]{2,1,0:T(8,128)(2,1)S(1)} %get-tuple-element.32), channel_id=1, source_target_pairs={{0,3},{1,0},{2,1},{3,2},{4,7},{5,4},{6,5},{7,6},{8,11},{9,8},{10,9... | collective-permute-start | bytes 983048 | tf_op jit(solution)/shard_map/ppermute | solution.py:188
  122.7 18.6 %collective-permute-done.11 = bf16[10,128,128]{2,1,0:T(8,128)(2,1)S(1)} collective-permute-done((bf16[10,128,128]{2,1,0:T(8,128)(2,1)S(1)}, bf16[10,128,128]{2,1,0:T(8,128)(2,1)S(1)}, u32[]{:S(2)}, u32[]{:S(2)}) %collective-permute-start.11) | collective-permute-done | bytes 327712 | tf_op jit(solution)/shard_map/ppermute | solution.py:188
  141.3 0.2 copy.20
  141.7 0.2 copy.23
  142.1 0.2 copy.25
  142.8 1.0 copy-done.2
  143.9 0.7 constant_dynamic-update-slice_fusion
  (45 shorter events, 1.8 us)
Async XLA Ops:
  0.0 9.4 %copy-start = (bf16[512,1280]{1,0:T(8,128)(2,1)S(1)}, bf16[512,1280]{1,0:T(8,128)(2,1)}, u32[]{:S(2)}) copy-start(bf16[512,1280]{1,0:T(8,128)(2,1)} %a_2_.5) | copy-start | bytes 3932164
  0.0 9.5 %copy-start.4 = (s32[1,6]{1,0:T(1,128)S(1)}, s32[1,6]{1,0:T(1,128)}, u32[]{:S(2)}) copy-start(s32[1,6]{1,0:T(1,128)} %param.11) | copy-start | bytes 76
  0.0 13.3 %copy-start.1 = (bf16[512,1280]{1,0:T(8,128)(2,1)S(1)}, bf16[512,1280]{1,0:T(8,128)(2,1)}, u32[]{:S(2)}) copy-start(bf16[512,1280]{1,0:T(8,128)(2,1)} %a_4_.5) | copy-start | bytes 3932164
  2.4 28.9 %collective-permute-start = (bf16[128,1280]{1,0:T(8,128)(2,1)}, bf16[128,1280]{1,0:T(8,128)(2,1)S(1)}, u32[]{:S(2)}, u32[]{:S(2)}) collective-permute-start(bf16[128,1280]{1,0:T(8,128)(2,1)} %get-tuple-element.28), channel_id=1, source_target_pairs={{0,1},{1,2},{2,3},{3,0},{4,5},{5,6},{6,7},{7,4},{8,9},{9,10},{10,1... | collective-permute-start | bytes 983048 | tf_op jit(solution)/shard_map/ppermute | solution.py:104
  5.4 24.2 %collective-permute-start.1 = (bf16[128,1280]{1,0:T(8,128)(2,1)}, bf16[128,1280]{1,0:T(8,128)(2,1)}, u32[]{:S(2)}, u32[]{:S(2)}) collective-permute-start(bf16[128,1280]{1,0:T(8,128)(2,1)} %get-tuple-element.30), channel_id=1, source_target_pairs={{0,2},{1,3},{2,0},{3,1},{4,6},{5,7},{6,4},{7,5},{8,10},{9,11},{10,... | collective-permute-start | bytes 983048 | tf_op jit(solution)/shard_map/ppermute | solution.py:104
  8.0 21.6 %collective-permute-start.2 = (bf16[128,1280]{1,0:T(8,128)(2,1)}, bf16[128,1280]{1,0:T(8,128)(2,1)}, u32[]{:S(2)}, u32[]{:S(2)}) collective-permute-start(bf16[128,1280]{1,0:T(8,128)(2,1)} %get-tuple-element.29), channel_id=1, source_target_pairs={{0,3},{1,0},{2,1},{3,2},{4,7},{5,4},{6,5},{7,6},{8,11},{9,8},{10,9... | collective-permute-start | bytes 983048 | tf_op jit(solution)/shard_map/ppermute | solution.py:104
  9.4 40.3 %collective-permute-start.3 = (bf16[512,1280]{1,0:T(8,128)(2,1)S(1)}, bf16[512,1280]{1,0:T(8,128)(2,1)}, u32[]{:S(2)}, u32[]{:S(2)}) collective-permute-start(bf16[512,1280]{1,0:T(8,128)(2,1)S(1)} %copy-done), channel_id=1, source_target_pairs={{0,4},{4,0},{8,12},{12,8},{1,5},{5,1},{9,13},{13,9},{2,6},{6,2},{1... | collective-permute-start | bytes 3932168 | tf_op jit(solution)/shard_map/ppermute | solution.py:132
  9.8 3.6 %collective-permute-start.7 = (s32[4]{0:T(128)S(1)}, s32[4]{0:T(128)S(1)}, u32[]{:S(2)}, u32[]{:S(2)}) collective-permute-start(s32[4]{0:T(128)S(1)} %fusion.5), channel_id=1, source_target_pairs={{0,8},{4,12},{8,0},{12,4},{1,9},{5,13},{9,1},{13,5},{2,10},{6,14},... | collective-permute-start | bytes 56 | tf_op jit(solution)/shard_map/ppermute | solution.py:125
  13.3 20.5 %copy-start.3 = (s32[4]{0:T(128)}, s32[4]{0:T(128)S(1)}, u32[]{:S(2)}) copy-start(s32[4]{0:T(128)S(1)} %collective-permute-done.7.a_0_) | copy-start | bytes 52
  13.3 36.3 %collective-permute-start.4 = (bf16[512,1280]{1,0:T(8,128)(2,1)S(1)}, bf16[512,1280]{1,0:T(8,128)(2,1)}, u32[]{:S(2)}, u32[]{:S(2)}) collective-permute-start(bf16[512,1280]{1,0:T(8,128)(2,1)S(1)} %copy-done.1), channel_id=1, source_target_pairs={{0,4},{4,0},{8,12},{12,8},{1,5},{5,1},{9,13},{13,9},{2,6},{6,2},{1... | collective-permute-start | bytes 3932168 | tf_op jit(solution)/shard_map/ppermute | solution.py:132
  29.7 20.0 %collective-permute-start.5 = (bf16[512,1280]{1,0:T(8,128)(2,1)}, bf16[512,1280]{1,0:T(8,128)(2,1)}, u32[]{:S(2)}, u32[]{:S(2)}) collective-permute-start(bf16[512,1280]{1,0:T(8,128)(2,1)} %a_6_.5), channel_id=1, source_target_pairs={{0,4},{4,0},{8,12},{12,8},{1,5},{5,1},{9,13},{13,9},{2,6},{6,2},{1... | collective-permute-start | bytes 3932168 | tf_op jit(solution)/shard_map/ppermute | solution.py:132
  29.7 20.0 %collective-permute-start.6 = (bf16[512,1280]{1,0:T(8,128)(2,1)}, bf16[512,1280]{1,0:T(8,128)(2,1)}, u32[]{:S(2)}, u32[]{:S(2)}) collective-permute-start(bf16[512,1280]{1,0:T(8,128)(2,1)} %a_8_.5), channel_id=1, source_target_pairs={{0,4},{4,0},{8,12},{12,8},{1,5},{5,1},{9,13},{13,9},{2,6},{6,2},{1... | collective-permute-start | bytes 3932168 | tf_op jit(solution)/shard_map/ppermute | solution.py:132
  31.3 16.8 %collective-permute-start.8 = (bf16[256,1280]{1,0:T(8,128)(2,1)S(1)}, bf16[256,1280]{1,0:T(8,128)(2,1)}, u32[]{:S(2)}, u32[]{:S(2)}) collective-permute-start(bf16[256,1280]{1,0:T(8,128)(2,1)S(1)} %pad_maximum_fusion.1), channel_id=1, source_target_pairs={{0,8},{4,12},{8,0},{12,4},{1,9},{5,13},{9,1},{13,5},{2,10},{6,14},... | collective-permute-start | bytes 1966088 | tf_op jit(solution)/shard_map/ppermute | solution.py:128
  48.1 16.1 %collective-permute-start.12 = (bf16[256,1280]{1,0:T(8,128)(2,1)}, bf16[256,1280]{1,0:T(8,128)(2,1)}, u32[]{:S(2)}, u32[]{:S(2)}) collective-permute-start(bf16[256,1280]{1,0:T(8,128)(2,1)} %pad_maximum_fusion.2), channel_id=1, source_target_pairs={{0,8},{4,12},{8,0},{12,4},{1,9},{5,13},{9,1},{13,5},{2,10},{6,14},... | collective-permute-start | bytes 1966088 | tf_op jit(solution)/shard_map/ppermute | solution.py:127
  62.6 17.4 %copy-start.5 = (f32[10,8,256]{2,1,0:T(8,128)S(1)}, f32[10,8,256]{2,1,0:T(8,128)}, u32[]{:S(2)}) copy-start(f32[10,8,256]{2,1,0:T(8,128)} %get-tuple-element.13) | copy-start | bytes 245764
  62.6 44.4 %collective-permute-start.10 = (bf16[10,256,128]{2,1,0:T(8,128)(2,1)}, bf16[10,256,128]{2,1,0:T(8,128)(2,1)S(1)}, u32[]{:S(2)}, u32[]{:S(2)}) collective-permute-start(bf16[10,256,128]{2,1,0:T(8,128)(2,1)} %get-tuple-element.14), channel_id=1, source_target_pairs={{0,8},{4,12},{8,0},{12,4},{1,9},{5,13},{9,1},{13,5},{2,10},{6,14},... | collective-permute-start | bytes 1966088 | tf_op jit(solution)/shard_map/ppermute | solution.py:170
  77.2 29.9 %collective-permute-start.14 = (bf16[10,256,128]{2,1,0:T(8,128)(2,1)}, bf16[10,256,128]{2,1,0:T(8,128)(2,1)S(1)}, u32[]{:S(2)}, u32[]{:S(2)}) collective-permute-start(bf16[10,256,128]{2,1,0:T(8,128)(2,1)} %get-tuple-element.16), channel_id=1, source_target_pairs={{0,8},{4,12},{8,0},{12,4},{1,9},{5,13},{9,1},{13,5},{2,10},{6,14},... | collective-permute-start | bytes 1966088 | tf_op jit(solution)/shard_map/ppermute | solution.py:170
  80.1 26.9 %collective-permute-start.9 = (f32[10,8,256]{2,1,0:T(8,128)S(1)}, f32[10,8,256]{2,1,0:T(8,128)S(1)}, u32[]{:S(2)}, u32[]{:S(2)}) collective-permute-start(f32[10,8,256]{2,1,0:T(8,128)S(1)} %copy-done.5), channel_id=1, source_target_pairs={{0,8},{4,12},{8,0},{12,4},{1,9},{5,13},{9,1},{13,5},{2,10},{6,14},... | collective-permute-start | bytes 245768 | tf_op jit(solution)/shard_map/ppermute | solution.py:170
  80.1 26.9 %collective-permute-start.13 = (f32[10,8,256]{2,1,0:T(8,128)}, f32[10,8,256]{2,1,0:T(8,128)S(1)}, u32[]{:S(2)}, u32[]{:S(2)}) collective-permute-start(f32[10,8,256]{2,1,0:T(8,128)} %get-tuple-element.15), channel_id=1, source_target_pairs={{0,8},{4,12},{8,0},{12,4},{1,9},{5,13},{9,1},{13,5},{2,10},{6,14},... | collective-permute-start | bytes 245768 | tf_op jit(solution)/shard_map/ppermute | solution.py:170
  111.7 29.6 %collective-permute-start.11 = (bf16[10,128,128]{2,1,0:T(8,128)(2,1)S(1)}, bf16[10,128,128]{2,1,0:T(8,128)(2,1)S(1)}, u32[]{:S(2)}, u32[]{:S(2)}) collective-permute-start(bf16[10,128,128]{2,1,0:T(8,128)(2,1)S(1)} %get-tuple-element.34), channel_id=1, source_target_pairs={{0,2},{1,3},{2,0},{3,1},{4,6},{5,7},{6,4},{7,5},{8,10},{9,11},{10,... | collective-permute-start | bytes 983048 | tf_op jit(solution)/shard_map/ppermute | solution.py:188
  118.8 22.9 %collective-permute-start.15 = (bf16[10,128,128]{2,1,0:T(8,128)(2,1)S(1)}, bf16[10,128,128]{2,1,0:T(8,128)(2,1)S(1)}, u32[]{:S(2)}, u32[]{:S(2)}) collective-permute-start(bf16[10,128,128]{2,1,0:T(8,128)(2,1)S(1)} %get-tuple-element.32), channel_id=1, source_target_pairs={{0,3},{1,0},{2,1},{3,2},{4,7},{5,4},{6,5},{7,6},{8,11},{9,8},{10,9... | collective-permute-start | bytes 983048 | tf_op jit(solution)/shard_map/ppermute | solution.py:188
  122.3 19.8 %collective-permute-start.16 = (bf16[10,128,128]{2,1,0:T(8,128)(2,1)S(1)}, bf16[10,128,128]{2,1,0:T(8,128)(2,1)S(1)}, u32[]{:S(2)}, u32[]{:S(2)}) collective-permute-start(bf16[10,128,128]{2,1,0:T(8,128)(2,1)S(1)} %get-tuple-element.33), channel_id=1, source_target_pairs={{0,1},{1,2},{2,3},{3,0},{4,5},{5,6},{6,7},{7,4},{8,9},{9,10},{10,1... | collective-permute-start | bytes 983048 | tf_op jit(solution)/shard_map/ppermute | solution.py:188
  142.8 1.1 copy-start.2
